TPU v7x, 32 devices: a whole 2x2x4 slice. The times are simulated.
32 devices in a mesh: slab: 8 (over z, y), yz: 4 (over x, core).
Axes of the slice: x: 2, y: 2, z: 4, core: 2. Of those that a mesh axis runs over, the one named last changes fastest.
Arguments:
- field_e: float32 [3, 32, 32, 128], P(None, 'slab', 'yz'), may hold values from -6 to 6
- field_h: float32 [3, 32, 32, 128], P(None, 'slab', 'yz'), may hold values from -6 to 6
- permittivity: float32 [3, 32, 32, 128], P(None, 'slab', 'yz'), may hold values from 1 to 12
- conductivity: float32 [32, 32, 128], P('slab', 'yz'), may hold values from 0.02 to 1
- forward_e: float32 [8, 4, 2, 3, 64], P('slab', 'yz'), may hold values from -6 to 6
- slot_cell: int32 [8, 4, 8, 8], P('slab', 'yz'), may hold values from 0 to 4096, as said below
- recv_param: int32 [8, 4, 8, 8], P('slab', 'yz'), may hold values from 0 to 128, as said below
Outputs:
- new_e: float32 [3, 32, 32, 128], P(None, 'slab', 'yz')
- new_h: float32 [3, 32, 32, 128], P(None, 'slab', 'yz')
- gradient: float32 [8, 4, 128], P('slab', 'yz')
Inputs may be any that keep to these rules, and one draw needn't show every extreme that they name: Slot c from device (s, y) to owner d of the same yz index is filled when slot_cell[s, y, d, c] < 4096, which holds exactly when recv_param[d, y, s, c] < 128; filled slots of a pair come first. In every draw one owner receives 8 filled slots from every source and some pair has no filled slot. `recv_param`: see slot_cell.
All inputs are finite; a program needn't handle non-finite values.
Results may differ from a plain program's by a relative error of at most 0.0001.
Values sent between devices are 32-bit elements; how exact they have to be, the bound alone decides.
No kernel may reach another device: no remote copies, remote signals or barrier semaphores. Data moves between devices by JAX's collectives and lax.ppermute only.
A program may use at most 64 MiB of HBM per device.

v0:
```python
import jax
import jax.numpy as jnp
from jax import lax
from jax.sharding import PartitionSpec as P

STEPS = 2
PAR_DEV = 128


CH_GAIN = 0.5
CE_GAIN = 0.5


def from_behind(array, axis, by):
    count = lax.axis_size(axis)
    pairs = [(i, i + by) for i in range(count) if 0 <= i + by < count]
    return lax.ppermute(array, axis, pairs)


def diff_ahead(values, edges, along):
    extent = values.shape[along]
    return jnp.concatenate([lax.slice_in_dim(values, 1, extent, axis=along), edges], along) - values


def diff_behind(values, edges, along):
    extent = values.shape[along]
    return values - jnp.concatenate(
        [edges, lax.slice_in_dim(values, 0, extent - 1, axis=along)], along
    )


def curl_ahead(field, x_edges, y_edges):
    z_zeros = jnp.zeros_like(field[0][:, :, 0:1])
    curl_x = diff_ahead(field[2], y_edges[1], 1) - diff_ahead(field[1], z_zeros, 2)
    curl_y = diff_ahead(field[0], z_zeros, 2) - diff_ahead(field[2], x_edges[1], 0)
    curl_z = diff_ahead(field[1], x_edges[0], 0) - diff_ahead(field[0], y_edges[0], 1)
    return jnp.stack([curl_x, curl_y, curl_z])


def curl_behind(field, x_edges, y_edges):
    z_zeros = jnp.zeros_like(field[0][:, :, 0:1])
    curl_x = diff_behind(field[2], y_edges[1], 1) - diff_behind(field[1], z_zeros, 2)
    curl_y = diff_behind(field[0], z_zeros, 2) - diff_behind(field[2], x_edges[1], 0)
    curl_z = diff_behind(field[1], x_edges[0], 0) - diff_behind(field[0], y_edges[0], 1)
    return jnp.stack([curl_x, curl_y, curl_z])


def shards(field_e, field_h, permittivity, conductivity, forward_e, slot_cell, recv_param):
    depth_x = field_e.shape[1]
    depth_y = field_e.shape[2]
    sources = recv_param.shape[2]
    capacity = recv_param.shape[3]
    ratio = 0.5 * conductivity[None] / permittivity
    keep_rate = (1.0 - ratio) / (1.0 + ratio)
    curl_gain = CE_GAIN / (permittivity * (1.0 + ratio))
    cell_index = slot_cell.reshape(-1)
    segments = recv_param.reshape(-1)
    gradient = jnp.zeros((PAR_DEV + 1,), jnp.float32)
    for step_index in range(STEPS):
        x_edges = from_behind(field_e[1:3, 0:1], "slab", -1)
        y_edges = from_behind(field_e[0:3:2, :, 0:1], "yz", -1)
        field_h = field_h - CH_GAIN * curl_ahead(field_e, x_edges, y_edges)
        x_edges = from_behind(field_h[1:3, depth_x - 1 : depth_x], "slab", 1)
        y_edges = from_behind(field_h[0:3:2, :, depth_y - 1 : depth_y], "yz", 1)
        field_e = keep_rate * field_e + curl_gain * curl_behind(field_h, x_edges, y_edges)
        flattened = jnp.concatenate([field_e.reshape(3, -1), jnp.zeros((3, 1), jnp.float32)], 1)
        picked = jnp.take(flattened, cell_index, axis=1)
        products = jnp.sum(picked * forward_e[0, 0, step_index], axis=0)
        received = lax.all_to_all(
            products.reshape(sources, capacity), "slab", split_axis=0, concat_axis=0, tiled=True
        )
        gradient = gradient + jax.ops.segment_sum(
            received.reshape(-1), segments, num_segments=PAR_DEV + 1
        )
    return (field_e, field_h, gradient[:PAR_DEV].reshape(1, 1, PAR_DEV))


def solution(mesh):
    return jax.shard_map(
        shards,
        mesh=mesh,
        in_specs=(
            P(None, "slab", "yz", None),
            P(None, "slab", "yz", None),
            P(None, "slab", "yz", None),
            P("slab", "yz", None),
            P("slab", "yz", None, None, None),
            P("slab", "yz", None, None),
            P("slab", "yz", None, None),
        ),
        out_specs=(P(None, "slab", "yz", None), P(None, "slab", "yz", None), P("slab", "yz", None)),
        check_vma=False,
    )
```

profile of v0, /device:TPU:2, one launch (start us, length us, event | category | flops | bytes accessed | tf_op | source)
XLA Modules:
  0.0 70.6 jit_solution(17802159824943974842)
XLA Ops:
  0.6 0.7 slice.235
  1.3 1.3 %collective-permute-start.1 = (f32[2,1,8,128]{3,2,1,0:T(8,128)S(1)}, f32[2,1,8,128]{3,2,1,0:T(8,128)S(1)}, u32[]{:S(2)}, u32[]{:S(2)}) collective-permute-start(f32[2,1,8,128]{3,2,1,0:T(8,128)S(1)} %slice.235), channel_id=1, source_target_pairs={{4,0},{8,4},{12,8},{16,12},{20,16},{24,20},{28,24},{5,1},{9,5},{13... | collective-permute-start | bytes 24584 | tf_op jit(solution)/shard_map/ppermute | solution.py:17
  2.6 0.8 %slice.227 = f32[2,4,1,128]{3,2,1,0:T(1,128)S(1)} slice(f32[3,4,8,128]{3,2,1,0:T(8,128)} %param.9), slice={[0:3:2], [0:4:1], [0:1:1], [0:128:1]} | slice | bytes 8192 | tf_op jit(solution)/shard_map/slice | solution.py:61
  3.4 1.9 %collective-permute-start = (f32[2,4,1,128]{3,2,1,0:T(1,128)S(1)}, f32[2,4,1,128]{3,2,1,0:T(1,128)S(1)}, u32[]{:S(2)}, u32[]{:S(2)}) collective-permute-start(f32[2,4,1,128]{3,2,1,0:T(1,128)S(1)} %slice.227), channel_id=1, source_target_pairs={{1,0},{2,1},{3,2},{5,4},{6,5},{7,6},{9,8},{10,9},{11,10},{13,12},{... | collective-permute-start | bytes 12296 | tf_op jit(solution)/shard_map/ppermute | solution.py:17
  5.3 0.7 %slice_bitcast_fusion.14 = f32[4,8,128]{2,1,0:T(8,128)S(1)} fusion(f32[3,4,8,128]{3,2,1,0:T(8,128)} %param.9), kind=kLoop, calls=%fused_computation.67 | loop fusion | bytes 32768 | tf_op jit(solution)/shard_map/squeeze | solution.py:35
  6.0 0.7 %slice_bitcast_fusion.19 = (f32[3,8,128]{2,1,0:T(8,128)S(1)}, f32[1,3,8,128]{3,2,1,0:T(8,128)S(1)}) fusion(f32[3,4,8,128]{3,2,1,0:T(8,128)} %param.9), kind=kLoop, calls=%fused_computation.72 | loop fusion | bytes 49152 | tf_op jit(solution)/shard_map/slice | solution.py:22
  6.8 0.8 %reshape.78 = s32[64]{0:T(128)S(1)} reshape(s32[1,1,8,8]{3,2,1,0:T(8,128)} %param.14) | data formatting | bytes 512 | tf_op jit(solution)/shard_map/reshape | solution.py:56
  7.5 0.7 %broadcast_multiply_fusion = f32[4,8,128]{2,1,0:T(8,128)S(1)} fusion(f32[4,8,128]{2,1,0:T(8,128)} %param.12), kind=kLoop, calls=%fused_computation.73 | loop fusion | flops 4096 | bytes 32768 | tf_op jit(solution)/shard_map/mul | solution.py:53
  8.3 0.8 %fusion.31 = (f32[1,1,1,3,64]{4,2,3,1,0:T(1,128)S(1)}, f32[1,1,1,3,64]{4,2,3,1,0:T(1,128)S(1)}) fusion(f32[1,1,2,3,64]{4,2,3,1,0:T(2,128)} %param.13), kind=kLoop, calls=%fused_computation.90 | loop fusion | bytes 3072 | tf_op jit(solution)/shard_map/slice | solution.py:68
  9.3 0.8 %slice_bitcast_fusion.15 = (f32[4,8,128]{2,1,0:T(8,128)S(1)}, f32[1,4,8,128]{3,2,1,0:T(8,128)S(1)}, f32[4,8,128]{2,1,0:T(8,128)S(1)}) fusion(f32[3,4,8,128]{3,2,1,0:T(8,128)} %param.9, f32[1,4,1,128]{3,2,1,0:T(1,128)S(1)} %get-tuple-element.49, f32[1,4,7,128]{3,2,1,0:T(8,128)S(1)} %slice_bitcast_fusion.6, f32[1,1,8,128]{3,2,1,0:T(8,128)S(1)} %get-tuple-element.41, ...), kind=kLoop, calls=%fused_computation.68 | loop fusion | flops 20480 | bytes 131072 | tf_op jit(solution)/shard_map/squeeze | solution.py:34
  10.2 0.8 %fusion.7 = (f32[1,4,8,128]{3,2,1,0:T(8,128)S(1)}, f32[1,4,8,128]{3,2,1,0:T(8,128)S(1)}) fusion(f32[4,1,128]{2,1,0:T(1,128)S(1)} %get-tuple-element.48, f32[4,7,128]{2,1,0:T(8,128)S(1)} %slice.296, f32[4,8,127]{2,1,0:T(8,128)S(1)} %slice.298, f32[3,4,8,128]{3,2,1,0:T(8,128)} %param.9, f32[1,8,128]{2,1,0:T(8,128)S(1)} %get-tuple-element.40, ...), kind=kLoop, calls=%fused_computation.26 | loop fusion | flops 32768 | bytes 147200 | tf_op jit(solution)/shard_map/stack | solution.py:37
  11.0 0.8 %fusion = f32[3,4,8,128]{3,2,1,0:T(8,128)S(1)} fusion(f32[3,4,8,128]{3,2,1,0:T(8,128)} %param.10, f32[1,4,8,128]{3,2,1,0:T(8,128)S(1)} %get-tuple-element.30, f32[1,4,8,128]{3,2,1,0:T(8,128)S(1)} %get-tuple-element.28, f32[1,4,8,128]{3,2,1,0:T(8,128)S(1)} %get-tuple-element.27), kind=kLoop, calls=%fused_computation.4 | loop fusion | flops 49152 | bytes 147456 | tf_op jit(solution)/shard_map/sub | solution.py:62
  11.8 4.5 %collective-permute-start.3 = (f32[2,1,8,128]{3,2,1,0:T(8,128)S(1)}, f32[2,1,8,128]{3,2,1,0:T(8,128)S(1)}, u32[]{:S(2)}, u32[]{:S(2)}) collective-permute-start(f32[2,1,8,128]{3,2,1,0:T(8,128)S(1)} %slice.311), channel_id=1, source_target_pairs={{0,4},{4,8},{8,12},{12,16},{16,20},{20,24},{24,28},{1,5},{5,9},{9,... | collective-permute-start | bytes 24584 | tf_op jit(solution)/shard_map/ppermute | solution.py:17
  16.4 2.1 %collective-permute-start.2 = (f32[2,4,1,128]{3,1,2,0:T(4,128)S(1)}, f32[2,4,1,128]{3,1,2,0:T(4,128)S(1)}, u32[]{:S(2)}, u32[]{:S(2)}) collective-permute-start(f32[2,4,1,128]{3,1,2,0:T(4,128)S(1)} %bitcast.154), channel_id=1, source_target_pairs={{0,1},{1,2},{2,3},{4,5},{5,6},{6,7},{8,9},{9,10},{10,11},{12,13},{... | collective-permute-start | bytes 12296 | tf_op jit(solution)/shard_map/ppermute | solution.py:17
  18.5 2.8 %collective-permute-done.2 = f32[2,4,1,128]{3,1,2,0:T(4,128)S(1)} collective-permute-done((f32[2,4,1,128]{3,1,2,0:T(4,128)S(1)}, f32[2,4,1,128]{3,1,2,0:T(4,128)S(1)}, u32[]{:S(2)}, u32[]{:S(2)}) %collective-permute-start.2) | collective-permute-done | bytes 4128 | tf_op jit(solution)/shard_map/ppermute | solution.py:17
  21.4 0.9 %fusion.1 = f32[3,4,8,128]{3,2,1,0:T(8,128)S(1)} fusion(f32[1,4,8,128]{3,2,1,0:T(8,128)S(1)} %get-tuple-element.23, f32[1,4,8,128]{3,2,1,0:T(8,128)S(1)} %get-tuple-element.21, f32[1,4,8,128]{3,2,1,0:T(8,128)S(1)} %get-tuple-element.20, f32[3,4,8,128]{3,2,1,0:T(8,128)} %param.9, f32[3,4,8,128]{3,2,1,0:T(8,128)} %param.11, ...), kind=kLoop, calls=%fused_computation.6 | loop fusion | flops 135168 | bytes 212992 | tf_op jit(solution)/shard_map/add | solution.py:65
  22.3 1.9 %collective-permute-start.4 = (f32[2,4,1,128]{3,1,2,0:T(4,128)S(1)}, f32[2,4,1,128]{3,1,2,0:T(4,128)S(1)}, u32[]{:S(2)}, u32[]{:S(2)}) collective-permute-start(f32[2,4,1,128]{3,1,2,0:T(4,128)S(1)} %bitcast.153), channel_id=1, source_target_pairs={{1,0},{2,1},{3,2},{5,4},{6,5},{7,6},{9,8},{10,9},{11,10},{13,12},{... | collective-permute-start | bytes 12296 | tf_op jit(solution)/shard_map/ppermute | solution.py:17
  25.0 1.3 %collective-permute-start.5 = (f32[2,1,8,128]{3,2,1,0:T(8,128)S(1)}, f32[2,1,8,128]{3,2,1,0:T(8,128)S(1)}, u32[]{:S(2)}, u32[]{:S(2)}) collective-permute-start(f32[2,1,8,128]{3,2,1,0:T(8,128)S(1)} %slice.326), channel_id=1, source_target_pairs={{4,0},{8,4},{12,8},{16,12},{20,16},{24,20},{28,24},{5,1},{9,5},{13... | collective-permute-start | bytes 24584 | tf_op jit(solution)/shard_map/ppermute | solution.py:17
  26.3 1.5 %concatenate.129 = f32[3,4097]{0,1:T(8,128)} pad(f32[3,4096]{0,1:T(8,128)S(1)} %bitcast.139, f32[]{:T(128)} %constant.0.clone.1), padding=0_0x0_1 | pad | bytes 98320 | tf_op jit(solution)/shard_map/concatenate | solution.py:66
  27.8 2.2 %gather_fusion = f32[64,3]{1,0:T(8,128)S(1)} fusion(f32[3,4097]{0,1:T(8,128)} %concatenate.129, s32[1024]{0:T(1024)S(1)} %pad_clamp_fusion), kind=kCustom, calls=%fused_computation.clone | custom fusion | bytes 1792 | tf_op jit(solution)/shard_map/jit(_take)/gather | solution.py:67
  30.0 0.9 %collective-permute-done.5 = f32[2,1,8,128]{3,2,1,0:T(8,128)S(1)} collective-permute-done((f32[2,1,8,128]{3,2,1,0:T(8,128)S(1)}, f32[2,1,8,128]{3,2,1,0:T(8,128)S(1)}, u32[]{:S(2)}, u32[]{:S(2)}) %collective-permute-start.5) | collective-permute-done | bytes 8224 | tf_op jit(solution)/shard_map/ppermute | solution.py:17
  31.1 4.8 %collective-permute-start.7 = (f32[2,1,8,128]{3,2,1,0:T(8,128)S(1)}, f32[2,1,8,128]{3,2,1,0:T(8,128)S(1)}, u32[]{:S(2)}, u32[]{:S(2)}) collective-permute-start(f32[2,1,8,128]{3,2,1,0:T(8,128)S(1)} %slice.339), channel_id=1, source_target_pairs={{0,4},{4,8},{8,12},{12,16},{16,20},{20,24},{24,28},{1,5},{5,9},{9,... | collective-permute-start | bytes 24584 | tf_op jit(solution)/shard_map/ppermute | solution.py:17
  36.0 1.9 %collective-permute-start.6 = (f32[2,4,1,128]{3,1,2,0:T(4,128)S(1)}, f32[2,4,1,128]{3,1,2,0:T(4,128)S(1)}, u32[]{:S(2)}, u32[]{:S(2)}) collective-permute-start(f32[2,4,1,128]{3,1,2,0:T(4,128)S(1)} %bitcast.155), channel_id=1, source_target_pairs={{0,1},{1,2},{2,3},{4,5},{5,6},{6,7},{8,9},{9,10},{10,11},{12,13},{... | collective-permute-start | bytes 12296 | tf_op jit(solution)/shard_map/ppermute | solution.py:17
  37.9 3.0 %collective-permute-done.6 = f32[2,4,1,128]{3,1,2,0:T(4,128)S(1)} collective-permute-done((f32[2,4,1,128]{3,1,2,0:T(4,128)S(1)}, f32[2,4,1,128]{3,1,2,0:T(4,128)S(1)}, u32[]{:S(2)}, u32[]{:S(2)}) %collective-permute-start.6) | collective-permute-done | bytes 4128 | tf_op jit(solution)/shard_map/ppermute | solution.py:17
  41.7 1.5 %concatenate.130 = f32[3,4097]{0,1:T(8,128)} pad(f32[3,4096]{0,1:T(8,128)S(1)} %bitcast.140, f32[]{:T(128)} %constant.0.clone.1), padding=0_0x0_1 | pad | bytes 98320 | tf_op jit(solution)/shard_map/concatenate | solution.py:66
  43.2 2.2 %gather_fusion.1 = f32[64,3]{1,0:T(8,128)S(1)} fusion(f32[3,4097]{0,1:T(8,128)} %concatenate.130, s32[1024]{0:T(1024)S(1)} %pad_clamp_fusion), kind=kCustom, calls=%fused_computation.1.clone | custom fusion | bytes 1792 | tf_op jit(solution)/shard_map/jit(_take)/gather | solution.py:67
  45.5 0.7 all_to_all.12
  46.2 5.4 %all-to-all-start = ((f32[8,1,8]{2,1,0:T(1,128)}), f32[8,1,8]{2,1,0:T(1,128)S(1)}, u32[]{:S(2)}, u32[]{:S(2)}) async-start(f32[8,1,8]{2,1,0:T(1,128)} %bitcast.44), calls=%async_computation | async-start | bytes 8192 | tf_op jit(solution)/shard_map/all_to_all | solution.py:69
  52.4 5.7 %all-to-all-done = f32[8,1,8]{2,1,0:T(1,128)S(1)} async-done(((f32[8,1,8]{2,1,0:T(1,128)}), f32[8,1,8]{2,1,0:T(1,128)S(1)}, u32[]{:S(2)}, u32[]{:S(2)}) %all-to-all-start) | async-done | bytes 288 | tf_op jit(solution)/shard_map/all_to_all | solution.py:69
  58.1 3.3 %all-to-all-start.1 = ((f32[8,1,8]{2,1,0:T(1,128)}), f32[8,1,8]{2,1,0:T(1,128)S(1)}, u32[]{:S(2)}, u32[]{:S(2)}) async-start(f32[8,1,8]{2,1,0:T(1,128)} %bitcast.48), calls=%async_computation.1 | async-start | bytes 8192 | tf_op jit(solution)/shard_map/all_to_all | solution.py:69
  62.7 5.1 %all-to-all-done.1 = f32[8,1,8]{2,1,0:T(1,128)S(1)} async-done(((f32[8,1,8]{2,1,0:T(1,128)}), f32[8,1,8]{2,1,0:T(1,128)S(1)}, u32[]{:S(2)}, u32[]{:S(2)}) %all-to-all-start.1) | async-done | bytes 288 | tf_op jit(solution)/shard_map/all_to_all | solution.py:69
  68.6 1.4 %scatter_custom_fusion = f32[129]{0:T(256)S(1)} fusion(s32[128]{0:T(128)S(1)} %add_bitcast_fusion, f32[128]{0:T(128)S(1)} %pad_maximum_fusion, f32[]{:T(128)} %constant.0.clone.1), kind=kCustom, calls=%fused_computation.85 | custom fusion | flops 128 | bytes 520 | tf_op jit(solution)/shard_map/add | solution.py:72
  (71 shorter events, 5.8 us)
Async XLA Ops:
  1.3 8.0 %collective-permute-start.1 = (f32[2,1,8,128]{3,2,1,0:T(8,128)S(1)}, f32[2,1,8,128]{3,2,1,0:T(8,128)S(1)}, u32[]{:S(2)}, u32[]{:S(2)}) collective-permute-start(f32[2,1,8,128]{3,2,1,0:T(8,128)S(1)} %slice.235), channel_id=1, source_target_pairs={{4,0},{8,4},{12,8},{16,12},{20,16},{24,20},{28,24},{5,1},{9,5},{13... | collective-permute-start | bytes 24584 | tf_op jit(solution)/shard_map/ppermute | solution.py:17
  3.4 5.9 %collective-permute-start = (f32[2,4,1,128]{3,2,1,0:T(1,128)S(1)}, f32[2,4,1,128]{3,2,1,0:T(1,128)S(1)}, u32[]{:S(2)}, u32[]{:S(2)}) collective-permute-start(f32[2,4,1,128]{3,2,1,0:T(1,128)S(1)} %slice.227), channel_id=1, source_target_pairs={{1,0},{2,1},{3,2},{5,4},{6,5},{7,6},{9,8},{10,9},{11,10},{13,12},{... | collective-permute-start | bytes 12296 | tf_op jit(solution)/shard_map/ppermute | solution.py:17
  11.8 9.5 %collective-permute-start.3 = (f32[2,1,8,128]{3,2,1,0:T(8,128)S(1)}, f32[2,1,8,128]{3,2,1,0:T(8,128)S(1)}, u32[]{:S(2)}, u32[]{:S(2)}) collective-permute-start(f32[2,1,8,128]{3,2,1,0:T(8,128)S(1)} %slice.311), channel_id=1, source_target_pairs={{0,4},{4,8},{8,12},{12,16},{16,20},{20,24},{24,28},{1,5},{5,9},{9,... | collective-permute-start | bytes 24584 | tf_op jit(solution)/shard_map/ppermute | solution.py:17
  16.4 4.9 %collective-permute-start.2 = (f32[2,4,1,128]{3,1,2,0:T(4,128)S(1)}, f32[2,4,1,128]{3,1,2,0:T(4,128)S(1)}, u32[]{:S(2)}, u32[]{:S(2)}) collective-permute-start(f32[2,4,1,128]{3,1,2,0:T(4,128)S(1)} %bitcast.154), channel_id=1, source_target_pairs={{0,1},{1,2},{2,3},{4,5},{5,6},{6,7},{8,9},{9,10},{10,11},{12,13},{... | collective-permute-start | bytes 12296 | tf_op jit(solution)/shard_map/ppermute | solution.py:17
  22.3 7.7 %collective-permute-start.4 = (f32[2,4,1,128]{3,1,2,0:T(4,128)S(1)}, f32[2,4,1,128]{3,1,2,0:T(4,128)S(1)}, u32[]{:S(2)}, u32[]{:S(2)}) collective-permute-start(f32[2,4,1,128]{3,1,2,0:T(4,128)S(1)} %bitcast.153), channel_id=1, source_target_pairs={{1,0},{2,1},{3,2},{5,4},{6,5},{7,6},{9,8},{10,9},{11,10},{13,12},{... | collective-permute-start | bytes 12296 | tf_op jit(solution)/shard_map/ppermute | solution.py:17
  25.0 6.0 %collective-permute-start.5 = (f32[2,1,8,128]{3,2,1,0:T(8,128)S(1)}, f32[2,1,8,128]{3,2,1,0:T(8,128)S(1)}, u32[]{:S(2)}, u32[]{:S(2)}) collective-permute-start(f32[2,1,8,128]{3,2,1,0:T(8,128)S(1)} %slice.326), channel_id=1, source_target_pairs={{4,0},{8,4},{12,8},{16,12},{20,16},{24,20},{28,24},{5,1},{9,5},{13... | collective-permute-start | bytes 24584 | tf_op jit(solution)/shard_map/ppermute | solution.py:17
  26.3 4.8 %copy-start.1 = (f32[3,4,8,128]{3,2,1,0:T(8,128)S(1)}, f32[3,4,8,128]{3,2,1,0:T(8,128)}, u32[]{:S(2)}) copy-start(f32[3,4,8,128]{3,2,1,0:T(8,128)} %param.10) | copy-start | bytes 147460
  26.3 14.7 %copy-start.2 = (f32[3,4,8,128]{3,2,1,0:T(8,128)S(1)}, f32[3,4,8,128]{3,2,1,0:T(8,128)}, u32[]{:S(2)}) copy-start(f32[3,4,8,128]{3,2,1,0:T(8,128)} %param.11) | copy-start | bytes 147460
  31.1 12.1 %copy-start = (f32[3,4,8,128]{3,2,1,0:T(8,128)}, f32[3,4,8,128]{3,2,1,0:T(8,128)S(1)}, u32[]{:S(2)}) copy-start(f32[3,4,8,128]{3,2,1,0:T(8,128)S(1)} %fusion.2) | copy-start | bytes 147460
  31.1 9.8 %collective-permute-start.7 = (f32[2,1,8,128]{3,2,1,0:T(8,128)S(1)}, f32[2,1,8,128]{3,2,1,0:T(8,128)S(1)}, u32[]{:S(2)}, u32[]{:S(2)}) collective-permute-start(f32[2,1,8,128]{3,2,1,0:T(8,128)S(1)} %slice.339), channel_id=1, source_target_pairs={{0,4},{4,8},{8,12},{12,16},{16,20},{20,24},{24,28},{1,5},{5,9},{9,... | collective-permute-start | bytes 24584 | tf_op jit(solution)/shard_map/ppermute | solution.py:17
  36.0 4.9 %collective-permute-start.6 = (f32[2,4,1,128]{3,1,2,0:T(4,128)S(1)}, f32[2,4,1,128]{3,1,2,0:T(4,128)S(1)}, u32[]{:S(2)}, u32[]{:S(2)}) collective-permute-start(f32[2,4,1,128]{3,1,2,0:T(4,128)S(1)} %bitcast.155), channel_id=1, source_target_pairs={{0,1},{1,2},{2,3},{4,5},{5,6},{6,7},{8,9},{9,10},{10,11},{12,13},{... | collective-permute-start | bytes 12296 | tf_op jit(solution)/shard_map/ppermute | solution.py:17
  41.0 2.1 %copy-start.3 = (f32[3,4,8,128]{3,2,1,0:T(8,128)}, f32[3,4,8,128]{3,2,1,0:T(8,128)S(1)}, u32[]{:S(2)}) copy-start(f32[3,4,8,128]{3,2,1,0:T(8,128)S(1)} %fusion.3) | copy-start | bytes 147460
  41.7 10.0 %copy-start.4 = (s32[1,1,8,8]{3,2,1,0:T(8,128)S(1)}, s32[1,1,8,8]{3,2,1,0:T(8,128)}, u32[]{:S(2)}) copy-start(s32[1,1,8,8]{3,2,1,0:T(8,128)} %param.15) | copy-start | bytes 772
  46.2 11.9 %all-to-all-start = ((f32[8,1,8]{2,1,0:T(1,128)}), f32[8,1,8]{2,1,0:T(1,128)S(1)}, u32[]{:S(2)}, u32[]{:S(2)}) async-start(f32[8,1,8]{2,1,0:T(1,128)} %bitcast.44), calls=%async_computation | async-start | bytes 8192 | tf_op jit(solution)/shard_map/all_to_all | solution.py:69
  58.1 9.7 %all-to-all-start.1 = ((f32[8,1,8]{2,1,0:T(1,128)}), f32[8,1,8]{2,1,0:T(1,128)S(1)}, u32[]{:S(2)}, u32[]{:S(2)}) async-start(f32[8,1,8]{2,1,0:T(1,128)} %bitcast.48), calls=%async_computation.1 | async-start | bytes 8192 | tf_op jit(solution)/shard_map/all_to_all | solution.py:69
where the time goes:
time: 71.8 us; the launch traced here: 70.6 us
  starting transfers between devices  28.5 us (40%)
  waiting for transfers between devices  17.5 us (24%)
  local copies, waits for them, and re-layouts  16.3 us (23%)
  other arithmetic  7.3 us (10%)
  between operations  1.01 us (1%)
    ppermute x8, starting transfers between devices, from_behind(): return lax.ppermute(array, axis, pairs)  19.8 us
    all_to_all x2, waiting for transfers between devices, shards(): lax.all_to_all(products.reshape(sources, capacity), 'slab', split_axis=0,...  10.8 us
    all_to_all x2, starting transfers between devices, shards(): lax.all_to_all(products.reshape(sources, capacity), 'slab', split_axis=0,...  8.7 us
    ppermute x8, waiting for transfers between devices, from_behind(): return lax.ppermute(array, axis, pairs)  6.73 us
    gather x2, local copies, waits for them, and re-layouts, shards(): picked = jnp.take(flattened, cell_index, axis=1)  4.38 us
    concatenate x2, local copies, waits for them, and re-layouts, shards(): jnp.concatenate([field_e.reshape(3, -1), jnp.zeros((3, 1), jnp.float32)], 1)  2.96 us
    all_to_all x3, local copies, waits for them, and re-layouts, shards(): lax.all_to_all(products.reshape(sources, capacity), 'slab', split_axis=0,...  1.87 us
  transfers between devices with their start and end apart: 10, of which 5 were waited for; matrix products, arithmetic and copies ran while one was open for 15% of the time, Pallas kernels for 0%

commit v1 on v0

v1 whole, which is shorter than its diff:
```python
import jax
import jax.numpy as jnp
from jax import lax
from jax.sharding import PartitionSpec as P

STEPS = 2
PAR_DEV = 128
HALO = 2

CH_GAIN = 0.5
CE_GAIN = 0.5


def recv_from(array, axis, offset):
    count = lax.axis_size(axis)
    pairs = [(i + offset, i) for i in range(count) if 0 <= i + offset < count]
    return lax.ppermute(array, axis, pairs)


def diff_ahead(values, along):
    extent = values.shape[along]
    edge = jnp.zeros_like(lax.slice_in_dim(values, 0, 1, axis=along))
    return jnp.concatenate([lax.slice_in_dim(values, 1, extent, axis=along), edge], along) - values


def diff_behind(values, along):
    extent = values.shape[along]
    edge = jnp.zeros_like(lax.slice_in_dim(values, 0, 1, axis=along))
    return values - jnp.concatenate([edge, lax.slice_in_dim(values, 0, extent - 1, axis=along)], along)


def curl_ahead(field):
    curl_x = diff_ahead(field[2], 1) - diff_ahead(field[1], 2)
    curl_y = diff_ahead(field[0], 2) - diff_ahead(field[2], 0)
    curl_z = diff_ahead(field[1], 0) - diff_ahead(field[0], 1)
    return jnp.stack([curl_x, curl_y, curl_z])


def curl_behind(field):
    curl_x = diff_behind(field[2], 1) - diff_behind(field[1], 2)
    curl_y = diff_behind(field[0], 2) - diff_behind(field[2], 0)
    curl_z = diff_behind(field[1], 0) - diff_behind(field[0], 1)
    return jnp.stack([curl_x, curl_y, curl_z])


def with_halo(stack, depth_x, depth_y):
    low = recv_from(stack[:, depth_x - HALO : depth_x], "slab", -1)
    high = recv_from(stack[:, 0:HALO], "slab", 1)
    stack = jnp.concatenate([low, stack, high], 1)
    low = recv_from(stack[:, :, depth_y - HALO : depth_y], "yz", -1)
    high = recv_from(stack[:, :, 0:HALO], "yz", 1)
    return jnp.concatenate([low, stack, high], 2)


def shards(field_e, field_h, permittivity, conductivity, forward_e, slot_cell, recv_param):
    depth_x = field_e.shape[1]
    depth_y = field_e.shape[2]
    sources = recv_param.shape[2]
    capacity = recv_param.shape[3]
    n_x = lax.axis_size("slab") * depth_x
    n_y = lax.axis_size("yz") * depth_y
    stack = jnp.concatenate([field_e, field_h, permittivity, conductivity[None]], 0)
    stack = with_halo(stack, depth_x, depth_y)
    field_e, field_h = stack[0:3], stack[3:6]
    gx = lax.axis_index("slab") * depth_x - HALO + lax.broadcasted_iota(jnp.int32, (1, depth_x + 2 * HALO, 1, 1), 1)
    gy = lax.axis_index("yz") * depth_y - HALO + lax.broadcasted_iota(jnp.int32, (1, 1, depth_y + 2 * HALO, 1), 2)
    inside = (gx >= 0) & (gx < n_x) & (gy >= 0) & (gy < n_y)
    permittivity = jnp.where(inside, stack[6:9], 1.0)
    conductivity = stack[9:10]
    ratio = 0.5 * conductivity / permittivity
    keep_rate = (1.0 - ratio) / (1.0 + ratio)
    curl_gain = CE_GAIN / (permittivity * (1.0 + ratio))
    local = (slice(None), slice(HALO, HALO + depth_x), slice(HALO, HALO + depth_y))
    picked_steps = []
    for step_index in range(STEPS):
        field_h = jnp.where(inside, field_h - CH_GAIN * curl_ahead(field_e), 0.0)
        field_e = jnp.where(inside, keep_rate * field_e + curl_gain * curl_behind(field_h), 0.0)
        picked_steps.append(field_e[local].reshape(3, -1))
    flattened = jnp.stack(picked_steps)
    flattened = jnp.concatenate([flattened, jnp.zeros((STEPS, 3, 1), jnp.float32)], 2)
    picked = jnp.take(flattened, slot_cell.reshape(-1), axis=2)
    products = jnp.sum(picked * forward_e[0, 0], axis=1)
    products = products.reshape(STEPS, sources, capacity).transpose(1, 0, 2)
    received = lax.all_to_all(products, "slab", split_axis=0, concat_axis=0, tiled=True)
    segments = jnp.broadcast_to(recv_param.reshape(sources, 1, capacity), (sources, STEPS, capacity))
    gradient = jax.ops.segment_sum(received.reshape(-1), segments.reshape(-1), num_segments=PAR_DEV + 1)
    return (field_e[local], field_h[local], gradient[:PAR_DEV].reshape(1, 1, PAR_DEV))


def solution(mesh):
    return jax.shard_map(
        shards,
        mesh=mesh,
        in_specs=(
            P(None, "slab", "yz", None),
            P(None, "slab", "yz", None),
            P(None, "slab", "yz", None),
            P("slab", "yz", None),
            P("slab", "yz", None, None, None),
            P("slab", "yz", None, None),
            P("slab", "yz", None, None),
        ),
        out_specs=(P(None, "slab", "yz", None), P(None, "slab", "yz", None), P("slab", "yz", None)),
        check_vma=False,
    )
```

time: 71.8 us -> 51.9 us (0.72)
  starting transfers between devices: 28.5 us -> 17.2 us
  waiting for transfers between devices: 17.5 us -> 9.1 us
  other arithmetic: 7.3 us -> 13.7 us
  local copies, waits for them, and re-layouts: 16.3 us -> 10.4 us
    ppermute x8 -> x4, starting transfers between devices: 19.8 us -> 10.2 us  [recv_from(): return lax.ppermute(array, axis, pairs)]
    another operation x1, other arithmetic: 0.08 us -> 8.24 us  [shards(): flattened = jnp.stack(picked_steps)]
    all_to_all x2 -> x1, waiting for transfers between devices: 10.8 us -> 5.77 us  [shards(): lax.all_to_all(products, 'slab', split_axis=0, concat_axis=0, tiled=True)]
    ppermute x8 -> x4, waiting for transfers between devices: 6.73 us -> 3.33 us  [recv_from(): return lax.ppermute(array, axis, pairs)]
    concatenate x6 -> x0, local copies, waits for them, and re-layouts: 2.97 us -> none  [the longest x2 2.96 us: shards(): jnp.concatenate([field_e.reshape(3, -1), jnp.zeros((3, 1), jnp.float32)], 1)]
    another operation x1 -> x3, local copies, waits for them, and re-layouts: 0.08 us -> 2.73 us  [the longest x2 2.64 us: shards(): flattened = jnp.stack(picked_steps)]
    add x3 -> x0, other arithmetic: 2.31 us -> none  [the longest x1 1.43 us: shards(): gradient + jax.ops.segment_sum(received.reshape(-1), segments, num_segmen...]
    all_to_all x3 -> x0, local copies, waits for them, and re-layouts: 1.87 us -> none  [shards(): lax.all_to_all(products.reshape(sources, capacity), 'slab', split_axis=0,...]
  transfers between devices with their start and end apart: 10 -> 5, of which waited for: 5 -> 2; matrix products, arithmetic and copies ran while one was open for 15% -> 6% of each run, Pallas kernels for 0% -> 0%
where the time goes in v1:
time: 51.9 us; the launch traced here: 51.2 us
  starting transfers between devices  17.2 us (33%)
  other arithmetic  13.7 us (26%)
  local copies, waits for them, and re-layouts  10.4 us (20%)
  waiting for transfers between devices  9.1 us (18%)
  between operations  0.91 us (2%)
    ppermute x4, starting transfers between devices, recv_from(): return lax.ppermute(array, axis, pairs)  10.2 us
    another operation x1, other arithmetic, shards(): flattened = jnp.stack(picked_steps)  8.24 us
    all_to_all x1, starting transfers between devices, shards(): lax.all_to_all(products, 'slab', split_axis=0, concat_axis=0, tiled=True)  7.02 us
    all_to_all x1, waiting for transfers between devices, shards(): lax.all_to_all(products, 'slab', split_axis=0, concat_axis=0, tiled=True)  5.77 us
    ppermute x4, waiting for transfers between devices, recv_from(): return lax.ppermute(array, axis, pairs)  3.33 us
    gather x1, local copies, waits for them, and re-layouts, shards(): picked = jnp.take(flattened, slot_cell.reshape(-1), axis=2)  2.83 us
    another operation x2, local copies, waits for them, and re-layouts, shards(): flattened = jnp.stack(picked_steps)  2.64 us
    reshape x2, local copies, waits for them, and re-layouts, shards(): picked = jnp.take(flattened, slot_cell.reshape(-1), axis=2)  1.53 us
  transfers between devices with their start and end apart: 5, of which 2 were waited for; matrix products, arithmetic and copies ran while one was open for 6% of the time, Pallas kernels for 0%

profile of v1, /device:TPU:2, one launch (start us, length us, event | category | flops | bytes accessed | tf_op | source)
XLA Modules:
  0.0 51.2 jit_solution(9626943895551162265)
XLA Ops:
  0.6 0.9 %pad_maximum_fusion.1 = f32[10,4,8,128]{3,2,1,0:T(8,128)S(1)} fusion(f32[1,4,8,128]{3,2,1,0:T(8,128)} %bitcast.154, f32[3,4,8,128]{3,2,1,0:T(8,128)} %param.9, f32[3,4,8,128]{3,2,1,0:T(8,128)} %param.8, f32[3,4,8,128]{3,2,1,0:T(8,128)} %param.7), kind=kLoop, calls=%fused_computation.17 | loop fusion | flops 122880 | bytes 327680 | tf_op jit(solution)/shard_map/concatenate | solution.py:62
  1.5 1.3 %collective-permute-start.1 = (f32[10,2,8,128]{3,2,1,0:T(8,128)S(1)}, f32[10,2,8,128]{3,2,1,0:T(8,128)S(1)}, u32[]{:S(2)}, u32[]{:S(2)}) collective-permute-start(f32[10,2,8,128]{3,2,1,0:T(8,128)S(1)} %get-tuple-element.44), channel_id=1, source_target_pairs={{4,0},{8,4},{12,8},{16,12},{20,16},{24,20},{28,24},{5,1},{9,5},{13... | collective-permute-start | bytes 245768 | tf_op jit(solution)/shard_map/ppermute | solution.py:17
  2.8 4.6 %collective-permute-start = (f32[10,2,8,128]{3,2,1,0:T(8,128)S(1)}, f32[10,2,8,128]{3,2,1,0:T(8,128)S(1)}, u32[]{:S(2)}, u32[]{:S(2)}) collective-permute-start(f32[10,2,8,128]{3,2,1,0:T(8,128)S(1)} %get-tuple-element.43), channel_id=1, source_target_pairs={{0,4},{4,8},{8,12},{12,16},{16,20},{20,24},{24,28},{1,5},{5,9},{9,... | collective-permute-start | bytes 245768 | tf_op jit(solution)/shard_map/ppermute | solution.py:17
  7.4 0.8 %reshape.141 = s32[64,1]{0,1:T(1,128)S(1)} reshape(s32[1,1,8,8]{3,2,1,0:T(8,128)} %param.12) | data formatting | bytes 512 | tf_op jit(solution)/shard_map/reshape | solution.py:81
  8.2 0.8 %reshape.140 = s32[64]{0:T(128)S(1)} reshape(s32[1,1,8,8]{3,2,1,0:T(8,128)} %param.12) | data formatting | bytes 512 | tf_op jit(solution)/shard_map/reshape | solution.py:81
  9.1 0.8 %copy.23 = f32[1,1,2,3,64]{3,2,4,1,0:T(2,128)S(1)} copy(f32[1,1,2,3,64]{4,2,3,1,0:T(2,128)} %param.11) | data formatting | bytes 3072 | tf_op args[4]
  9.9 1.0 %pad_maximum_fusion.7 = (f32[10,8,2,128]{3,2,1,0:T(2,128)S(1)}, f32[10,8,2,128]{3,2,1,0:T(2,128)S(1)}) fusion(f32[10,2,8,128]{3,2,1,0:T(8,128)S(1)} %collective-permute-done.1, f32[10,2,8,128]{3,2,1,0:T(8,128)S(1)} %collective-permute-done, f32[1,4,8,128]{3,2,1,0:T(8,128)} %bitcast.155, f32[3,4,8,128]{3,2,1,0:T(8,128)} %param.9, f32[3,4,8,128]{3,2,1,0:T(8,128)} %param.8, ...), kind=kLoop, calls=%fused_computation.23 | loop fusion | flops 204800 | bytes 491520 | tf_op jit(solution)/shard_map/slice | solution.py:50
  11.0 1.9 %collective-permute-start.3 = (f32[10,8,2,128]{3,2,1,0:T(2,128)S(1)}, f32[10,8,2,128]{3,2,1,0:T(2,128)S(1)}, u32[]{:S(2)}, u32[]{:S(2)}) collective-permute-start(f32[10,8,2,128]{3,2,1,0:T(2,128)S(1)} %get-tuple-element.16), channel_id=1, source_target_pairs={{1,0},{2,1},{3,2},{5,4},{6,5},{7,6},{9,8},{10,9},{11,10},{13,12},{... | collective-permute-start | bytes 245768 | tf_op jit(solution)/shard_map/ppermute | solution.py:17
  12.9 2.4 %collective-permute-start.2 = (f32[10,8,2,128]{3,2,1,0:T(2,128)S(1)}, f32[10,8,2,128]{3,2,1,0:T(2,128)S(1)}, u32[]{:S(2)}, u32[]{:S(2)}) collective-permute-start(f32[10,8,2,128]{3,2,1,0:T(2,128)S(1)} %get-tuple-element.15), channel_id=1, source_target_pairs={{0,1},{1,2},{2,3},{4,5},{5,6},{6,7},{8,9},{9,10},{10,11},{12,13},{... | collective-permute-start | bytes 245768 | tf_op jit(solution)/shard_map/ppermute | solution.py:17
  15.3 3.3 %collective-permute-done.2 = f32[10,8,2,128]{3,2,1,0:T(2,128)S(1)} collective-permute-done((f32[10,8,2,128]{3,2,1,0:T(2,128)S(1)}, f32[10,8,2,128]{3,2,1,0:T(2,128)S(1)}, u32[]{:S(2)}, u32[]{:S(2)}) %collective-permute-start.2) | collective-permute-done | bytes 81952 | tf_op jit(solution)/shard_map/ppermute | solution.py:17
  18.6 1.0 %pad_maximum_fusion = f32[10,8,12,128]{3,2,1,0:T(8,128)S(1)} fusion(f32[10,8,2,128]{3,2,1,0:T(2,128)S(1)} %collective-permute-done.3, f32[10,2,8,128]{3,2,1,0:T(8,128)S(1)} %collective-permute-done.1, f32[1,4,8,128]{3,2,1,0:T(8,128)} %bitcast.156, f32[3,4,8,128]{3,2,1,0:T(8,128)} %param.9, f32[3,4,8,128]{3,2,1,0:T(8,128)} %param.8, ...), kind=kLoop, calls=%fused_computation.3 | loop fusion | flops 860160 | bytes 983040 | tf_op jit(solution)/shard_map/concatenate | solution.py:52
  19.7 0.1 slice.261
  19.9 0.1 fusion
  20.1 0.1 subtract_bitcast_fusion.8
  20.2 0.2 fusion.2
  20.5 0.1 slice.277
  20.6 0.1 fusion.4
  20.8 0.1 subtract_bitcast_fusion.2
  20.9 0.1 fusion.14
  21.0 0.6 %copy.27 = f32[3,4,8,128]{0,3,2,1:T(8,128)S(1)} copy(f32[3,4,8,128]{3,2,1,0:T(8,128)S(1)} %get-tuple-element.18) | data formatting | bytes 98304 | tf_op jit(solution)/shard_map/stack;reshape | solution.py:79
  21.6 2.0 %copy.26 = f32[3,4,8,128]{0,3,2,1:T(8,128)} copy(f32[3,4,8,128]{3,2,1,0:T(8,128)S(1)} %get-tuple-element.17) | data formatting | bytes 98304 | tf_op jit(solution)/shard_map/stack;reshape | solution.py:79
  23.6 8.2 %select_maximum_fusion = f32[2,3,4097]{1,0,2:T(2,128)} fusion(f32[1,3,4096]{1,0,2:T(1,128)S(1)} %bitcast.144, f32[1,3,4096]{1,0,2:T(1,128)} %bitcast.145), kind=kLoop, calls=%fused_computation.2 | loop fusion | flops 98328 | bytes 196632 | tf_op jit(solution)/shard_map/stack | solution.py:79
  31.9 2.8 %gather_fusion = f32[64,2,3]{2,1,0:T(2,128)S(1)} fusion(f32[2,3,4097]{1,0,2:T(2,128)} %select_maximum_fusion, s32[1024]{0:T(1024)S(1)} %pad_clamp_fusion), kind=kCustom, calls=%fused_computation | custom fusion | bytes 3328 | tf_op jit(solution)/shard_map/jit(_take)/gather | solution.py:81
  34.7 0.2 fusion.6
  35.0 0.7 %copy.25 = f32[8,2,8]{2,1,0:T(2,128)} copy(f32[8,2,8]{1,2,0:T(8,128)S(1)} %bitcast.157) | data formatting | bytes 1024 | tf_op jit(solution)/shard_map/transpose | solution.py:83
  35.7 7.0 %all-to-all-start = ((f32[8,2,8]{2,1,0:T(2,128)}), f32[8,2,8]{2,1,0:T(2,128)S(1)}, u32[]{:S(2)}, u32[]{:S(2)}) async-start(f32[8,2,8]{2,1,0:T(2,128)} %copy.25), calls=%async_computation | async-start | bytes 16384 | tf_op jit(solution)/shard_map/all_to_all | solution.py:84
  42.7 0.1 reshape.155
  42.8 0.6 %slice.296 = f32[3,4,8,128]{3,2,1,0:T(8,128)} slice(f32[3,8,12,128]{3,2,1,0:T(8,128)S(1)} %fusion.4), slice={[0:3], [2:6], [2:10], [0:128]} | slice | bytes 98304 | tf_op jit(solution)/shard_map/slice | solution.py:87
  43.4 5.8 %all-to-all-done = f32[8,2,8]{2,1,0:T(2,128)S(1)} async-done(((f32[8,2,8]{2,1,0:T(2,128)}), f32[8,2,8]{2,1,0:T(2,128)S(1)}, u32[]{:S(2)}, u32[]{:S(2)}) %all-to-all-start) | async-done | bytes 544 | tf_op jit(solution)/shard_map/all_to_all | solution.py:84
  49.2 0.1 reshape.157
  49.3 1.4 %scatter_custom_fusion = f32[129]{0:T(256)S(1)} fusion(s32[128]{0:T(128)S(1)} %reshape.155, f32[128]{0:T(128)S(1)} %reshape.157, f32[]{:T(128)} %constant.24.clone.1), kind=kCustom, calls=%fused_computation.74 | custom fusion | flops 128 | bytes 520 | tf_op jit(solution)/shard_map/scatter-add | solution.py:86
  50.7 0.5 %slice_bitcast_fusion.20 = f32[1,1,128]{2,1,0:T(1,128)} fusion(f32[129]{0:T(256)S(1)} %scatter_custom_fusion), kind=kLoop, calls=%fused_computation.73 | loop fusion | bytes 1024 | tf_op jit(solution)/shard_map/reshape | solution.py:87
  (32 shorter events, 0.6 us)
Async XLA Ops:
  1.5 8.4 %collective-permute-start.1 = (f32[10,2,8,128]{3,2,1,0:T(8,128)S(1)}, f32[10,2,8,128]{3,2,1,0:T(8,128)S(1)}, u32[]{:S(2)}, u32[]{:S(2)}) collective-permute-start(f32[10,2,8,128]{3,2,1,0:T(8,128)S(1)} %get-tuple-element.44), channel_id=1, source_target_pairs={{4,0},{8,4},{12,8},{16,12},{20,16},{24,20},{28,24},{5,1},{9,5},{13... | collective-permute-start | bytes 245768 | tf_op jit(solution)/shard_map/ppermute | solution.py:17
  2.8 7.1 %collective-permute-start = (f32[10,2,8,128]{3,2,1,0:T(8,128)S(1)}, f32[10,2,8,128]{3,2,1,0:T(8,128)S(1)}, u32[]{:S(2)}, u32[]{:S(2)}) collective-permute-start(f32[10,2,8,128]{3,2,1,0:T(8,128)S(1)} %get-tuple-element.43), channel_id=1, source_target_pairs={{0,4},{4,8},{8,12},{12,16},{16,20},{20,24},{24,28},{1,5},{5,9},{9,... | collective-permute-start | bytes 245768 | tf_op jit(solution)/shard_map/ppermute | solution.py:17
  11.0 4.4 %collective-permute-start.3 = (f32[10,8,2,128]{3,2,1,0:T(2,128)S(1)}, f32[10,8,2,128]{3,2,1,0:T(2,128)S(1)}, u32[]{:S(2)}, u32[]{:S(2)}) collective-permute-start(f32[10,8,2,128]{3,2,1,0:T(2,128)S(1)} %get-tuple-element.16), channel_id=1, source_target_pairs={{1,0},{2,1},{3,2},{5,4},{6,5},{7,6},{9,8},{10,9},{11,10},{13,12},{... | collective-permute-start | bytes 245768 | tf_op jit(solution)/shard_map/ppermute | solution.py:17
  12.9 5.8 %collective-permute-start.2 = (f32[10,8,2,128]{3,2,1,0:T(2,128)S(1)}, f32[10,8,2,128]{3,2,1,0:T(2,128)S(1)}, u32[]{:S(2)}, u32[]{:S(2)}) collective-permute-start(f32[10,8,2,128]{3,2,1,0:T(2,128)S(1)} %get-tuple-element.15), channel_id=1, source_target_pairs={{0,1},{1,2},{2,3},{4,5},{5,6},{6,7},{8,9},{9,10},{10,11},{12,13},{... | collective-permute-start | bytes 245768 | tf_op jit(solution)/shard_map/ppermute | solution.py:17
  21.0 10.9 %copy-start = (f32[3,4,8,128]{3,2,1,0:T(8,128)}, f32[3,4,8,128]{3,2,1,0:T(8,128)S(1)}, u32[]{:S(2)}) copy-start(f32[3,4,8,128]{3,2,1,0:T(8,128)S(1)} %get-tuple-element.18) | copy-start | bytes 147460
  23.6 19.0 %copy-start.1 = (s32[1,1,8,8]{3,2,1,0:T(8,128)S(1)}, s32[1,1,8,8]{3,2,1,0:T(8,128)}, u32[]{:S(2)}) copy-start(s32[1,1,8,8]{3,2,1,0:T(8,128)} %param.13) | copy-start | bytes 772
  35.7 13.5 %all-to-all-start = ((f32[8,2,8]{2,1,0:T(2,128)}), f32[8,2,8]{2,1,0:T(2,128)S(1)}, u32[]{:S(2)}, u32[]{:S(2)}) async-start(f32[8,2,8]{2,1,0:T(2,128)} %copy.25), calls=%async_computation | async-start | bytes 16384 | tf_op jit(solution)/shard_map/all_to_all | solution.py:84

commit v2 on v1

v2 whole, which is shorter than its diff:
```python
import functools

import jax
import jax.numpy as jnp
from jax import lax
from jax.experimental import pallas as pl
from jax.experimental.pallas import tpu as pltpu
from jax.sharding import PartitionSpec as P

STEPS = 2
PAR_DEV = 128
HALO = 2
LANES = 128

CH_GAIN = 0.5
CE_GAIN = 0.5


def recv_from(array, axis, offset):
    count = lax.axis_size(axis)
    pairs = [(i + offset, i) for i in range(count) if 0 <= i + offset < count]
    return lax.ppermute(array, axis, pairs)


def ahead(values, axis):
    extent = values.shape[axis]
    if axis == 0:
        return jnp.concatenate([values[1:], values[:1]], 0)
    shifted = pltpu.roll(values, extent - 1, axis)
    if axis == 2:
        lane = lax.broadcasted_iota(jnp.int32, values.shape, 2)
        shifted = jnp.where(lane == extent - 1, 0.0, shifted)
    return shifted


def behind(values, axis):
    extent = values.shape[axis]
    if axis == 0:
        return jnp.concatenate([values[extent - 1 :], values[: extent - 1]], 0)
    shifted = pltpu.roll(values, 1, axis)
    if axis == 2:
        lane = lax.broadcasted_iota(jnp.int32, values.shape, 2)
        shifted = jnp.where(lane == 0, 0.0, shifted)
    return shifted


def leapfrog_kernel(
    dims, offsets, e_ref, h_ref, perm_ref, cond_ref, xlo_ref, xhi_ref, ylo_ref, yhi_ref,
    cell_ref, fwd_ref, e_out, h_out, prod_out, ring,
):
    depth_x, depth_y, n_x, n_y = dims
    ring_x, ring_y = ring.shape[1], ring.shape[2]
    ring[0:3, 0:depth_x, 0:depth_y] = e_ref[...]
    ring[3:6, 0:depth_x, 0:depth_y] = h_ref[...]
    ring[6:9, 0:depth_x, 0:depth_y] = perm_ref[...]
    ring[9:10, 0:depth_x, 0:depth_y] = cond_ref[...]
    ring[:, depth_x : depth_x + HALO, 0:depth_y] = xhi_ref[...]
    ring[:, ring_x - HALO : ring_x, 0:depth_y] = xlo_ref[...]
    ring[:, :, depth_y : depth_y + HALO] = yhi_ref[...]
    ring[:, :, depth_y + HALO : ring_y - HALO] = jnp.zeros(
        (ring.shape[0], ring_x, ring_y - depth_y - 2 * HALO, LANES), jnp.float32
    )
    ring[:, :, ring_y - HALO : ring_y] = ylo_ref[...]

    shape = (ring_x, ring_y, LANES)
    xi = lax.broadcasted_iota(jnp.int32, shape, 0)
    yi = lax.broadcasted_iota(jnp.int32, shape, 1)
    gx = offsets[0] + jnp.where(xi < depth_x + HALO, xi, xi - ring_x)
    gy = offsets[1] + jnp.where(yi < depth_y + HALO, yi, yi - ring_y)
    y_real = (yi < depth_y + HALO) | (yi >= ring_y - HALO)
    inside = (gx >= 0) & (gx < n_x) & (gy >= 0) & (gy < n_y) & y_real

    field_e = [ring[c] for c in range(3)]
    field_h = [ring[3 + c] for c in range(3)]
    conductivity = ring[9]
    keep_rate, curl_gain = [], []
    for c in range(3):
        permittivity = jnp.where(inside, ring[6 + c], 1.0)
        ratio = 0.5 * conductivity / permittivity
        keep_rate.append((1.0 - ratio) / (1.0 + ratio))
        curl_gain.append(CE_GAIN / (permittivity * (1.0 + ratio)))

    cells = cell_ref[...]
    rows = depth_x * depth_y
    lane_pick = (lax.broadcasted_iota(jnp.int32, (LANES, cells.shape[1]), 0) == (cells % LANES)).astype(jnp.float32)
    row_pick = lax.broadcasted_iota(jnp.int32, (rows, cells.shape[1]), 0) == (cells // LANES)

    for step_index in range(STEPS):
        e0, e1, e2 = field_e
        curl = (
            (ahead(e2, 1) - e2) - (ahead(e1, 2) - e1),
            (ahead(e0, 2) - e0) - (ahead(e2, 0) - e2),
            (ahead(e1, 0) - e1) - (ahead(e0, 1) - e0),
        )
        field_h = [jnp.where(inside, field_h[c] - CH_GAIN * curl[c], 0.0) for c in range(3)]
        h0, h1, h2 = field_h
        curl = (
            (h2 - behind(h2, 1)) - (h1 - behind(h1, 2)),
            (h0 - behind(h0, 2)) - (h2 - behind(h2, 0)),
            (h1 - behind(h1, 0)) - (h0 - behind(h0, 1)),
        )
        field_e = [
            jnp.where(inside, keep_rate[c] * field_e[c] + curl_gain[c] * curl[c], 0.0) for c in range(3)
        ]
        product = None
        for c in range(3):
            block = field_e[c][0:depth_x, 0:depth_y].reshape(rows, LANES)
            by_lane = jnp.dot(block, lane_pick, precision=lax.Precision.HIGHEST, preferred_element_type=jnp.float32)
            picked = jnp.sum(jnp.where(row_pick, by_lane, 0.0), axis=0, keepdims=True)
            term = picked * fwd_ref[step_index, c : c + 1, :]
            product = term if product is None else product + term
        prod_out[step_index : step_index + 1, :] = product

    for c in range(3):
        e_out[c] = field_e[c][0:depth_x, 0:depth_y]
        h_out[c] = field_h[c][0:depth_x, 0:depth_y]


def leapfrog(offsets, field_e, field_h, permittivity, conductivity, xlo, xhi, ylo, yhi, cells, fwd, n_x, n_y):
    _, depth_x, depth_y, _ = field_e.shape
    ring_x = depth_x + 2 * HALO
    ring_y = -(-(depth_y + 2 * HALO) // 8) * 8
    vmem = pl.BlockSpec(memory_space=pltpu.VMEM)
    smem = pl.BlockSpec(memory_space=pltpu.SMEM)
    kernel = functools.partial(leapfrog_kernel, (depth_x, depth_y, n_x, n_y))
    return pl.pallas_call(
        kernel,
        out_shape=(
            jax.ShapeDtypeStruct(field_e.shape, jnp.float32),
            jax.ShapeDtypeStruct(field_h.shape, jnp.float32),
            jax.ShapeDtypeStruct((STEPS, cells.shape[1]), jnp.float32),
        ),
        in_specs=[smem] + [vmem] * 10,
        out_specs=(vmem, vmem, vmem),
        scratch_shapes=[pltpu.VMEM((10, ring_x, ring_y, LANES), jnp.float32)],
    )(offsets, field_e, field_h, permittivity, conductivity, xlo, xhi, ylo, yhi, cells, fwd)


def shards(field_e, field_h, permittivity, conductivity, forward_e, slot_cell, recv_param):
    depth_x = field_e.shape[1]
    depth_y = field_e.shape[2]
    sources = recv_param.shape[2]
    capacity = recv_param.shape[3]
    n_x = lax.axis_size("slab") * depth_x
    n_y = lax.axis_size("yz") * depth_y
    parts = (field_e, field_h, permittivity, conductivity[None])
    xlo = recv_from(jnp.concatenate([p[:, depth_x - HALO :] for p in parts], 0), "slab", -1)
    xhi = recv_from(jnp.concatenate([p[:, :HALO] for p in parts], 0), "slab", 1)
    def rows(start):
        center = jnp.concatenate([p[:, :, start : start + HALO] for p in parts], 0)
        return jnp.concatenate([center, xhi[:, :, start : start + HALO], xlo[:, :, start : start + HALO]], 1)

    ylo = recv_from(rows(depth_y - HALO), "yz", -1)
    yhi = recv_from(rows(0), "yz", 1)
    offsets = jnp.stack([lax.axis_index("slab") * depth_x, lax.axis_index("yz") * depth_y]).astype(jnp.int32)
    new_e, new_h, products = leapfrog(
        offsets, field_e, field_h, permittivity, conductivity[None], xlo, xhi, ylo, yhi,
        slot_cell.reshape(1, -1), forward_e[0, 0], n_x, n_y,
    )
    products = products.reshape(STEPS, sources, capacity)
    received = lax.all_to_all(products, "slab", split_axis=1, concat_axis=1, tiled=True)
    segments = jnp.broadcast_to(recv_param.reshape(1, sources, capacity), (STEPS, sources, capacity))
    gradient = jax.ops.segment_sum(received.reshape(-1), segments.reshape(-1), num_segments=PAR_DEV + 1)
    return (new_e, new_h, gradient[:PAR_DEV].reshape(1, 1, PAR_DEV))


def solution(mesh):
    return jax.shard_map(
        shards,
        mesh=mesh,
        in_specs=(
            P(None, "slab", "yz", None),
            P(None, "slab", "yz", None),
            P(None, "slab", "yz", None),
            P("slab", "yz", None),
            P("slab", "yz", None, None, None),
            P("slab", "yz", None, None),
            P("slab", "yz", None, None),
        ),
        out_specs=(P(None, "slab", "yz", None), P(None, "slab", "yz", None), P("slab", "yz", None)),
        check_vma=False,
    )
```

time: 51.9 us -> 39.5 us (0.76)
  other arithmetic: 13.7 us -> 2.08 us
  local copies, waits for them, and re-layouts: 10.4 us -> 7.5 us
  Pallas kernels: 0 us -> 2.32 us
    another operation x5 -> x1, other arithmetic: 8.56 us -> 0.56 us  [shards(): jnp.stack([lax.axis_index('slab') * depth_x, lax.axis_index('yz') * depth...]
    unnamed x5 -> x25, local copies, waits for them, and re-layouts: 0.8 us -> 3.92 us
    gather x1 -> x0, local copies, waits for them, and re-layouts: 2.83 us -> none  [shards(): picked = jnp.take(flattened, slot_cell.reshape(-1), axis=2)]
    another operation x2 -> x0, local copies, waits for them, and re-layouts: 2.64 us -> none  [shards(): flattened = jnp.stack(picked_steps)]
    pallas_call x0 -> x1, Pallas kernels: none -> 2.32 us  [leapfrog(): pl.pallas_call(kernel, out_shape=(jax.ShapeDtypeStruct(field_e.shape, jnp...]
    concatenate x2 -> x4, other arithmetic: 1.86 us -> 0.1 us  [the longest x2 0.08 us: rows(): jnp.concatenate([center, xhi[:, :, start:start + HALO], xlo[:, :, start:s...]
    slice x2 -> x0, other arithmetic: 1.09 us -> none  [the longest x1 1.01 us: with_halo(): low = recv_from(stack[:, :, depth_y - HALO:depth_y], 'yz', -1)]
    transpose x1 -> x0, local copies, waits for them, and re-layouts: 0.71 us -> none  [shards(): products = products.reshape(STEPS, sources, capacity).transpose(1, 0, 2)]
  transfers between devices with their start and end apart: 5 -> 5, of which waited for: 2 -> 2; matrix products, arithmetic and copies ran while one was open for 6% -> 5% of each run, Pallas kernels for 0% -> 0%
where the time goes in v2:
time: 39.5 us; the launch traced here: 39 us
  starting transfers between devices  17.1 us (43%)
  waiting for transfers between devices  9.2 us (23%)
  local copies, waits for them, and re-layouts  7.5 us (19%)
  Pallas kernels  2.32 us (6%)
  other arithmetic  2.08 us (5%)
  between operations  0.8 us (2%)
    ppermute x4, starting transfers between devices, recv_from(): return lax.ppermute(array, axis, pairs)  10.3 us
    all_to_all x1, starting transfers between devices, shards(): lax.all_to_all(products, 'slab', split_axis=1, concat_axis=1, tiled=True)  6.8 us
    all_to_all x1, waiting for transfers between devices, shards(): lax.all_to_all(products, 'slab', split_axis=1, concat_axis=1, tiled=True)  6.41 us
    unnamed x25, local copies, waits for them, and re-layouts  3.92 us
    ppermute x4, waiting for transfers between devices, recv_from(): return lax.ppermute(array, axis, pairs)  2.79 us
    pallas_call x1, Pallas kernels, leapfrog(): pl.pallas_call(kernel, out_shape=(jax.ShapeDtypeStruct(field_e.shape, jnp...  2.32 us
    slice x3, local copies, waits for them, and re-layouts, shards(): xhi = recv_from(jnp.concatenate([p[:, :HALO] for p in parts], 0), 'slab', 1)  1.49 us
    scatter-add x1, other arithmetic, shards(): jax.ops.segment_sum(received.reshape(-1), segments.reshape(-1), num_segme...  1.43 us
  transfers between devices with their start and end apart: 5, of which 2 were waited for; matrix products, arithmetic and copies ran while one was open for 5% of the time, Pallas kernels for 0%

profile of v2, /device:TPU:2, one launch (start us, length us, event | category | flops | bytes accessed | tf_op | source)
XLA Modules:
  0.0 39.0 jit_solution(5674853202967746843)
XLA Ops:
  0.6 0.7 %fusion.11 = (f32[1,2,8,128]{3,2,1,0:T(8,128)S(1)}, f32[1,2,8,128]{3,2,1,0:T(8,128)S(1)}) fusion(f32[1,4,8,128]{3,2,1,0:T(8,128)} %bitcast.11), kind=kLoop, calls=%fused_computation.19 | loop fusion | bytes 32768 | tf_op jit(solution)/shard_map/slice | solution.py:148
  1.4 0.8 %fusion.9 = (f32[3,2,8,128]{3,2,1,0:T(8,128)S(1)}, f32[3,2,8,128]{3,2,1,0:T(8,128)S(1)}) fusion(f32[3,4,8,128]{3,2,1,0:T(8,128)} %perm_ref.1), kind=kLoop, calls=%fused_computation.17 | loop fusion | bytes 98304 | tf_op jit(solution)/shard_map/slice | solution.py:148
  2.1 0.1 copy-done.1
  2.2 0.0 copy-done.2
  2.2 1.3 %collective-permute-start.1 = (f32[10,2,8,128]{3,2,1,0:T(8,128)S(1)}, f32[10,2,8,128]{3,2,1,0:T(8,128)S(1)}, u32[]{:S(2)}, u32[]{:S(2)}) collective-permute-start(f32[10,2,8,128]{3,2,1,0:T(8,128)S(1)} %pad_maximum_fusion.1), channel_id=1, source_target_pairs={{4,0},{8,4},{12,8},{16,12},{20,16},{24,20},{28,24},{5,1},{9,5},{13... | collective-permute-start | bytes 245768 | tf_op jit(solution)/shard_map/ppermute | solution.py:22
  3.5 0.0 copy-start
  3.5 4.7 %collective-permute-start = (f32[10,2,8,128]{3,2,1,0:T(8,128)S(1)}, f32[10,2,8,128]{3,2,1,0:T(8,128)S(1)}, u32[]{:S(2)}, u32[]{:S(2)}) collective-permute-start(f32[10,2,8,128]{3,2,1,0:T(8,128)S(1)} %pad_maximum_fusion), channel_id=1, source_target_pairs={{0,4},{4,8},{8,12},{12,16},{16,20},{20,24},{24,28},{1,5},{5,9},{9,... | collective-permute-start | bytes 245768 | tf_op jit(solution)/shard_map/ppermute | solution.py:22
  8.3 0.0 copy-start.5
  8.3 0.7 %copy-done.5 = f32[4,8,128]{2,1,0:T(8,128)S(1)} copy-done((f32[4,8,128]{2,1,0:T(8,128)S(1)}, f32[4,8,128]{2,1,0:T(8,128)}, u32[]{:S(2)}) %copy-start.5) | copy-done | bytes 16408
  9.0 0.7 %copy-done.10 = f32[1,1,2,3,64]{4,2,3,1,0:T(2,128)S(1)} copy-done((f32[1,1,2,3,64]{4,2,3,1,0:T(2,128)S(1)}, f32[1,1,2,3,64]{4,2,3,1,0:T(2,128)}, u32[]{:S(2)}) %copy-start.10) | copy-done | bytes 1560
  9.7 0.6 %copy.15 = f32[1,1,2,3,64]{4,3,2,1,0:T(4,128)} copy(f32[1,1,2,3,64]{4,2,3,1,0:T(2,128)S(1)} %copy-done.10) | data formatting | bytes 3072 | tf_op args[4]
  10.3 0.7 %reshape.20.cell_ref = s32[1,64]{1,0:T(1,128)} reshape(s32[1,1,8,8]{3,2,1,0:T(8,128)S(1)} %copy-done.9) | data formatting | bytes 512 | tf_op jit(solution)/shard_map/reshape | solution.py:158
  10.9 0.0 collective-permute-done.1.xhi_ref
  11.0 0.0 collective-permute-done.xlo_ref
  11.0 0.6 %copy-done.3 = f32[10,2,8,128]{3,2,1,0:T(8,128)} copy-done((f32[10,2,8,128]{3,2,1,0:T(8,128)}, f32[10,2,8,128]{3,2,1,0:T(8,128)S(1)}, u32[]{:S(2)}) %copy-start.3) | copy-done | bytes 81944
  11.6 1.9 %collective-permute-start.3 = (f32[10,8,2,128]{3,2,1,0:T(2,128)S(1)}, f32[10,8,2,128]{3,2,1,0:T(2,128)S(1)}, u32[]{:S(2)}, u32[]{:S(2)}) collective-permute-start(f32[10,8,2,128]{3,2,1,0:T(2,128)S(1)} %pad_maximum_fusion.3), channel_id=1, source_target_pairs={{1,0},{2,1},{3,2},{5,4},{6,5},{7,6},{9,8},{10,9},{11,10},{13,12},{... | collective-permute-start | bytes 245768 | tf_op jit(solution)/shard_map/ppermute | solution.py:22
  13.6 2.4 %collective-permute-start.2 = (f32[10,8,2,128]{3,2,1,0:T(2,128)S(1)}, f32[10,8,2,128]{3,2,1,0:T(2,128)S(1)}, u32[]{:S(2)}, u32[]{:S(2)}) collective-permute-start(f32[10,8,2,128]{3,2,1,0:T(2,128)S(1)} %pad_maximum_fusion.2), channel_id=1, source_target_pairs={{0,1},{1,2},{2,3},{4,5},{5,6},{6,7},{8,9},{9,10},{10,11},{12,13},{... | collective-permute-start | bytes 245768 | tf_op jit(solution)/shard_map/ppermute | solution.py:22
  16.0 0.6 %pad_add_fusion.offsets = s32[2]{0:T(128)} fusion(s32[1]{0:T(128)} %bitcast.1, s32[1]{0:T(128)} %bitcast), kind=kLoop, calls=%fused_computation.6 | loop fusion | flops 2 | bytes 16 | tf_op jit(solution)/shard_map/stack | solution.py:155
  16.6 0.0 collective-permute-done.3.yhi_ref
  16.6 2.8 %collective-permute-done.2.ylo_ref = f32[10,8,2,128]{3,2,1,0:T(2,128)S(1)} collective-permute-done((f32[10,8,2,128]{3,2,1,0:T(2,128)S(1)}, f32[10,8,2,128]{3,2,1,0:T(2,128)S(1)}, u32[]{:S(2)}, u32[]{:S(2)}) %collective-permute-start.2) | collective-permute-done | bytes 81952 | tf_op jit(solution)/shard_map/ppermute | solution.py:22
  19.4 0.0 copy-done.6
  19.4 0.6 %copy-done.7 = f32[10,8,2,128]{3,2,1,0:T(2,128)} copy-done((f32[10,8,2,128]{3,2,1,0:T(2,128)}, f32[10,8,2,128]{3,2,1,0:T(2,128)S(1)}, u32[]{:S(2)}) %copy-start.7) | copy-done | bytes 81944
  20.0 2.3 %shard_map.94 = (f32[3,4,8,128]{3,2,1,0:T(8,128)}, f32[3,4,8,128]{3,2,1,0:T(8,128)}, f32[2,64]{1,0:T(2,128)}) custom-call(s32[2]{0:T(128)} %pad_add_fusion.offsets, f32[3,4,8,128]{3,2,1,0:T(8,128)} %e_ref.1, f32[3,4,8,128]{3,2,1,0:T(8,128)} %h_ref.1, f32[3,4,8,128]{3,2,1,0:T(8,128)} %perm_ref.1, f32[1,4,8,128]{3,2,1,0:T(8,128)} %bitcast.12, ...), custom_call_target="tpu_custom_call" | custom-call | tf_op jit(solution)/shard_map/pallas_call | solution.py:126
  22.3 0.7 %copy-done.11 = f32[2,64]{1,0:T(2,128)S(1)} copy-done((f32[2,64]{1,0:T(2,128)S(1)}, f32[2,64]{1,0:T(2,128)}, u32[]{:S(2)}) %copy-start.11) | copy-done | bytes 536
  23.0 0.1 reshape.21
  23.0 0.6 %copy.12 = f32[2,8,8]{2,0,1:T(2,128)} copy(f32[2,8,8]{2,1,0:T(8,128)S(1)} %reshape.21) | data formatting | bytes 1024 | tf_op jit(solution)/shard_map/reshape | solution.py:160
  23.6 6.8 %all-to-all-start = ((f32[2,8,8]{2,0,1:T(2,128)}), f32[2,8,8]{2,0,1:T(2,128)S(1)}, u32[]{:S(2)}, u32[]{:S(2)}) async-start(f32[2,8,8]{2,0,1:T(2,128)} %copy.12), calls=%async_computation | async-start | bytes 16384 | tf_op jit(solution)/shard_map/all_to_all | solution.py:161
  30.5 0.1 reshape.26
  30.6 6.4 %all-to-all-done = f32[2,8,8]{2,0,1:T(2,128)S(1)} async-done(((f32[2,8,8]{2,0,1:T(2,128)}), f32[2,8,8]{2,0,1:T(2,128)S(1)}, u32[]{:S(2)}, u32[]{:S(2)}) %all-to-all-start) | async-done | bytes 544 | tf_op jit(solution)/shard_map/all_to_all | solution.py:161
  37.0 0.1 reshape.28
  37.1 1.4 %scatter_custom_fusion = f32[129]{0:T(256)S(1)} fusion(s32[128]{0:T(128)S(1)} %reshape.26, f32[128]{0:T(128)S(1)} %reshape.28, f32[]{:T(128)} %constant.14.clone.1), kind=kCustom, calls=%fused_computation.8 | custom fusion | flops 128 | bytes 520 | tf_op jit(solution)/shard_map/scatter-add | solution.py:163
  38.5 0.5 %slice_bitcast_fusion = f32[1,1,128]{2,1,0:T(1,128)} fusion(f32[129]{0:T(256)S(1)} %scatter_custom_fusion), kind=kLoop, calls=%fused_computation.7 | loop fusion | bytes 1024 | tf_op jit(solution)/shard_map/reshape | solution.py:164
  (26 shorter events, 0.2 us)
Async XLA Ops:
  1.3 0.8 %copy-start.1 = (f32[3,4,8,128]{3,2,1,0:T(8,128)S(1)}, f32[3,4,8,128]{3,2,1,0:T(8,128)}, u32[]{:S(2)}) copy-start(f32[3,4,8,128]{3,2,1,0:T(8,128)} %e_ref.1) | copy-start | bytes 147460
  1.4 0.9 %copy-start.2 = (f32[3,4,8,128]{3,2,1,0:T(8,128)S(1)}, f32[3,4,8,128]{3,2,1,0:T(8,128)}, u32[]{:S(2)}) copy-start(f32[3,4,8,128]{3,2,1,0:T(8,128)} %h_ref.1) | copy-start | bytes 147460
  2.2 8.7 %collective-permute-start.1 = (f32[10,2,8,128]{3,2,1,0:T(8,128)S(1)}, f32[10,2,8,128]{3,2,1,0:T(8,128)S(1)}, u32[]{:S(2)}, u32[]{:S(2)}) collective-permute-start(f32[10,2,8,128]{3,2,1,0:T(8,128)S(1)} %pad_maximum_fusion.1), channel_id=1, source_target_pairs={{4,0},{8,4},{12,8},{16,12},{20,16},{24,20},{28,24},{5,1},{9,5},{13... | collective-permute-start | bytes 245768 | tf_op jit(solution)/shard_map/ppermute | solution.py:22
  3.5 4.7 %copy-start = (f32[3,4,8,128]{3,2,1,0:T(8,128)S(1)}, f32[3,4,8,128]{3,2,1,0:T(8,128)}, u32[]{:S(2)}) copy-start(f32[3,4,8,128]{3,2,1,0:T(8,128)} %perm_ref.1) | copy-start | bytes 147460
  3.5 7.4 %collective-permute-start = (f32[10,2,8,128]{3,2,1,0:T(8,128)S(1)}, f32[10,2,8,128]{3,2,1,0:T(8,128)S(1)}, u32[]{:S(2)}, u32[]{:S(2)}) collective-permute-start(f32[10,2,8,128]{3,2,1,0:T(8,128)S(1)} %pad_maximum_fusion), channel_id=1, source_target_pairs={{0,4},{4,8},{8,12},{12,16},{16,20},{20,24},{24,28},{1,5},{5,9},{9,... | collective-permute-start | bytes 245768 | tf_op jit(solution)/shard_map/ppermute | solution.py:22
  8.3 0.7 %copy-start.5 = (f32[4,8,128]{2,1,0:T(8,128)S(1)}, f32[4,8,128]{2,1,0:T(8,128)}, u32[]{:S(2)}) copy-start(f32[4,8,128]{2,1,0:T(8,128)} %param.10) | copy-start | bytes 49156
  9.0 0.7 %copy-start.10 = (f32[1,1,2,3,64]{4,2,3,1,0:T(2,128)S(1)}, f32[1,1,2,3,64]{4,2,3,1,0:T(2,128)}, u32[]{:S(2)}) copy-start(f32[1,1,2,3,64]{4,2,3,1,0:T(2,128)} %param.11) | copy-start | bytes 4612
  9.0 1.3 %copy-start.9 = (s32[1,1,8,8]{3,2,1,0:T(8,128)S(1)}, s32[1,1,8,8]{3,2,1,0:T(8,128)}, u32[]{:S(2)}) copy-start(s32[1,1,8,8]{3,2,1,0:T(8,128)} %param.12) | copy-start | bytes 772
  10.9 0.6 %copy-start.3 = (f32[10,2,8,128]{3,2,1,0:T(8,128)}, f32[10,2,8,128]{3,2,1,0:T(8,128)S(1)}, u32[]{:S(2)}) copy-start(f32[10,2,8,128]{3,2,1,0:T(8,128)S(1)} %collective-permute-done.1.xhi_ref) | copy-start | bytes 245764
  11.0 0.6 %copy-start.4 = (f32[10,2,8,128]{3,2,1,0:T(8,128)}, f32[10,2,8,128]{3,2,1,0:T(8,128)S(1)}, u32[]{:S(2)}) copy-start(f32[10,2,8,128]{3,2,1,0:T(8,128)S(1)} %collective-permute-done.xlo_ref) | copy-start | bytes 245764
  11.6 5.0 %collective-permute-start.3 = (f32[10,8,2,128]{3,2,1,0:T(2,128)S(1)}, f32[10,8,2,128]{3,2,1,0:T(2,128)S(1)}, u32[]{:S(2)}, u32[]{:S(2)}) collective-permute-start(f32[10,8,2,128]{3,2,1,0:T(2,128)S(1)} %pad_maximum_fusion.3), channel_id=1, source_target_pairs={{1,0},{2,1},{3,2},{5,4},{6,5},{7,6},{9,8},{10,9},{11,10},{13,12},{... | collective-permute-start | bytes 245768 | tf_op jit(solution)/shard_map/ppermute | solution.py:22
  13.6 5.8 %collective-permute-start.2 = (f32[10,8,2,128]{3,2,1,0:T(2,128)S(1)}, f32[10,8,2,128]{3,2,1,0:T(2,128)S(1)}, u32[]{:S(2)}, u32[]{:S(2)}) collective-permute-start(f32[10,8,2,128]{3,2,1,0:T(2,128)S(1)} %pad_maximum_fusion.2), channel_id=1, source_target_pairs={{0,1},{1,2},{2,3},{4,5},{5,6},{6,7},{8,9},{9,10},{10,11},{12,13},{... | collective-permute-start | bytes 245768 | tf_op jit(solution)/shard_map/ppermute | solution.py:22
  16.6 2.8 %copy-start.6 = (f32[10,8,2,128]{3,2,1,0:T(2,128)}, f32[10,8,2,128]{3,2,1,0:T(2,128)S(1)}, u32[]{:S(2)}) copy-start(f32[10,8,2,128]{3,2,1,0:T(2,128)S(1)} %collective-permute-done.3.yhi_ref) | copy-start | bytes 245764
  19.4 0.6 %copy-start.7 = (f32[10,8,2,128]{3,2,1,0:T(2,128)}, f32[10,8,2,128]{3,2,1,0:T(2,128)S(1)}, u32[]{:S(2)}) copy-start(f32[10,8,2,128]{3,2,1,0:T(2,128)S(1)} %collective-permute-done.2.ylo_ref) | copy-start | bytes 245764
  22.3 0.7 %copy-start.11 = (f32[2,64]{1,0:T(2,128)S(1)}, f32[2,64]{1,0:T(2,128)}, u32[]{:S(2)}) copy-start(f32[2,64]{1,0:T(2,128)} %get-tuple-element.8) | copy-start | bytes 1540
  23.0 7.4 %copy-start.8 = (s32[1,1,8,8]{3,2,1,0:T(8,128)S(1)}, s32[1,1,8,8]{3,2,1,0:T(8,128)}, u32[]{:S(2)}) copy-start(s32[1,1,8,8]{3,2,1,0:T(8,128)} %param.13) | copy-start | bytes 772
  23.6 13.3 %all-to-all-start = ((f32[2,8,8]{2,0,1:T(2,128)}), f32[2,8,8]{2,0,1:T(2,128)S(1)}, u32[]{:S(2)}, u32[]{:S(2)}) async-start(f32[2,8,8]{2,0,1:T(2,128)} %copy.12), calls=%async_computation | async-start | bytes 16384 | tf_op jit(solution)/shard_map/all_to_all | solution.py:161

commit v3 on v2

--- a/solution.py
+++ b/solution.py
@@ -11,6 +11,7 @@
 PAR_DEV = 128
 HALO = 2
 LANES = 128
+MAX_PERMUTE_RING = 8
 
 CH_GAIN = 0.5
 CE_GAIN = 0.5
@@ -136,6 +137,21 @@
     )(offsets, field_e, field_h, permittivity, conductivity, xlo, xhi, ylo, yhi, cells, fwd)
 
 
+def exchange_by_permutes(products, segments, count):
+    me = lax.axis_index("slab")
+    doubled = jnp.concatenate([products, products], 1)
+    rotated = lax.dynamic_slice_in_dim(doubled, me, count, axis=1)
+    pieces = [rotated[:, 0]]
+    for shift in range(1, count):
+        pairs = [(i, (i + shift) % count) for i in range(count)]
+        pieces.append(lax.ppermute(rotated[:, shift], "slab", pairs))
+    received = jnp.stack(pieces, 1)
+    backwards = segments[::-1]
+    doubled = jnp.concatenate([backwards, backwards], 0)
+    sources = lax.dynamic_slice_in_dim(doubled, count - 1 - me, count, axis=0)
+    return received, sources
+
+
 def shards(field_e, field_h, permittivity, conductivity, forward_e, slot_cell, recv_param):
     depth_x = field_e.shape[1]
     depth_y = field_e.shape[2]
@@ -158,8 +174,12 @@
         slot_cell.reshape(1, -1), forward_e[0, 0], n_x, n_y,
     )
     products = products.reshape(STEPS, sources, capacity)
-    received = lax.all_to_all(products, "slab", split_axis=1, concat_axis=1, tiled=True)
-    segments = jnp.broadcast_to(recv_param.reshape(1, sources, capacity), (STEPS, sources, capacity))
+    segments = recv_param.reshape(sources, capacity)
+    if sources <= MAX_PERMUTE_RING:
+        received, segments = exchange_by_permutes(products, segments, sources)
+    else:
+        received = lax.all_to_all(products, "slab", split_axis=1, concat_axis=1, tiled=True)
+    segments = jnp.broadcast_to(segments[None], (STEPS, sources, capacity))
     gradient = jax.ops.segment_sum(received.reshape(-1), segments.reshape(-1), num_segments=PAR_DEV + 1)
     return (new_e, new_h, gradient[:PAR_DEV].reshape(1, 1, PAR_DEV))
 

time: 39.5 us -> 43.6 us (1.10)
  starting transfers between devices: 17.1 us -> 23.6 us
  waiting for transfers between devices: 9.2 us -> 7.39 us
  local copies, waits for them, and re-layouts: 7.5 us -> 6.83 us
    ppermute x0 -> x7, starting transfers between devices: none -> 13.3 us  [exchange_by_permutes(): pieces.append(lax.ppermute(rotated[:, shift], 'slab', pairs))]
    all_to_all x1 -> x0, starting transfers between devices: 6.8 us -> none  [shards(): lax.all_to_all(products, 'slab', split_axis=1, concat_axis=1, tiled=True)]
    all_to_all x1 -> x0, waiting for transfers between devices: 6.41 us -> none  [shards(): lax.all_to_all(products, 'slab', split_axis=1, concat_axis=1, tiled=True)]
    ppermute x0 -> x7, waiting for transfers between devices: none -> 4.68 us  [exchange_by_permutes(): pieces.append(lax.ppermute(rotated[:, shift], 'slab', pairs))]
    reshape x2 -> x1, local copies, waits for them, and re-layouts: 0.68 us -> 0.08 us  [shards(): products = products.reshape(STEPS, sources, capacity)]
  transfers between devices with their start and end apart: 5 -> 11, of which waited for: 2 -> 4; matrix products, arithmetic and copies ran while one was open for 5% -> 5% of each run, Pallas kernels for 0% -> 0%
where the time goes in v3:
time: 43.6 us; the launch traced here: 43.1 us
  starting transfers between devices  23.6 us (54%)
  waiting for transfers between devices  7.39 us (17%)
  local copies, waits for them, and re-layouts  6.83 us (16%)
  Pallas kernels  2.29 us (5%)
  other arithmetic  2.19 us (5%)
  between operations  0.87 us (2%)
    ppermute x7, starting transfers between devices, exchange_by_permutes(): pieces.append(lax.ppermute(rotated[:, shift], 'slab', pairs))  13.3 us
    ppermute x4, starting transfers between devices, recv_from(): return lax.ppermute(array, axis, pairs)  10.3 us
    ppermute x7, waiting for transfers between devices, exchange_by_permutes(): pieces.append(lax.ppermute(rotated[:, shift], 'slab', pairs))  4.68 us
    unnamed x25, local copies, waits for them, and re-layouts  3.88 us
    ppermute x4, waiting for transfers between devices, recv_from(): return lax.ppermute(array, axis, pairs)  2.7 us
    pallas_call x1, Pallas kernels, leapfrog(): pl.pallas_call(kernel, out_shape=(jax.ShapeDtypeStruct(field_e.shape, jnp...  2.29 us
    slice x3, local copies, waits for them, and re-layouts, shards(): xhi = recv_from(jnp.concatenate([p[:, :HALO] for p in parts], 0), 'slab', 1)  1.49 us
    scatter-add x1, other arithmetic, shards(): jax.ops.segment_sum(received.reshape(-1), segments.reshape(-1), num_segme...  1.43 us
  transfers between devices with their start and end apart: 11, of which 4 were waited for; matrix products, arithmetic and copies ran while one was open for 5% of the time, Pallas kernels for 0%

profile of v3, /device:TPU:2, one launch (start us, length us, event | category | flops | bytes accessed | tf_op | source)
XLA Modules:
  0.0 43.1 jit_solution(1875156131699437337)
XLA Ops:
  0.6 0.7 %fusion.13 = (f32[1,2,8,128]{3,2,1,0:T(8,128)S(1)}, f32[1,2,8,128]{3,2,1,0:T(8,128)S(1)}) fusion(f32[1,4,8,128]{3,2,1,0:T(8,128)} %bitcast.39), kind=kLoop, calls=%fused_computation.25 | loop fusion | bytes 32768 | tf_op jit(solution)/shard_map/slice | solution.py:164
  1.4 0.8 %fusion.11 = (f32[3,2,8,128]{3,2,1,0:T(8,128)S(1)}, f32[3,2,8,128]{3,2,1,0:T(8,128)S(1)}) fusion(f32[3,4,8,128]{3,2,1,0:T(8,128)} %perm_ref.1), kind=kLoop, calls=%fused_computation.23 | loop fusion | bytes 98304 | tf_op jit(solution)/shard_map/slice | solution.py:164
  2.1 0.1 copy-done.1
  2.2 1.3 %collective-permute-start.1 = (f32[10,2,8,128]{3,2,1,0:T(8,128)S(1)}, f32[10,2,8,128]{3,2,1,0:T(8,128)S(1)}, u32[]{:S(2)}, u32[]{:S(2)}) collective-permute-start(f32[10,2,8,128]{3,2,1,0:T(8,128)S(1)} %pad_maximum_fusion.1), channel_id=1, source_target_pairs={{4,0},{8,4},{12,8},{16,12},{20,16},{24,20},{28,24},{5,1},{9,5},{13... | collective-permute-start | bytes 245768 | tf_op jit(solution)/shard_map/ppermute | solution.py:23
  3.6 4.7 %collective-permute-start = (f32[10,2,8,128]{3,2,1,0:T(8,128)S(1)}, f32[10,2,8,128]{3,2,1,0:T(8,128)S(1)}, u32[]{:S(2)}, u32[]{:S(2)}) collective-permute-start(f32[10,2,8,128]{3,2,1,0:T(8,128)S(1)} %pad_maximum_fusion), channel_id=1, source_target_pairs={{0,4},{4,8},{8,12},{12,16},{16,20},{20,24},{24,28},{1,5},{5,9},{9,... | collective-permute-start | bytes 245768 | tf_op jit(solution)/shard_map/ppermute | solution.py:23
  8.4 0.7 %copy-done.10 = f32[1,1,2,3,64]{4,2,3,1,0:T(2,128)S(1)} copy-done((f32[1,1,2,3,64]{4,2,3,1,0:T(2,128)S(1)}, f32[1,1,2,3,64]{4,2,3,1,0:T(2,128)}, u32[]{:S(2)}) %copy-start.10) | copy-done | bytes 1560
  9.0 0.6 %copy.19 = f32[1,1,2,3,64]{4,3,2,1,0:T(4,128)} copy(f32[1,1,2,3,64]{4,2,3,1,0:T(2,128)S(1)} %copy-done.10) | data formatting | bytes 3072 | tf_op args[4]
  9.6 0.6 %reshape.22.cell_ref = s32[1,64]{1,0:T(1,128)} reshape(s32[1,1,8,8]{3,2,1,0:T(8,128)S(1)} %copy-done.8) | data formatting | bytes 512 | tf_op jit(solution)/shard_map/reshape | solution.py:174
  10.2 0.7 %copy-done.9 = s32[1,1,8,8]{3,2,1,0:T(8,128)S(1)} copy-done((s32[1,1,8,8]{3,2,1,0:T(8,128)S(1)}, s32[1,1,8,8]{3,2,1,0:T(8,128)}, u32[]{:S(2)}) %copy-start.9) | copy-done | bytes 280
  10.9 0.1 reshape.29
  11.1 0.6 %copy-done.3 = f32[10,2,8,128]{3,2,1,0:T(8,128)} copy-done((f32[10,2,8,128]{3,2,1,0:T(8,128)}, f32[10,2,8,128]{3,2,1,0:T(8,128)S(1)}, u32[]{:S(2)}) %copy-start.3) | copy-done | bytes 81944
  11.7 1.9 %collective-permute-start.3 = (f32[10,8,2,128]{3,2,1,0:T(2,128)S(1)}, f32[10,8,2,128]{3,2,1,0:T(2,128)S(1)}, u32[]{:S(2)}, u32[]{:S(2)}) collective-permute-start(f32[10,8,2,128]{3,2,1,0:T(2,128)S(1)} %pad_maximum_fusion.3), channel_id=1, source_target_pairs={{1,0},{2,1},{3,2},{5,4},{6,5},{7,6},{9,8},{10,9},{11,10},{13,12},{... | collective-permute-start | bytes 245768 | tf_op jit(solution)/shard_map/ppermute | solution.py:23
  13.7 2.4 %collective-permute-start.2 = (f32[10,8,2,128]{3,2,1,0:T(2,128)S(1)}, f32[10,8,2,128]{3,2,1,0:T(2,128)S(1)}, u32[]{:S(2)}, u32[]{:S(2)}) collective-permute-start(f32[10,8,2,128]{3,2,1,0:T(2,128)S(1)} %pad_maximum_fusion.2), channel_id=1, source_target_pairs={{0,1},{1,2},{2,3},{4,5},{5,6},{6,7},{8,9},{9,10},{10,11},{12,13},{... | collective-permute-start | bytes 245768 | tf_op jit(solution)/shard_map/ppermute | solution.py:23
  16.1 0.6 %pad_add_fusion.offsets = s32[2]{0:T(128)} fusion(s32[1]{0:T(128)} %bitcast.1, s32[1]{0:T(128)} %bitcast), kind=kLoop, calls=%fused_computation.12 | loop fusion | flops 2 | bytes 16 | tf_op jit(solution)/shard_map/stack | solution.py:171
  16.7 2.7 %collective-permute-done.2.ylo_ref = f32[10,8,2,128]{3,2,1,0:T(2,128)S(1)} collective-permute-done((f32[10,8,2,128]{3,2,1,0:T(2,128)S(1)}, f32[10,8,2,128]{3,2,1,0:T(2,128)S(1)}, u32[]{:S(2)}, u32[]{:S(2)}) %collective-permute-start.2) | collective-permute-done | bytes 81952 | tf_op jit(solution)/shard_map/ppermute | solution.py:23
  19.4 0.6 %copy-done.7 = f32[10,8,2,128]{3,2,1,0:T(2,128)} copy-done((f32[10,8,2,128]{3,2,1,0:T(2,128)}, f32[10,8,2,128]{3,2,1,0:T(2,128)S(1)}, u32[]{:S(2)}) %copy-start.7) | copy-done | bytes 81944
  20.1 2.3 %shard_map.94 = (f32[3,4,8,128]{3,2,1,0:T(8,128)}, f32[3,4,8,128]{3,2,1,0:T(8,128)}, f32[2,64]{1,0:T(2,128)}) custom-call(s32[2]{0:T(128)} %pad_add_fusion.offsets, f32[3,4,8,128]{3,2,1,0:T(8,128)} %e_ref.1, f32[3,4,8,128]{3,2,1,0:T(8,128)} %h_ref.1, f32[3,4,8,128]{3,2,1,0:T(8,128)} %perm_ref.1, f32[1,4,8,128]{3,2,1,0:T(8,128)} %bitcast.40, ...), custom_call_target="tpu_custom_call" | custom-call | tf_op jit(solution)/shard_map/pallas_call | solution.py:127
  22.4 0.6 %copy-done.11 = f32[2,64]{1,0:T(2,128)S(1)} copy-done((f32[2,64]{1,0:T(2,128)S(1)}, f32[2,64]{1,0:T(2,128)}, u32[]{:S(2)}) %copy-start.11) | copy-done | bytes 536
  23.0 0.1 reshape.24
  23.1 3.5 %collective-permute-start.5 = (f32[2,8]{1,0:T(2,128)S(1)}, f32[2,8]{1,0:T(2,128)S(1)}, u32[]{:S(2)}, u32[]{:S(2)}) collective-permute-start(f32[2,8]{1,0:T(2,128)S(1)} %bitcast.56), channel_id=1, source_target_pairs={{0,8},{4,12},{8,16},{12,20},{16,24},{20,28},{24,0},{28,4},{1,9},{5... | collective-permute-start | bytes 200 | tf_op jit(solution)/shard_map/ppermute | solution.py:147
  26.6 1.6 %collective-permute-start.6 = (f32[2,8]{1,0:T(2,128)S(1)}, f32[2,8]{1,0:T(2,128)S(1)}, u32[]{:S(2)}, u32[]{:S(2)}) collective-permute-start(f32[2,8]{1,0:T(2,128)S(1)} %bitcast.54), channel_id=1, source_target_pairs={{0,12},{4,16},{8,20},{12,24},{16,28},{20,0},{24,4},{28,8},{1,13},{... | collective-permute-start | bytes 200 | tf_op jit(solution)/shard_map/ppermute | solution.py:147
  28.2 1.2 %collective-permute-start.7 = (f32[2,8]{1,0:T(2,128)S(1)}, f32[2,8]{1,0:T(2,128)S(1)}, u32[]{:S(2)}, u32[]{:S(2)}) collective-permute-start(f32[2,8]{1,0:T(2,128)S(1)} %bitcast.52), channel_id=1, source_target_pairs={{0,16},{4,20},{8,24},{12,28},{16,0},{20,4},{24,8},{28,12},{1,17},{... | collective-permute-start | bytes 200 | tf_op jit(solution)/shard_map/ppermute | solution.py:147
  29.4 3.6 %collective-permute-start.8 = (f32[2,8]{1,0:T(2,128)S(1)}, f32[2,8]{1,0:T(2,128)S(1)}, u32[]{:S(2)}, u32[]{:S(2)}) collective-permute-start(f32[2,8]{1,0:T(2,128)S(1)} %bitcast.50), channel_id=1, source_target_pairs={{0,20},{4,24},{8,28},{12,0},{16,4},{20,8},{24,12},{28,16},{1,21},{... | collective-permute-start | bytes 200 | tf_op jit(solution)/shard_map/ppermute | solution.py:147
  33.0 1.3 %collective-permute-start.9 = (f32[2,8]{1,0:T(2,128)S(1)}, f32[2,8]{1,0:T(2,128)S(1)}, u32[]{:S(2)}, u32[]{:S(2)}) collective-permute-start(f32[2,8]{1,0:T(2,128)S(1)} %bitcast.48), channel_id=1, source_target_pairs={{0,24},{4,28},{8,0},{12,4},{16,8},{20,12},{24,16},{28,20},{1,25},{... | collective-permute-start | bytes 200 | tf_op jit(solution)/shard_map/ppermute | solution.py:147
  34.4 0.4 %collective-permute-start.10 = (f32[2,8]{1,0:T(2,128)S(1)}, f32[2,8]{1,0:T(2,128)S(1)}, u32[]{:S(2)}, u32[]{:S(2)}) collective-permute-start(f32[2,8]{1,0:T(2,128)S(1)} %bitcast.46), channel_id=1, source_target_pairs={{0,28},{4,0},{8,4},{12,8},{16,12},{20,16},{24,20},{28,24},{1,29},{... | collective-permute-start | bytes 200 | tf_op jit(solution)/shard_map/ppermute | solution.py:147
  34.8 1.6 %collective-permute-start.4 = (f32[2,8]{1,0:T(2,128)S(1)}, f32[2,8]{1,0:T(2,128)S(1)}, u32[]{:S(2)}, u32[]{:S(2)}) collective-permute-start(f32[2,8]{1,0:T(2,128)S(1)} %bitcast.44), channel_id=1, source_target_pairs={{0,4},{4,8},{8,12},{12,16},{16,20},{20,24},{24,28},{28,0},{1,5},{5... | collective-permute-start | bytes 200 | tf_op jit(solution)/shard_map/ppermute | solution.py:147
  36.4 0.2 collective-permute-done.9
  36.6 1.4 %collective-permute-done.10 = f32[2,8]{1,0:T(2,128)S(1)} collective-permute-done((f32[2,8]{1,0:T(2,128)S(1)}, f32[2,8]{1,0:T(2,128)S(1)}, u32[]{:S(2)}, u32[]{:S(2)}) %collective-permute-start.10) | collective-permute-done | bytes 96 | tf_op jit(solution)/shard_map/ppermute | solution.py:147
  37.9 3.1 %collective-permute-done.4 = f32[2,8]{1,0:T(2,128)S(1)} collective-permute-done((f32[2,8]{1,0:T(2,128)S(1)}, f32[2,8]{1,0:T(2,128)S(1)}, u32[]{:S(2)}, u32[]{:S(2)}) %collective-permute-start.4) | collective-permute-done | bytes 96 | tf_op jit(solution)/shard_map/ppermute | solution.py:147
  41.1 0.1 reshape.31
  41.2 1.4 %scatter_custom_fusion = f32[129]{0:T(256)S(1)} fusion(s32[128]{0:T(128)S(1)} %reshape.29, f32[128]{0:T(128)S(1)} %reshape.31, f32[]{:T(128)} %constant.18.clone.1), kind=kCustom, calls=%fused_computation.14 | custom fusion | flops 128 | bytes 520 | tf_op jit(solution)/shard_map/scatter-add | solution.py:183
  42.6 0.5 %slice_bitcast_fusion = f32[1,1,128]{2,1,0:T(1,128)} fusion(f32[129]{0:T(256)S(1)} %scatter_custom_fusion), kind=kLoop, calls=%fused_computation.13 | loop fusion | bytes 1024 | tf_op jit(solution)/shard_map/reshape | solution.py:184
  (41 shorter events, 0.3 us)
Async XLA Ops:
  1.3 0.8 %copy-start.1 = (f32[3,4,8,128]{3,2,1,0:T(8,128)S(1)}, f32[3,4,8,128]{3,2,1,0:T(8,128)}, u32[]{:S(2)}) copy-start(f32[3,4,8,128]{3,2,1,0:T(8,128)} %e_ref.1) | copy-start | bytes 147460
  1.4 0.9 %copy-start.2 = (f32[3,4,8,128]{3,2,1,0:T(8,128)S(1)}, f32[3,4,8,128]{3,2,1,0:T(8,128)}, u32[]{:S(2)}) copy-start(f32[3,4,8,128]{3,2,1,0:T(8,128)} %h_ref.1) | copy-start | bytes 147460
  2.2 8.8 %collective-permute-start.1 = (f32[10,2,8,128]{3,2,1,0:T(8,128)S(1)}, f32[10,2,8,128]{3,2,1,0:T(8,128)S(1)}, u32[]{:S(2)}, u32[]{:S(2)}) collective-permute-start(f32[10,2,8,128]{3,2,1,0:T(8,128)S(1)} %pad_maximum_fusion.1), channel_id=1, source_target_pairs={{4,0},{8,4},{12,8},{16,12},{20,16},{24,20},{28,24},{5,1},{9,5},{13... | collective-permute-start | bytes 245768 | tf_op jit(solution)/shard_map/ppermute | solution.py:23
  3.5 4.7 %copy-start.5 = (f32[4,8,128]{2,1,0:T(8,128)S(1)}, f32[4,8,128]{2,1,0:T(8,128)}, u32[]{:S(2)}) copy-start(f32[4,8,128]{2,1,0:T(8,128)} %param.10) | copy-start | bytes 49156
  3.5 4.8 %copy-start = (f32[3,4,8,128]{3,2,1,0:T(8,128)S(1)}, f32[3,4,8,128]{3,2,1,0:T(8,128)}, u32[]{:S(2)}) copy-start(f32[3,4,8,128]{3,2,1,0:T(8,128)} %perm_ref.1) | copy-start | bytes 147460
  3.6 7.5 %collective-permute-start = (f32[10,2,8,128]{3,2,1,0:T(8,128)S(1)}, f32[10,2,8,128]{3,2,1,0:T(8,128)S(1)}, u32[]{:S(2)}, u32[]{:S(2)}) collective-permute-start(f32[10,2,8,128]{3,2,1,0:T(8,128)S(1)} %pad_maximum_fusion), channel_id=1, source_target_pairs={{0,4},{4,8},{8,12},{12,16},{16,20},{20,24},{24,28},{1,5},{5,9},{9,... | collective-permute-start | bytes 245768 | tf_op jit(solution)/shard_map/ppermute | solution.py:23
  8.3 0.7 %copy-start.10 = (f32[1,1,2,3,64]{4,2,3,1,0:T(2,128)S(1)}, f32[1,1,2,3,64]{4,2,3,1,0:T(2,128)}, u32[]{:S(2)}) copy-start(f32[1,1,2,3,64]{4,2,3,1,0:T(2,128)} %param.11) | copy-start | bytes 4612
  8.3 1.3 %copy-start.8 = (s32[1,1,8,8]{3,2,1,0:T(8,128)S(1)}, s32[1,1,8,8]{3,2,1,0:T(8,128)}, u32[]{:S(2)}) copy-start(s32[1,1,8,8]{3,2,1,0:T(8,128)} %param.12) | copy-start | bytes 772
  10.2 0.7 %copy-start.9 = (s32[1,1,8,8]{3,2,1,0:T(8,128)S(1)}, s32[1,1,8,8]{3,2,1,0:T(8,128)}, u32[]{:S(2)}) copy-start(s32[1,1,8,8]{3,2,1,0:T(8,128)} %param.13) | copy-start | bytes 772
  11.0 0.6 %copy-start.3 = (f32[10,2,8,128]{3,2,1,0:T(8,128)}, f32[10,2,8,128]{3,2,1,0:T(8,128)S(1)}, u32[]{:S(2)}) copy-start(f32[10,2,8,128]{3,2,1,0:T(8,128)S(1)} %collective-permute-done.1.xhi_ref) | copy-start | bytes 245764
  11.1 0.6 %copy-start.4 = (f32[10,2,8,128]{3,2,1,0:T(8,128)}, f32[10,2,8,128]{3,2,1,0:T(8,128)S(1)}, u32[]{:S(2)}) copy-start(f32[10,2,8,128]{3,2,1,0:T(8,128)S(1)} %collective-permute-done.xlo_ref) | copy-start | bytes 245764
  11.7 5.0 %collective-permute-start.3 = (f32[10,8,2,128]{3,2,1,0:T(2,128)S(1)}, f32[10,8,2,128]{3,2,1,0:T(2,128)S(1)}, u32[]{:S(2)}, u32[]{:S(2)}) collective-permute-start(f32[10,8,2,128]{3,2,1,0:T(2,128)S(1)} %pad_maximum_fusion.3), channel_id=1, source_target_pairs={{1,0},{2,1},{3,2},{5,4},{6,5},{7,6},{9,8},{10,9},{11,10},{13,12},{... | collective-permute-start | bytes 245768 | tf_op jit(solution)/shard_map/ppermute | solution.py:23
  13.7 5.8 %collective-permute-start.2 = (f32[10,8,2,128]{3,2,1,0:T(2,128)S(1)}, f32[10,8,2,128]{3,2,1,0:T(2,128)S(1)}, u32[]{:S(2)}, u32[]{:S(2)}) collective-permute-start(f32[10,8,2,128]{3,2,1,0:T(2,128)S(1)} %pad_maximum_fusion.2), channel_id=1, source_target_pairs={{0,1},{1,2},{2,3},{4,5},{5,6},{6,7},{8,9},{9,10},{10,11},{12,13},{... | collective-permute-start | bytes 245768 | tf_op jit(solution)/shard_map/ppermute | solution.py:23
  16.7 2.7 %copy-start.6 = (f32[10,8,2,128]{3,2,1,0:T(2,128)}, f32[10,8,2,128]{3,2,1,0:T(2,128)S(1)}, u32[]{:S(2)}) copy-start(f32[10,8,2,128]{3,2,1,0:T(2,128)S(1)} %collective-permute-done.3.yhi_ref) | copy-start | bytes 245764
  19.4 0.6 %copy-start.7 = (f32[10,8,2,128]{3,2,1,0:T(2,128)}, f32[10,8,2,128]{3,2,1,0:T(2,128)S(1)}, u32[]{:S(2)}) copy-start(f32[10,8,2,128]{3,2,1,0:T(2,128)S(1)} %collective-permute-done.2.ylo_ref) | copy-start | bytes 245764
  22.4 0.6 %copy-start.11 = (f32[2,64]{1,0:T(2,128)S(1)}, f32[2,64]{1,0:T(2,128)}, u32[]{:S(2)}) copy-start(f32[2,64]{1,0:T(2,128)} %get-tuple-element.8) | copy-start | bytes 1540
  23.1 11.3 %collective-permute-start.5 = (f32[2,8]{1,0:T(2,128)S(1)}, f32[2,8]{1,0:T(2,128)S(1)}, u32[]{:S(2)}, u32[]{:S(2)}) collective-permute-start(f32[2,8]{1,0:T(2,128)S(1)} %bitcast.56), channel_id=1, source_target_pairs={{0,8},{4,12},{8,16},{12,20},{16,24},{20,28},{24,0},{28,4},{1,9},{5... | collective-permute-start | bytes 200 | tf_op jit(solution)/shard_map/ppermute | solution.py:147
  26.6 8.2 %collective-permute-start.6 = (f32[2,8]{1,0:T(2,128)S(1)}, f32[2,8]{1,0:T(2,128)S(1)}, u32[]{:S(2)}, u32[]{:S(2)}) collective-permute-start(f32[2,8]{1,0:T(2,128)S(1)} %bitcast.54), channel_id=1, source_target_pairs={{0,12},{4,16},{8,20},{12,24},{16,28},{20,0},{24,4},{28,8},{1,13},{... | collective-permute-start | bytes 200 | tf_op jit(solution)/shard_map/ppermute | solution.py:147
  28.2 8.2 %collective-permute-start.7 = (f32[2,8]{1,0:T(2,128)S(1)}, f32[2,8]{1,0:T(2,128)S(1)}, u32[]{:S(2)}, u32[]{:S(2)}) collective-permute-start(f32[2,8]{1,0:T(2,128)S(1)} %bitcast.52), channel_id=1, source_target_pairs={{0,16},{4,20},{8,24},{12,28},{16,0},{20,4},{24,8},{28,12},{1,17},{... | collective-permute-start | bytes 200 | tf_op jit(solution)/shard_map/ppermute | solution.py:147
  29.4 7.0 %collective-permute-start.8 = (f32[2,8]{1,0:T(2,128)S(1)}, f32[2,8]{1,0:T(2,128)S(1)}, u32[]{:S(2)}, u32[]{:S(2)}) collective-permute-start(f32[2,8]{1,0:T(2,128)S(1)} %bitcast.50), channel_id=1, source_target_pairs={{0,20},{4,24},{8,28},{12,0},{16,4},{20,8},{24,12},{28,16},{1,21},{... | collective-permute-start | bytes 200 | tf_op jit(solution)/shard_map/ppermute | solution.py:147
  33.0 3.6 %collective-permute-start.9 = (f32[2,8]{1,0:T(2,128)S(1)}, f32[2,8]{1,0:T(2,128)S(1)}, u32[]{:S(2)}, u32[]{:S(2)}) collective-permute-start(f32[2,8]{1,0:T(2,128)S(1)} %bitcast.48), channel_id=1, source_target_pairs={{0,24},{4,28},{8,0},{12,4},{16,8},{20,12},{24,16},{28,20},{1,25},{... | collective-permute-start | bytes 200 | tf_op jit(solution)/shard_map/ppermute | solution.py:147
  34.4 3.6 %collective-permute-start.10 = (f32[2,8]{1,0:T(2,128)S(1)}, f32[2,8]{1,0:T(2,128)S(1)}, u32[]{:S(2)}, u32[]{:S(2)}) collective-permute-start(f32[2,8]{1,0:T(2,128)S(1)} %bitcast.46), channel_id=1, source_target_pairs={{0,28},{4,0},{8,4},{12,8},{16,12},{20,16},{24,20},{28,24},{1,29},{... | collective-permute-start | bytes 200 | tf_op jit(solution)/shard_map/ppermute | solution.py:147
  34.8 6.3 %collective-permute-start.4 = (f32[2,8]{1,0:T(2,128)S(1)}, f32[2,8]{1,0:T(2,128)S(1)}, u32[]{:S(2)}, u32[]{:S(2)}) collective-permute-start(f32[2,8]{1,0:T(2,128)S(1)} %bitcast.44), channel_id=1, source_target_pairs={{0,4},{4,8},{8,12},{12,16},{16,20},{20,24},{24,28},{28,0},{1,5},{5... | collective-permute-start | bytes 200 | tf_op jit(solution)/shard_map/ppermute | solution.py:147

commit v4 on v2

--- a/solution.py
+++ b/solution.py
@@ -136,6 +136,32 @@
     )(offsets, field_e, field_h, permittivity, conductivity, xlo, xhi, ylo, yhi, cells, fwd)
 
 
+def xor_rows(array, me, count, axis):
+    bit = 1
+    while bit < count:
+        shape = array.shape[:axis] + (count // (2 * bit), 2, bit) + array.shape[axis + 1 :]
+        split = array.reshape(shape)
+        swapped = jnp.flip(split, axis + 1).reshape(array.shape)
+        array = jnp.where((me // bit) % 2 == 1, swapped, array)
+        bit *= 2
+    return array
+
+
+def exchange_by_halving(products, segments, count):
+    me = lax.axis_index("slab")
+    held = xor_rows(products, me, count, 1)[:, :, None]
+    bit = count // 2
+    while bit >= 1:
+        owners = held.shape[1]
+        keep = held[:, : owners // 2]
+        send = held[:, owners // 2 :]
+        pairs = [(i, i ^ bit) for i in range(count)]
+        got = lax.ppermute(send, "slab", pairs)
+        held = jnp.stack([keep, got], 3).reshape(keep.shape[:2] + (keep.shape[2] * 2,) + keep.shape[3:])
+        bit //= 2
+    return held[:, 0], xor_rows(segments, me, count, 0)
+
+
 def shards(field_e, field_h, permittivity, conductivity, forward_e, slot_cell, recv_param):
     depth_x = field_e.shape[1]
     depth_y = field_e.shape[2]
@@ -158,8 +184,12 @@
         slot_cell.reshape(1, -1), forward_e[0, 0], n_x, n_y,
     )
     products = products.reshape(STEPS, sources, capacity)
-    received = lax.all_to_all(products, "slab", split_axis=1, concat_axis=1, tiled=True)
-    segments = jnp.broadcast_to(recv_param.reshape(1, sources, capacity), (STEPS, sources, capacity))
+    segments = recv_param.reshape(sources, capacity)
+    if sources & (sources - 1) == 0:
+        received, segments = exchange_by_halving(products, segments, sources)
+    else:
+        received = lax.all_to_all(products, "slab", split_axis=1, concat_axis=1, tiled=True)
+    segments = jnp.broadcast_to(segments[None], received.shape)
     gradient = jax.ops.segment_sum(received.reshape(-1), segments.reshape(-1), num_segments=PAR_DEV + 1)
     return (new_e, new_h, gradient[:PAR_DEV].reshape(1, 1, PAR_DEV))
 

time: 39.5 us -> 39.8 us (level)
  the two profiles are of different devices: /device:TPU:2 before, /device:TPU:6 now
where the time goes in v4:
time: 39.8 us; the launch traced here: 39.3 us
  starting transfers between devices  15.8 us (40%)
  waiting for transfers between devices  10.8 us (27%)
  local copies, waits for them, and re-layouts  7.3 us (18%)
  Pallas kernels  2.31 us (6%)
  other arithmetic  2.23 us (6%)
  between operations  0.92 us (2%)
    ppermute x4, starting transfers between devices, recv_from(): return lax.ppermute(array, axis, pairs)  11.4 us
    ppermute x3, waiting for transfers between devices, exchange_by_halving(): got = lax.ppermute(send, 'slab', pairs)  7.41 us
    ppermute x3, starting transfers between devices, exchange_by_halving(): got = lax.ppermute(send, 'slab', pairs)  4.37 us
    unnamed x25, local copies, waits for them, and re-layouts  3.99 us
    ppermute x4, waiting for transfers between devices, recv_from(): return lax.ppermute(array, axis, pairs)  3.35 us
    pallas_call x1, Pallas kernels, leapfrog(): pl.pallas_call(kernel, out_shape=(jax.ShapeDtypeStruct(field_e.shape, jnp...  2.31 us
    slice x3, local copies, waits for them, and re-layouts, shards(): xhi = recv_from(jnp.concatenate([p[:, :HALO] for p in parts], 0), 'slab', 1)  1.49 us
    scatter-add x1, other arithmetic, shards(): jax.ops.segment_sum(received.reshape(-1), segments.reshape(-1), num_segme...  1.43 us
  transfers between devices with their start and end apart: 7, of which 5 were waited for; matrix products, arithmetic and copies ran while one was open for 5% of the time, Pallas kernels for 0%

profile of v4, /device:TPU:6, one launch (start us, length us, event | category | flops | bytes accessed | tf_op | source)
XLA Modules:
  0.0 39.3 jit_solution(7203650303019470660)
XLA Ops:
  0.6 0.7 %fusion.13 = (f32[1,2,8,128]{3,2,1,0:T(8,128)S(1)}, f32[1,2,8,128]{3,2,1,0:T(8,128)S(1)}) fusion(f32[1,4,8,128]{3,2,1,0:T(8,128)} %bitcast.57), kind=kLoop, calls=%fused_computation.34 | loop fusion | bytes 32768 | tf_op jit(solution)/shard_map/slice | solution.py:174
  1.4 0.8 %fusion.11 = (f32[3,2,8,128]{3,2,1,0:T(8,128)S(1)}, f32[3,2,8,128]{3,2,1,0:T(8,128)S(1)}) fusion(f32[3,4,8,128]{3,2,1,0:T(8,128)} %perm_ref.1), kind=kLoop, calls=%fused_computation.32 | loop fusion | bytes 98304 | tf_op jit(solution)/shard_map/slice | solution.py:174
  2.2 3.4 %collective-permute-start = (f32[10,2,8,128]{3,2,1,0:T(8,128)S(1)}, f32[10,2,8,128]{3,2,1,0:T(8,128)S(1)}, u32[]{:S(2)}, u32[]{:S(2)}) collective-permute-start(f32[10,2,8,128]{3,2,1,0:T(8,128)S(1)} %pad_maximum_fusion), channel_id=1, source_target_pairs={{0,4},{4,8},{8,12},{12,16},{16,20},{20,24},{24,28},{1,5},{5,9},{9,... | collective-permute-start | bytes 245768 | tf_op jit(solution)/shard_map/ppermute | solution.py:22
  5.7 2.4 %collective-permute-start.1 = (f32[10,2,8,128]{3,2,1,0:T(8,128)S(1)}, f32[10,2,8,128]{3,2,1,0:T(8,128)S(1)}, u32[]{:S(2)}, u32[]{:S(2)}) collective-permute-start(f32[10,2,8,128]{3,2,1,0:T(8,128)S(1)} %pad_maximum_fusion.1), channel_id=1, source_target_pairs={{4,0},{8,4},{12,8},{16,12},{20,16},{24,20},{28,24},{5,1},{9,5},{13... | collective-permute-start | bytes 245768 | tf_op jit(solution)/shard_map/ppermute | solution.py:22
  8.2 0.7 %copy-done.5 = f32[4,8,128]{2,1,0:T(8,128)S(1)} copy-done((f32[4,8,128]{2,1,0:T(8,128)S(1)}, f32[4,8,128]{2,1,0:T(8,128)}, u32[]{:S(2)}) %copy-start.5) | copy-done | bytes 16408
  8.9 0.7 %copy-done.10 = s32[1,1,8,8]{3,2,1,0:T(8,128)S(1)} copy-done((s32[1,1,8,8]{3,2,1,0:T(8,128)S(1)}, s32[1,1,8,8]{3,2,1,0:T(8,128)}, u32[]{:S(2)}) %copy-start.10) | copy-done | bytes 280
  9.6 0.6 %reshape.180.cell_ref = s32[1,64]{1,0:T(1,128)} reshape(s32[1,1,8,8]{3,2,1,0:T(8,128)S(1)} %copy-done.10) | data formatting | bytes 512 | tf_op jit(solution)/shard_map/reshape | solution.py:184
  10.2 0.6 %copy.17 = f32[1,1,2,3,64]{4,3,2,1,0:T(4,128)} copy(f32[1,1,2,3,64]{4,2,3,1,0:T(2,128)S(1)} %copy-done.11) | data formatting | bytes 3072 | tf_op args[4]
  10.8 0.1 copy-done.8
  11.0 2.0 %collective-permute-done.1.xhi_ref = f32[10,2,8,128]{3,2,1,0:T(8,128)S(1)} collective-permute-done((f32[10,2,8,128]{3,2,1,0:T(8,128)S(1)}, f32[10,2,8,128]{3,2,1,0:T(8,128)S(1)}, u32[]{:S(2)}, u32[]{:S(2)}) %collective-permute-start.1) | collective-permute-done | bytes 81952 | tf_op jit(solution)/shard_map/ppermute | solution.py:22
  13.0 0.6 %copy-done.4 = f32[10,2,8,128]{3,2,1,0:T(8,128)} copy-done((f32[10,2,8,128]{3,2,1,0:T(8,128)}, f32[10,2,8,128]{3,2,1,0:T(8,128)S(1)}, u32[]{:S(2)}) %copy-start.4) | copy-done | bytes 81944
  13.6 1.9 %collective-permute-start.2 = (f32[10,8,2,128]{3,2,1,0:T(2,128)S(1)}, f32[10,8,2,128]{3,2,1,0:T(2,128)S(1)}, u32[]{:S(2)}, u32[]{:S(2)}) collective-permute-start(f32[10,8,2,128]{3,2,1,0:T(2,128)S(1)} %pad_maximum_fusion.2), channel_id=1, source_target_pairs={{0,1},{1,2},{2,3},{4,5},{5,6},{6,7},{8,9},{9,10},{10,11},{12,13},{... | collective-permute-start | bytes 245768 | tf_op jit(solution)/shard_map/ppermute | solution.py:22
  15.5 3.6 %collective-permute-start.3 = (f32[10,8,2,128]{3,2,1,0:T(2,128)S(1)}, f32[10,8,2,128]{3,2,1,0:T(2,128)S(1)}, u32[]{:S(2)}, u32[]{:S(2)}) collective-permute-start(f32[10,8,2,128]{3,2,1,0:T(2,128)S(1)} %pad_maximum_fusion.3), channel_id=1, source_target_pairs={{1,0},{2,1},{3,2},{5,4},{6,5},{7,6},{9,8},{10,9},{11,10},{13,12},{... | collective-permute-start | bytes 245768 | tf_op jit(solution)/shard_map/ppermute | solution.py:22
  19.2 0.7 %pad_add_fusion.offsets = s32[2]{0:T(128)} fusion(s32[1]{0:T(128)} %bitcast.1, s32[1]{0:T(128)} %bitcast), kind=kLoop, calls=%fused_computation.21 | loop fusion | flops 2 | bytes 16 | tf_op jit(solution)/shard_map/stack | solution.py:181
  19.8 1.4 %collective-permute-done.3.yhi_ref = f32[10,8,2,128]{3,2,1,0:T(2,128)S(1)} collective-permute-done((f32[10,8,2,128]{3,2,1,0:T(2,128)S(1)}, f32[10,8,2,128]{3,2,1,0:T(2,128)S(1)}, u32[]{:S(2)}, u32[]{:S(2)}) %collective-permute-start.3) | collective-permute-done | bytes 81952 | tf_op jit(solution)/shard_map/ppermute | solution.py:22
  21.2 0.6 %copy-done.7 = f32[10,8,2,128]{3,2,1,0:T(2,128)} copy-done((f32[10,8,2,128]{3,2,1,0:T(2,128)}, f32[10,8,2,128]{3,2,1,0:T(2,128)S(1)}, u32[]{:S(2)}) %copy-start.7) | copy-done | bytes 81944
  21.8 2.3 %shard_map.94 = (f32[3,4,8,128]{3,2,1,0:T(8,128)}, f32[3,4,8,128]{3,2,1,0:T(8,128)}, f32[2,64]{1,0:T(2,128)}) custom-call(s32[2]{0:T(128)} %pad_add_fusion.offsets, f32[3,4,8,128]{3,2,1,0:T(8,128)} %e_ref.1, f32[3,4,8,128]{3,2,1,0:T(8,128)} %h_ref.1, f32[3,4,8,128]{3,2,1,0:T(8,128)} %perm_ref.1, f32[1,4,8,128]{3,2,1,0:T(8,128)} %bitcast.58, ...), custom_call_target="tpu_custom_call" | custom-call | tf_op jit(solution)/shard_map/pallas_call | solution.py:126
  24.1 0.7 %copy-done.9 = f32[2,64]{1,0:T(2,128)S(1)} copy-done((f32[2,64]{1,0:T(2,128)S(1)}, f32[2,64]{1,0:T(2,128)}, u32[]{:S(2)}) %copy-start.9) | copy-done | bytes 536
  24.8 0.1 reshape_reshape.7
  24.9 0.1 reshape.191
  25.0 0.1 reshape.194
  25.1 0.1 reshape.198
  25.3 2.7 %collective-permute-start.4 = (f32[2,4,1,8]{3,1,0,2:T(4,128)S(1)}, f32[2,4,1,8]{3,1,0,2:T(4,128)S(1)}, u32[]{:S(2)}, u32[]{:S(2)}) collective-permute-start(f32[2,4,1,8]{3,1,0,2:T(4,128)S(1)} %get-tuple-element.34), channel_id=1, source_target_pairs={{0,16},{4,20},{8,24},{12,28},{16,0},{20,4},{24,8},{28,12},{1,17},{... | collective-permute-start | bytes 776 | tf_op jit(solution)/shard_map/ppermute | solution.py:159
  27.9 1.9 %collective-permute-done.4 = f32[2,4,1,8]{3,1,0,2:T(4,128)S(1)} collective-permute-done((f32[2,4,1,8]{3,1,0,2:T(4,128)S(1)}, f32[2,4,1,8]{3,1,0,2:T(4,128)S(1)}, u32[]{:S(2)}, u32[]{:S(2)}) %collective-permute-start.4) | collective-permute-done | bytes 288 | tf_op jit(solution)/shard_map/ppermute | solution.py:159
  29.9 1.6 %collective-permute-start.5 = (f32[2,2,2,8]{3,2,1,0:T(2,128)S(1)}, f32[2,2,2,8]{3,2,1,0:T(2,128)S(1)}, u32[]{:S(2)}, u32[]{:S(2)}) collective-permute-start(f32[2,2,2,8]{3,2,1,0:T(2,128)S(1)} %get-tuple-element.32), channel_id=1, source_target_pairs={{0,8},{4,12},{8,0},{12,4},{16,24},{20,28},{24,16},{28,20},{1,9},{5... | collective-permute-start | bytes 776 | tf_op jit(solution)/shard_map/ppermute | solution.py:159
  31.5 2.0 %collective-permute-done.5 = f32[2,2,2,8]{3,2,1,0:T(2,128)S(1)} collective-permute-done((f32[2,2,2,8]{3,2,1,0:T(2,128)S(1)}, f32[2,2,2,8]{3,2,1,0:T(2,128)S(1)}, u32[]{:S(2)}, u32[]{:S(2)}) %collective-permute-start.5) | collective-permute-done | bytes 288 | tf_op jit(solution)/shard_map/ppermute | solution.py:159
  33.6 0.1 collective-permute-start.6
  33.7 0.1 reshape.204
  33.7 3.5 %collective-permute-done.6 = f32[2,1,4,8]{3,2,1,0:T(4,128)S(1)} collective-permute-done((f32[2,1,4,8]{3,2,1,0:T(4,128)S(1)}, f32[2,1,4,8]{3,2,1,0:T(4,128)S(1)}, u32[]{:S(2)}, u32[]{:S(2)}) %collective-permute-start.6) | collective-permute-done | bytes 288 | tf_op jit(solution)/shard_map/ppermute | solution.py:159
  37.2 0.1 reshape.206
  37.3 1.4 %scatter_custom_fusion = f32[129]{0:T(256)S(1)} fusion(s32[128]{0:T(128)S(1)} %reshape.204, f32[128]{0:T(128)S(1)} %reshape.206, f32[]{:T(128)} %constant.71.clone.1), kind=kCustom, calls=%fused_computation.23 | custom fusion | flops 128 | bytes 520 | tf_op jit(solution)/shard_map/scatter-add | solution.py:193
  38.8 0.5 %slice_bitcast_fusion.3 = f32[1,1,128]{2,1,0:T(1,128)} fusion(f32[129]{0:T(256)S(1)} %scatter_custom_fusion), kind=kLoop, calls=%fused_computation.22 | loop fusion | bytes 1024 | tf_op jit(solution)/shard_map/reshape | solution.py:194
  (52 shorter events, 0.5 us)
Async XLA Ops:
  1.3 0.8 %copy-start.1 = (f32[3,4,8,128]{3,2,1,0:T(8,128)S(1)}, f32[3,4,8,128]{3,2,1,0:T(8,128)}, u32[]{:S(2)}) copy-start(f32[3,4,8,128]{3,2,1,0:T(8,128)} %e_ref.1) | copy-start | bytes 147460
  1.4 0.9 %copy-start.2 = (f32[3,4,8,128]{3,2,1,0:T(8,128)S(1)}, f32[3,4,8,128]{3,2,1,0:T(8,128)}, u32[]{:S(2)}) copy-start(f32[3,4,8,128]{3,2,1,0:T(8,128)} %h_ref.1) | copy-start | bytes 147460
  2.2 8.7 %collective-permute-start = (f32[10,2,8,128]{3,2,1,0:T(8,128)S(1)}, f32[10,2,8,128]{3,2,1,0:T(8,128)S(1)}, u32[]{:S(2)}, u32[]{:S(2)}) collective-permute-start(f32[10,2,8,128]{3,2,1,0:T(8,128)S(1)} %pad_maximum_fusion), channel_id=1, source_target_pairs={{0,4},{4,8},{8,12},{12,16},{16,20},{20,24},{24,28},{1,5},{5,9},{9,... | collective-permute-start | bytes 245768 | tf_op jit(solution)/shard_map/ppermute | solution.py:22
  5.7 2.5 %copy-start = (f32[3,4,8,128]{3,2,1,0:T(8,128)S(1)}, f32[3,4,8,128]{3,2,1,0:T(8,128)}, u32[]{:S(2)}) copy-start(f32[3,4,8,128]{3,2,1,0:T(8,128)} %perm_ref.1) | copy-start | bytes 147460
  5.7 7.2 %collective-permute-start.1 = (f32[10,2,8,128]{3,2,1,0:T(8,128)S(1)}, f32[10,2,8,128]{3,2,1,0:T(8,128)S(1)}, u32[]{:S(2)}, u32[]{:S(2)}) collective-permute-start(f32[10,2,8,128]{3,2,1,0:T(8,128)S(1)} %pad_maximum_fusion.1), channel_id=1, source_target_pairs={{4,0},{8,4},{12,8},{16,12},{20,16},{24,20},{28,24},{5,1},{9,5},{13... | collective-permute-start | bytes 245768 | tf_op jit(solution)/shard_map/ppermute | solution.py:22
  8.1 0.7 %copy-start.5 = (f32[4,8,128]{2,1,0:T(8,128)S(1)}, f32[4,8,128]{2,1,0:T(8,128)}, u32[]{:S(2)}) copy-start(f32[4,8,128]{2,1,0:T(8,128)} %param.10) | copy-start | bytes 49156
  8.9 0.7 %copy-start.10 = (s32[1,1,8,8]{3,2,1,0:T(8,128)S(1)}, s32[1,1,8,8]{3,2,1,0:T(8,128)}, u32[]{:S(2)}) copy-start(s32[1,1,8,8]{3,2,1,0:T(8,128)} %param.12) | copy-start | bytes 772
  8.9 1.3 %copy-start.11 = (f32[1,1,2,3,64]{4,2,3,1,0:T(2,128)S(1)}, f32[1,1,2,3,64]{4,2,3,1,0:T(2,128)}, u32[]{:S(2)}) copy-start(f32[1,1,2,3,64]{4,2,3,1,0:T(2,128)} %param.11) | copy-start | bytes 4612
  10.2 0.7 %copy-start.8 = (s32[1,1,8,8]{3,2,1,0:T(8,128)S(1)}, s32[1,1,8,8]{3,2,1,0:T(8,128)}, u32[]{:S(2)}) copy-start(s32[1,1,8,8]{3,2,1,0:T(8,128)} %param.13) | copy-start | bytes 772
  10.9 2.0 %copy-start.3 = (f32[10,2,8,128]{3,2,1,0:T(8,128)}, f32[10,2,8,128]{3,2,1,0:T(8,128)S(1)}, u32[]{:S(2)}) copy-start(f32[10,2,8,128]{3,2,1,0:T(8,128)S(1)} %collective-permute-done.xlo_ref) | copy-start | bytes 245764
  12.9 0.6 %copy-start.4 = (f32[10,2,8,128]{3,2,1,0:T(8,128)}, f32[10,2,8,128]{3,2,1,0:T(8,128)S(1)}, u32[]{:S(2)}) copy-start(f32[10,2,8,128]{3,2,1,0:T(8,128)S(1)} %collective-permute-done.1.xhi_ref) | copy-start | bytes 245764
  13.6 6.3 %collective-permute-start.2 = (f32[10,8,2,128]{3,2,1,0:T(2,128)S(1)}, f32[10,8,2,128]{3,2,1,0:T(2,128)S(1)}, u32[]{:S(2)}, u32[]{:S(2)}) collective-permute-start(f32[10,8,2,128]{3,2,1,0:T(2,128)S(1)} %pad_maximum_fusion.2), channel_id=1, source_target_pairs={{0,1},{1,2},{2,3},{4,5},{5,6},{6,7},{8,9},{9,10},{10,11},{12,13},{... | collective-permute-start | bytes 245768 | tf_op jit(solution)/shard_map/ppermute | solution.py:22
  15.5 5.7 %collective-permute-start.3 = (f32[10,8,2,128]{3,2,1,0:T(2,128)S(1)}, f32[10,8,2,128]{3,2,1,0:T(2,128)S(1)}, u32[]{:S(2)}, u32[]{:S(2)}) collective-permute-start(f32[10,8,2,128]{3,2,1,0:T(2,128)S(1)} %pad_maximum_fusion.3), channel_id=1, source_target_pairs={{1,0},{2,1},{3,2},{5,4},{6,5},{7,6},{9,8},{10,9},{11,10},{13,12},{... | collective-permute-start | bytes 245768 | tf_op jit(solution)/shard_map/ppermute | solution.py:22
  19.8 1.4 %copy-start.6 = (f32[10,8,2,128]{3,2,1,0:T(2,128)}, f32[10,8,2,128]{3,2,1,0:T(2,128)S(1)}, u32[]{:S(2)}) copy-start(f32[10,8,2,128]{3,2,1,0:T(2,128)S(1)} %collective-permute-done.2.ylo_ref) | copy-start | bytes 245764
  21.2 0.6 %copy-start.7 = (f32[10,8,2,128]{3,2,1,0:T(2,128)}, f32[10,8,2,128]{3,2,1,0:T(2,128)S(1)}, u32[]{:S(2)}) copy-start(f32[10,8,2,128]{3,2,1,0:T(2,128)S(1)} %collective-permute-done.3.yhi_ref) | copy-start | bytes 245764
  24.1 0.7 %copy-start.9 = (f32[2,64]{1,0:T(2,128)S(1)}, f32[2,64]{1,0:T(2,128)}, u32[]{:S(2)}) copy-start(f32[2,64]{1,0:T(2,128)} %get-tuple-element.8) | copy-start | bytes 1540
  25.3 4.6 %collective-permute-start.4 = (f32[2,4,1,8]{3,1,0,2:T(4,128)S(1)}, f32[2,4,1,8]{3,1,0,2:T(4,128)S(1)}, u32[]{:S(2)}, u32[]{:S(2)}) collective-permute-start(f32[2,4,1,8]{3,1,0,2:T(4,128)S(1)} %get-tuple-element.34), channel_id=1, source_target_pairs={{0,16},{4,20},{8,24},{12,28},{16,0},{20,4},{24,8},{28,12},{1,17},{... | collective-permute-start | bytes 776 | tf_op jit(solution)/shard_map/ppermute | solution.py:159
  29.9 3.7 %collective-permute-start.5 = (f32[2,2,2,8]{3,2,1,0:T(2,128)S(1)}, f32[2,2,2,8]{3,2,1,0:T(2,128)S(1)}, u32[]{:S(2)}, u32[]{:S(2)}) collective-permute-start(f32[2,2,2,8]{3,2,1,0:T(2,128)S(1)} %get-tuple-element.32), channel_id=1, source_target_pairs={{0,8},{4,12},{8,0},{12,4},{16,24},{20,28},{24,16},{28,20},{1,9},{5... | collective-permute-start | bytes 776 | tf_op jit(solution)/shard_map/ppermute | solution.py:159
  33.6 3.7 %collective-permute-start.6 = (f32[2,1,4,8]{3,2,1,0:T(4,128)S(1)}, f32[2,1,4,8]{3,2,1,0:T(4,128)S(1)}, u32[]{:S(2)}, u32[]{:S(2)}) collective-permute-start(f32[2,1,4,8]{3,2,1,0:T(4,128)S(1)} %get-tuple-element.30), channel_id=1, source_target_pairs={{0,4},{4,0},{8,12},{12,8},{16,20},{20,16},{24,28},{28,24},{1,5},{5... | collective-permute-start | bytes 776 | tf_op jit(solution)/shard_map/ppermute | solution.py:159

commit v5 on v4

--- a/solution.py
+++ b/solution.py
@@ -46,8 +46,16 @@
 
 def leapfrog_kernel(
     dims, offsets, e_ref, h_ref, perm_ref, cond_ref, xlo_ref, xhi_ref, ylo_ref, yhi_ref,
-    cell_ref, fwd_ref, e_out, h_out, prod_out, ring,
+    cell_ref, fwd_ref, e_out, h_out, prod_out, ring, *staged,
 ):
+    sources = (e_ref, h_ref, perm_ref, cond_ref, xlo_ref, xhi_ref, ylo_ref, yhi_ref, cell_ref, fwd_ref)
+    buffers, sems = staged[:-1], staged[-1]
+    copies = [pltpu.make_async_copy(src, buf, sems.at[i]) for i, (src, buf) in enumerate(zip(sources, buffers))]
+    for copy in copies:
+        copy.start()
+    for copy in copies:
+        copy.wait()
+    e_ref, h_ref, perm_ref, cond_ref, xlo_ref, xhi_ref, ylo_ref, yhi_ref, cell_ref, fwd_ref = buffers
     depth_x, depth_y, n_x, n_y = dims
     ring_x, ring_y = ring.shape[1], ring.shape[2]
     ring[0:3, 0:depth_x, 0:depth_y] = e_ref[...]
@@ -120,7 +128,9 @@
     _, depth_x, depth_y, _ = field_e.shape
     ring_x = depth_x + 2 * HALO
     ring_y = -(-(depth_y + 2 * HALO) // 8) * 8
-    vmem = pl.BlockSpec(memory_space=pltpu.VMEM)
+    whole = pl.BlockSpec()
+    anywhere = pl.BlockSpec(memory_space=pl.ANY)
+    operands = (field_e, field_h, permittivity, conductivity, xlo, xhi, ylo, yhi, cells, fwd)
     smem = pl.BlockSpec(memory_space=pltpu.SMEM)
     kernel = functools.partial(leapfrog_kernel, (depth_x, depth_y, n_x, n_y))
     return pl.pallas_call(
@@ -130,10 +140,12 @@
             jax.ShapeDtypeStruct(field_h.shape, jnp.float32),
             jax.ShapeDtypeStruct((STEPS, cells.shape[1]), jnp.float32),
         ),
-        in_specs=[smem] + [vmem] * 10,
-        out_specs=(vmem, vmem, vmem),
-        scratch_shapes=[pltpu.VMEM((10, ring_x, ring_y, LANES), jnp.float32)],
-    )(offsets, field_e, field_h, permittivity, conductivity, xlo, xhi, ylo, yhi, cells, fwd)
+        in_specs=[smem] + [anywhere] * 10,
+        out_specs=(whole, whole, whole),
+        scratch_shapes=[pltpu.VMEM((10, ring_x, ring_y, LANES), jnp.float32)]
+        + [pltpu.VMEM(a.shape, a.dtype) for a in operands]
+        + [pltpu.SemaphoreType.DMA((len(operands),))],
+    )(offsets, *operands)
 
 
 def xor_rows(array, me, count, axis):
@@ -189,9 +201,10 @@
         received, segments = exchange_by_halving(products, segments, sources)
     else:
         received = lax.all_to_all(products, "slab", split_axis=1, concat_axis=1, tiled=True)
-    segments = jnp.broadcast_to(segments[None], received.shape)
-    gradient = jax.ops.segment_sum(received.reshape(-1), segments.reshape(-1), num_segments=PAR_DEV + 1)
-    return (new_e, new_h, gradient[:PAR_DEV].reshape(1, 1, PAR_DEV))
+    segments = jnp.broadcast_to(segments[None], received.shape).reshape(-1, 1)
+    params = lax.broadcasted_iota(jnp.int32, (1, PAR_DEV), 1)
+    gradient = jnp.sum(jnp.where(segments == params, received.reshape(-1, 1), 0.0), axis=0)
+    return (new_e, new_h, gradient.reshape(1, 1, PAR_DEV))
 
 
 def solution(mesh):

time: 39.8 us -> 39.3 us (0.987)
  other arithmetic: 2.23 us -> 1.44 us
  Pallas kernels: 2.31 us -> 3.06 us
  waiting for transfers between devices: 10.8 us -> 10.2 us
    scatter-add x1 -> x0, other arithmetic: 1.43 us -> none  [shards(): jax.ops.segment_sum(received.reshape(-1), segments.reshape(-1), num_segme...]
    pallas_call x1, Pallas kernels: 2.31 us -> 3.06 us  [leapfrog(): pl.pallas_call(kernel, out_shape=(jax.ShapeDtypeStruct(field_e.shape, jnp...]
    reduce_sum x0 -> x1, other arithmetic: none -> 0.63 us  [shards(): jnp.sum(jnp.where(segments == params, received.reshape(-1, 1), 0.0), axis=0)]
    unnamed x25, local copies, waits for them, and re-layouts: 3.99 us -> 4.57 us
    ppermute x4, waiting for transfers between devices: 3.35 us -> 2.79 us  [recv_from(): return lax.ppermute(array, axis, pairs)]
    reshape x1 -> x0, local copies, waits for them, and re-layouts: 0.51 us -> none  [shards(): return (new_e, new_h, gradient[:PAR_DEV].reshape(1, 1, PAR_DEV))]
where the time goes in v5:
time: 39.3 us; the launch traced here: 38.7 us
  starting transfers between devices  15.8 us (40%)
  waiting for transfers between devices  10.2 us (26%)
  local copies, waits for them, and re-layouts  7.37 us (19%)
  Pallas kernels  3.06 us (8%)
  other arithmetic  1.44 us (4%)
  between operations  0.91 us (2%)
    ppermute x4, starting transfers between devices, recv_from(): return lax.ppermute(array, axis, pairs)  11.4 us
    ppermute x3, waiting for transfers between devices, exchange_by_halving(): got = lax.ppermute(send, 'slab', pairs)  7.41 us
    unnamed x25, local copies, waits for them, and re-layouts  4.57 us
    ppermute x3, starting transfers between devices, exchange_by_halving(): got = lax.ppermute(send, 'slab', pairs)  4.37 us
    pallas_call x1, Pallas kernels, leapfrog(): pl.pallas_call(kernel, out_shape=(jax.ShapeDtypeStruct(field_e.shape, jnp...  3.06 us
    ppermute x4, waiting for transfers between devices, recv_from(): return lax.ppermute(array, axis, pairs)  2.79 us
    slice x3, local copies, waits for them, and re-layouts, shards(): xhi = recv_from(jnp.concatenate([p[:, :HALO] for p in parts], 0), 'slab', 1)  1.49 us
  transfers between devices with their start and end apart: 7, of which 5 were waited for; matrix products, arithmetic and copies ran while one was open for 5% of the time, Pallas kernels for 0%

profile of v5, /device:TPU:6, one launch (start us, length us, event | category | flops | bytes accessed | tf_op | source)
XLA Modules:
  0.0 38.7 jit_solution(1789165498232019032)
XLA Ops:
  0.6 0.7 %fusion.11 = (f32[1,2,8,128]{3,2,1,0:T(8,128)S(1)}, f32[1,2,8,128]{3,2,1,0:T(8,128)S(1)}) fusion(f32[1,4,8,128]{3,2,1,0:T(8,128)} %bitcast.56), kind=kLoop, calls=%fused_computation.32 | loop fusion | bytes 32768 | tf_op jit(solution)/shard_map/slice | solution.py:186
  1.4 0.8 %fusion.9 = (f32[3,2,8,128]{3,2,1,0:T(8,128)S(1)}, f32[3,2,8,128]{3,2,1,0:T(8,128)S(1)}) fusion(f32[3,4,8,128]{3,2,1,0:T(8,128)} %perm_ref.1), kind=kLoop, calls=%fused_computation.30 | loop fusion | bytes 98304 | tf_op jit(solution)/shard_map/slice | solution.py:186
  2.1 0.1 copy-done.1
  2.2 3.4 %collective-permute-start = (f32[10,2,8,128]{3,2,1,0:T(8,128)S(1)}, f32[10,2,8,128]{3,2,1,0:T(8,128)S(1)}, u32[]{:S(2)}, u32[]{:S(2)}) collective-permute-start(f32[10,2,8,128]{3,2,1,0:T(8,128)S(1)} %pad_maximum_fusion), channel_id=1, source_target_pairs={{0,4},{4,8},{8,12},{12,16},{16,20},{20,24},{24,28},{1,5},{5,9},{9,... | collective-permute-start | bytes 245768 | tf_op jit(solution)/shard_map/ppermute | solution.py:22
  5.7 2.4 %collective-permute-start.1 = (f32[10,2,8,128]{3,2,1,0:T(8,128)S(1)}, f32[10,2,8,128]{3,2,1,0:T(8,128)S(1)}, u32[]{:S(2)}, u32[]{:S(2)}) collective-permute-start(f32[10,2,8,128]{3,2,1,0:T(8,128)S(1)} %pad_maximum_fusion.1), channel_id=1, source_target_pairs={{4,0},{8,4},{12,8},{16,12},{20,16},{24,20},{28,24},{5,1},{9,5},{13... | collective-permute-start | bytes 245768 | tf_op jit(solution)/shard_map/ppermute | solution.py:22
  8.2 0.7 %copy-done.5 = f32[4,8,128]{2,1,0:T(8,128)S(1)} copy-done((f32[4,8,128]{2,1,0:T(8,128)S(1)}, f32[4,8,128]{2,1,0:T(8,128)}, u32[]{:S(2)}) %copy-start.5) | copy-done | bytes 16408
  8.9 0.7 %copy-done.10 = s32[1,1,8,8]{3,2,1,0:T(8,128)S(1)} copy-done((s32[1,1,8,8]{3,2,1,0:T(8,128)S(1)}, s32[1,1,8,8]{3,2,1,0:T(8,128)}, u32[]{:S(2)}) %copy-start.10) | copy-done | bytes 280
  9.6 0.6 %reshape.183.cell_ref = s32[1,64]{1,0:T(1,128)} reshape(s32[1,1,8,8]{3,2,1,0:T(8,128)S(1)} %copy-done.10) | data formatting | bytes 512 | tf_op jit(solution)/shard_map/reshape | solution.py:196
  10.2 0.6 %copy.21 = f32[1,1,2,3,64]{4,3,2,1,0:T(4,128)} copy(f32[1,1,2,3,64]{4,2,3,1,0:T(2,128)S(1)} %copy-done.11) | data formatting | bytes 3072 | tf_op args[4]
  10.8 0.7 %copy-done.8 = s32[1,1,8,8]{3,2,1,0:T(8,128)S(1)} copy-done((s32[1,1,8,8]{3,2,1,0:T(8,128)S(1)}, s32[1,1,8,8]{3,2,1,0:T(8,128)}, u32[]{:S(2)}) %copy-start.8) | copy-done | bytes 280
  11.5 1.4 %collective-permute-done.1.xhi_ref = f32[10,2,8,128]{3,2,1,0:T(8,128)S(1)} collective-permute-done((f32[10,2,8,128]{3,2,1,0:T(8,128)S(1)}, f32[10,2,8,128]{3,2,1,0:T(8,128)S(1)}, u32[]{:S(2)}, u32[]{:S(2)}) %collective-permute-start.1) | collective-permute-done | bytes 81952 | tf_op jit(solution)/shard_map/ppermute | solution.py:22
  13.0 0.6 %copy-done.4 = f32[10,2,8,128]{3,2,1,0:T(8,128)} copy-done((f32[10,2,8,128]{3,2,1,0:T(8,128)}, f32[10,2,8,128]{3,2,1,0:T(8,128)S(1)}, u32[]{:S(2)}) %copy-start.4) | copy-done | bytes 81944
  13.6 1.9 %collective-permute-start.2 = (f32[10,8,2,128]{3,2,1,0:T(2,128)S(1)}, f32[10,8,2,128]{3,2,1,0:T(2,128)S(1)}, u32[]{:S(2)}, u32[]{:S(2)}) collective-permute-start(f32[10,8,2,128]{3,2,1,0:T(2,128)S(1)} %pad_maximum_fusion.2), channel_id=1, source_target_pairs={{0,1},{1,2},{2,3},{4,5},{5,6},{6,7},{8,9},{9,10},{10,11},{12,13},{... | collective-permute-start | bytes 245768 | tf_op jit(solution)/shard_map/ppermute | solution.py:22
  15.5 3.6 %collective-permute-start.3 = (f32[10,8,2,128]{3,2,1,0:T(2,128)S(1)}, f32[10,8,2,128]{3,2,1,0:T(2,128)S(1)}, u32[]{:S(2)}, u32[]{:S(2)}) collective-permute-start(f32[10,8,2,128]{3,2,1,0:T(2,128)S(1)} %pad_maximum_fusion.3), channel_id=1, source_target_pairs={{1,0},{2,1},{3,2},{5,4},{6,5},{7,6},{9,8},{10,9},{11,10},{13,12},{... | collective-permute-start | bytes 245768 | tf_op jit(solution)/shard_map/ppermute | solution.py:22
  19.2 0.7 %pad_add_fusion.offsets = s32[2]{0:T(128)} fusion(s32[1]{0:T(128)} %bitcast.1, s32[1]{0:T(128)} %bitcast), kind=kLoop, calls=%fused_computation.22 | loop fusion | flops 2 | bytes 16 | tf_op jit(solution)/shard_map/stack | solution.py:193
  19.8 1.4 %collective-permute-done.3.yhi_ref = f32[10,8,2,128]{3,2,1,0:T(2,128)S(1)} collective-permute-done((f32[10,8,2,128]{3,2,1,0:T(2,128)S(1)}, f32[10,8,2,128]{3,2,1,0:T(2,128)S(1)}, u32[]{:S(2)}, u32[]{:S(2)}) %collective-permute-start.3) | collective-permute-done | bytes 81952 | tf_op jit(solution)/shard_map/ppermute | solution.py:22
  21.2 0.6 %copy-done.7 = f32[10,8,2,128]{3,2,1,0:T(2,128)} copy-done((f32[10,8,2,128]{3,2,1,0:T(2,128)}, f32[10,8,2,128]{3,2,1,0:T(2,128)S(1)}, u32[]{:S(2)}) %copy-start.7) | copy-done | bytes 81944
  21.8 3.1 %shard_map.94 = (f32[3,4,8,128]{3,2,1,0:T(8,128)}, f32[3,4,8,128]{3,2,1,0:T(8,128)}, f32[2,64]{1,0:T(2,128)}) custom-call(s32[2]{0:T(128)} %pad_add_fusion.offsets, f32[3,4,8,128]{3,2,1,0:T(8,128)} %e_ref.1, f32[3,4,8,128]{3,2,1,0:T(8,128)} %h_ref.1, f32[3,4,8,128]{3,2,1,0:T(8,128)} %perm_ref.1, f32[1,4,8,128]{3,2,1,0:T(8,128)} %bitcast.57, ...), custom_call_target="tpu_custom_call" | custom-call | tf_op jit(solution)/shard_map/pallas_call | solution.py:136
  24.9 0.6 %copy-done.9 = f32[2,64]{1,0:T(2,128)S(1)} copy-done((f32[2,64]{1,0:T(2,128)S(1)}, f32[2,64]{1,0:T(2,128)}, u32[]{:S(2)}) %copy-start.9) | copy-done | bytes 536
  25.6 0.1 reshape_reshape.7
  25.6 0.1 reshape.194
  25.7 0.1 reshape.197
  25.8 0.1 reshape.201
  26.0 2.7 %collective-permute-start.4 = (f32[2,4,1,8]{3,1,0,2:T(4,128)S(1)}, f32[2,4,1,8]{3,1,0,2:T(4,128)S(1)}, u32[]{:S(2)}, u32[]{:S(2)}) collective-permute-start(f32[2,4,1,8]{3,1,0,2:T(4,128)S(1)} %get-tuple-element.34), channel_id=1, source_target_pairs={{0,16},{4,20},{8,24},{12,28},{16,0},{20,4},{24,8},{28,12},{1,17},{... | collective-permute-start | bytes 776 | tf_op jit(solution)/shard_map/ppermute | solution.py:171
  28.7 1.9 %collective-permute-done.4 = f32[2,4,1,8]{3,1,0,2:T(4,128)S(1)} collective-permute-done((f32[2,4,1,8]{3,1,0,2:T(4,128)S(1)}, f32[2,4,1,8]{3,1,0,2:T(4,128)S(1)}, u32[]{:S(2)}, u32[]{:S(2)}) %collective-permute-start.4) | collective-permute-done | bytes 288 | tf_op jit(solution)/shard_map/ppermute | solution.py:171
  30.6 1.6 %collective-permute-start.5 = (f32[2,2,2,8]{3,2,1,0:T(2,128)S(1)}, f32[2,2,2,8]{3,2,1,0:T(2,128)S(1)}, u32[]{:S(2)}, u32[]{:S(2)}) collective-permute-start(f32[2,2,2,8]{3,2,1,0:T(2,128)S(1)} %get-tuple-element.32), channel_id=1, source_target_pairs={{0,8},{4,12},{8,0},{12,4},{16,24},{20,28},{24,16},{28,20},{1,9},{5... | collective-permute-start | bytes 776 | tf_op jit(solution)/shard_map/ppermute | solution.py:171
  32.3 2.0 %collective-permute-done.5 = f32[2,2,2,8]{3,2,1,0:T(2,128)S(1)} collective-permute-done((f32[2,2,2,8]{3,2,1,0:T(2,128)S(1)}, f32[2,2,2,8]{3,2,1,0:T(2,128)S(1)}, u32[]{:S(2)}, u32[]{:S(2)}) %collective-permute-start.5) | collective-permute-done | bytes 288 | tf_op jit(solution)/shard_map/ppermute | solution.py:171
  34.3 0.1 collective-permute-start.6
  34.4 0.1 eq.37
  34.5 3.5 %collective-permute-done.6 = f32[2,1,4,8]{3,2,1,0:T(4,128)S(1)} collective-permute-done((f32[2,1,4,8]{3,2,1,0:T(4,128)S(1)}, f32[2,1,4,8]{3,2,1,0:T(4,128)S(1)}, u32[]{:S(2)}, u32[]{:S(2)}) %collective-permute-start.6) | collective-permute-done | bytes 288 | tf_op jit(solution)/shard_map/ppermute | solution.py:171
  38.0 0.1 broadcast_in_dim.27
  38.1 0.6 %select_reduce_fusion = f32[128]{0:T(128)} fusion(f32[128]{0:T(128)S(1)} %broadcast_in_dim.27, s32[128]{0:T(128)S(1)} %eq.37), kind=kLoop, calls=%fused_computation.4 | loop fusion | flops 49024 | bytes 1536 | tf_op jit(solution)/shard_map/reduce_sum | solution.py:206
  (51 shorter events, 0.4 us)
Async XLA Ops:
  1.3 0.8 %copy-start.1 = (f32[3,4,8,128]{3,2,1,0:T(8,128)S(1)}, f32[3,4,8,128]{3,2,1,0:T(8,128)}, u32[]{:S(2)}) copy-start(f32[3,4,8,128]{3,2,1,0:T(8,128)} %e_ref.1) | copy-start | bytes 147460
  1.4 0.9 %copy-start.2 = (f32[3,4,8,128]{3,2,1,0:T(8,128)S(1)}, f32[3,4,8,128]{3,2,1,0:T(8,128)}, u32[]{:S(2)}) copy-start(f32[3,4,8,128]{3,2,1,0:T(8,128)} %h_ref.1) | copy-start | bytes 147460
  2.2 9.3 %collective-permute-start = (f32[10,2,8,128]{3,2,1,0:T(8,128)S(1)}, f32[10,2,8,128]{3,2,1,0:T(8,128)S(1)}, u32[]{:S(2)}, u32[]{:S(2)}) collective-permute-start(f32[10,2,8,128]{3,2,1,0:T(8,128)S(1)} %pad_maximum_fusion), channel_id=1, source_target_pairs={{0,4},{4,8},{8,12},{12,16},{16,20},{20,24},{24,28},{1,5},{5,9},{9,... | collective-permute-start | bytes 245768 | tf_op jit(solution)/shard_map/ppermute | solution.py:22
  5.7 2.5 %copy-start = (f32[3,4,8,128]{3,2,1,0:T(8,128)S(1)}, f32[3,4,8,128]{3,2,1,0:T(8,128)}, u32[]{:S(2)}) copy-start(f32[3,4,8,128]{3,2,1,0:T(8,128)} %perm_ref.1) | copy-start | bytes 147460
  5.7 7.2 %collective-permute-start.1 = (f32[10,2,8,128]{3,2,1,0:T(8,128)S(1)}, f32[10,2,8,128]{3,2,1,0:T(8,128)S(1)}, u32[]{:S(2)}, u32[]{:S(2)}) collective-permute-start(f32[10,2,8,128]{3,2,1,0:T(8,128)S(1)} %pad_maximum_fusion.1), channel_id=1, source_target_pairs={{4,0},{8,4},{12,8},{16,12},{20,16},{24,20},{28,24},{5,1},{9,5},{13... | collective-permute-start | bytes 245768 | tf_op jit(solution)/shard_map/ppermute | solution.py:22
  8.1 0.7 %copy-start.5 = (f32[4,8,128]{2,1,0:T(8,128)S(1)}, f32[4,8,128]{2,1,0:T(8,128)}, u32[]{:S(2)}) copy-start(f32[4,8,128]{2,1,0:T(8,128)} %param.10) | copy-start | bytes 49156
  8.9 0.7 %copy-start.10 = (s32[1,1,8,8]{3,2,1,0:T(8,128)S(1)}, s32[1,1,8,8]{3,2,1,0:T(8,128)}, u32[]{:S(2)}) copy-start(s32[1,1,8,8]{3,2,1,0:T(8,128)} %param.12) | copy-start | bytes 772
  8.9 1.3 %copy-start.11 = (f32[1,1,2,3,64]{4,2,3,1,0:T(2,128)S(1)}, f32[1,1,2,3,64]{4,2,3,1,0:T(2,128)}, u32[]{:S(2)}) copy-start(f32[1,1,2,3,64]{4,2,3,1,0:T(2,128)} %param.11) | copy-start | bytes 4612
  10.8 0.7 %copy-start.8 = (s32[1,1,8,8]{3,2,1,0:T(8,128)S(1)}, s32[1,1,8,8]{3,2,1,0:T(8,128)}, u32[]{:S(2)}) copy-start(s32[1,1,8,8]{3,2,1,0:T(8,128)} %param.13) | copy-start | bytes 772
  11.5 1.5 %copy-start.3 = (f32[10,2,8,128]{3,2,1,0:T(8,128)}, f32[10,2,8,128]{3,2,1,0:T(8,128)S(1)}, u32[]{:S(2)}) copy-start(f32[10,2,8,128]{3,2,1,0:T(8,128)S(1)} %collective-permute-done.xlo_ref) | copy-start | bytes 245764
  12.9 0.6 %copy-start.4 = (f32[10,2,8,128]{3,2,1,0:T(8,128)}, f32[10,2,8,128]{3,2,1,0:T(8,128)S(1)}, u32[]{:S(2)}) copy-start(f32[10,2,8,128]{3,2,1,0:T(8,128)S(1)} %collective-permute-done.1.xhi_ref) | copy-start | bytes 245764
  13.6 6.3 %collective-permute-start.2 = (f32[10,8,2,128]{3,2,1,0:T(2,128)S(1)}, f32[10,8,2,128]{3,2,1,0:T(2,128)S(1)}, u32[]{:S(2)}, u32[]{:S(2)}) collective-permute-start(f32[10,8,2,128]{3,2,1,0:T(2,128)S(1)} %pad_maximum_fusion.2), channel_id=1, source_target_pairs={{0,1},{1,2},{2,3},{4,5},{5,6},{6,7},{8,9},{9,10},{10,11},{12,13},{... | collective-permute-start | bytes 245768 | tf_op jit(solution)/shard_map/ppermute | solution.py:22
  15.5 5.7 %collective-permute-start.3 = (f32[10,8,2,128]{3,2,1,0:T(2,128)S(1)}, f32[10,8,2,128]{3,2,1,0:T(2,128)S(1)}, u32[]{:S(2)}, u32[]{:S(2)}) collective-permute-start(f32[10,8,2,128]{3,2,1,0:T(2,128)S(1)} %pad_maximum_fusion.3), channel_id=1, source_target_pairs={{1,0},{2,1},{3,2},{5,4},{6,5},{7,6},{9,8},{10,9},{11,10},{13,12},{... | collective-permute-start | bytes 245768 | tf_op jit(solution)/shard_map/ppermute | solution.py:22
  19.8 1.4 %copy-start.6 = (f32[10,8,2,128]{3,2,1,0:T(2,128)}, f32[10,8,2,128]{3,2,1,0:T(2,128)S(1)}, u32[]{:S(2)}) copy-start(f32[10,8,2,128]{3,2,1,0:T(2,128)S(1)} %collective-permute-done.2.ylo_ref) | copy-start | bytes 245764
  21.2 0.6 %copy-start.7 = (f32[10,8,2,128]{3,2,1,0:T(2,128)}, f32[10,8,2,128]{3,2,1,0:T(2,128)S(1)}, u32[]{:S(2)}) copy-start(f32[10,8,2,128]{3,2,1,0:T(2,128)S(1)} %collective-permute-done.3.yhi_ref) | copy-start | bytes 245764
  24.9 0.7 %copy-start.9 = (f32[2,64]{1,0:T(2,128)S(1)}, f32[2,64]{1,0:T(2,128)}, u32[]{:S(2)}) copy-start(f32[2,64]{1,0:T(2,128)} %get-tuple-element.8) | copy-start | bytes 1540
  26.0 4.6 %collective-permute-start.4 = (f32[2,4,1,8]{3,1,0,2:T(4,128)S(1)}, f32[2,4,1,8]{3,1,0,2:T(4,128)S(1)}, u32[]{:S(2)}, u32[]{:S(2)}) collective-permute-start(f32[2,4,1,8]{3,1,0,2:T(4,128)S(1)} %get-tuple-element.34), channel_id=1, source_target_pairs={{0,16},{4,20},{8,24},{12,28},{16,0},{20,4},{24,8},{28,12},{1,17},{... | collective-permute-start | bytes 776 | tf_op jit(solution)/shard_map/ppermute | solution.py:171
  30.6 3.7 %collective-permute-start.5 = (f32[2,2,2,8]{3,2,1,0:T(2,128)S(1)}, f32[2,2,2,8]{3,2,1,0:T(2,128)S(1)}, u32[]{:S(2)}, u32[]{:S(2)}) collective-permute-start(f32[2,2,2,8]{3,2,1,0:T(2,128)S(1)} %get-tuple-element.32), channel_id=1, source_target_pairs={{0,8},{4,12},{8,0},{12,4},{16,24},{20,28},{24,16},{28,20},{1,9},{5... | collective-permute-start | bytes 776 | tf_op jit(solution)/shard_map/ppermute | solution.py:171
  34.3 3.7 %collective-permute-start.6 = (f32[2,1,4,8]{3,2,1,0:T(4,128)S(1)}, f32[2,1,4,8]{3,2,1,0:T(4,128)S(1)}, u32[]{:S(2)}, u32[]{:S(2)}) collective-permute-start(f32[2,1,4,8]{3,2,1,0:T(4,128)S(1)} %get-tuple-element.30), channel_id=1, source_target_pairs={{0,4},{4,0},{8,12},{12,8},{16,20},{20,16},{24,28},{28,24},{1,5},{5... | collective-permute-start | bytes 776 | tf_op jit(solution)/shard_map/ppermute | solution.py:171

commit v6 on v4

--- a/solution.py
+++ b/solution.py
@@ -189,9 +189,10 @@
         received, segments = exchange_by_halving(products, segments, sources)
     else:
         received = lax.all_to_all(products, "slab", split_axis=1, concat_axis=1, tiled=True)
-    segments = jnp.broadcast_to(segments[None], received.shape)
-    gradient = jax.ops.segment_sum(received.reshape(-1), segments.reshape(-1), num_segments=PAR_DEV + 1)
-    return (new_e, new_h, gradient[:PAR_DEV].reshape(1, 1, PAR_DEV))
+    segments = jnp.broadcast_to(segments[None], received.shape).reshape(-1, 1)
+    params = lax.broadcasted_iota(jnp.int32, (1, PAR_DEV), 1)
+    gradient = jnp.sum(jnp.where(segments == params, received.reshape(-1, 1), 0.0), axis=0)
+    return (new_e, new_h, gradient.reshape(1, 1, PAR_DEV))
 
 
 def solution(mesh):

time: 39.8 us -> 38.5 us (0.967)
  other arithmetic: 2.23 us -> 1.44 us
  waiting for transfers between devices: 10.8 us -> 10.2 us
    scatter-add x1 -> x0, other arithmetic: 1.43 us -> none  [shards(): jax.ops.segment_sum(received.reshape(-1), segments.reshape(-1), num_segme...]
    reduce_sum x0 -> x1, other arithmetic: none -> 0.63 us  [shards(): jnp.sum(jnp.where(segments == params, received.reshape(-1, 1), 0.0), axis=0)]
    unnamed x25, local copies, waits for them, and re-layouts: 3.99 us -> 4.58 us
    ppermute x4, waiting for transfers between devices: 3.35 us -> 2.79 us  [recv_from(): return lax.ppermute(array, axis, pairs)]
    reshape x1 -> x0, local copies, waits for them, and re-layouts: 0.51 us -> none  [shards(): return (new_e, new_h, gradient[:PAR_DEV].reshape(1, 1, PAR_DEV))]
  transfers between devices with their start and end apart: 7 -> 7, of which waited for: 5 -> 5; matrix products, arithmetic and copies ran while one was open for 5% -> 6% of each run, Pallas kernels for 0% -> 0%
where the time goes in v6:
time: 38.5 us; the launch traced here: 38 us
  starting transfers between devices  15.8 us (41%)
  waiting for transfers between devices  10.2 us (26%)
  local copies, waits for them, and re-layouts  7.37 us (19%)
  Pallas kernels  2.31 us (6%)
  other arithmetic  1.44 us (4%)
  between operations  0.89 us (2%)
    ppermute x4, starting transfers between devices, recv_from(): return lax.ppermute(array, axis, pairs)  11.4 us
    ppermute x3, waiting for transfers between devices, exchange_by_halving(): got = lax.ppermute(send, 'slab', pairs)  7.41 us
    unnamed x25, local copies, waits for them, and re-layouts  4.58 us
    ppermute x3, starting transfers between devices, exchange_by_halving(): got = lax.ppermute(send, 'slab', pairs)  4.37 us
    ppermute x4, waiting for transfers between devices, recv_from(): return lax.ppermute(array, axis, pairs)  2.79 us
    pallas_call x1, Pallas kernels, leapfrog(): pl.pallas_call(kernel, out_shape=(jax.ShapeDtypeStruct(field_e.shape, jnp...  2.31 us
    slice x3, local copies, waits for them, and re-layouts, shards(): xhi = recv_from(jnp.concatenate([p[:, :HALO] for p in parts], 0), 'slab', 1)  1.49 us
  transfers between devices with their start and end apart: 7, of which 5 were waited for; matrix products, arithmetic and copies ran while one was open for 6% of the time, Pallas kernels for 0%

profile of v6, /device:TPU:6, one launch (start us, length us, event | category | flops | bytes accessed | tf_op | source)
XLA Modules:
  0.0 38.0 jit_solution(1445880777148005561)
XLA Ops:
  0.6 0.7 %fusion.11 = (f32[1,2,8,128]{3,2,1,0:T(8,128)S(1)}, f32[1,2,8,128]{3,2,1,0:T(8,128)S(1)}) fusion(f32[1,4,8,128]{3,2,1,0:T(8,128)} %bitcast.56), kind=kLoop, calls=%fused_computation.32 | loop fusion | bytes 32768 | tf_op jit(solution)/shard_map/slice | solution.py:174
  1.4 0.8 %fusion.9 = (f32[3,2,8,128]{3,2,1,0:T(8,128)S(1)}, f32[3,2,8,128]{3,2,1,0:T(8,128)S(1)}) fusion(f32[3,4,8,128]{3,2,1,0:T(8,128)} %perm_ref.1), kind=kLoop, calls=%fused_computation.30 | loop fusion | bytes 98304 | tf_op jit(solution)/shard_map/slice | solution.py:174
  2.1 0.1 copy-done.1
  2.2 3.4 %collective-permute-start = (f32[10,2,8,128]{3,2,1,0:T(8,128)S(1)}, f32[10,2,8,128]{3,2,1,0:T(8,128)S(1)}, u32[]{:S(2)}, u32[]{:S(2)}) collective-permute-start(f32[10,2,8,128]{3,2,1,0:T(8,128)S(1)} %pad_maximum_fusion), channel_id=1, source_target_pairs={{0,4},{4,8},{8,12},{12,16},{16,20},{20,24},{24,28},{1,5},{5,9},{9,... | collective-permute-start | bytes 245768 | tf_op jit(solution)/shard_map/ppermute | solution.py:22
  5.7 2.4 %collective-permute-start.1 = (f32[10,2,8,128]{3,2,1,0:T(8,128)S(1)}, f32[10,2,8,128]{3,2,1,0:T(8,128)S(1)}, u32[]{:S(2)}, u32[]{:S(2)}) collective-permute-start(f32[10,2,8,128]{3,2,1,0:T(8,128)S(1)} %pad_maximum_fusion.1), channel_id=1, source_target_pairs={{4,0},{8,4},{12,8},{16,12},{20,16},{24,20},{28,24},{5,1},{9,5},{13... | collective-permute-start | bytes 245768 | tf_op jit(solution)/shard_map/ppermute | solution.py:22
  8.2 0.7 %copy-done.5 = f32[4,8,128]{2,1,0:T(8,128)S(1)} copy-done((f32[4,8,128]{2,1,0:T(8,128)S(1)}, f32[4,8,128]{2,1,0:T(8,128)}, u32[]{:S(2)}) %copy-start.5) | copy-done | bytes 16408
  8.9 0.7 %copy-done.10 = s32[1,1,8,8]{3,2,1,0:T(8,128)S(1)} copy-done((s32[1,1,8,8]{3,2,1,0:T(8,128)S(1)}, s32[1,1,8,8]{3,2,1,0:T(8,128)}, u32[]{:S(2)}) %copy-start.10) | copy-done | bytes 280
  9.6 0.6 %reshape.183.cell_ref = s32[1,64]{1,0:T(1,128)} reshape(s32[1,1,8,8]{3,2,1,0:T(8,128)S(1)} %copy-done.10) | data formatting | bytes 512 | tf_op jit(solution)/shard_map/reshape | solution.py:184
  10.2 0.6 %copy.21 = f32[1,1,2,3,64]{4,3,2,1,0:T(4,128)} copy(f32[1,1,2,3,64]{4,2,3,1,0:T(2,128)S(1)} %copy-done.11) | data formatting | bytes 3072 | tf_op args[4]
  10.8 0.7 %copy-done.8 = s32[1,1,8,8]{3,2,1,0:T(8,128)S(1)} copy-done((s32[1,1,8,8]{3,2,1,0:T(8,128)S(1)}, s32[1,1,8,8]{3,2,1,0:T(8,128)}, u32[]{:S(2)}) %copy-start.8) | copy-done | bytes 280
  11.5 1.4 %collective-permute-done.1.xhi_ref = f32[10,2,8,128]{3,2,1,0:T(8,128)S(1)} collective-permute-done((f32[10,2,8,128]{3,2,1,0:T(8,128)S(1)}, f32[10,2,8,128]{3,2,1,0:T(8,128)S(1)}, u32[]{:S(2)}, u32[]{:S(2)}) %collective-permute-start.1) | collective-permute-done | bytes 81952 | tf_op jit(solution)/shard_map/ppermute | solution.py:22
  13.0 0.6 %copy-done.4 = f32[10,2,8,128]{3,2,1,0:T(8,128)} copy-done((f32[10,2,8,128]{3,2,1,0:T(8,128)}, f32[10,2,8,128]{3,2,1,0:T(8,128)S(1)}, u32[]{:S(2)}) %copy-start.4) | copy-done | bytes 81944
  13.6 1.9 %collective-permute-start.2 = (f32[10,8,2,128]{3,2,1,0:T(2,128)S(1)}, f32[10,8,2,128]{3,2,1,0:T(2,128)S(1)}, u32[]{:S(2)}, u32[]{:S(2)}) collective-permute-start(f32[10,8,2,128]{3,2,1,0:T(2,128)S(1)} %pad_maximum_fusion.2), channel_id=1, source_target_pairs={{0,1},{1,2},{2,3},{4,5},{5,6},{6,7},{8,9},{9,10},{10,11},{12,13},{... | collective-permute-start | bytes 245768 | tf_op jit(solution)/shard_map/ppermute | solution.py:22
  15.5 3.6 %collective-permute-start.3 = (f32[10,8,2,128]{3,2,1,0:T(2,128)S(1)}, f32[10,8,2,128]{3,2,1,0:T(2,128)S(1)}, u32[]{:S(2)}, u32[]{:S(2)}) collective-permute-start(f32[10,8,2,128]{3,2,1,0:T(2,128)S(1)} %pad_maximum_fusion.3), channel_id=1, source_target_pairs={{1,0},{2,1},{3,2},{5,4},{6,5},{7,6},{9,8},{10,9},{11,10},{13,12},{... | collective-permute-start | bytes 245768 | tf_op jit(solution)/shard_map/ppermute | solution.py:22
  19.2 0.7 %pad_add_fusion.offsets = s32[2]{0:T(128)} fusion(s32[1]{0:T(128)} %bitcast.1, s32[1]{0:T(128)} %bitcast), kind=kLoop, calls=%fused_computation.22 | loop fusion | flops 2 | bytes 16 | tf_op jit(solution)/shard_map/stack | solution.py:181
  19.8 1.4 %collective-permute-done.3.yhi_ref = f32[10,8,2,128]{3,2,1,0:T(2,128)S(1)} collective-permute-done((f32[10,8,2,128]{3,2,1,0:T(2,128)S(1)}, f32[10,8,2,128]{3,2,1,0:T(2,128)S(1)}, u32[]{:S(2)}, u32[]{:S(2)}) %collective-permute-start.3) | collective-permute-done | bytes 81952 | tf_op jit(solution)/shard_map/ppermute | solution.py:22
  21.2 0.6 %copy-done.7 = f32[10,8,2,128]{3,2,1,0:T(2,128)} copy-done((f32[10,8,2,128]{3,2,1,0:T(2,128)}, f32[10,8,2,128]{3,2,1,0:T(2,128)S(1)}, u32[]{:S(2)}) %copy-start.7) | copy-done | bytes 81944
  21.8 2.3 %shard_map.94 = (f32[3,4,8,128]{3,2,1,0:T(8,128)}, f32[3,4,8,128]{3,2,1,0:T(8,128)}, f32[2,64]{1,0:T(2,128)}) custom-call(s32[2]{0:T(128)} %pad_add_fusion.offsets, f32[3,4,8,128]{3,2,1,0:T(8,128)} %e_ref.1, f32[3,4,8,128]{3,2,1,0:T(8,128)} %h_ref.1, f32[3,4,8,128]{3,2,1,0:T(8,128)} %perm_ref.1, f32[1,4,8,128]{3,2,1,0:T(8,128)} %bitcast.57, ...), custom_call_target="tpu_custom_call" | custom-call | tf_op jit(solution)/shard_map/pallas_call | solution.py:126
  24.1 0.7 %copy-done.9 = f32[2,64]{1,0:T(2,128)S(1)} copy-done((f32[2,64]{1,0:T(2,128)S(1)}, f32[2,64]{1,0:T(2,128)}, u32[]{:S(2)}) %copy-start.9) | copy-done | bytes 536
  24.8 0.1 reshape_reshape.7
  24.9 0.1 reshape.194
  25.0 0.1 reshape.197
  25.1 0.1 reshape.201
  25.3 2.7 %collective-permute-start.4 = (f32[2,4,1,8]{3,1,0,2:T(4,128)S(1)}, f32[2,4,1,8]{3,1,0,2:T(4,128)S(1)}, u32[]{:S(2)}, u32[]{:S(2)}) collective-permute-start(f32[2,4,1,8]{3,1,0,2:T(4,128)S(1)} %get-tuple-element.34), channel_id=1, source_target_pairs={{0,16},{4,20},{8,24},{12,28},{16,0},{20,4},{24,8},{28,12},{1,17},{... | collective-permute-start | bytes 776 | tf_op jit(solution)/shard_map/ppermute | solution.py:159
  27.9 1.9 %collective-permute-done.4 = f32[2,4,1,8]{3,1,0,2:T(4,128)S(1)} collective-permute-done((f32[2,4,1,8]{3,1,0,2:T(4,128)S(1)}, f32[2,4,1,8]{3,1,0,2:T(4,128)S(1)}, u32[]{:S(2)}, u32[]{:S(2)}) %collective-permute-start.4) | collective-permute-done | bytes 288 | tf_op jit(solution)/shard_map/ppermute | solution.py:159
  29.9 1.6 %collective-permute-start.5 = (f32[2,2,2,8]{3,2,1,0:T(2,128)S(1)}, f32[2,2,2,8]{3,2,1,0:T(2,128)S(1)}, u32[]{:S(2)}, u32[]{:S(2)}) collective-permute-start(f32[2,2,2,8]{3,2,1,0:T(2,128)S(1)} %get-tuple-element.32), channel_id=1, source_target_pairs={{0,8},{4,12},{8,0},{12,4},{16,24},{20,28},{24,16},{28,20},{1,9},{5... | collective-permute-start | bytes 776 | tf_op jit(solution)/shard_map/ppermute | solution.py:159
  31.5 2.0 %collective-permute-done.5 = f32[2,2,2,8]{3,2,1,0:T(2,128)S(1)} collective-permute-done((f32[2,2,2,8]{3,2,1,0:T(2,128)S(1)}, f32[2,2,2,8]{3,2,1,0:T(2,128)S(1)}, u32[]{:S(2)}, u32[]{:S(2)}) %collective-permute-start.5) | collective-permute-done | bytes 288 | tf_op jit(solution)/shard_map/ppermute | solution.py:159
  33.6 0.1 collective-permute-start.6
  33.7 0.1 eq.37
  33.7 3.5 %collective-permute-done.6 = f32[2,1,4,8]{3,2,1,0:T(4,128)S(1)} collective-permute-done((f32[2,1,4,8]{3,2,1,0:T(4,128)S(1)}, f32[2,1,4,8]{3,2,1,0:T(4,128)S(1)}, u32[]{:S(2)}, u32[]{:S(2)}) %collective-permute-start.6) | collective-permute-done | bytes 288 | tf_op jit(solution)/shard_map/ppermute | solution.py:159
  37.2 0.1 broadcast_in_dim.27
  37.3 0.6 %select_reduce_fusion = f32[128]{0:T(128)} fusion(f32[128]{0:T(128)S(1)} %broadcast_in_dim.27, s32[128]{0:T(128)S(1)} %eq.37), kind=kLoop, calls=%fused_computation.4 | loop fusion | flops 49024 | bytes 1536 | tf_op jit(solution)/shard_map/reduce_sum | solution.py:194
  (51 shorter events, 0.4 us)
Async XLA Ops:
  1.3 0.8 %copy-start.1 = (f32[3,4,8,128]{3,2,1,0:T(8,128)S(1)}, f32[3,4,8,128]{3,2,1,0:T(8,128)}, u32[]{:S(2)}) copy-start(f32[3,4,8,128]{3,2,1,0:T(8,128)} %e_ref.1) | copy-start | bytes 147460
  1.4 0.9 %copy-start.2 = (f32[3,4,8,128]{3,2,1,0:T(8,128)S(1)}, f32[3,4,8,128]{3,2,1,0:T(8,128)}, u32[]{:S(2)}) copy-start(f32[3,4,8,128]{3,2,1,0:T(8,128)} %h_ref.1) | copy-start | bytes 147460
  2.2 9.3 %collective-permute-start = (f32[10,2,8,128]{3,2,1,0:T(8,128)S(1)}, f32[10,2,8,128]{3,2,1,0:T(8,128)S(1)}, u32[]{:S(2)}, u32[]{:S(2)}) collective-permute-start(f32[10,2,8,128]{3,2,1,0:T(8,128)S(1)} %pad_maximum_fusion), channel_id=1, source_target_pairs={{0,4},{4,8},{8,12},{12,16},{16,20},{20,24},{24,28},{1,5},{5,9},{9,... | collective-permute-start | bytes 245768 | tf_op jit(solution)/shard_map/ppermute | solution.py:22
  5.7 2.5 %copy-start = (f32[3,4,8,128]{3,2,1,0:T(8,128)S(1)}, f32[3,4,8,128]{3,2,1,0:T(8,128)}, u32[]{:S(2)}) copy-start(f32[3,4,8,128]{3,2,1,0:T(8,128)} %perm_ref.1) | copy-start | bytes 147460
  5.7 7.2 %collective-permute-start.1 = (f32[10,2,8,128]{3,2,1,0:T(8,128)S(1)}, f32[10,2,8,128]{3,2,1,0:T(8,128)S(1)}, u32[]{:S(2)}, u32[]{:S(2)}) collective-permute-start(f32[10,2,8,128]{3,2,1,0:T(8,128)S(1)} %pad_maximum_fusion.1), channel_id=1, source_target_pairs={{4,0},{8,4},{12,8},{16,12},{20,16},{24,20},{28,24},{5,1},{9,5},{13... | collective-permute-start | bytes 245768 | tf_op jit(solution)/shard_map/ppermute | solution.py:22
  8.1 0.7 %copy-start.5 = (f32[4,8,128]{2,1,0:T(8,128)S(1)}, f32[4,8,128]{2,1,0:T(8,128)}, u32[]{:S(2)}) copy-start(f32[4,8,128]{2,1,0:T(8,128)} %param.10) | copy-start | bytes 49156
  8.9 0.7 %copy-start.10 = (s32[1,1,8,8]{3,2,1,0:T(8,128)S(1)}, s32[1,1,8,8]{3,2,1,0:T(8,128)}, u32[]{:S(2)}) copy-start(s32[1,1,8,8]{3,2,1,0:T(8,128)} %param.12) | copy-start | bytes 772
  8.9 1.3 %copy-start.11 = (f32[1,1,2,3,64]{4,2,3,1,0:T(2,128)S(1)}, f32[1,1,2,3,64]{4,2,3,1,0:T(2,128)}, u32[]{:S(2)}) copy-start(f32[1,1,2,3,64]{4,2,3,1,0:T(2,128)} %param.11) | copy-start | bytes 4612
  10.8 0.7 %copy-start.8 = (s32[1,1,8,8]{3,2,1,0:T(8,128)S(1)}, s32[1,1,8,8]{3,2,1,0:T(8,128)}, u32[]{:S(2)}) copy-start(s32[1,1,8,8]{3,2,1,0:T(8,128)} %param.13) | copy-start | bytes 772
  11.5 1.5 %copy-start.3 = (f32[10,2,8,128]{3,2,1,0:T(8,128)}, f32[10,2,8,128]{3,2,1,0:T(8,128)S(1)}, u32[]{:S(2)}) copy-start(f32[10,2,8,128]{3,2,1,0:T(8,128)S(1)} %collective-permute-done.xlo_ref) | copy-start | bytes 245764
  12.9 0.6 %copy-start.4 = (f32[10,2,8,128]{3,2,1,0:T(8,128)}, f32[10,2,8,128]{3,2,1,0:T(8,128)S(1)}, u32[]{:S(2)}) copy-start(f32[10,2,8,128]{3,2,1,0:T(8,128)S(1)} %collective-permute-done.1.xhi_ref) | copy-start | bytes 245764
  13.6 6.3 %collective-permute-start.2 = (f32[10,8,2,128]{3,2,1,0:T(2,128)S(1)}, f32[10,8,2,128]{3,2,1,0:T(2,128)S(1)}, u32[]{:S(2)}, u32[]{:S(2)}) collective-permute-start(f32[10,8,2,128]{3,2,1,0:T(2,128)S(1)} %pad_maximum_fusion.2), channel_id=1, source_target_pairs={{0,1},{1,2},{2,3},{4,5},{5,6},{6,7},{8,9},{9,10},{10,11},{12,13},{... | collective-permute-start | bytes 245768 | tf_op jit(solution)/shard_map/ppermute | solution.py:22
  15.5 5.7 %collective-permute-start.3 = (f32[10,8,2,128]{3,2,1,0:T(2,128)S(1)}, f32[10,8,2,128]{3,2,1,0:T(2,128)S(1)}, u32[]{:S(2)}, u32[]{:S(2)}) collective-permute-start(f32[10,8,2,128]{3,2,1,0:T(2,128)S(1)} %pad_maximum_fusion.3), channel_id=1, source_target_pairs={{1,0},{2,1},{3,2},{5,4},{6,5},{7,6},{9,8},{10,9},{11,10},{13,12},{... | collective-permute-start | bytes 245768 | tf_op jit(solution)/shard_map/ppermute | solution.py:22
  19.8 1.4 %copy-start.6 = (f32[10,8,2,128]{3,2,1,0:T(2,128)}, f32[10,8,2,128]{3,2,1,0:T(2,128)S(1)}, u32[]{:S(2)}) copy-start(f32[10,8,2,128]{3,2,1,0:T(2,128)S(1)} %collective-permute-done.2.ylo_ref) | copy-start | bytes 245764
  21.2 0.6 %copy-start.7 = (f32[10,8,2,128]{3,2,1,0:T(2,128)}, f32[10,8,2,128]{3,2,1,0:T(2,128)S(1)}, u32[]{:S(2)}) copy-start(f32[10,8,2,128]{3,2,1,0:T(2,128)S(1)} %collective-permute-done.3.yhi_ref) | copy-start | bytes 245764
  24.1 0.7 %copy-start.9 = (f32[2,64]{1,0:T(2,128)S(1)}, f32[2,64]{1,0:T(2,128)}, u32[]{:S(2)}) copy-start(f32[2,64]{1,0:T(2,128)} %get-tuple-element.8) | copy-start | bytes 1540
  25.3 4.6 %collective-permute-start.4 = (f32[2,4,1,8]{3,1,0,2:T(4,128)S(1)}, f32[2,4,1,8]{3,1,0,2:T(4,128)S(1)}, u32[]{:S(2)}, u32[]{:S(2)}) collective-permute-start(f32[2,4,1,8]{3,1,0,2:T(4,128)S(1)} %get-tuple-element.34), channel_id=1, source_target_pairs={{0,16},{4,20},{8,24},{12,28},{16,0},{20,4},{24,8},{28,12},{1,17},{... | collective-permute-start | bytes 776 | tf_op jit(solution)/shard_map/ppermute | solution.py:159
  29.9 3.7 %collective-permute-start.5 = (f32[2,2,2,8]{3,2,1,0:T(2,128)S(1)}, f32[2,2,2,8]{3,2,1,0:T(2,128)S(1)}, u32[]{:S(2)}, u32[]{:S(2)}) collective-permute-start(f32[2,2,2,8]{3,2,1,0:T(2,128)S(1)} %get-tuple-element.32), channel_id=1, source_target_pairs={{0,8},{4,12},{8,0},{12,4},{16,24},{20,28},{24,16},{28,20},{1,9},{5... | collective-permute-start | bytes 776 | tf_op jit(solution)/shard_map/ppermute | solution.py:159
  33.6 3.7 %collective-permute-start.6 = (f32[2,1,4,8]{3,2,1,0:T(4,128)S(1)}, f32[2,1,4,8]{3,2,1,0:T(4,128)S(1)}, u32[]{:S(2)}, u32[]{:S(2)}) collective-permute-start(f32[2,1,4,8]{3,2,1,0:T(4,128)S(1)} %get-tuple-element.30), channel_id=1, source_target_pairs={{0,4},{4,0},{8,12},{12,8},{16,20},{20,16},{24,28},{28,24},{1,5},{5... | collective-permute-start | bytes 776 | tf_op jit(solution)/shard_map/ppermute | solution.py:159

commit v7 on v6

--- a/solution.py
+++ b/solution.py
@@ -11,6 +11,7 @@
 PAR_DEV = 128
 HALO = 2
 LANES = 128
+RADIX = 4
 
 CH_GAIN = 0.5
 CE_GAIN = 0.5
@@ -151,7 +152,7 @@
     me = lax.axis_index("slab")
     held = xor_rows(products, me, count, 1)[:, :, None]
     bit = count // 2
-    while bit >= 1:
+    while bit >= RADIX:
         owners = held.shape[1]
         keep = held[:, : owners // 2]
         send = held[:, owners // 2 :]
@@ -159,7 +160,13 @@
         got = lax.ppermute(send, "slab", pairs)
         held = jnp.stack([keep, got], 3).reshape(keep.shape[:2] + (keep.shape[2] * 2,) + keep.shape[3:])
         bit //= 2
-    return held[:, 0], xor_rows(segments, me, count, 0)
+    owners = held.shape[1]
+    pieces = [held[:, 0]]
+    for q in range(1, owners):
+        pieces.append(lax.ppermute(held[:, q], "slab", [(i, i ^ q) for i in range(count)]))
+    held = jnp.stack(pieces, 2)
+    held = held.reshape(held.shape[:1] + (held.shape[1] * owners,) + held.shape[3:])
+    return held, xor_rows(segments, me, count, 0)
 
 
 def shards(field_e, field_h, permittivity, conductivity, forward_e, slot_cell, recv_param):

time: 38.5 us -> 37.7 us (0.979)
  the two profiles are of different devices: /device:TPU:6 before, /device:TPU:2 now
where the time goes in v7:
time: 37.7 us; the launch traced here: 37.2 us
  starting transfers between devices  17.1 us (45%)
  waiting for transfers between devices  8.81 us (23%)
  local copies, waits for them, and re-layouts  6.67 us (18%)
  Pallas kernels  2.31 us (6%)
  other arithmetic  1.43 us (4%)
  between operations  0.96 us (3%)
    ppermute x4, starting transfers between devices, recv_from(): return lax.ppermute(array, axis, pairs)  10.3 us
    ppermute x3, starting transfers between devices, exchange_by_halving(): lax.ppermute(held[:, q], 'slab', [(i, i ^ q) for i in range(count)])  4.14 us
    unnamed x25, local copies, waits for them, and re-layouts  3.88 us
    ppermute x4, waiting for transfers between devices, recv_from(): return lax.ppermute(array, axis, pairs)  3.61 us
    ppermute x3, waiting for transfers between devices, exchange_by_halving(): lax.ppermute(held[:, q], 'slab', [(i, i ^ q) for i in range(count)])  3.39 us
    ppermute x1, starting transfers between devices, exchange_by_halving(): got = lax.ppermute(send, 'slab', pairs)  2.65 us
    pallas_call x1, Pallas kernels, leapfrog(): pl.pallas_call(kernel, out_shape=(jax.ShapeDtypeStruct(field_e.shape, jnp...  2.31 us
    ppermute x1, waiting for transfers between devices, exchange_by_halving(): got = lax.ppermute(send, 'slab', pairs)  1.82 us
  transfers between devices with their start and end apart: 8, of which 6 were waited for; matrix products, arithmetic and copies ran while one was open for 6% of the time, Pallas kernels for 0%

profile of v7, /device:TPU:2, one launch (start us, length us, event | category | flops | bytes accessed | tf_op | source)
XLA Modules:
  0.0 37.2 jit_solution(6307159234239458967)
XLA Ops:
  0.6 0.7 %fusion.11 = (f32[1,2,8,128]{3,2,1,0:T(8,128)S(1)}, f32[1,2,8,128]{3,2,1,0:T(8,128)S(1)}) fusion(f32[1,4,8,128]{3,2,1,0:T(8,128)} %bitcast.58), kind=kLoop, calls=%fused_computation.33 | loop fusion | bytes 32768 | tf_op jit(solution)/shard_map/slice | solution.py:181
  1.4 0.8 %fusion.9 = (f32[3,2,8,128]{3,2,1,0:T(8,128)S(1)}, f32[3,2,8,128]{3,2,1,0:T(8,128)S(1)}) fusion(f32[3,4,8,128]{3,2,1,0:T(8,128)} %perm_ref.1), kind=kLoop, calls=%fused_computation.31 | loop fusion | bytes 98304 | tf_op jit(solution)/shard_map/slice | solution.py:181
  2.2 3.4 %collective-permute-start = (f32[10,2,8,128]{3,2,1,0:T(8,128)S(1)}, f32[10,2,8,128]{3,2,1,0:T(8,128)S(1)}, u32[]{:S(2)}, u32[]{:S(2)}) collective-permute-start(f32[10,2,8,128]{3,2,1,0:T(8,128)S(1)} %pad_maximum_fusion), channel_id=1, source_target_pairs={{0,4},{4,8},{8,12},{12,16},{16,20},{20,24},{24,28},{1,5},{5,9},{9,... | collective-permute-start | bytes 245768 | tf_op jit(solution)/shard_map/ppermute | solution.py:23
  5.7 1.3 %collective-permute-start.1 = (f32[10,2,8,128]{3,2,1,0:T(8,128)S(1)}, f32[10,2,8,128]{3,2,1,0:T(8,128)S(1)}, u32[]{:S(2)}, u32[]{:S(2)}) collective-permute-start(f32[10,2,8,128]{3,2,1,0:T(8,128)S(1)} %pad_maximum_fusion.1), channel_id=1, source_target_pairs={{4,0},{8,4},{12,8},{16,12},{20,16},{24,20},{28,24},{5,1},{9,5},{13... | collective-permute-start | bytes 245768 | tf_op jit(solution)/shard_map/ppermute | solution.py:23
  7.1 0.7 %copy-done.8 = s32[1,1,8,8]{3,2,1,0:T(8,128)S(1)} copy-done((s32[1,1,8,8]{3,2,1,0:T(8,128)S(1)}, s32[1,1,8,8]{3,2,1,0:T(8,128)}, u32[]{:S(2)}) %copy-start.8) | copy-done | bytes 280
  7.9 0.7 %copy-done.10 = s32[1,1,8,8]{3,2,1,0:T(8,128)S(1)} copy-done((s32[1,1,8,8]{3,2,1,0:T(8,128)S(1)}, s32[1,1,8,8]{3,2,1,0:T(8,128)}, u32[]{:S(2)}) %copy-start.10) | copy-done | bytes 280
  8.6 0.6 %reshape.180.cell_ref = s32[1,64]{1,0:T(1,128)} reshape(s32[1,1,8,8]{3,2,1,0:T(8,128)S(1)} %copy-done.10) | data formatting | bytes 512 | tf_op jit(solution)/shard_map/reshape | solution.py:191
  9.2 0.6 %copy.19 = f32[1,1,2,3,64]{4,3,2,1,0:T(4,128)} copy(f32[1,1,2,3,64]{4,2,3,1,0:T(2,128)S(1)} %copy-done.11) | data formatting | bytes 3072 | tf_op args[4]
  9.8 2.2 %collective-permute-done.1.xhi_ref = f32[10,2,8,128]{3,2,1,0:T(8,128)S(1)} collective-permute-done((f32[10,2,8,128]{3,2,1,0:T(8,128)S(1)}, f32[10,2,8,128]{3,2,1,0:T(8,128)S(1)}, u32[]{:S(2)}, u32[]{:S(2)}) %collective-permute-start.1) | collective-permute-done | bytes 81952 | tf_op jit(solution)/shard_map/ppermute | solution.py:23
  12.1 0.6 %copy-done.4 = f32[10,2,8,128]{3,2,1,0:T(8,128)} copy-done((f32[10,2,8,128]{3,2,1,0:T(8,128)}, f32[10,2,8,128]{3,2,1,0:T(8,128)S(1)}, u32[]{:S(2)}) %copy-start.4) | copy-done | bytes 81944
  12.7 1.9 %collective-permute-start.2 = (f32[10,8,2,128]{3,2,1,0:T(2,128)S(1)}, f32[10,8,2,128]{3,2,1,0:T(2,128)S(1)}, u32[]{:S(2)}, u32[]{:S(2)}) collective-permute-start(f32[10,8,2,128]{3,2,1,0:T(2,128)S(1)} %pad_maximum_fusion.2), channel_id=1, source_target_pairs={{0,1},{1,2},{2,3},{4,5},{5,6},{6,7},{8,9},{9,10},{10,11},{12,13},{... | collective-permute-start | bytes 245768 | tf_op jit(solution)/shard_map/ppermute | solution.py:23
  14.6 3.6 %collective-permute-start.3 = (f32[10,8,2,128]{3,2,1,0:T(2,128)S(1)}, f32[10,8,2,128]{3,2,1,0:T(2,128)S(1)}, u32[]{:S(2)}, u32[]{:S(2)}) collective-permute-start(f32[10,8,2,128]{3,2,1,0:T(2,128)S(1)} %pad_maximum_fusion.3), channel_id=1, source_target_pairs={{1,0},{2,1},{3,2},{5,4},{6,5},{7,6},{9,8},{10,9},{11,10},{13,12},{... | collective-permute-start | bytes 245768 | tf_op jit(solution)/shard_map/ppermute | solution.py:23
  18.3 0.7 %pad_add_fusion.offsets = s32[2]{0:T(128)} fusion(s32[1]{0:T(128)} %bitcast.1, s32[1]{0:T(128)} %bitcast), kind=kLoop, calls=%fused_computation.23 | loop fusion | flops 2 | bytes 16 | tf_op jit(solution)/shard_map/stack | solution.py:188
  18.9 1.4 %collective-permute-done.3.yhi_ref = f32[10,8,2,128]{3,2,1,0:T(2,128)S(1)} collective-permute-done((f32[10,8,2,128]{3,2,1,0:T(2,128)S(1)}, f32[10,8,2,128]{3,2,1,0:T(2,128)S(1)}, u32[]{:S(2)}, u32[]{:S(2)}) %collective-permute-start.3) | collective-permute-done | bytes 81952 | tf_op jit(solution)/shard_map/ppermute | solution.py:23
  20.3 0.6 %copy-done.7 = f32[10,8,2,128]{3,2,1,0:T(2,128)} copy-done((f32[10,8,2,128]{3,2,1,0:T(2,128)}, f32[10,8,2,128]{3,2,1,0:T(2,128)S(1)}, u32[]{:S(2)}) %copy-start.7) | copy-done | bytes 81944
  20.9 2.3 %shard_map.94 = (f32[3,4,8,128]{3,2,1,0:T(8,128)}, f32[3,4,8,128]{3,2,1,0:T(8,128)}, f32[2,64]{1,0:T(2,128)}) custom-call(s32[2]{0:T(128)} %pad_add_fusion.offsets, f32[3,4,8,128]{3,2,1,0:T(8,128)} %e_ref.1, f32[3,4,8,128]{3,2,1,0:T(8,128)} %h_ref.1, f32[3,4,8,128]{3,2,1,0:T(8,128)} %perm_ref.1, f32[1,4,8,128]{3,2,1,0:T(8,128)} %bitcast.59, ...), custom_call_target="tpu_custom_call" | custom-call | tf_op jit(solution)/shard_map/pallas_call | solution.py:127
  23.3 0.7 %copy-done.9 = f32[2,64]{1,0:T(2,128)S(1)} copy-done((f32[2,64]{1,0:T(2,128)S(1)}, f32[2,64]{1,0:T(2,128)}, u32[]{:S(2)}) %copy-start.9) | copy-done | bytes 536
  23.9 0.1 reshape_reshape.8
  24.0 0.1 reshape.191
  24.1 0.1 reshape.194
  24.2 0.1 reshape.198
  24.4 2.7 %collective-permute-start.4 = (f32[2,4,1,8]{3,1,0,2:T(4,128)S(1)}, f32[2,4,1,8]{3,1,0,2:T(4,128)S(1)}, u32[]{:S(2)}, u32[]{:S(2)}) collective-permute-start(f32[2,4,1,8]{3,1,0,2:T(4,128)S(1)} %get-tuple-element.34), channel_id=1, source_target_pairs={{0,16},{4,20},{8,24},{12,28},{16,0},{20,4},{24,8},{28,12},{1,17},{... | collective-permute-start | bytes 776 | tf_op jit(solution)/shard_map/ppermute | solution.py:160
  27.0 0.1 eq.37
  27.1 1.8 %collective-permute-done.4 = f32[2,4,1,8]{3,1,0,2:T(4,128)S(1)} collective-permute-done((f32[2,4,1,8]{3,1,0,2:T(4,128)S(1)}, f32[2,4,1,8]{3,1,0,2:T(4,128)S(1)}, u32[]{:S(2)}, u32[]{:S(2)}) %collective-permute-start.4) | collective-permute-done | bytes 288 | tf_op jit(solution)/shard_map/ppermute | solution.py:160
  29.0 3.5 %collective-permute-start.7 = (f32[2,2,8]{2,1,0:T(2,128)S(1)}, f32[2,2,8]{2,1,0:T(2,128)S(1)}, u32[]{:S(2)}, u32[]{:S(2)}) collective-permute-start(f32[2,2,8]{2,1,0:T(2,128)S(1)} %get-tuple-element.30), channel_id=1, source_target_pairs={{0,12},{4,8},{8,4},{12,0},{16,28},{20,24},{24,20},{28,16},{1,13},{... | collective-permute-start | bytes 392 | tf_op jit(solution)/shard_map/ppermute | solution.py:166
  32.5 0.4 %collective-permute-start.6 = (f32[2,2,8]{2,1,0:T(2,128)S(1)}, f32[2,2,8]{2,1,0:T(2,128)S(1)}, u32[]{:S(2)}, u32[]{:S(2)}) collective-permute-start(f32[2,2,8]{2,1,0:T(2,128)S(1)} %get-tuple-element.31), channel_id=1, source_target_pairs={{0,8},{4,12},{8,0},{12,4},{16,24},{20,28},{24,16},{28,20},{1,9},{5... | collective-permute-start | bytes 392 | tf_op jit(solution)/shard_map/ppermute | solution.py:166
  32.9 0.2 collective-permute-start.5
  33.1 0.9 %collective-permute-done.7 = f32[2,2,8]{2,1,0:T(2,128)S(1)} collective-permute-done((f32[2,2,8]{2,1,0:T(2,128)S(1)}, f32[2,2,8]{2,1,0:T(2,128)S(1)}, u32[]{:S(2)}, u32[]{:S(2)}) %collective-permute-start.7) | collective-permute-done | bytes 160 | tf_op jit(solution)/shard_map/ppermute | solution.py:166
  34.0 2.0 %collective-permute-done.6 = f32[2,2,8]{2,1,0:T(2,128)S(1)} collective-permute-done((f32[2,2,8]{2,1,0:T(2,128)S(1)}, f32[2,2,8]{2,1,0:T(2,128)S(1)}, u32[]{:S(2)}, u32[]{:S(2)}) %collective-permute-start.6) | collective-permute-done | bytes 160 | tf_op jit(solution)/shard_map/ppermute | solution.py:166
  36.0 0.4 %collective-permute-done.5 = f32[2,2,8]{2,1,0:T(2,128)S(1)} collective-permute-done((f32[2,2,8]{2,1,0:T(2,128)S(1)}, f32[2,2,8]{2,1,0:T(2,128)S(1)}, u32[]{:S(2)}, u32[]{:S(2)}) %collective-permute-start.5) | collective-permute-done | bytes 160 | tf_op jit(solution)/shard_map/ppermute | solution.py:166
  36.5 0.1 broadcast_in_dim.27
  36.6 0.6 %select_reduce_fusion = f32[128]{0:T(128)} fusion(f32[128]{0:T(128)S(1)} %broadcast_in_dim.27, s32[128]{0:T(128)S(1)} %eq.37), kind=kLoop, calls=%fused_computation.4 | loop fusion | flops 49024 | bytes 1536 | tf_op jit(solution)/shard_map/reduce_sum | solution.py:201
  (50 shorter events, 0.5 us)
Async XLA Ops:
  1.3 0.8 %copy-start.1 = (f32[3,4,8,128]{3,2,1,0:T(8,128)S(1)}, f32[3,4,8,128]{3,2,1,0:T(8,128)}, u32[]{:S(2)}) copy-start(f32[3,4,8,128]{3,2,1,0:T(8,128)} %e_ref.1) | copy-start | bytes 147460
  1.4 0.9 %copy-start.2 = (f32[3,4,8,128]{3,2,1,0:T(8,128)S(1)}, f32[3,4,8,128]{3,2,1,0:T(8,128)}, u32[]{:S(2)}) copy-start(f32[3,4,8,128]{3,2,1,0:T(8,128)} %h_ref.1) | copy-start | bytes 147460
  2.2 7.6 %collective-permute-start = (f32[10,2,8,128]{3,2,1,0:T(8,128)S(1)}, f32[10,2,8,128]{3,2,1,0:T(8,128)S(1)}, u32[]{:S(2)}, u32[]{:S(2)}) collective-permute-start(f32[10,2,8,128]{3,2,1,0:T(8,128)S(1)} %pad_maximum_fusion), channel_id=1, source_target_pairs={{0,4},{4,8},{8,12},{12,16},{16,20},{20,24},{24,28},{1,5},{5,9},{9,... | collective-permute-start | bytes 245768 | tf_op jit(solution)/shard_map/ppermute | solution.py:23
  5.7 1.3 %copy-start.5 = (f32[4,8,128]{2,1,0:T(8,128)S(1)}, f32[4,8,128]{2,1,0:T(8,128)}, u32[]{:S(2)}) copy-start(f32[4,8,128]{2,1,0:T(8,128)} %param.10) | copy-start | bytes 49156
  5.7 1.4 %copy-start = (f32[3,4,8,128]{3,2,1,0:T(8,128)S(1)}, f32[3,4,8,128]{3,2,1,0:T(8,128)}, u32[]{:S(2)}) copy-start(f32[3,4,8,128]{3,2,1,0:T(8,128)} %perm_ref.1) | copy-start | bytes 147460
  5.7 6.3 %collective-permute-start.1 = (f32[10,2,8,128]{3,2,1,0:T(8,128)S(1)}, f32[10,2,8,128]{3,2,1,0:T(8,128)S(1)}, u32[]{:S(2)}, u32[]{:S(2)}) collective-permute-start(f32[10,2,8,128]{3,2,1,0:T(8,128)S(1)} %pad_maximum_fusion.1), channel_id=1, source_target_pairs={{4,0},{8,4},{12,8},{16,12},{20,16},{24,20},{28,24},{5,1},{9,5},{13... | collective-permute-start | bytes 245768 | tf_op jit(solution)/shard_map/ppermute | solution.py:23
  7.1 0.7 %copy-start.8 = (s32[1,1,8,8]{3,2,1,0:T(8,128)S(1)}, s32[1,1,8,8]{3,2,1,0:T(8,128)}, u32[]{:S(2)}) copy-start(s32[1,1,8,8]{3,2,1,0:T(8,128)} %param.13) | copy-start | bytes 772
  7.9 0.7 %copy-start.10 = (s32[1,1,8,8]{3,2,1,0:T(8,128)S(1)}, s32[1,1,8,8]{3,2,1,0:T(8,128)}, u32[]{:S(2)}) copy-start(s32[1,1,8,8]{3,2,1,0:T(8,128)} %param.12) | copy-start | bytes 772
  7.9 1.3 %copy-start.11 = (f32[1,1,2,3,64]{4,2,3,1,0:T(2,128)S(1)}, f32[1,1,2,3,64]{4,2,3,1,0:T(2,128)}, u32[]{:S(2)}) copy-start(f32[1,1,2,3,64]{4,2,3,1,0:T(2,128)} %param.11) | copy-start | bytes 4612
  9.8 2.3 %copy-start.3 = (f32[10,2,8,128]{3,2,1,0:T(8,128)}, f32[10,2,8,128]{3,2,1,0:T(8,128)S(1)}, u32[]{:S(2)}) copy-start(f32[10,2,8,128]{3,2,1,0:T(8,128)S(1)} %collective-permute-done.xlo_ref) | copy-start | bytes 245764
  12.0 0.6 %copy-start.4 = (f32[10,2,8,128]{3,2,1,0:T(8,128)}, f32[10,2,8,128]{3,2,1,0:T(8,128)S(1)}, u32[]{:S(2)}) copy-start(f32[10,2,8,128]{3,2,1,0:T(8,128)S(1)} %collective-permute-done.1.xhi_ref) | copy-start | bytes 245764
  12.7 6.3 %collective-permute-start.2 = (f32[10,8,2,128]{3,2,1,0:T(2,128)S(1)}, f32[10,8,2,128]{3,2,1,0:T(2,128)S(1)}, u32[]{:S(2)}, u32[]{:S(2)}) collective-permute-start(f32[10,8,2,128]{3,2,1,0:T(2,128)S(1)} %pad_maximum_fusion.2), channel_id=1, source_target_pairs={{0,1},{1,2},{2,3},{4,5},{5,6},{6,7},{8,9},{9,10},{10,11},{12,13},{... | collective-permute-start | bytes 245768 | tf_op jit(solution)/shard_map/ppermute | solution.py:23
  14.6 5.7 %collective-permute-start.3 = (f32[10,8,2,128]{3,2,1,0:T(2,128)S(1)}, f32[10,8,2,128]{3,2,1,0:T(2,128)S(1)}, u32[]{:S(2)}, u32[]{:S(2)}) collective-permute-start(f32[10,8,2,128]{3,2,1,0:T(2,128)S(1)} %pad_maximum_fusion.3), channel_id=1, source_target_pairs={{1,0},{2,1},{3,2},{5,4},{6,5},{7,6},{9,8},{10,9},{11,10},{13,12},{... | collective-permute-start | bytes 245768 | tf_op jit(solution)/shard_map/ppermute | solution.py:23
  18.9 1.4 %copy-start.6 = (f32[10,8,2,128]{3,2,1,0:T(2,128)}, f32[10,8,2,128]{3,2,1,0:T(2,128)S(1)}, u32[]{:S(2)}) copy-start(f32[10,8,2,128]{3,2,1,0:T(2,128)S(1)} %collective-permute-done.2.ylo_ref) | copy-start | bytes 245764
  20.3 0.6 %copy-start.7 = (f32[10,8,2,128]{3,2,1,0:T(2,128)}, f32[10,8,2,128]{3,2,1,0:T(2,128)S(1)}, u32[]{:S(2)}) copy-start(f32[10,8,2,128]{3,2,1,0:T(2,128)S(1)} %collective-permute-done.3.yhi_ref) | copy-start | bytes 245764
  23.2 0.7 %copy-start.9 = (f32[2,64]{1,0:T(2,128)S(1)}, f32[2,64]{1,0:T(2,128)}, u32[]{:S(2)}) copy-start(f32[2,64]{1,0:T(2,128)} %get-tuple-element.8) | copy-start | bytes 1540
  24.4 4.6 %collective-permute-start.4 = (f32[2,4,1,8]{3,1,0,2:T(4,128)S(1)}, f32[2,4,1,8]{3,1,0,2:T(4,128)S(1)}, u32[]{:S(2)}, u32[]{:S(2)}) collective-permute-start(f32[2,4,1,8]{3,1,0,2:T(4,128)S(1)} %get-tuple-element.34), channel_id=1, source_target_pairs={{0,16},{4,20},{8,24},{12,28},{16,0},{20,4},{24,8},{28,12},{1,17},{... | collective-permute-start | bytes 776 | tf_op jit(solution)/shard_map/ppermute | solution.py:160
  29.0 5.1 %collective-permute-start.7 = (f32[2,2,8]{2,1,0:T(2,128)S(1)}, f32[2,2,8]{2,1,0:T(2,128)S(1)}, u32[]{:S(2)}, u32[]{:S(2)}) collective-permute-start(f32[2,2,8]{2,1,0:T(2,128)S(1)} %get-tuple-element.30), channel_id=1, source_target_pairs={{0,12},{4,8},{8,4},{12,0},{16,28},{20,24},{24,20},{28,16},{1,13},{... | collective-permute-start | bytes 392 | tf_op jit(solution)/shard_map/ppermute | solution.py:166
  32.5 3.6 %collective-permute-start.6 = (f32[2,2,8]{2,1,0:T(2,128)S(1)}, f32[2,2,8]{2,1,0:T(2,128)S(1)}, u32[]{:S(2)}, u32[]{:S(2)}) collective-permute-start(f32[2,2,8]{2,1,0:T(2,128)S(1)} %get-tuple-element.31), channel_id=1, source_target_pairs={{0,8},{4,12},{8,0},{12,4},{16,24},{20,28},{24,16},{28,20},{1,9},{5... | collective-permute-start | bytes 392 | tf_op jit(solution)/shard_map/ppermute | solution.py:166
  32.9 3.6 %collective-permute-start.5 = (f32[2,2,8]{2,1,0:T(2,128)S(1)}, f32[2,2,8]{2,1,0:T(2,128)S(1)}, u32[]{:S(2)}, u32[]{:S(2)}) collective-permute-start(f32[2,2,8]{2,1,0:T(2,128)S(1)} %get-tuple-element.32), channel_id=1, source_target_pairs={{0,4},{4,0},{8,12},{12,8},{16,20},{20,16},{24,28},{28,24},{1,5},{5... | collective-permute-start | bytes 392 | tf_op jit(solution)/shard_map/ppermute | solution.py:166

commit v8 on v7

--- a/solution.py
+++ b/solution.py
@@ -11,7 +11,7 @@
 PAR_DEV = 128
 HALO = 2
 LANES = 128
-RADIX = 4
+RADIX = 8
 
 CH_GAIN = 0.5
 CE_GAIN = 0.5

time: 37.7 us -> 42.3 us (1.12)
  starting transfers between devices: 17.1 us -> 22.1 us
  waiting for transfers between devices: 8.81 us -> 8.27 us
    ppermute x3 -> x7, starting transfers between devices: 4.14 us -> 11.8 us  [exchange_by_halving(): lax.ppermute(held[:, q], 'slab', [(i, i ^ q) for i in range(count)])]
    ppermute x1 -> x0, starting transfers between devices: 2.65 us -> none  [exchange_by_halving(): got = lax.ppermute(send, 'slab', pairs)]
    ppermute x1 -> x0, waiting for transfers between devices: 1.82 us -> none  [exchange_by_halving(): got = lax.ppermute(send, 'slab', pairs)]
    ppermute x3 -> x7, waiting for transfers between devices: 3.39 us -> 4.76 us  [exchange_by_halving(): lax.ppermute(held[:, q], 'slab', [(i, i ^ q) for i in range(count)])]
    unnamed x25 -> x31, local copies, waits for them, and re-layouts: 3.88 us -> 3.9 us
  transfers between devices with their start and end apart: 8 -> 11, of which waited for: 6 -> 5; matrix products, arithmetic and copies ran while one was open for 6% -> 5% of each run, Pallas kernels for 0% -> 0%
where the time goes in v8:
time: 42.3 us; the launch traced here: 41.7 us
  starting transfers between devices  22.1 us (52%)
  waiting for transfers between devices  8.27 us (20%)
  local copies, waits for them, and re-layouts  6.65 us (16%)
  Pallas kernels  2.29 us (5%)
  other arithmetic  1.41 us (3%)
  between operations  1 us (2%)
    ppermute x7, starting transfers between devices, exchange_by_halving(): lax.ppermute(held[:, q], 'slab', [(i, i ^ q) for i in range(count)])  11.8 us
    ppermute x4, starting transfers between devices, recv_from(): return lax.ppermute(array, axis, pairs)  10.3 us
    ppermute x7, waiting for transfers between devices, exchange_by_halving(): lax.ppermute(held[:, q], 'slab', [(i, i ^ q) for i in range(count)])  4.76 us
    unnamed x31, local copies, waits for them, and re-layouts  3.9 us
    ppermute x4, waiting for transfers between devices, recv_from(): return lax.ppermute(array, axis, pairs)  3.51 us
    pallas_call x1, Pallas kernels, leapfrog(): pl.pallas_call(kernel, out_shape=(jax.ShapeDtypeStruct(field_e.shape, jnp...  2.29 us
    slice x3, local copies, waits for them, and re-layouts, shards(): xhi = recv_from(jnp.concatenate([p[:, :HALO] for p in parts], 0), 'slab', 1)  1.49 us
  transfers between devices with their start and end apart: 11, of which 5 were waited for; matrix products, arithmetic and copies ran while one was open for 5% of the time, Pallas kernels for 0%

profile of v8, /device:TPU:2, one launch (start us, length us, event | category | flops | bytes accessed | tf_op | source)
XLA Modules:
  0.0 41.7 jit_solution(1601507182213082706)
XLA Ops:
  0.6 0.7 %fusion.11 = (f32[1,2,8,128]{3,2,1,0:T(8,128)S(1)}, f32[1,2,8,128]{3,2,1,0:T(8,128)S(1)}) fusion(f32[1,4,8,128]{3,2,1,0:T(8,128)} %bitcast.73), kind=kLoop, calls=%fused_computation.33 | loop fusion | bytes 32768 | tf_op jit(solution)/shard_map/slice | solution.py:181
  1.4 0.8 %fusion.9 = (f32[3,2,8,128]{3,2,1,0:T(8,128)S(1)}, f32[3,2,8,128]{3,2,1,0:T(8,128)S(1)}) fusion(f32[3,4,8,128]{3,2,1,0:T(8,128)} %perm_ref.1), kind=kLoop, calls=%fused_computation.31 | loop fusion | bytes 98304 | tf_op jit(solution)/shard_map/slice | solution.py:181
  2.2 3.4 %collective-permute-start = (f32[10,2,8,128]{3,2,1,0:T(8,128)S(1)}, f32[10,2,8,128]{3,2,1,0:T(8,128)S(1)}, u32[]{:S(2)}, u32[]{:S(2)}) collective-permute-start(f32[10,2,8,128]{3,2,1,0:T(8,128)S(1)} %pad_maximum_fusion), channel_id=1, source_target_pairs={{0,4},{4,8},{8,12},{12,16},{16,20},{20,24},{24,28},{1,5},{5,9},{9,... | collective-permute-start | bytes 245768 | tf_op jit(solution)/shard_map/ppermute | solution.py:23
  5.7 1.3 %collective-permute-start.1 = (f32[10,2,8,128]{3,2,1,0:T(8,128)S(1)}, f32[10,2,8,128]{3,2,1,0:T(8,128)S(1)}, u32[]{:S(2)}, u32[]{:S(2)}) collective-permute-start(f32[10,2,8,128]{3,2,1,0:T(8,128)S(1)} %pad_maximum_fusion.1), channel_id=1, source_target_pairs={{4,0},{8,4},{12,8},{16,12},{20,16},{24,20},{28,24},{5,1},{9,5},{13... | collective-permute-start | bytes 245768 | tf_op jit(solution)/shard_map/ppermute | solution.py:23
  7.2 0.7 %copy-done.8 = s32[1,1,8,8]{3,2,1,0:T(8,128)S(1)} copy-done((s32[1,1,8,8]{3,2,1,0:T(8,128)S(1)}, s32[1,1,8,8]{3,2,1,0:T(8,128)}, u32[]{:S(2)}) %copy-start.8) | copy-done | bytes 280
  7.9 0.7 %copy-done.10 = s32[1,1,8,8]{3,2,1,0:T(8,128)S(1)} copy-done((s32[1,1,8,8]{3,2,1,0:T(8,128)S(1)}, s32[1,1,8,8]{3,2,1,0:T(8,128)}, u32[]{:S(2)}) %copy-start.10) | copy-done | bytes 280
  8.6 0.6 %reshape.177.cell_ref = s32[1,64]{1,0:T(1,128)} reshape(s32[1,1,8,8]{3,2,1,0:T(8,128)S(1)} %copy-done.10) | data formatting | bytes 512 | tf_op jit(solution)/shard_map/reshape | solution.py:191
  9.2 0.6 %copy.29 = f32[1,1,2,3,64]{4,3,2,1,0:T(4,128)} copy(f32[1,1,2,3,64]{4,2,3,1,0:T(2,128)S(1)} %copy-done.11) | data formatting | bytes 3072 | tf_op args[4]
  9.8 0.1 eq.37
  9.9 2.1 %collective-permute-done.1.xhi_ref = f32[10,2,8,128]{3,2,1,0:T(8,128)S(1)} collective-permute-done((f32[10,2,8,128]{3,2,1,0:T(8,128)S(1)}, f32[10,2,8,128]{3,2,1,0:T(8,128)S(1)}, u32[]{:S(2)}, u32[]{:S(2)}) %collective-permute-start.1) | collective-permute-done | bytes 81952 | tf_op jit(solution)/shard_map/ppermute | solution.py:23
  12.1 0.6 %copy-done.4 = f32[10,2,8,128]{3,2,1,0:T(8,128)} copy-done((f32[10,2,8,128]{3,2,1,0:T(8,128)}, f32[10,2,8,128]{3,2,1,0:T(8,128)S(1)}, u32[]{:S(2)}) %copy-start.4) | copy-done | bytes 81944
  12.7 1.9 %collective-permute-start.2 = (f32[10,8,2,128]{3,2,1,0:T(2,128)S(1)}, f32[10,8,2,128]{3,2,1,0:T(2,128)S(1)}, u32[]{:S(2)}, u32[]{:S(2)}) collective-permute-start(f32[10,8,2,128]{3,2,1,0:T(2,128)S(1)} %pad_maximum_fusion.2), channel_id=1, source_target_pairs={{0,1},{1,2},{2,3},{4,5},{5,6},{6,7},{8,9},{9,10},{10,11},{12,13},{... | collective-permute-start | bytes 245768 | tf_op jit(solution)/shard_map/ppermute | solution.py:23
  14.6 3.6 %collective-permute-start.3 = (f32[10,8,2,128]{3,2,1,0:T(2,128)S(1)}, f32[10,8,2,128]{3,2,1,0:T(2,128)S(1)}, u32[]{:S(2)}, u32[]{:S(2)}) collective-permute-start(f32[10,8,2,128]{3,2,1,0:T(2,128)S(1)} %pad_maximum_fusion.3), channel_id=1, source_target_pairs={{1,0},{2,1},{3,2},{5,4},{6,5},{7,6},{9,8},{10,9},{11,10},{13,12},{... | collective-permute-start | bytes 245768 | tf_op jit(solution)/shard_map/ppermute | solution.py:23
  18.3 0.6 %pad_add_fusion.offsets = s32[2]{0:T(128)} fusion(s32[1]{0:T(128)} %bitcast.1, s32[1]{0:T(128)} %bitcast), kind=kLoop, calls=%fused_computation.23 | loop fusion | flops 2 | bytes 16 | tf_op jit(solution)/shard_map/stack | solution.py:188
  18.9 1.4 %collective-permute-done.3.yhi_ref = f32[10,8,2,128]{3,2,1,0:T(2,128)S(1)} collective-permute-done((f32[10,8,2,128]{3,2,1,0:T(2,128)S(1)}, f32[10,8,2,128]{3,2,1,0:T(2,128)S(1)}, u32[]{:S(2)}, u32[]{:S(2)}) %collective-permute-start.3) | collective-permute-done | bytes 81952 | tf_op jit(solution)/shard_map/ppermute | solution.py:23
  20.3 0.6 %copy-done.7 = f32[10,8,2,128]{3,2,1,0:T(2,128)} copy-done((f32[10,8,2,128]{3,2,1,0:T(2,128)}, f32[10,8,2,128]{3,2,1,0:T(2,128)S(1)}, u32[]{:S(2)}) %copy-start.7) | copy-done | bytes 81944
  20.9 2.3 %shard_map.94 = (f32[3,4,8,128]{3,2,1,0:T(8,128)}, f32[3,4,8,128]{3,2,1,0:T(8,128)}, f32[2,64]{1,0:T(2,128)}) custom-call(s32[2]{0:T(128)} %pad_add_fusion.offsets, f32[3,4,8,128]{3,2,1,0:T(8,128)} %e_ref.1, f32[3,4,8,128]{3,2,1,0:T(8,128)} %h_ref.1, f32[3,4,8,128]{3,2,1,0:T(8,128)} %perm_ref.1, f32[1,4,8,128]{3,2,1,0:T(8,128)} %bitcast.74, ...), custom_call_target="tpu_custom_call" | custom-call | tf_op jit(solution)/shard_map/pallas_call | solution.py:127
  23.2 0.6 %copy-done.9 = f32[2,64]{1,0:T(2,128)S(1)} copy-done((f32[2,64]{1,0:T(2,128)S(1)}, f32[2,64]{1,0:T(2,128)}, u32[]{:S(2)}) %copy-start.9) | copy-done | bytes 536
  23.9 0.1 reshape_reshape.8
  24.0 0.1 reshape.188
  24.0 0.1 reshape.191
  24.3 2.5 %collective-permute-start.4 = (f32[2,1,8]{2,0,1:T(2,128)S(1)}, f32[2,1,8]{2,0,1:T(2,128)S(1)}, u32[]{:S(2)}, u32[]{:S(2)}) collective-permute-start(f32[2,1,8]{2,0,1:T(2,128)S(1)} %bitcast.97), channel_id=1, source_target_pairs={{0,4},{4,0},{8,12},{12,8},{16,20},{20,16},{24,28},{28,24},{1,5},{5... | collective-permute-start | bytes 200 | tf_op jit(solution)/shard_map/ppermute | solution.py:166
  26.8 1.6 %collective-permute-start.5 = (f32[2,1,8]{2,0,1:T(2,128)S(1)}, f32[2,1,8]{2,0,1:T(2,128)S(1)}, u32[]{:S(2)}, u32[]{:S(2)}) collective-permute-start(f32[2,1,8]{2,0,1:T(2,128)S(1)} %bitcast.96), channel_id=1, source_target_pairs={{0,8},{4,12},{8,0},{12,4},{16,24},{20,28},{24,16},{28,20},{1,9},{5... | collective-permute-start | bytes 200 | tf_op jit(solution)/shard_map/ppermute | solution.py:166
  28.4 2.6 %collective-permute-start.7 = (f32[2,1,8]{2,0,1:T(2,128)S(1)}, f32[2,1,8]{2,0,1:T(2,128)S(1)}, u32[]{:S(2)}, u32[]{:S(2)}) collective-permute-start(f32[2,1,8]{2,0,1:T(2,128)S(1)} %bitcast.94), channel_id=1, source_target_pairs={{0,16},{4,20},{8,24},{12,28},{16,0},{20,4},{24,8},{28,12},{1,17},{... | collective-permute-start | bytes 200 | tf_op jit(solution)/shard_map/ppermute | solution.py:166
  31.0 1.7 %collective-permute-start.8 = (f32[2,1,8]{2,0,1:T(2,128)S(1)}, f32[2,1,8]{2,0,1:T(2,128)S(1)}, u32[]{:S(2)}, u32[]{:S(2)}) collective-permute-start(f32[2,1,8]{2,0,1:T(2,128)S(1)} %bitcast.93), channel_id=1, source_target_pairs={{0,20},{4,16},{8,28},{12,24},{16,4},{20,0},{24,12},{28,8},{1,21},{... | collective-permute-start | bytes 200 | tf_op jit(solution)/shard_map/ppermute | solution.py:166
  32.7 2.0 %collective-permute-start.9 = (f32[2,1,8]{2,0,1:T(2,128)S(1)}, f32[2,1,8]{2,0,1:T(2,128)S(1)}, u32[]{:S(2)}, u32[]{:S(2)}) collective-permute-start(f32[2,1,8]{2,0,1:T(2,128)S(1)} %bitcast.92), channel_id=1, source_target_pairs={{0,24},{4,28},{8,16},{12,20},{16,8},{20,12},{24,0},{28,4},{1,25},{... | collective-permute-start | bytes 200 | tf_op jit(solution)/shard_map/ppermute | solution.py:166
  34.7 1.5 %collective-permute-start.10 = (f32[2,1,8]{2,0,1:T(2,128)S(1)}, f32[2,1,8]{2,0,1:T(2,128)S(1)}, u32[]{:S(2)}, u32[]{:S(2)}) collective-permute-start(f32[2,1,8]{2,0,1:T(2,128)S(1)} %bitcast.91), channel_id=1, source_target_pairs={{0,28},{4,24},{8,20},{12,16},{16,12},{20,8},{24,4},{28,0},{1,29},{... | collective-permute-start | bytes 200 | tf_op jit(solution)/shard_map/ppermute | solution.py:166
  36.2 0.1 collective-permute-done.8
  36.3 1.7 %collective-permute-done.9 = f32[2,1,8]{2,0,1:T(2,128)S(1)} collective-permute-done((f32[2,1,8]{2,0,1:T(2,128)S(1)}, f32[2,1,8]{2,0,1:T(2,128)S(1)}, u32[]{:S(2)}, u32[]{:S(2)}) %collective-permute-start.9) | collective-permute-done | bytes 96 | tf_op jit(solution)/shard_map/ppermute | solution.py:166
  38.1 2.9 %collective-permute-done.10 = f32[2,1,8]{2,0,1:T(2,128)S(1)} collective-permute-done((f32[2,1,8]{2,0,1:T(2,128)S(1)}, f32[2,1,8]{2,0,1:T(2,128)S(1)}, u32[]{:S(2)}, u32[]{:S(2)}) %collective-permute-start.10) | collective-permute-done | bytes 96 | tf_op jit(solution)/shard_map/ppermute | solution.py:166
  41.0 0.1 broadcast_in_dim.27
  41.1 0.6 %select_reduce_fusion = f32[128]{0:T(128)} fusion(f32[128]{0:T(128)S(1)} %broadcast_in_dim.27, s32[128]{0:T(128)S(1)} %eq.37), kind=kLoop, calls=%fused_computation.4 | loop fusion | flops 49024 | bytes 1536 | tf_op jit(solution)/shard_map/reduce_sum | solution.py:201
  (59 shorter events, 0.6 us)
Async XLA Ops:
  1.3 0.8 %copy-start.1 = (f32[3,4,8,128]{3,2,1,0:T(8,128)S(1)}, f32[3,4,8,128]{3,2,1,0:T(8,128)}, u32[]{:S(2)}) copy-start(f32[3,4,8,128]{3,2,1,0:T(8,128)} %e_ref.1) | copy-start | bytes 147460
  1.4 0.9 %copy-start.2 = (f32[3,4,8,128]{3,2,1,0:T(8,128)S(1)}, f32[3,4,8,128]{3,2,1,0:T(8,128)}, u32[]{:S(2)}) copy-start(f32[3,4,8,128]{3,2,1,0:T(8,128)} %h_ref.1) | copy-start | bytes 147460
  2.2 7.7 %collective-permute-start = (f32[10,2,8,128]{3,2,1,0:T(8,128)S(1)}, f32[10,2,8,128]{3,2,1,0:T(8,128)S(1)}, u32[]{:S(2)}, u32[]{:S(2)}) collective-permute-start(f32[10,2,8,128]{3,2,1,0:T(8,128)S(1)} %pad_maximum_fusion), channel_id=1, source_target_pairs={{0,4},{4,8},{8,12},{12,16},{16,20},{20,24},{24,28},{1,5},{5,9},{9,... | collective-permute-start | bytes 245768 | tf_op jit(solution)/shard_map/ppermute | solution.py:23
  5.7 1.3 %copy-start.5 = (f32[4,8,128]{2,1,0:T(8,128)S(1)}, f32[4,8,128]{2,1,0:T(8,128)}, u32[]{:S(2)}) copy-start(f32[4,8,128]{2,1,0:T(8,128)} %param.10) | copy-start | bytes 49156
  5.7 1.4 %copy-start = (f32[3,4,8,128]{3,2,1,0:T(8,128)S(1)}, f32[3,4,8,128]{3,2,1,0:T(8,128)}, u32[]{:S(2)}) copy-start(f32[3,4,8,128]{3,2,1,0:T(8,128)} %perm_ref.1) | copy-start | bytes 147460
  5.7 6.3 %collective-permute-start.1 = (f32[10,2,8,128]{3,2,1,0:T(8,128)S(1)}, f32[10,2,8,128]{3,2,1,0:T(8,128)S(1)}, u32[]{:S(2)}, u32[]{:S(2)}) collective-permute-start(f32[10,2,8,128]{3,2,1,0:T(8,128)S(1)} %pad_maximum_fusion.1), channel_id=1, source_target_pairs={{4,0},{8,4},{12,8},{16,12},{20,16},{24,20},{28,24},{5,1},{9,5},{13... | collective-permute-start | bytes 245768 | tf_op jit(solution)/shard_map/ppermute | solution.py:23
  7.1 0.7 %copy-start.8 = (s32[1,1,8,8]{3,2,1,0:T(8,128)S(1)}, s32[1,1,8,8]{3,2,1,0:T(8,128)}, u32[]{:S(2)}) copy-start(s32[1,1,8,8]{3,2,1,0:T(8,128)} %param.13) | copy-start | bytes 772
  7.9 0.7 %copy-start.10 = (s32[1,1,8,8]{3,2,1,0:T(8,128)S(1)}, s32[1,1,8,8]{3,2,1,0:T(8,128)}, u32[]{:S(2)}) copy-start(s32[1,1,8,8]{3,2,1,0:T(8,128)} %param.12) | copy-start | bytes 772
  7.9 1.3 %copy-start.11 = (f32[1,1,2,3,64]{4,2,3,1,0:T(2,128)S(1)}, f32[1,1,2,3,64]{4,2,3,1,0:T(2,128)}, u32[]{:S(2)}) copy-start(f32[1,1,2,3,64]{4,2,3,1,0:T(2,128)} %param.11) | copy-start | bytes 4612
  9.9 2.2 %copy-start.3 = (f32[10,2,8,128]{3,2,1,0:T(8,128)}, f32[10,2,8,128]{3,2,1,0:T(8,128)S(1)}, u32[]{:S(2)}) copy-start(f32[10,2,8,128]{3,2,1,0:T(8,128)S(1)} %collective-permute-done.xlo_ref) | copy-start | bytes 245764
  12.0 0.6 %copy-start.4 = (f32[10,2,8,128]{3,2,1,0:T(8,128)}, f32[10,2,8,128]{3,2,1,0:T(8,128)S(1)}, u32[]{:S(2)}) copy-start(f32[10,2,8,128]{3,2,1,0:T(8,128)S(1)} %collective-permute-done.1.xhi_ref) | copy-start | bytes 245764
  12.7 6.3 %collective-permute-start.2 = (f32[10,8,2,128]{3,2,1,0:T(2,128)S(1)}, f32[10,8,2,128]{3,2,1,0:T(2,128)S(1)}, u32[]{:S(2)}, u32[]{:S(2)}) collective-permute-start(f32[10,8,2,128]{3,2,1,0:T(2,128)S(1)} %pad_maximum_fusion.2), channel_id=1, source_target_pairs={{0,1},{1,2},{2,3},{4,5},{5,6},{6,7},{8,9},{9,10},{10,11},{12,13},{... | collective-permute-start | bytes 245768 | tf_op jit(solution)/shard_map/ppermute | solution.py:23
  14.6 5.7 %collective-permute-start.3 = (f32[10,8,2,128]{3,2,1,0:T(2,128)S(1)}, f32[10,8,2,128]{3,2,1,0:T(2,128)S(1)}, u32[]{:S(2)}, u32[]{:S(2)}) collective-permute-start(f32[10,8,2,128]{3,2,1,0:T(2,128)S(1)} %pad_maximum_fusion.3), channel_id=1, source_target_pairs={{1,0},{2,1},{3,2},{5,4},{6,5},{7,6},{9,8},{10,9},{11,10},{13,12},{... | collective-permute-start | bytes 245768 | tf_op jit(solution)/shard_map/ppermute | solution.py:23
  18.9 1.4 %copy-start.6 = (f32[10,8,2,128]{3,2,1,0:T(2,128)}, f32[10,8,2,128]{3,2,1,0:T(2,128)S(1)}, u32[]{:S(2)}) copy-start(f32[10,8,2,128]{3,2,1,0:T(2,128)S(1)} %collective-permute-done.2.ylo_ref) | copy-start | bytes 245764
  20.3 0.6 %copy-start.7 = (f32[10,8,2,128]{3,2,1,0:T(2,128)}, f32[10,8,2,128]{3,2,1,0:T(2,128)S(1)}, u32[]{:S(2)}) copy-start(f32[10,8,2,128]{3,2,1,0:T(2,128)S(1)} %collective-permute-done.3.yhi_ref) | copy-start | bytes 245764
  23.2 0.6 %copy-start.9 = (f32[2,64]{1,0:T(2,128)S(1)}, f32[2,64]{1,0:T(2,128)}, u32[]{:S(2)}) copy-start(f32[2,64]{1,0:T(2,128)} %get-tuple-element.8) | copy-start | bytes 1540
  24.3 8.3 %collective-permute-start.4 = (f32[2,1,8]{2,0,1:T(2,128)S(1)}, f32[2,1,8]{2,0,1:T(2,128)S(1)}, u32[]{:S(2)}, u32[]{:S(2)}) collective-permute-start(f32[2,1,8]{2,0,1:T(2,128)S(1)} %bitcast.97), channel_id=1, source_target_pairs={{0,4},{4,0},{8,12},{12,8},{16,20},{20,16},{24,28},{28,24},{1,5},{5... | collective-permute-start | bytes 200 | tf_op jit(solution)/shard_map/ppermute | solution.py:166
  26.8 7.9 %collective-permute-start.5 = (f32[2,1,8]{2,0,1:T(2,128)S(1)}, f32[2,1,8]{2,0,1:T(2,128)S(1)}, u32[]{:S(2)}, u32[]{:S(2)}) collective-permute-start(f32[2,1,8]{2,0,1:T(2,128)S(1)} %bitcast.96), channel_id=1, source_target_pairs={{0,8},{4,12},{8,0},{12,4},{16,24},{20,28},{24,16},{28,20},{1,9},{5... | collective-permute-start | bytes 200 | tf_op jit(solution)/shard_map/ppermute | solution.py:166
  28.4 7.8 %collective-permute-start.6 = (f32[2,1,8]{2,0,1:T(2,128)S(1)}, f32[2,1,8]{2,0,1:T(2,128)S(1)}, u32[]{:S(2)}, u32[]{:S(2)}) collective-permute-start(f32[2,1,8]{2,0,1:T(2,128)S(1)} %bitcast.95), channel_id=1, source_target_pairs={{0,12},{4,8},{8,4},{12,0},{16,28},{20,24},{24,20},{28,16},{1,13},{... | collective-permute-start | bytes 200 | tf_op jit(solution)/shard_map/ppermute | solution.py:166
  28.4 7.8 %collective-permute-start.7 = (f32[2,1,8]{2,0,1:T(2,128)S(1)}, f32[2,1,8]{2,0,1:T(2,128)S(1)}, u32[]{:S(2)}, u32[]{:S(2)}) collective-permute-start(f32[2,1,8]{2,0,1:T(2,128)S(1)} %bitcast.94), channel_id=1, source_target_pairs={{0,16},{4,20},{8,24},{12,28},{16,0},{20,4},{24,8},{28,12},{1,17},{... | collective-permute-start | bytes 200 | tf_op jit(solution)/shard_map/ppermute | solution.py:166
  31.0 5.4 %collective-permute-start.8 = (f32[2,1,8]{2,0,1:T(2,128)S(1)}, f32[2,1,8]{2,0,1:T(2,128)S(1)}, u32[]{:S(2)}, u32[]{:S(2)}) collective-permute-start(f32[2,1,8]{2,0,1:T(2,128)S(1)} %bitcast.93), channel_id=1, source_target_pairs={{0,20},{4,16},{8,28},{12,24},{16,4},{20,0},{24,12},{28,8},{1,21},{... | collective-permute-start | bytes 200 | tf_op jit(solution)/shard_map/ppermute | solution.py:166
  32.7 5.4 %collective-permute-start.9 = (f32[2,1,8]{2,0,1:T(2,128)S(1)}, f32[2,1,8]{2,0,1:T(2,128)S(1)}, u32[]{:S(2)}, u32[]{:S(2)}) collective-permute-start(f32[2,1,8]{2,0,1:T(2,128)S(1)} %bitcast.92), channel_id=1, source_target_pairs={{0,24},{4,28},{8,16},{12,20},{16,8},{20,12},{24,0},{28,4},{1,25},{... | collective-permute-start | bytes 200 | tf_op jit(solution)/shard_map/ppermute | solution.py:166
  34.7 6.3 %collective-permute-start.10 = (f32[2,1,8]{2,0,1:T(2,128)S(1)}, f32[2,1,8]{2,0,1:T(2,128)S(1)}, u32[]{:S(2)}, u32[]{:S(2)}) collective-permute-start(f32[2,1,8]{2,0,1:T(2,128)S(1)} %bitcast.91), channel_id=1, source_target_pairs={{0,28},{4,24},{8,20},{12,16},{16,12},{20,8},{24,4},{28,0},{1,29},{... | collective-permute-start | bytes 200 | tf_op jit(solution)/shard_map/ppermute | solution.py:166

commit v9 on v7

--- a/solution.py
+++ b/solution.py
@@ -43,6 +43,18 @@
         lane = lax.broadcasted_iota(jnp.int32, values.shape, 2)
         shifted = jnp.where(lane == 0, 0.0, shifted)
     return shifted
+
+
+def swap_halos(first, last, axis):
+    count = lax.axis_size(axis)
+    odd = lax.axis_index(axis) % 2 == 1
+    inner = [(i, i ^ 1) for i in range(count) if i ^ 1 < count]
+    outer = [p for i in range(1, count - 1, 2) for p in ((i, i + 1), (i + 1, i))]
+    got_inner = lax.ppermute(jnp.where(odd, first, last), axis, inner)
+    got_outer = lax.ppermute(jnp.where(odd, last, first), axis, outer)
+    low = jnp.where(odd, got_inner, got_outer)
+    high = jnp.where(odd, got_outer, got_inner)
+    return low, high
 
 
 def leapfrog_kernel(
@@ -177,14 +189,16 @@
     n_x = lax.axis_size("slab") * depth_x
     n_y = lax.axis_size("yz") * depth_y
     parts = (field_e, field_h, permittivity, conductivity[None])
-    xlo = recv_from(jnp.concatenate([p[:, depth_x - HALO :] for p in parts], 0), "slab", -1)
-    xhi = recv_from(jnp.concatenate([p[:, :HALO] for p in parts], 0), "slab", 1)
+    xlo, xhi = swap_halos(
+        jnp.concatenate([p[:, :HALO] for p in parts], 0),
+        jnp.concatenate([p[:, depth_x - HALO :] for p in parts], 0),
+        "slab",
+    )
     def rows(start):
         center = jnp.concatenate([p[:, :, start : start + HALO] for p in parts], 0)
         return jnp.concatenate([center, xhi[:, :, start : start + HALO], xlo[:, :, start : start + HALO]], 1)
 
-    ylo = recv_from(rows(depth_y - HALO), "yz", -1)
-    yhi = recv_from(rows(0), "yz", 1)
+    ylo, yhi = swap_halos(rows(0), rows(depth_y - HALO), "yz")
     offsets = jnp.stack([lax.axis_index("slab") * depth_x, lax.axis_index("yz") * depth_y]).astype(jnp.int32)
     new_e, new_h, products = leapfrog(
         offsets, field_e, field_h, permittivity, conductivity[None], xlo, xhi, ylo, yhi,

time: 37.7 us -> 34.2 us (0.907)
  starting transfers between devices: 17.1 us -> 14.1 us
  waiting for transfers between devices: 8.81 us -> 7.51 us
  other arithmetic: 1.43 us -> 2.14 us
    ppermute x4, starting transfers between devices: 10.3 us -> 7.62 us  [the longest x2 4.42 us: swap_halos(): got_inner = lax.ppermute(jnp.where(odd, first, last), axis, inner)]
    unnamed x25 -> x21, local copies, waits for them, and re-layouts: 3.88 us -> 5.48 us
    slice x3, local copies, waits for them, and re-layouts: 1.49 us -> 0.01 us  [shards(): p[:, :HALO]]
    ppermute x4, waiting for transfers between devices: 3.61 us -> 2.61 us  [the longest x2 2.61 us: swap_halos(): got_outer = lax.ppermute(jnp.where(odd, last, first), axis, outer)]
    select_n x0 -> x5, other arithmetic: none -> 0.84 us  [the longest x2 0.68 us: swap_halos(): high = jnp.where(odd, got_outer, got_inner)]
    ppermute x3, starting transfers between devices: 4.14 us -> 3.55 us  [exchange_by_halving(): lax.ppermute(held[:, q], 'slab', [(i, i ^ q) for i in range(count)])]
  transfers between devices with their start and end apart: 8 -> 8, of which waited for: 6 -> 5; matrix products, arithmetic and copies ran while one was open for 6% -> 6% of each run, Pallas kernels for 0% -> 0%
where the time goes in v9:
time: 34.2 us; the launch traced here: 33.8 us
  starting transfers between devices  14.1 us (41%)
  waiting for transfers between devices  7.51 us (22%)
  local copies, waits for them, and re-layouts  6.82 us (20%)
  Pallas kernels  2.32 us (7%)
  other arithmetic  2.14 us (6%)
  between operations  0.92 us (3%)
    unnamed x21, local copies, waits for them, and re-layouts  5.48 us
    ppermute x2, starting transfers between devices, swap_halos(): got_inner = lax.ppermute(jnp.where(odd, first, last), axis, inner)  4.42 us
    ppermute x3, starting transfers between devices, exchange_by_halving(): lax.ppermute(held[:, q], 'slab', [(i, i ^ q) for i in range(count)])  3.55 us
    ppermute x3, waiting for transfers between devices, exchange_by_halving(): lax.ppermute(held[:, q], 'slab', [(i, i ^ q) for i in range(count)])  3.34 us
    ppermute x2, starting transfers between devices, swap_halos(): got_outer = lax.ppermute(jnp.where(odd, last, first), axis, outer)  3.2 us
    ppermute x1, starting transfers between devices, exchange_by_halving(): got = lax.ppermute(send, 'slab', pairs)  2.92 us
    ppermute x2, waiting for transfers between devices, swap_halos(): got_outer = lax.ppermute(jnp.where(odd, last, first), axis, outer)  2.61 us
    pallas_call x1, Pallas kernels, leapfrog(): pl.pallas_call(kernel, out_shape=(jax.ShapeDtypeStruct(field_e.shape, jnp...  2.32 us
  transfers between devices with their start and end apart: 8, of which 5 were waited for; matrix products, arithmetic and copies ran while one was open for 6% of the time, Pallas kernels for 0%

profile of v9, /device:TPU:2, one launch (start us, length us, event | category | flops | bytes accessed | tf_op | source)
XLA Modules:
  0.0 33.8 jit_solution(16575700308009764895)
XLA Ops:
  0.7 0.7 %copy-done.5 = f32[4,8,128]{2,1,0:T(8,128)S(1)} copy-done((f32[4,8,128]{2,1,0:T(8,128)S(1)}, f32[4,8,128]{2,1,0:T(8,128)}, u32[]{:S(2)}) %copy-start.5) | copy-done | bytes 16408
  1.4 0.1 copy-done.2
  1.5 0.8 %copy-done.3 = f32[3,4,8,128]{3,2,1,0:T(8,128)S(1)} copy-done((f32[3,4,8,128]{3,2,1,0:T(8,128)S(1)}, f32[3,4,8,128]{3,2,1,0:T(8,128)}, u32[]{:S(2)}) %copy-start.3) | copy-done | bytes 49176
  2.3 0.7 %collective-permute-start.1 = (f32[10,2,8,128]{3,2,1,0:T(8,128)S(1)}, f32[10,2,8,128]{3,2,1,0:T(8,128)S(1)}, u32[]{:S(2)}, u32[]{:S(2)}) collective-permute-start(f32[10,2,8,128]{3,2,1,0:T(8,128)S(1)} %get-tuple-element.13), channel_id=1, source_target_pairs={{4,8},{8,4},{12,16},{16,12},{20,24},{24,20},{5,9},{9,5},{13,17},{1... | collective-permute-start | bytes 245768 | tf_op jit(solution)/shard_map/ppermute | solution.py:54
  3.0 4.3 %collective-permute-start = (f32[10,2,8,128]{3,2,1,0:T(8,128)S(1)}, f32[10,2,8,128]{3,2,1,0:T(8,128)S(1)}, u32[]{:S(2)}, u32[]{:S(2)}) collective-permute-start(f32[10,2,8,128]{3,2,1,0:T(8,128)S(1)} %get-tuple-element.14), channel_id=1, source_target_pairs={{0,4},{4,0},{8,12},{12,8},{16,20},{20,16},{24,28},{28,24},{1,5},{5... | collective-permute-start | bytes 245768 | tf_op jit(solution)/shard_map/ppermute | solution.py:53
  7.4 0.7 %copy-done.6 = s32[1,1,8,8]{3,2,1,0:T(8,128)S(1)} copy-done((s32[1,1,8,8]{3,2,1,0:T(8,128)S(1)}, s32[1,1,8,8]{3,2,1,0:T(8,128)}, u32[]{:S(2)}) %copy-start.6) | copy-done | bytes 280
  8.2 0.7 %copy-done.8 = s32[1,1,8,8]{3,2,1,0:T(8,128)S(1)} copy-done((s32[1,1,8,8]{3,2,1,0:T(8,128)S(1)}, s32[1,1,8,8]{3,2,1,0:T(8,128)}, u32[]{:S(2)}) %copy-start.8) | copy-done | bytes 280
  8.8 0.6 %reshape.180.cell_ref = s32[1,64]{1,0:T(1,128)} reshape(s32[1,1,8,8]{3,2,1,0:T(8,128)S(1)} %copy-done.8) | data formatting | bytes 512 | tf_op jit(solution)/shard_map/reshape | solution.py:205
  9.5 0.7 %copy-done.9 = f32[1,1,2,3,64]{4,2,3,1,0:T(2,128)S(1)} copy-done((f32[1,1,2,3,64]{4,2,3,1,0:T(2,128)S(1)}, f32[1,1,2,3,64]{4,2,3,1,0:T(2,128)}, u32[]{:S(2)}) %copy-start.9) | copy-done | bytes 1560
  10.2 0.6 %copy.19 = f32[1,1,2,3,64]{4,3,2,1,0:T(4,128)} copy(f32[1,1,2,3,64]{4,2,3,1,0:T(2,128)S(1)} %copy-done.9) | data formatting | bytes 3072 | tf_op args[4]
  10.9 0.6 %copy-done = f32[10,2,8,128]{3,2,1,0:T(8,128)} copy-done((f32[10,2,8,128]{3,2,1,0:T(8,128)}, f32[10,2,8,128]{3,2,1,0:T(8,128)S(1)}, u32[]{:S(2)}) %copy-start) | copy-done | bytes 81944
  11.7 2.5 %collective-permute-start.3 = (f32[10,8,2,128]{3,2,1,0:T(2,128)S(1)}, f32[10,8,2,128]{3,2,1,0:T(2,128)S(1)}, u32[]{:S(2)}, u32[]{:S(2)}) collective-permute-start(f32[10,8,2,128]{3,2,1,0:T(2,128)S(1)} %broadcast_select_fusion.2), channel_id=1, source_target_pairs={{1,2},{2,1},{5,6},{6,5},{9,10},{10,9},{13,14},{14,13},{17,18},{18,... | collective-permute-start | bytes 245768 | tf_op jit(solution)/shard_map/ppermute | solution.py:54
  14.2 0.6 %pad_add_fusion.offsets = s32[2]{0:T(128)} fusion(s32[1]{0:T(128)} %bitcast.1, s32[1]{0:T(128)} %bitcast), kind=kLoop, calls=%fused_computation.31 | loop fusion | flops 2 | bytes 16 | tf_op jit(solution)/shard_map/stack | solution.py:202
  14.8 2.6 %collective-permute-done.3 = f32[10,8,2,128]{3,2,1,0:T(2,128)S(1)} collective-permute-done((f32[10,8,2,128]{3,2,1,0:T(2,128)S(1)}, f32[10,8,2,128]{3,2,1,0:T(2,128)S(1)}, u32[]{:S(2)}, u32[]{:S(2)}) %collective-permute-start.3) | collective-permute-done | bytes 81952 | tf_op jit(solution)/shard_map/ppermute | solution.py:54
  17.4 0.7 %broadcast_select_fusion = (f32[10,2,8,128]{3,2,1,0:T(8,128)}, f32[10,2,8,128]{3,2,1,0:T(8,128)}) fusion(f32[10,2,8,128]{3,2,1,0:T(8,128)S(1)} %bitcast.68, f32[10,2,8,128]{3,2,1,0:T(8,128)S(1)} %bitcast.67, pred[]{:T(512)S(6)} %eq.41), kind=kLoop, calls=%fused_computation.4 | loop fusion | flops 40960 | bytes 327681 | tf_op jit(solution)/shard_map/jit(_where)/select_n | solution.py:56
  18.1 2.3 %shard_map.94 = (f32[3,4,8,128]{3,2,1,0:T(8,128)}, f32[3,4,8,128]{3,2,1,0:T(8,128)}, f32[2,64]{1,0:T(2,128)}) custom-call(s32[2]{0:T(128)} %pad_add_fusion.offsets, f32[3,4,8,128]{3,2,1,0:T(8,128)} %e_ref.1, f32[3,4,8,128]{3,2,1,0:T(8,128)} %h_ref.1, f32[3,4,8,128]{3,2,1,0:T(8,128)} %perm_ref.1, f32[1,4,8,128]{3,2,1,0:T(8,128)} %bitcast.64, ...), custom_call_target="tpu_custom_call" | custom-call | tf_op jit(solution)/shard_map/pallas_call | solution.py:139
  20.4 0.7 %copy-done.7 = f32[2,64]{1,0:T(2,128)S(1)} copy-done((f32[2,64]{1,0:T(2,128)S(1)}, f32[2,64]{1,0:T(2,128)}, u32[]{:S(2)}) %copy-start.7) | copy-done | bytes 536
  21.1 0.1 reshape.198
  21.2 0.1 reshape.194
  21.3 0.1 reshape.191
  21.4 0.1 reshape_reshape.8
  21.6 2.9 %collective-permute-start.4 = (f32[2,4,1,8]{3,1,0,2:T(4,128)S(1)}, f32[2,4,1,8]{3,1,0,2:T(4,128)S(1)}, u32[]{:S(2)}, u32[]{:S(2)}) collective-permute-start(f32[2,4,1,8]{3,1,0,2:T(4,128)S(1)} %get-tuple-element.40), channel_id=1, source_target_pairs={{0,16},{4,20},{8,24},{12,28},{16,0},{20,4},{24,8},{28,12},{1,17},{... | collective-permute-start | bytes 776 | tf_op jit(solution)/shard_map/ppermute | solution.py:172
  24.5 0.1 eq.44
  24.6 1.6 %collective-permute-done.4 = f32[2,4,1,8]{3,1,0,2:T(4,128)S(1)} collective-permute-done((f32[2,4,1,8]{3,1,0,2:T(4,128)S(1)}, f32[2,4,1,8]{3,1,0,2:T(4,128)S(1)}, u32[]{:S(2)}, u32[]{:S(2)}) %collective-permute-start.4) | collective-permute-done | bytes 288 | tf_op jit(solution)/shard_map/ppermute | solution.py:172
  26.2 2.9 %collective-permute-start.7 = (f32[2,2,8]{2,1,0:T(2,128)S(1)}, f32[2,2,8]{2,1,0:T(2,128)S(1)}, u32[]{:S(2)}, u32[]{:S(2)}) collective-permute-start(f32[2,2,8]{2,1,0:T(2,128)S(1)} %get-tuple-element.36), channel_id=1, source_target_pairs={{0,12},{4,8},{8,4},{12,0},{16,28},{20,24},{24,20},{28,16},{1,13},{... | collective-permute-start | bytes 392 | tf_op jit(solution)/shard_map/ppermute | solution.py:178
  29.0 0.4 %collective-permute-start.6 = (f32[2,2,8]{2,1,0:T(2,128)S(1)}, f32[2,2,8]{2,1,0:T(2,128)S(1)}, u32[]{:S(2)}, u32[]{:S(2)}) collective-permute-start(f32[2,2,8]{2,1,0:T(2,128)S(1)} %get-tuple-element.37), channel_id=1, source_target_pairs={{0,8},{4,12},{8,0},{12,4},{16,24},{20,28},{24,16},{28,20},{1,9},{5... | collective-permute-start | bytes 392 | tf_op jit(solution)/shard_map/ppermute | solution.py:178
  29.5 0.2 collective-permute-start.5
  29.7 1.0 %collective-permute-done.7 = f32[2,2,8]{2,1,0:T(2,128)S(1)} collective-permute-done((f32[2,2,8]{2,1,0:T(2,128)S(1)}, f32[2,2,8]{2,1,0:T(2,128)S(1)}, u32[]{:S(2)}, u32[]{:S(2)}) %collective-permute-start.7) | collective-permute-done | bytes 160 | tf_op jit(solution)/shard_map/ppermute | solution.py:178
  30.7 1.9 %collective-permute-done.6 = f32[2,2,8]{2,1,0:T(2,128)S(1)} collective-permute-done((f32[2,2,8]{2,1,0:T(2,128)S(1)}, f32[2,2,8]{2,1,0:T(2,128)S(1)}, u32[]{:S(2)}, u32[]{:S(2)}) %collective-permute-start.6) | collective-permute-done | bytes 160 | tf_op jit(solution)/shard_map/ppermute | solution.py:178
  32.6 0.4 %collective-permute-done.5 = f32[2,2,8]{2,1,0:T(2,128)S(1)} collective-permute-done((f32[2,2,8]{2,1,0:T(2,128)S(1)}, f32[2,2,8]{2,1,0:T(2,128)S(1)}, u32[]{:S(2)}, u32[]{:S(2)}) %collective-permute-start.5) | collective-permute-done | bytes 160 | tf_op jit(solution)/shard_map/ppermute | solution.py:178
  33.1 0.1 broadcast_in_dim.27
  33.2 0.6 %select_reduce_fusion = f32[128]{0:T(128)} fusion(f32[128]{0:T(128)S(1)} %broadcast_in_dim.27, s32[128]{0:T(128)S(1)} %eq.44), kind=kLoop, calls=%fused_computation.8 | loop fusion | flops 49024 | bytes 1536 | tf_op jit(solution)/shard_map/reduce_sum | solution.py:215
  (47 shorter events, 0.6 us)
Async XLA Ops:
  0.6 0.7 %copy-start.5 = (f32[4,8,128]{2,1,0:T(8,128)S(1)}, f32[4,8,128]{2,1,0:T(8,128)}, u32[]{:S(2)}) copy-start(f32[4,8,128]{2,1,0:T(8,128)} %param.10) | copy-start | bytes 49156
  0.6 0.8 %copy-start.2 = (f32[3,4,8,128]{3,2,1,0:T(8,128)S(1)}, f32[3,4,8,128]{3,2,1,0:T(8,128)}, u32[]{:S(2)}) copy-start(f32[3,4,8,128]{3,2,1,0:T(8,128)} %perm_ref.1) | copy-start | bytes 147460
  1.4 0.8 %copy-start.3 = (f32[3,4,8,128]{3,2,1,0:T(8,128)S(1)}, f32[3,4,8,128]{3,2,1,0:T(8,128)}, u32[]{:S(2)}) copy-start(f32[3,4,8,128]{3,2,1,0:T(8,128)} %e_ref.1) | copy-start | bytes 147460
  1.4 0.8 %copy-start.4 = (f32[3,4,8,128]{3,2,1,0:T(8,128)S(1)}, f32[3,4,8,128]{3,2,1,0:T(8,128)}, u32[]{:S(2)}) copy-start(f32[3,4,8,128]{3,2,1,0:T(8,128)} %h_ref.1) | copy-start | bytes 147460
  2.3 8.5 %collective-permute-start.1 = (f32[10,2,8,128]{3,2,1,0:T(8,128)S(1)}, f32[10,2,8,128]{3,2,1,0:T(8,128)S(1)}, u32[]{:S(2)}, u32[]{:S(2)}) collective-permute-start(f32[10,2,8,128]{3,2,1,0:T(8,128)S(1)} %get-tuple-element.13), channel_id=1, source_target_pairs={{4,8},{8,4},{12,16},{16,12},{20,24},{24,20},{5,9},{9,5},{13,17},{1... | collective-permute-start | bytes 245768 | tf_op jit(solution)/shard_map/ppermute | solution.py:54
  3.0 7.8 %collective-permute-start = (f32[10,2,8,128]{3,2,1,0:T(8,128)S(1)}, f32[10,2,8,128]{3,2,1,0:T(8,128)S(1)}, u32[]{:S(2)}, u32[]{:S(2)}) collective-permute-start(f32[10,2,8,128]{3,2,1,0:T(8,128)S(1)} %get-tuple-element.14), channel_id=1, source_target_pairs={{0,4},{4,0},{8,12},{12,8},{16,20},{20,16},{24,28},{28,24},{1,5},{5... | collective-permute-start | bytes 245768 | tf_op jit(solution)/shard_map/ppermute | solution.py:53
  7.4 0.7 %copy-start.6 = (s32[1,1,8,8]{3,2,1,0:T(8,128)S(1)}, s32[1,1,8,8]{3,2,1,0:T(8,128)}, u32[]{:S(2)}) copy-start(s32[1,1,8,8]{3,2,1,0:T(8,128)} %param.13) | copy-start | bytes 772
  8.2 0.7 %copy-start.8 = (s32[1,1,8,8]{3,2,1,0:T(8,128)S(1)}, s32[1,1,8,8]{3,2,1,0:T(8,128)}, u32[]{:S(2)}) copy-start(s32[1,1,8,8]{3,2,1,0:T(8,128)} %param.12) | copy-start | bytes 772
  9.5 0.7 %copy-start.9 = (f32[1,1,2,3,64]{4,2,3,1,0:T(2,128)S(1)}, f32[1,1,2,3,64]{4,2,3,1,0:T(2,128)}, u32[]{:S(2)}) copy-start(f32[1,1,2,3,64]{4,2,3,1,0:T(2,128)} %param.11) | copy-start | bytes 4612
  10.8 0.6 %copy-start = (f32[10,2,8,128]{3,2,1,0:T(8,128)}, f32[10,2,8,128]{3,2,1,0:T(8,128)S(1)}, u32[]{:S(2)}) copy-start(f32[10,2,8,128]{3,2,1,0:T(8,128)S(1)} %get-tuple-element.11.xhi_ref) | copy-start | bytes 245764
  10.8 0.7 %copy-start.1 = (f32[10,2,8,128]{3,2,1,0:T(8,128)}, f32[10,2,8,128]{3,2,1,0:T(8,128)S(1)}, u32[]{:S(2)}) copy-start(f32[10,2,8,128]{3,2,1,0:T(8,128)S(1)} %get-tuple-element.12.xlo_ref) | copy-start | bytes 245764
  11.6 3.2 %collective-permute-start.2 = (f32[10,8,2,128]{3,2,1,0:T(2,128)S(1)}, f32[10,8,2,128]{3,2,1,0:T(2,128)S(1)}, u32[]{:S(2)}, u32[]{:S(2)}) collective-permute-start(f32[10,8,2,128]{3,2,1,0:T(2,128)S(1)} %broadcast_select_fusion.3), channel_id=1, source_target_pairs={{0,1},{1,0},{2,3},{3,2},{4,5},{5,4},{6,7},{7,6},{8,9},{9,8},{10,11... | collective-permute-start | bytes 245768 | tf_op jit(solution)/shard_map/ppermute | solution.py:53
  11.7 5.8 %collective-permute-start.3 = (f32[10,8,2,128]{3,2,1,0:T(2,128)S(1)}, f32[10,8,2,128]{3,2,1,0:T(2,128)S(1)}, u32[]{:S(2)}, u32[]{:S(2)}) collective-permute-start(f32[10,8,2,128]{3,2,1,0:T(2,128)S(1)} %broadcast_select_fusion.2), channel_id=1, source_target_pairs={{1,2},{2,1},{5,6},{6,5},{9,10},{10,9},{13,14},{14,13},{17,18},{18,... | collective-permute-start | bytes 245768 | tf_op jit(solution)/shard_map/ppermute | solution.py:54
  20.4 0.7 %copy-start.7 = (f32[2,64]{1,0:T(2,128)S(1)}, f32[2,64]{1,0:T(2,128)}, u32[]{:S(2)}) copy-start(f32[2,64]{1,0:T(2,128)} %get-tuple-element.8) | copy-start | bytes 1540
  21.6 4.6 %collective-permute-start.4 = (f32[2,4,1,8]{3,1,0,2:T(4,128)S(1)}, f32[2,4,1,8]{3,1,0,2:T(4,128)S(1)}, u32[]{:S(2)}, u32[]{:S(2)}) collective-permute-start(f32[2,4,1,8]{3,1,0,2:T(4,128)S(1)} %get-tuple-element.40), channel_id=1, source_target_pairs={{0,16},{4,20},{8,24},{12,28},{16,0},{20,4},{24,8},{28,12},{1,17},{... | collective-permute-start | bytes 776 | tf_op jit(solution)/shard_map/ppermute | solution.py:172
  26.2 4.5 %collective-permute-start.7 = (f32[2,2,8]{2,1,0:T(2,128)S(1)}, f32[2,2,8]{2,1,0:T(2,128)S(1)}, u32[]{:S(2)}, u32[]{:S(2)}) collective-permute-start(f32[2,2,8]{2,1,0:T(2,128)S(1)} %get-tuple-element.36), channel_id=1, source_target_pairs={{0,12},{4,8},{8,4},{12,0},{16,28},{20,24},{24,20},{28,16},{1,13},{... | collective-permute-start | bytes 392 | tf_op jit(solution)/shard_map/ppermute | solution.py:178
  29.0 3.6 %collective-permute-start.6 = (f32[2,2,8]{2,1,0:T(2,128)S(1)}, f32[2,2,8]{2,1,0:T(2,128)S(1)}, u32[]{:S(2)}, u32[]{:S(2)}) collective-permute-start(f32[2,2,8]{2,1,0:T(2,128)S(1)} %get-tuple-element.37), channel_id=1, source_target_pairs={{0,8},{4,12},{8,0},{12,4},{16,24},{20,28},{24,16},{28,20},{1,9},{5... | collective-permute-start | bytes 392 | tf_op jit(solution)/shard_map/ppermute | solution.py:178
  29.5 3.6 %collective-permute-start.5 = (f32[2,2,8]{2,1,0:T(2,128)S(1)}, f32[2,2,8]{2,1,0:T(2,128)S(1)}, u32[]{:S(2)}, u32[]{:S(2)}) collective-permute-start(f32[2,2,8]{2,1,0:T(2,128)S(1)} %get-tuple-element.38), channel_id=1, source_target_pairs={{0,4},{4,0},{8,12},{12,8},{16,20},{20,16},{24,28},{28,24},{1,5},{5... | collective-permute-start | bytes 392 | tf_op jit(solution)/shard_map/ppermute | solution.py:178

commit v10 on v9

--- a/solution.py
+++ b/solution.py
@@ -52,34 +52,39 @@
     outer = [p for i in range(1, count - 1, 2) for p in ((i, i + 1), (i + 1, i))]
     got_inner = lax.ppermute(jnp.where(odd, first, last), axis, inner)
     got_outer = lax.ppermute(jnp.where(odd, last, first), axis, outer)
-    low = jnp.where(odd, got_inner, got_outer)
-    high = jnp.where(odd, got_outer, got_inner)
-    return low, high
+    return got_inner, got_outer
+
+
+def low_high(got_inner, got_outer, odd):
+    return jnp.where(odd, got_inner, got_outer), jnp.where(odd, got_outer, got_inner)
 
 
 def leapfrog_kernel(
-    dims, offsets, e_ref, h_ref, perm_ref, cond_ref, xlo_ref, xhi_ref, ylo_ref, yhi_ref,
+    dims, e_ref, h_ref, perm_ref, cond_ref, x_inner_ref, x_outer_ref, y_inner_ref, y_outer_ref,
     cell_ref, fwd_ref, e_out, h_out, prod_out, ring,
 ):
     depth_x, depth_y, n_x, n_y = dims
     ring_x, ring_y = ring.shape[1], ring.shape[2]
+    slab, yz = lax.axis_index("slab"), lax.axis_index("yz")
+    xlo, xhi = low_high(x_inner_ref[...], x_outer_ref[...], slab % 2 == 1)
+    ylo, yhi = low_high(y_inner_ref[...], y_outer_ref[...], yz % 2 == 1)
     ring[0:3, 0:depth_x, 0:depth_y] = e_ref[...]
     ring[3:6, 0:depth_x, 0:depth_y] = h_ref[...]
     ring[6:9, 0:depth_x, 0:depth_y] = perm_ref[...]
     ring[9:10, 0:depth_x, 0:depth_y] = cond_ref[...]
-    ring[:, depth_x : depth_x + HALO, 0:depth_y] = xhi_ref[...]
-    ring[:, ring_x - HALO : ring_x, 0:depth_y] = xlo_ref[...]
-    ring[:, :, depth_y : depth_y + HALO] = yhi_ref[...]
+    ring[:, depth_x : depth_x + HALO, 0:depth_y] = xhi
+    ring[:, ring_x - HALO : ring_x, 0:depth_y] = xlo
+    ring[:, :, depth_y : depth_y + HALO] = yhi
     ring[:, :, depth_y + HALO : ring_y - HALO] = jnp.zeros(
         (ring.shape[0], ring_x, ring_y - depth_y - 2 * HALO, LANES), jnp.float32
     )
-    ring[:, :, ring_y - HALO : ring_y] = ylo_ref[...]
+    ring[:, :, ring_y - HALO : ring_y] = ylo
 
     shape = (ring_x, ring_y, LANES)
     xi = lax.broadcasted_iota(jnp.int32, shape, 0)
     yi = lax.broadcasted_iota(jnp.int32, shape, 1)
-    gx = offsets[0] + jnp.where(xi < depth_x + HALO, xi, xi - ring_x)
-    gy = offsets[1] + jnp.where(yi < depth_y + HALO, yi, yi - ring_y)
+    gx = slab * depth_x + jnp.where(xi < depth_x + HALO, xi, xi - ring_x)
+    gy = yz * depth_y + jnp.where(yi < depth_y + HALO, yi, yi - ring_y)
     y_real = (yi < depth_y + HALO) | (yi >= ring_y - HALO)
     inside = (gx >= 0) & (gx < n_x) & (gy >= 0) & (gy < n_y) & y_real
 
@@ -129,12 +134,11 @@
         h_out[c] = field_h[c][0:depth_x, 0:depth_y]
 
 
-def leapfrog(offsets, field_e, field_h, permittivity, conductivity, xlo, xhi, ylo, yhi, cells, fwd, n_x, n_y):
+def leapfrog(field_e, field_h, permittivity, conductivity, xlo, xhi, ylo, yhi, cells, fwd, n_x, n_y):
     _, depth_x, depth_y, _ = field_e.shape
     ring_x = depth_x + 2 * HALO
     ring_y = -(-(depth_y + 2 * HALO) // 8) * 8
     vmem = pl.BlockSpec(memory_space=pltpu.VMEM)
-    smem = pl.BlockSpec(memory_space=pltpu.SMEM)
     kernel = functools.partial(leapfrog_kernel, (depth_x, depth_y, n_x, n_y))
     return pl.pallas_call(
         kernel,
@@ -143,10 +147,10 @@
             jax.ShapeDtypeStruct(field_h.shape, jnp.float32),
             jax.ShapeDtypeStruct((STEPS, cells.shape[1]), jnp.float32),
         ),
-        in_specs=[smem] + [vmem] * 10,
+        in_specs=[vmem] * 10,
         out_specs=(vmem, vmem, vmem),
         scratch_shapes=[pltpu.VMEM((10, ring_x, ring_y, LANES), jnp.float32)],
-    )(offsets, field_e, field_h, permittivity, conductivity, xlo, xhi, ylo, yhi, cells, fwd)
+    )(field_e, field_h, permittivity, conductivity, xlo, xhi, ylo, yhi, cells, fwd)
 
 
 def xor_rows(array, me, count, axis):
@@ -189,19 +193,19 @@
     n_x = lax.axis_size("slab") * depth_x
     n_y = lax.axis_size("yz") * depth_y
     parts = (field_e, field_h, permittivity, conductivity[None])
-    xlo, xhi = swap_halos(
+    x_inner, x_outer = swap_halos(
         jnp.concatenate([p[:, :HALO] for p in parts], 0),
         jnp.concatenate([p[:, depth_x - HALO :] for p in parts], 0),
         "slab",
     )
+    xlo, xhi = low_high(x_inner, x_outer, lax.axis_index("slab") % 2 == 1)
     def rows(start):
         center = jnp.concatenate([p[:, :, start : start + HALO] for p in parts], 0)
         return jnp.concatenate([center, xhi[:, :, start : start + HALO], xlo[:, :, start : start + HALO]], 1)
 
-    ylo, yhi = swap_halos(rows(0), rows(depth_y - HALO), "yz")
-    offsets = jnp.stack([lax.axis_index("slab") * depth_x, lax.axis_index("yz") * depth_y]).astype(jnp.int32)
+    y_inner, y_outer = swap_halos(rows(0), rows(depth_y - HALO), "yz")
     new_e, new_h, products = leapfrog(
-        offsets, field_e, field_h, permittivity, conductivity[None], xlo, xhi, ylo, yhi,
+        field_e, field_h, permittivity, conductivity[None], x_inner, x_outer, y_inner, y_outer,
         slot_cell.reshape(1, -1), forward_e[0, 0], n_x, n_y,
     )
     products = products.reshape(STEPS, sources, capacity)

time: 34.2 us -> 34.1 us (level)
  other arithmetic: 2.14 us -> 0.86 us
  starting transfers between devices: 14.1 us -> 14.8 us
  local copies, waits for them, and re-layouts: 6.82 us -> 7.34 us
    ppermute x2, waiting for transfers between devices: 2.61 us -> 0.63 us  [swap_halos(): got_outer = lax.ppermute(jnp.where(odd, last, first), axis, outer)]
    ppermute x2, waiting for transfers between devices: 0.01 us -> 1.93 us  [swap_halos(): got_inner = lax.ppermute(jnp.where(odd, first, last), axis, inner)]
    ppermute x1, starting transfers between devices: 2.92 us -> 3.62 us  [exchange_by_halving(): got = lax.ppermute(send, 'slab', pairs)]
    select_n x2 -> x1, other arithmetic: 0.68 us -> 0.01 us  [low_high(): jnp.where(odd, got_outer, got_inner)]
    another operation x1 -> x0, other arithmetic: 0.61 us -> none  [shards(): jnp.stack([lax.axis_index('slab') * depth_x, lax.axis_index('yz') * depth...]
    unnamed x21 -> x25, local copies, waits for them, and re-layouts: 5.48 us -> 6.06 us
  transfers between devices with their start and end apart: 8 -> 8, of which waited for: 5 -> 6; matrix products, arithmetic and copies ran while one was open for 6% -> 4% of each run, Pallas kernels for 0% -> 0%
where the time goes in v10:
time: 34.1 us; the launch traced here: 33.7 us
  starting transfers between devices  14.8 us (43%)
  waiting for transfers between devices  7.44 us (22%)
  local copies, waits for them, and re-layouts  7.34 us (22%)
  Pallas kernels  2.28 us (7%)
  between operations  0.95 us (3%)
  other arithmetic  0.86 us (3%)
    unnamed x25, local copies, waits for them, and re-layouts  6.06 us
    ppermute x2, starting transfers between devices, swap_halos(): got_inner = lax.ppermute(jnp.where(odd, first, last), axis, inner)  4.42 us
    ppermute x1, starting transfers between devices, exchange_by_halving(): got = lax.ppermute(send, 'slab', pairs)  3.62 us
    ppermute x3, starting transfers between devices, exchange_by_halving(): lax.ppermute(held[:, q], 'slab', [(i, i ^ q) for i in range(count)])  3.57 us
    ppermute x3, waiting for transfers between devices, exchange_by_halving(): lax.ppermute(held[:, q], 'slab', [(i, i ^ q) for i in range(count)])  3.39 us
    ppermute x2, starting transfers between devices, swap_halos(): got_outer = lax.ppermute(jnp.where(odd, last, first), axis, outer)  3.2 us
    pallas_call x1, Pallas kernels, leapfrog(): pl.pallas_call(kernel, out_shape=(jax.ShapeDtypeStruct(field_e.shape, jnp...  2.28 us
    ppermute x2, waiting for transfers between devices, swap_halos(): got_inner = lax.ppermute(jnp.where(odd, first, last), axis, inner)  1.93 us
  transfers between devices with their start and end apart: 8, of which 6 were waited for; matrix products, arithmetic and copies ran while one was open for 4% of the time, Pallas kernels for 0%

profile of v10, /device:TPU:2, one launch (start us, length us, event | category | flops | bytes accessed | tf_op | source)
XLA Modules:
  0.0 33.7 jit_solution(5851249269740321158)
XLA Ops:
  0.7 0.7 %copy-done.5 = f32[4,8,128]{2,1,0:T(8,128)S(1)} copy-done((f32[4,8,128]{2,1,0:T(8,128)S(1)}, f32[4,8,128]{2,1,0:T(8,128)}, u32[]{:S(2)}) %copy-start.5) | copy-done | bytes 16408
  1.4 0.1 copy-done.2
  1.5 0.8 %copy-done.3 = f32[3,4,8,128]{3,2,1,0:T(8,128)S(1)} copy-done((f32[3,4,8,128]{3,2,1,0:T(8,128)S(1)}, f32[3,4,8,128]{3,2,1,0:T(8,128)}, u32[]{:S(2)}) %copy-start.3) | copy-done | bytes 49176
  2.3 0.7 %collective-permute-start.1 = (f32[10,2,8,128]{3,2,1,0:T(8,128)S(1)}, f32[10,2,8,128]{3,2,1,0:T(8,128)S(1)}, u32[]{:S(2)}, u32[]{:S(2)}) collective-permute-start(f32[10,2,8,128]{3,2,1,0:T(8,128)S(1)} %get-tuple-element.11), channel_id=1, source_target_pairs={{4,8},{8,4},{12,16},{16,12},{20,24},{24,20},{5,9},{9,5},{13,17},{1... | collective-permute-start | bytes 245768 | tf_op jit(solution)/shard_map/ppermute | solution.py:54
  3.0 4.3 %collective-permute-start = (f32[10,2,8,128]{3,2,1,0:T(8,128)S(1)}, f32[10,2,8,128]{3,2,1,0:T(8,128)S(1)}, u32[]{:S(2)}, u32[]{:S(2)}) collective-permute-start(f32[10,2,8,128]{3,2,1,0:T(8,128)S(1)} %get-tuple-element.12), channel_id=1, source_target_pairs={{0,4},{4,0},{8,12},{12,8},{16,20},{20,16},{24,28},{28,24},{1,5},{5... | collective-permute-start | bytes 245768 | tf_op jit(solution)/shard_map/ppermute | solution.py:53
  7.4 0.7 %copy-done.8 = s32[1,1,8,8]{3,2,1,0:T(8,128)S(1)} copy-done((s32[1,1,8,8]{3,2,1,0:T(8,128)S(1)}, s32[1,1,8,8]{3,2,1,0:T(8,128)}, u32[]{:S(2)}) %copy-start.8) | copy-done | bytes 280
  8.1 1.9 %collective-permute-done.x_inner_ref = f32[10,2,8,128]{3,2,1,0:T(8,128)S(1)} collective-permute-done((f32[10,2,8,128]{3,2,1,0:T(8,128)S(1)}, f32[10,2,8,128]{3,2,1,0:T(8,128)S(1)}, u32[]{:S(2)}, u32[]{:S(2)}) %collective-permute-start) | collective-permute-done | bytes 81952 | tf_op jit(solution)/shard_map/ppermute | solution.py:53
  10.1 0.6 %copy-done.1 = f32[10,2,8,128]{3,2,1,0:T(8,128)} copy-done((f32[10,2,8,128]{3,2,1,0:T(8,128)}, f32[10,2,8,128]{3,2,1,0:T(8,128)S(1)}, u32[]{:S(2)}) %copy-start.1) | copy-done | bytes 81944
  11.0 2.5 %collective-permute-start.3 = (f32[10,8,2,128]{3,2,1,0:T(2,128)S(1)}, f32[10,8,2,128]{3,2,1,0:T(2,128)S(1)}, u32[]{:S(2)}, u32[]{:S(2)}) collective-permute-start(f32[10,8,2,128]{3,2,1,0:T(2,128)S(1)} %broadcast_select_fusion), channel_id=1, source_target_pairs={{1,2},{2,1},{5,6},{6,5},{9,10},{10,9},{13,14},{14,13},{17,18},{18,... | collective-permute-start | bytes 245768 | tf_op jit(solution)/shard_map/ppermute | solution.py:54
  13.6 0.7 %copy-done.10 = s32[1,1,8,8]{3,2,1,0:T(8,128)S(1)} copy-done((s32[1,1,8,8]{3,2,1,0:T(8,128)S(1)}, s32[1,1,8,8]{3,2,1,0:T(8,128)}, u32[]{:S(2)}) %copy-start.10) | copy-done | bytes 280
  14.2 0.6 %reshape.180.cell_ref = s32[1,64]{1,0:T(1,128)} reshape(s32[1,1,8,8]{3,2,1,0:T(8,128)S(1)} %copy-done.10) | data formatting | bytes 512 | tf_op jit(solution)/shard_map/reshape | solution.py:209
  14.8 0.7 %copy-done.11 = f32[1,1,2,3,64]{4,2,3,1,0:T(2,128)S(1)} copy-done((f32[1,1,2,3,64]{4,2,3,1,0:T(2,128)S(1)}, f32[1,1,2,3,64]{4,2,3,1,0:T(2,128)}, u32[]{:S(2)}) %copy-start.11) | copy-done | bytes 1560
  15.5 0.6 %copy.19 = f32[1,1,2,3,64]{4,3,2,1,0:T(4,128)} copy(f32[1,1,2,3,64]{4,2,3,1,0:T(2,128)S(1)} %copy-done.11) | data formatting | bytes 3072 | tf_op args[4]
  16.1 0.6 %collective-permute-done.3.y_outer_ref = f32[10,8,2,128]{3,2,1,0:T(2,128)S(1)} collective-permute-done((f32[10,8,2,128]{3,2,1,0:T(2,128)S(1)}, f32[10,8,2,128]{3,2,1,0:T(2,128)S(1)}, u32[]{:S(2)}, u32[]{:S(2)}) %collective-permute-start.3) | collective-permute-done | bytes 81952 | tf_op jit(solution)/shard_map/ppermute | solution.py:54
  16.7 0.6 %copy-done.7 = f32[10,8,2,128]{3,2,1,0:T(2,128)} copy-done((f32[10,8,2,128]{3,2,1,0:T(2,128)}, f32[10,8,2,128]{3,2,1,0:T(2,128)S(1)}, u32[]{:S(2)}) %copy-start.7) | copy-done | bytes 81944
  17.4 2.3 %shard_map.94 = (f32[3,4,8,128]{3,2,1,0:T(8,128)}, f32[3,4,8,128]{3,2,1,0:T(8,128)}, f32[2,64]{1,0:T(2,128)}) custom-call(f32[3,4,8,128]{3,2,1,0:T(8,128)} %e_ref.1, f32[3,4,8,128]{3,2,1,0:T(8,128)} %h_ref.1, f32[3,4,8,128]{3,2,1,0:T(8,128)} %perm_ref.1, f32[1,4,8,128]{3,2,1,0:T(8,128)} %bitcast.56, f32[10,2,8,128]{3,2,1,0:T(8,128)} %copy-done.1, ...), custom_call_target="tpu_custom_call" | custom-call | tf_op jit(solution)/shard_map/pallas_call | solution.py:143
  19.6 0.6 %copy-done.9 = f32[2,64]{1,0:T(2,128)S(1)} copy-done((f32[2,64]{1,0:T(2,128)S(1)}, f32[2,64]{1,0:T(2,128)}, u32[]{:S(2)}) %copy-start.9) | copy-done | bytes 536
  20.3 0.1 reshape.198
  20.4 0.1 reshape.194
  20.4 0.1 reshape.191
  20.5 0.1 reshape_reshape.8
  20.7 3.6 %collective-permute-start.4 = (f32[2,4,1,8]{3,1,0,2:T(4,128)S(1)}, f32[2,4,1,8]{3,1,0,2:T(4,128)S(1)}, u32[]{:S(2)}, u32[]{:S(2)}) collective-permute-start(f32[2,4,1,8]{3,1,0,2:T(4,128)S(1)} %get-tuple-element.38), channel_id=1, source_target_pairs={{0,16},{4,20},{8,24},{12,28},{16,0},{20,4},{24,8},{28,12},{1,17},{... | collective-permute-start | bytes 776 | tf_op jit(solution)/shard_map/ppermute | solution.py:176
  24.4 0.1 eq.46
  24.5 1.5 %collective-permute-done.4 = f32[2,4,1,8]{3,1,0,2:T(4,128)S(1)} collective-permute-done((f32[2,4,1,8]{3,1,0,2:T(4,128)S(1)}, f32[2,4,1,8]{3,1,0,2:T(4,128)S(1)}, u32[]{:S(2)}, u32[]{:S(2)}) %collective-permute-start.4) | collective-permute-done | bytes 288 | tf_op jit(solution)/shard_map/ppermute | solution.py:176
  26.0 2.9 %collective-permute-start.7 = (f32[2,2,8]{2,1,0:T(2,128)S(1)}, f32[2,2,8]{2,1,0:T(2,128)S(1)}, u32[]{:S(2)}, u32[]{:S(2)}) collective-permute-start(f32[2,2,8]{2,1,0:T(2,128)S(1)} %get-tuple-element.34), channel_id=1, source_target_pairs={{0,12},{4,8},{8,4},{12,0},{16,28},{20,24},{24,20},{28,16},{1,13},{... | collective-permute-start | bytes 392 | tf_op jit(solution)/shard_map/ppermute | solution.py:182
  28.9 0.4 %collective-permute-start.6 = (f32[2,2,8]{2,1,0:T(2,128)S(1)}, f32[2,2,8]{2,1,0:T(2,128)S(1)}, u32[]{:S(2)}, u32[]{:S(2)}) collective-permute-start(f32[2,2,8]{2,1,0:T(2,128)S(1)} %get-tuple-element.35), channel_id=1, source_target_pairs={{0,8},{4,12},{8,0},{12,4},{16,24},{20,28},{24,16},{28,20},{1,9},{5... | collective-permute-start | bytes 392 | tf_op jit(solution)/shard_map/ppermute | solution.py:182
  29.3 0.2 collective-permute-start.5
  29.5 1.0 %collective-permute-done.7 = f32[2,2,8]{2,1,0:T(2,128)S(1)} collective-permute-done((f32[2,2,8]{2,1,0:T(2,128)S(1)}, f32[2,2,8]{2,1,0:T(2,128)S(1)}, u32[]{:S(2)}, u32[]{:S(2)}) %collective-permute-start.7) | collective-permute-done | bytes 160 | tf_op jit(solution)/shard_map/ppermute | solution.py:182
  30.5 2.0 %collective-permute-done.6 = f32[2,2,8]{2,1,0:T(2,128)S(1)} collective-permute-done((f32[2,2,8]{2,1,0:T(2,128)S(1)}, f32[2,2,8]{2,1,0:T(2,128)S(1)}, u32[]{:S(2)}, u32[]{:S(2)}) %collective-permute-start.6) | collective-permute-done | bytes 160 | tf_op jit(solution)/shard_map/ppermute | solution.py:182
  32.5 0.4 %collective-permute-done.5 = f32[2,2,8]{2,1,0:T(2,128)S(1)} collective-permute-done((f32[2,2,8]{2,1,0:T(2,128)S(1)}, f32[2,2,8]{2,1,0:T(2,128)S(1)}, u32[]{:S(2)}, u32[]{:S(2)}) %collective-permute-start.5) | collective-permute-done | bytes 160 | tf_op jit(solution)/shard_map/ppermute | solution.py:182
  32.9 0.1 broadcast_in_dim.27
  33.0 0.6 %select_reduce_fusion = f32[128]{0:T(128)} fusion(f32[128]{0:T(128)S(1)} %broadcast_in_dim.27, s32[128]{0:T(128)S(1)} %eq.46), kind=kLoop, calls=%fused_computation.6 | loop fusion | flops 49024 | bytes 1536 | tf_op jit(solution)/shard_map/reduce_sum | solution.py:219
  (49 shorter events, 0.5 us)
Async XLA Ops:
  0.6 0.7 %copy-start.5 = (f32[4,8,128]{2,1,0:T(8,128)S(1)}, f32[4,8,128]{2,1,0:T(8,128)}, u32[]{:S(2)}) copy-start(f32[4,8,128]{2,1,0:T(8,128)} %param.10) | copy-start | bytes 49156
  0.6 0.8 %copy-start.2 = (f32[3,4,8,128]{3,2,1,0:T(8,128)S(1)}, f32[3,4,8,128]{3,2,1,0:T(8,128)}, u32[]{:S(2)}) copy-start(f32[3,4,8,128]{3,2,1,0:T(8,128)} %perm_ref.1) | copy-start | bytes 147460
  1.4 0.8 %copy-start.3 = (f32[3,4,8,128]{3,2,1,0:T(8,128)S(1)}, f32[3,4,8,128]{3,2,1,0:T(8,128)}, u32[]{:S(2)}) copy-start(f32[3,4,8,128]{3,2,1,0:T(8,128)} %e_ref.1) | copy-start | bytes 147460
  1.4 0.8 %copy-start.4 = (f32[3,4,8,128]{3,2,1,0:T(8,128)S(1)}, f32[3,4,8,128]{3,2,1,0:T(8,128)}, u32[]{:S(2)}) copy-start(f32[3,4,8,128]{3,2,1,0:T(8,128)} %h_ref.1) | copy-start | bytes 147460
  2.3 5.8 %collective-permute-start.1 = (f32[10,2,8,128]{3,2,1,0:T(8,128)S(1)}, f32[10,2,8,128]{3,2,1,0:T(8,128)S(1)}, u32[]{:S(2)}, u32[]{:S(2)}) collective-permute-start(f32[10,2,8,128]{3,2,1,0:T(8,128)S(1)} %get-tuple-element.11), channel_id=1, source_target_pairs={{4,8},{8,4},{12,16},{16,12},{20,24},{24,20},{5,9},{9,5},{13,17},{1... | collective-permute-start | bytes 245768 | tf_op jit(solution)/shard_map/ppermute | solution.py:54
  3.0 7.1 %collective-permute-start = (f32[10,2,8,128]{3,2,1,0:T(8,128)S(1)}, f32[10,2,8,128]{3,2,1,0:T(8,128)S(1)}, u32[]{:S(2)}, u32[]{:S(2)}) collective-permute-start(f32[10,2,8,128]{3,2,1,0:T(8,128)S(1)} %get-tuple-element.12), channel_id=1, source_target_pairs={{0,4},{4,0},{8,12},{12,8},{16,20},{20,16},{24,28},{28,24},{1,5},{5... | collective-permute-start | bytes 245768 | tf_op jit(solution)/shard_map/ppermute | solution.py:53
  7.3 0.7 %copy-start.8 = (s32[1,1,8,8]{3,2,1,0:T(8,128)S(1)}, s32[1,1,8,8]{3,2,1,0:T(8,128)}, u32[]{:S(2)}) copy-start(s32[1,1,8,8]{3,2,1,0:T(8,128)} %param.13) | copy-start | bytes 772
  8.1 2.0 %copy-start = (f32[10,2,8,128]{3,2,1,0:T(8,128)}, f32[10,2,8,128]{3,2,1,0:T(8,128)S(1)}, u32[]{:S(2)}) copy-start(f32[10,2,8,128]{3,2,1,0:T(8,128)S(1)} %collective-permute-done.1.x_outer_ref) | copy-start | bytes 245764
  10.1 0.6 %copy-start.1 = (f32[10,2,8,128]{3,2,1,0:T(8,128)}, f32[10,2,8,128]{3,2,1,0:T(8,128)S(1)}, u32[]{:S(2)}) copy-start(f32[10,2,8,128]{3,2,1,0:T(8,128)S(1)} %collective-permute-done.x_inner_ref) | copy-start | bytes 245764
  10.9 5.2 %collective-permute-start.2 = (f32[10,8,2,128]{3,2,1,0:T(2,128)S(1)}, f32[10,8,2,128]{3,2,1,0:T(2,128)S(1)}, u32[]{:S(2)}, u32[]{:S(2)}) collective-permute-start(f32[10,8,2,128]{3,2,1,0:T(2,128)S(1)} %broadcast_select_fusion.1), channel_id=1, source_target_pairs={{0,1},{1,0},{2,3},{3,2},{4,5},{5,4},{6,7},{7,6},{8,9},{9,8},{10,11... | collective-permute-start | bytes 245768 | tf_op jit(solution)/shard_map/ppermute | solution.py:53
  11.0 5.8 %collective-permute-start.3 = (f32[10,8,2,128]{3,2,1,0:T(2,128)S(1)}, f32[10,8,2,128]{3,2,1,0:T(2,128)S(1)}, u32[]{:S(2)}, u32[]{:S(2)}) collective-permute-start(f32[10,8,2,128]{3,2,1,0:T(2,128)S(1)} %broadcast_select_fusion), channel_id=1, source_target_pairs={{1,2},{2,1},{5,6},{6,5},{9,10},{10,9},{13,14},{14,13},{17,18},{18,... | collective-permute-start | bytes 245768 | tf_op jit(solution)/shard_map/ppermute | solution.py:54
  13.5 0.7 %copy-start.10 = (s32[1,1,8,8]{3,2,1,0:T(8,128)S(1)}, s32[1,1,8,8]{3,2,1,0:T(8,128)}, u32[]{:S(2)}) copy-start(s32[1,1,8,8]{3,2,1,0:T(8,128)} %param.12) | copy-start | bytes 772
  14.8 0.7 %copy-start.11 = (f32[1,1,2,3,64]{4,2,3,1,0:T(2,128)S(1)}, f32[1,1,2,3,64]{4,2,3,1,0:T(2,128)}, u32[]{:S(2)}) copy-start(f32[1,1,2,3,64]{4,2,3,1,0:T(2,128)} %param.11) | copy-start | bytes 4612
  16.1 0.6 %copy-start.6 = (f32[10,8,2,128]{3,2,1,0:T(2,128)}, f32[10,8,2,128]{3,2,1,0:T(2,128)S(1)}, u32[]{:S(2)}) copy-start(f32[10,8,2,128]{3,2,1,0:T(2,128)S(1)} %collective-permute-done.2.y_inner_ref) | copy-start | bytes 245764
  16.7 0.6 %copy-start.7 = (f32[10,8,2,128]{3,2,1,0:T(2,128)}, f32[10,8,2,128]{3,2,1,0:T(2,128)S(1)}, u32[]{:S(2)}) copy-start(f32[10,8,2,128]{3,2,1,0:T(2,128)S(1)} %collective-permute-done.3.y_outer_ref) | copy-start | bytes 245764
  19.6 0.6 %copy-start.9 = (f32[2,64]{1,0:T(2,128)S(1)}, f32[2,64]{1,0:T(2,128)}, u32[]{:S(2)}) copy-start(f32[2,64]{1,0:T(2,128)} %get-tuple-element.8) | copy-start | bytes 1540
  20.7 5.2 %collective-permute-start.4 = (f32[2,4,1,8]{3,1,0,2:T(4,128)S(1)}, f32[2,4,1,8]{3,1,0,2:T(4,128)S(1)}, u32[]{:S(2)}, u32[]{:S(2)}) collective-permute-start(f32[2,4,1,8]{3,1,0,2:T(4,128)S(1)} %get-tuple-element.38), channel_id=1, source_target_pairs={{0,16},{4,20},{8,24},{12,28},{16,0},{20,4},{24,8},{28,12},{1,17},{... | collective-permute-start | bytes 776 | tf_op jit(solution)/shard_map/ppermute | solution.py:176
  26.0 4.5 %collective-permute-start.7 = (f32[2,2,8]{2,1,0:T(2,128)S(1)}, f32[2,2,8]{2,1,0:T(2,128)S(1)}, u32[]{:S(2)}, u32[]{:S(2)}) collective-permute-start(f32[2,2,8]{2,1,0:T(2,128)S(1)} %get-tuple-element.34), channel_id=1, source_target_pairs={{0,12},{4,8},{8,4},{12,0},{16,28},{20,24},{24,20},{28,16},{1,13},{... | collective-permute-start | bytes 392 | tf_op jit(solution)/shard_map/ppermute | solution.py:182
  28.9 3.6 %collective-permute-start.6 = (f32[2,2,8]{2,1,0:T(2,128)S(1)}, f32[2,2,8]{2,1,0:T(2,128)S(1)}, u32[]{:S(2)}, u32[]{:S(2)}) collective-permute-start(f32[2,2,8]{2,1,0:T(2,128)S(1)} %get-tuple-element.35), channel_id=1, source_target_pairs={{0,8},{4,12},{8,0},{12,4},{16,24},{20,28},{24,16},{28,20},{1,9},{5... | collective-permute-start | bytes 392 | tf_op jit(solution)/shard_map/ppermute | solution.py:182
  29.3 3.6 %collective-permute-start.5 = (f32[2,2,8]{2,1,0:T(2,128)S(1)}, f32[2,2,8]{2,1,0:T(2,128)S(1)}, u32[]{:S(2)}, u32[]{:S(2)}) collective-permute-start(f32[2,2,8]{2,1,0:T(2,128)S(1)} %get-tuple-element.36), channel_id=1, source_target_pairs={{0,4},{4,0},{8,12},{12,8},{16,20},{20,16},{24,28},{28,24},{1,5},{5... | collective-permute-start | bytes 392 | tf_op jit(solution)/shard_map/ppermute | solution.py:182

commit v11 on v10

--- a/solution.py
+++ b/solution.py
@@ -98,7 +98,16 @@
         keep_rate.append((1.0 - ratio) / (1.0 + ratio))
         curl_gain.append(CE_GAIN / (permittivity * (1.0 + ratio)))
 
-    cells = cell_ref[...]
+    grid = cell_ref[...].astype(jnp.float32)
+    owners, capacity = grid.shape
+    slots = owners * capacity
+    slot = lax.broadcasted_iota(jnp.int32, (capacity, slots), 1)
+    spread = (slot % capacity == lax.broadcasted_iota(jnp.int32, (capacity, slots), 0)).astype(jnp.float32)
+    by_owner = jnp.dot(grid, spread, precision=lax.Precision.HIGHEST, preferred_element_type=jnp.float32)
+    mine = lax.broadcasted_iota(jnp.int32, (owners, slots), 1) // capacity == lax.broadcasted_iota(
+        jnp.int32, (owners, slots), 0
+    )
+    cells = jnp.sum(jnp.where(mine, by_owner, 0.0), axis=0, keepdims=True).astype(jnp.int32)
     rows = depth_x * depth_y
     lane_pick = (lax.broadcasted_iota(jnp.int32, (LANES, cells.shape[1]), 0) == (cells % LANES)).astype(jnp.float32)
     row_pick = lax.broadcasted_iota(jnp.int32, (rows, cells.shape[1]), 0) == (cells // LANES)
@@ -125,7 +134,7 @@
             block = field_e[c][0:depth_x, 0:depth_y].reshape(rows, LANES)
             by_lane = jnp.dot(block, lane_pick, precision=lax.Precision.HIGHEST, preferred_element_type=jnp.float32)
             picked = jnp.sum(jnp.where(row_pick, by_lane, 0.0), axis=0, keepdims=True)
-            term = picked * fwd_ref[step_index, c : c + 1, :]
+            term = picked * fwd_ref[c, step_index : step_index + 1, :]
             product = term if product is None else product + term
         prod_out[step_index : step_index + 1, :] = product
 
@@ -145,7 +154,7 @@
         out_shape=(
             jax.ShapeDtypeStruct(field_e.shape, jnp.float32),
             jax.ShapeDtypeStruct(field_h.shape, jnp.float32),
-            jax.ShapeDtypeStruct((STEPS, cells.shape[1]), jnp.float32),
+            jax.ShapeDtypeStruct((STEPS, cells.size), jnp.float32),
         ),
         in_specs=[vmem] * 10,
         out_specs=(vmem, vmem, vmem),
@@ -206,7 +215,7 @@
     y_inner, y_outer = swap_halos(rows(0), rows(depth_y - HALO), "yz")
     new_e, new_h, products = leapfrog(
         field_e, field_h, permittivity, conductivity[None], x_inner, x_outer, y_inner, y_outer,
-        slot_cell.reshape(1, -1), forward_e[0, 0], n_x, n_y,
+        slot_cell[0, 0], jnp.transpose(forward_e[0, 0], (1, 0, 2)), n_x, n_y,
     )
     products = products.reshape(STEPS, sources, capacity)
     segments = recv_param.reshape(sources, capacity)

time: 34.1 us -> 34.1 us (level)
  waiting for transfers between devices: 7.44 us -> 9.96 us
  local copies, waits for them, and re-layouts: 7.34 us -> 4.84 us
    ppermute x2, waiting for transfers between devices: 0.63 us -> 3.15 us  [swap_halos(): got_outer = lax.ppermute(jnp.where(odd, last, first), axis, outer)]
    unnamed x25 -> x20, local copies, waits for them, and re-layouts: 6.06 us -> 4.15 us
    reshape x1 -> x0, local copies, waits for them, and re-layouts: 0.59 us -> none  [shards(): slot_cell.reshape(1, -1)]
  transfers between devices with their start and end apart: 8 -> 8, of which waited for: 6 -> 6; matrix products, arithmetic and copies ran while one was open for 4% -> 1% of each run, Pallas kernels for 0% -> 0%
where the time goes in v11:
time: 34.1 us; the launch traced here: 33.8 us
  starting transfers between devices  14.8 us (43%)
  waiting for transfers between devices  9.96 us (29%)
  local copies, waits for them, and re-layouts  4.84 us (14%)
  Pallas kernels  2.34 us (7%)
  between operations  0.96 us (3%)
  other arithmetic  0.86 us (3%)
    ppermute x2, starting transfers between devices, swap_halos(): got_inner = lax.ppermute(jnp.where(odd, first, last), axis, inner)  4.42 us
    unnamed x20, local copies, waits for them, and re-layouts  4.15 us
    ppermute x1, starting transfers between devices, exchange_by_halving(): got = lax.ppermute(send, 'slab', pairs)  3.62 us
    ppermute x3, starting transfers between devices, exchange_by_halving(): lax.ppermute(held[:, q], 'slab', [(i, i ^ q) for i in range(count)])  3.57 us
    ppermute x3, waiting for transfers between devices, exchange_by_halving(): lax.ppermute(held[:, q], 'slab', [(i, i ^ q) for i in range(count)])  3.39 us
    ppermute x2, starting transfers between devices, swap_halos(): got_outer = lax.ppermute(jnp.where(odd, last, first), axis, outer)  3.2 us
    ppermute x2, waiting for transfers between devices, swap_halos(): got_outer = lax.ppermute(jnp.where(odd, last, first), axis, outer)  3.15 us
    pallas_call x1, Pallas kernels, leapfrog(): pl.pallas_call(kernel, out_shape=(jax.ShapeDtypeStruct(field_e.shape, jnp...  2.34 us
  transfers between devices with their start and end apart: 8, of which 6 were waited for; matrix products, arithmetic and copies ran while one was open for 1% of the time, Pallas kernels for 0%

profile of v11, /device:TPU:2, one launch (start us, length us, event | category | flops | bytes accessed | tf_op | source)
XLA Modules:
  0.0 33.8 jit_solution(3968715741325483699)
XLA Ops:
  0.7 0.7 %copy-done.5 = f32[4,8,128]{2,1,0:T(8,128)S(1)} copy-done((f32[4,8,128]{2,1,0:T(8,128)S(1)}, f32[4,8,128]{2,1,0:T(8,128)}, u32[]{:S(2)}) %copy-start.5) | copy-done | bytes 16408
  1.4 0.1 copy-done.2
  1.5 0.8 %copy-done.3 = f32[3,4,8,128]{3,2,1,0:T(8,128)S(1)} copy-done((f32[3,4,8,128]{3,2,1,0:T(8,128)S(1)}, f32[3,4,8,128]{3,2,1,0:T(8,128)}, u32[]{:S(2)}) %copy-start.3) | copy-done | bytes 49176
  2.2 0.0 copy-done.4
  2.3 0.7 %collective-permute-start.1 = (f32[10,2,8,128]{3,2,1,0:T(8,128)S(1)}, f32[10,2,8,128]{3,2,1,0:T(8,128)S(1)}, u32[]{:S(2)}, u32[]{:S(2)}) collective-permute-start(f32[10,2,8,128]{3,2,1,0:T(8,128)S(1)} %get-tuple-element.11), channel_id=1, source_target_pairs={{4,8},{8,4},{12,16},{16,12},{20,24},{24,20},{5,9},{9,5},{13,17},{1... | collective-permute-start | bytes 245768 | tf_op jit(solution)/shard_map/ppermute | solution.py:54
  3.0 4.3 %collective-permute-start = (f32[10,2,8,128]{3,2,1,0:T(8,128)S(1)}, f32[10,2,8,128]{3,2,1,0:T(8,128)S(1)}, u32[]{:S(2)}, u32[]{:S(2)}) collective-permute-start(f32[10,2,8,128]{3,2,1,0:T(8,128)S(1)} %get-tuple-element.12), channel_id=1, source_target_pairs={{0,4},{4,0},{8,12},{12,8},{16,20},{20,16},{24,28},{28,24},{1,5},{5... | collective-permute-start | bytes 245768 | tf_op jit(solution)/shard_map/ppermute | solution.py:53
  7.4 0.7 %copy-done.8 = s32[1,1,8,8]{3,2,1,0:T(8,128)S(1)} copy-done((s32[1,1,8,8]{3,2,1,0:T(8,128)S(1)}, s32[1,1,8,8]{3,2,1,0:T(8,128)}, u32[]{:S(2)}) %copy-start.8) | copy-done | bytes 280
  8.1 1.9 %collective-permute-done.x_inner_ref = f32[10,2,8,128]{3,2,1,0:T(8,128)S(1)} collective-permute-done((f32[10,2,8,128]{3,2,1,0:T(8,128)S(1)}, f32[10,2,8,128]{3,2,1,0:T(8,128)S(1)}, u32[]{:S(2)}, u32[]{:S(2)}) %collective-permute-start) | collective-permute-done | bytes 81952 | tf_op jit(solution)/shard_map/ppermute | solution.py:53
  10.1 0.6 %copy-done.1 = f32[10,2,8,128]{3,2,1,0:T(8,128)} copy-done((f32[10,2,8,128]{3,2,1,0:T(8,128)}, f32[10,2,8,128]{3,2,1,0:T(8,128)S(1)}, u32[]{:S(2)}) %copy-start.1) | copy-done | bytes 81944
  10.7 0.1 broadcast_select_fusion
  10.8 0.1 broadcast_select_fusion.1
  10.9 0.1 collective-permute-start.2
  11.0 2.5 %collective-permute-start.3 = (f32[10,8,2,128]{3,2,1,0:T(2,128)S(1)}, f32[10,8,2,128]{3,2,1,0:T(2,128)S(1)}, u32[]{:S(2)}, u32[]{:S(2)}) collective-permute-start(f32[10,8,2,128]{3,2,1,0:T(2,128)S(1)} %broadcast_select_fusion), channel_id=1, source_target_pairs={{1,2},{2,1},{5,6},{6,5},{9,10},{10,9},{13,14},{14,13},{17,18},{18,... | collective-permute-start | bytes 245768 | tf_op jit(solution)/shard_map/ppermute | solution.py:54
  13.6 3.1 %collective-permute-done.3.y_outer_ref = f32[10,8,2,128]{3,2,1,0:T(2,128)S(1)} collective-permute-done((f32[10,8,2,128]{3,2,1,0:T(2,128)S(1)}, f32[10,8,2,128]{3,2,1,0:T(2,128)S(1)}, u32[]{:S(2)}, u32[]{:S(2)}) %collective-permute-start.3) | collective-permute-done | bytes 81952 | tf_op jit(solution)/shard_map/ppermute | solution.py:54
  16.7 0.6 %copy-done.7 = f32[10,8,2,128]{3,2,1,0:T(2,128)} copy-done((f32[10,8,2,128]{3,2,1,0:T(2,128)}, f32[10,8,2,128]{3,2,1,0:T(2,128)S(1)}, u32[]{:S(2)}) %copy-start.7) | copy-done | bytes 81944
  17.4 2.3 %shard_map.94 = (f32[3,4,8,128]{3,2,1,0:T(8,128)}, f32[3,4,8,128]{3,2,1,0:T(8,128)}, f32[2,64]{1,0:T(2,128)}) custom-call(f32[3,4,8,128]{3,2,1,0:T(8,128)} %e_ref.1, f32[3,4,8,128]{3,2,1,0:T(8,128)} %h_ref.1, f32[3,4,8,128]{3,2,1,0:T(8,128)} %perm_ref.1, f32[1,4,8,128]{3,2,1,0:T(8,128)} %bitcast.55, f32[10,2,8,128]{3,2,1,0:T(8,128)} %copy-done.1, ...), custom_call_target="tpu_custom_call" | custom-call | tf_op jit(solution)/shard_map/pallas_call | solution.py:152
  19.7 0.7 %copy-done.9 = f32[2,64]{1,0:T(2,128)S(1)} copy-done((f32[2,64]{1,0:T(2,128)S(1)}, f32[2,64]{1,0:T(2,128)}, u32[]{:S(2)}) %copy-start.9) | copy-done | bytes 536
  20.4 0.1 reshape.194
  20.4 0.1 reshape.190
  20.5 0.1 reshape.187
  20.6 0.1 reshape_reshape.8
  20.8 3.6 %collective-permute-start.4 = (f32[2,4,1,8]{3,1,0,2:T(4,128)S(1)}, f32[2,4,1,8]{3,1,0,2:T(4,128)S(1)}, u32[]{:S(2)}, u32[]{:S(2)}) collective-permute-start(f32[2,4,1,8]{3,1,0,2:T(4,128)S(1)} %get-tuple-element.38), channel_id=1, source_target_pairs={{0,16},{4,20},{8,24},{12,28},{16,0},{20,4},{24,8},{28,12},{1,17},{... | collective-permute-start | bytes 776 | tf_op jit(solution)/shard_map/ppermute | solution.py:185
  24.5 0.1 eq.46
  24.5 1.5 %collective-permute-done.4 = f32[2,4,1,8]{3,1,0,2:T(4,128)S(1)} collective-permute-done((f32[2,4,1,8]{3,1,0,2:T(4,128)S(1)}, f32[2,4,1,8]{3,1,0,2:T(4,128)S(1)}, u32[]{:S(2)}, u32[]{:S(2)}) %collective-permute-start.4) | collective-permute-done | bytes 288 | tf_op jit(solution)/shard_map/ppermute | solution.py:185
  26.1 2.9 %collective-permute-start.7 = (f32[2,2,8]{2,1,0:T(2,128)S(1)}, f32[2,2,8]{2,1,0:T(2,128)S(1)}, u32[]{:S(2)}, u32[]{:S(2)}) collective-permute-start(f32[2,2,8]{2,1,0:T(2,128)S(1)} %get-tuple-element.34), channel_id=1, source_target_pairs={{0,12},{4,8},{8,4},{12,0},{16,28},{20,24},{24,20},{28,16},{1,13},{... | collective-permute-start | bytes 392 | tf_op jit(solution)/shard_map/ppermute | solution.py:191
  29.0 0.4 %collective-permute-start.6 = (f32[2,2,8]{2,1,0:T(2,128)S(1)}, f32[2,2,8]{2,1,0:T(2,128)S(1)}, u32[]{:S(2)}, u32[]{:S(2)}) collective-permute-start(f32[2,2,8]{2,1,0:T(2,128)S(1)} %get-tuple-element.35), channel_id=1, source_target_pairs={{0,8},{4,12},{8,0},{12,4},{16,24},{20,28},{24,16},{28,20},{1,9},{5... | collective-permute-start | bytes 392 | tf_op jit(solution)/shard_map/ppermute | solution.py:191
  29.4 0.2 collective-permute-start.5
  29.6 1.0 %collective-permute-done.7 = f32[2,2,8]{2,1,0:T(2,128)S(1)} collective-permute-done((f32[2,2,8]{2,1,0:T(2,128)S(1)}, f32[2,2,8]{2,1,0:T(2,128)S(1)}, u32[]{:S(2)}, u32[]{:S(2)}) %collective-permute-start.7) | collective-permute-done | bytes 160 | tf_op jit(solution)/shard_map/ppermute | solution.py:191
  30.6 2.0 %collective-permute-done.6 = f32[2,2,8]{2,1,0:T(2,128)S(1)} collective-permute-done((f32[2,2,8]{2,1,0:T(2,128)S(1)}, f32[2,2,8]{2,1,0:T(2,128)S(1)}, u32[]{:S(2)}, u32[]{:S(2)}) %collective-permute-start.6) | collective-permute-done | bytes 160 | tf_op jit(solution)/shard_map/ppermute | solution.py:191
  32.6 0.4 %collective-permute-done.5 = f32[2,2,8]{2,1,0:T(2,128)S(1)} collective-permute-done((f32[2,2,8]{2,1,0:T(2,128)S(1)}, f32[2,2,8]{2,1,0:T(2,128)S(1)}, u32[]{:S(2)}, u32[]{:S(2)}) %collective-permute-start.5) | collective-permute-done | bytes 160 | tf_op jit(solution)/shard_map/ppermute | solution.py:191
  33.0 0.1 broadcast_in_dim.27
  33.1 0.6 %select_reduce_fusion = f32[128]{0:T(128)} fusion(f32[128]{0:T(128)S(1)} %broadcast_in_dim.27, s32[128]{0:T(128)S(1)} %eq.46), kind=kLoop, calls=%fused_computation.6 | loop fusion | flops 49024 | bytes 1536 | tf_op jit(solution)/shard_map/reduce_sum | solution.py:228
  (43 shorter events, 0.3 us)
Async XLA Ops:
  0.6 0.7 %copy-start.5 = (f32[4,8,128]{2,1,0:T(8,128)S(1)}, f32[4,8,128]{2,1,0:T(8,128)}, u32[]{:S(2)}) copy-start(f32[4,8,128]{2,1,0:T(8,128)} %param.10) | copy-start | bytes 49156
  0.6 0.8 %copy-start.2 = (f32[3,4,8,128]{3,2,1,0:T(8,128)S(1)}, f32[3,4,8,128]{3,2,1,0:T(8,128)}, u32[]{:S(2)}) copy-start(f32[3,4,8,128]{3,2,1,0:T(8,128)} %perm_ref.1) | copy-start | bytes 147460
  1.4 0.8 %copy-start.3 = (f32[3,4,8,128]{3,2,1,0:T(8,128)S(1)}, f32[3,4,8,128]{3,2,1,0:T(8,128)}, u32[]{:S(2)}) copy-start(f32[3,4,8,128]{3,2,1,0:T(8,128)} %e_ref.1) | copy-start | bytes 147460
  1.4 0.8 %copy-start.4 = (f32[3,4,8,128]{3,2,1,0:T(8,128)S(1)}, f32[3,4,8,128]{3,2,1,0:T(8,128)}, u32[]{:S(2)}) copy-start(f32[3,4,8,128]{3,2,1,0:T(8,128)} %h_ref.1) | copy-start | bytes 147460
  2.3 5.8 %collective-permute-start.1 = (f32[10,2,8,128]{3,2,1,0:T(8,128)S(1)}, f32[10,2,8,128]{3,2,1,0:T(8,128)S(1)}, u32[]{:S(2)}, u32[]{:S(2)}) collective-permute-start(f32[10,2,8,128]{3,2,1,0:T(8,128)S(1)} %get-tuple-element.11), channel_id=1, source_target_pairs={{4,8},{8,4},{12,16},{16,12},{20,24},{24,20},{5,9},{9,5},{13,17},{1... | collective-permute-start | bytes 245768 | tf_op jit(solution)/shard_map/ppermute | solution.py:54
  3.0 7.1 %collective-permute-start = (f32[10,2,8,128]{3,2,1,0:T(8,128)S(1)}, f32[10,2,8,128]{3,2,1,0:T(8,128)S(1)}, u32[]{:S(2)}, u32[]{:S(2)}) collective-permute-start(f32[10,2,8,128]{3,2,1,0:T(8,128)S(1)} %get-tuple-element.12), channel_id=1, source_target_pairs={{0,4},{4,0},{8,12},{12,8},{16,20},{20,16},{24,28},{28,24},{1,5},{5... | collective-permute-start | bytes 245768 | tf_op jit(solution)/shard_map/ppermute | solution.py:53
  7.3 0.7 %copy-start.8 = (s32[1,1,8,8]{3,2,1,0:T(8,128)S(1)}, s32[1,1,8,8]{3,2,1,0:T(8,128)}, u32[]{:S(2)}) copy-start(s32[1,1,8,8]{3,2,1,0:T(8,128)} %param.13) | copy-start | bytes 772
  8.1 2.0 %copy-start = (f32[10,2,8,128]{3,2,1,0:T(8,128)}, f32[10,2,8,128]{3,2,1,0:T(8,128)S(1)}, u32[]{:S(2)}) copy-start(f32[10,2,8,128]{3,2,1,0:T(8,128)S(1)} %collective-permute-done.1.x_outer_ref) | copy-start | bytes 245764
  10.1 0.6 %copy-start.1 = (f32[10,2,8,128]{3,2,1,0:T(8,128)}, f32[10,2,8,128]{3,2,1,0:T(8,128)S(1)}, u32[]{:S(2)}) copy-start(f32[10,2,8,128]{3,2,1,0:T(8,128)S(1)} %collective-permute-done.x_inner_ref) | copy-start | bytes 245764
  10.9 2.7 %collective-permute-start.2 = (f32[10,8,2,128]{3,2,1,0:T(2,128)S(1)}, f32[10,8,2,128]{3,2,1,0:T(2,128)S(1)}, u32[]{:S(2)}, u32[]{:S(2)}) collective-permute-start(f32[10,8,2,128]{3,2,1,0:T(2,128)S(1)} %broadcast_select_fusion.1), channel_id=1, source_target_pairs={{0,1},{1,0},{2,3},{3,2},{4,5},{5,4},{6,7},{7,6},{8,9},{9,8},{10,11... | collective-permute-start | bytes 245768 | tf_op jit(solution)/shard_map/ppermute | solution.py:53
  11.0 5.8 %collective-permute-start.3 = (f32[10,8,2,128]{3,2,1,0:T(2,128)S(1)}, f32[10,8,2,128]{3,2,1,0:T(2,128)S(1)}, u32[]{:S(2)}, u32[]{:S(2)}) collective-permute-start(f32[10,8,2,128]{3,2,1,0:T(2,128)S(1)} %broadcast_select_fusion), channel_id=1, source_target_pairs={{1,2},{2,1},{5,6},{6,5},{9,10},{10,9},{13,14},{14,13},{17,18},{18,... | collective-permute-start | bytes 245768 | tf_op jit(solution)/shard_map/ppermute | solution.py:54
  13.6 3.2 %copy-start.6 = (f32[10,8,2,128]{3,2,1,0:T(2,128)}, f32[10,8,2,128]{3,2,1,0:T(2,128)S(1)}, u32[]{:S(2)}) copy-start(f32[10,8,2,128]{3,2,1,0:T(2,128)S(1)} %collective-permute-done.2.y_inner_ref) | copy-start | bytes 245764
  16.7 0.6 %copy-start.7 = (f32[10,8,2,128]{3,2,1,0:T(2,128)}, f32[10,8,2,128]{3,2,1,0:T(2,128)S(1)}, u32[]{:S(2)}) copy-start(f32[10,8,2,128]{3,2,1,0:T(2,128)S(1)} %collective-permute-done.3.y_outer_ref) | copy-start | bytes 245764
  19.7 0.7 %copy-start.9 = (f32[2,64]{1,0:T(2,128)S(1)}, f32[2,64]{1,0:T(2,128)}, u32[]{:S(2)}) copy-start(f32[2,64]{1,0:T(2,128)} %get-tuple-element.8) | copy-start | bytes 1540
  20.8 5.2 %collective-permute-start.4 = (f32[2,4,1,8]{3,1,0,2:T(4,128)S(1)}, f32[2,4,1,8]{3,1,0,2:T(4,128)S(1)}, u32[]{:S(2)}, u32[]{:S(2)}) collective-permute-start(f32[2,4,1,8]{3,1,0,2:T(4,128)S(1)} %get-tuple-element.38), channel_id=1, source_target_pairs={{0,16},{4,20},{8,24},{12,28},{16,0},{20,4},{24,8},{28,12},{1,17},{... | collective-permute-start | bytes 776 | tf_op jit(solution)/shard_map/ppermute | solution.py:185
  26.1 4.5 %collective-permute-start.7 = (f32[2,2,8]{2,1,0:T(2,128)S(1)}, f32[2,2,8]{2,1,0:T(2,128)S(1)}, u32[]{:S(2)}, u32[]{:S(2)}) collective-permute-start(f32[2,2,8]{2,1,0:T(2,128)S(1)} %get-tuple-element.34), channel_id=1, source_target_pairs={{0,12},{4,8},{8,4},{12,0},{16,28},{20,24},{24,20},{28,16},{1,13},{... | collective-permute-start | bytes 392 | tf_op jit(solution)/shard_map/ppermute | solution.py:191
  29.0 3.6 %collective-permute-start.6 = (f32[2,2,8]{2,1,0:T(2,128)S(1)}, f32[2,2,8]{2,1,0:T(2,128)S(1)}, u32[]{:S(2)}, u32[]{:S(2)}) collective-permute-start(f32[2,2,8]{2,1,0:T(2,128)S(1)} %get-tuple-element.35), channel_id=1, source_target_pairs={{0,8},{4,12},{8,0},{12,4},{16,24},{20,28},{24,16},{28,20},{1,9},{5... | collective-permute-start | bytes 392 | tf_op jit(solution)/shard_map/ppermute | solution.py:191
  29.4 3.6 %collective-permute-start.5 = (f32[2,2,8]{2,1,0:T(2,128)S(1)}, f32[2,2,8]{2,1,0:T(2,128)S(1)}, u32[]{:S(2)}, u32[]{:S(2)}) collective-permute-start(f32[2,2,8]{2,1,0:T(2,128)S(1)} %get-tuple-element.36), channel_id=1, source_target_pairs={{0,4},{4,0},{8,12},{12,8},{16,20},{20,16},{24,28},{28,24},{1,5},{5... | collective-permute-start | bytes 392 | tf_op jit(solution)/shard_map/ppermute | solution.py:191

commit v12 on v11

--- a/solution.py
+++ b/solution.py
@@ -92,11 +92,12 @@
     field_h = [ring[3 + c] for c in range(3)]
     conductivity = ring[9]
     keep_rate, curl_gain = [], []
+    half_loss = 0.5 * conductivity
     for c in range(3):
         permittivity = jnp.where(inside, ring[6 + c], 1.0)
-        ratio = 0.5 * conductivity / permittivity
-        keep_rate.append((1.0 - ratio) / (1.0 + ratio))
-        curl_gain.append(CE_GAIN / (permittivity * (1.0 + ratio)))
+        scale = 1.0 / (permittivity + half_loss)
+        keep_rate.append((permittivity - half_loss) * scale)
+        curl_gain.append(CE_GAIN * scale)
 
     grid = cell_ref[...].astype(jnp.float32)
     owners, capacity = grid.shape
@@ -112,6 +113,7 @@
     lane_pick = (lax.broadcasted_iota(jnp.int32, (LANES, cells.shape[1]), 0) == (cells % LANES)).astype(jnp.float32)
     row_pick = lax.broadcasted_iota(jnp.int32, (rows, cells.shape[1]), 0) == (cells // LANES)
 
+    blocks = []
     for step_index in range(STEPS):
         e0, e1, e2 = field_e
         curl = (
@@ -129,11 +131,16 @@
         field_e = [
             jnp.where(inside, keep_rate[c] * field_e[c] + curl_gain[c] * curl[c], 0.0) for c in range(3)
         ]
+        blocks.extend(field_e[c][0:depth_x, 0:depth_y].reshape(rows, LANES) for c in range(3))
+
+    by_lane = jnp.dot(
+        jnp.concatenate(blocks, 0), lane_pick, precision=lax.Precision.HIGHEST, preferred_element_type=jnp.float32
+    )
+    for step_index in range(STEPS):
         product = None
         for c in range(3):
-            block = field_e[c][0:depth_x, 0:depth_y].reshape(rows, LANES)
-            by_lane = jnp.dot(block, lane_pick, precision=lax.Precision.HIGHEST, preferred_element_type=jnp.float32)
-            picked = jnp.sum(jnp.where(row_pick, by_lane, 0.0), axis=0, keepdims=True)
+            part = by_lane[(3 * step_index + c) * rows : (3 * step_index + c + 1) * rows]
+            picked = jnp.sum(jnp.where(row_pick, part, 0.0), axis=0, keepdims=True)
             term = picked * fwd_ref[c, step_index : step_index + 1, :]
             product = term if product is None else product + term
         prod_out[step_index : step_index + 1, :] = product

time: 34.1 us -> 34 us (level)
  no operation moved by 1% of the time
where the time goes in v12:
time: 34 us; the launch traced here: 33.7 us
  starting transfers between devices  14.8 us (44%)
  waiting for transfers between devices  9.96 us (29%)
  local copies, waits for them, and re-layouts  4.84 us (14%)
  Pallas kernels  2.23 us (7%)
  between operations  0.96 us (3%)
  other arithmetic  0.86 us (3%)
    ppermute x2, starting transfers between devices, swap_halos(): got_inner = lax.ppermute(jnp.where(odd, first, last), axis, inner)  4.42 us
    unnamed x20, local copies, waits for them, and re-layouts  4.15 us
    ppermute x1, starting transfers between devices, exchange_by_halving(): got = lax.ppermute(send, 'slab', pairs)  3.62 us
    ppermute x3, starting transfers between devices, exchange_by_halving(): lax.ppermute(held[:, q], 'slab', [(i, i ^ q) for i in range(count)])  3.57 us
    ppermute x3, waiting for transfers between devices, exchange_by_halving(): lax.ppermute(held[:, q], 'slab', [(i, i ^ q) for i in range(count)])  3.39 us
    ppermute x2, starting transfers between devices, swap_halos(): got_outer = lax.ppermute(jnp.where(odd, last, first), axis, outer)  3.2 us
    ppermute x2, waiting for transfers between devices, swap_halos(): got_outer = lax.ppermute(jnp.where(odd, last, first), axis, outer)  3.15 us
    pallas_call x1, Pallas kernels, leapfrog(): pl.pallas_call(kernel, out_shape=(jax.ShapeDtypeStruct(field_e.shape, jnp...  2.23 us
  transfers between devices with their start and end apart: 8, of which 6 were waited for; matrix products, arithmetic and copies ran while one was open for 1% of the time, Pallas kernels for 0%

profile of v12, /device:TPU:2, one launch (start us, length us, event | category | flops | bytes accessed | tf_op | source)
XLA Modules:
  0.0 33.7 jit_solution(10320796671913772007)
XLA Ops:
  0.7 0.7 %copy-done.5 = f32[4,8,128]{2,1,0:T(8,128)S(1)} copy-done((f32[4,8,128]{2,1,0:T(8,128)S(1)}, f32[4,8,128]{2,1,0:T(8,128)}, u32[]{:S(2)}) %copy-start.5) | copy-done | bytes 16408
  1.4 0.1 copy-done.2
  1.5 0.8 %copy-done.3 = f32[3,4,8,128]{3,2,1,0:T(8,128)S(1)} copy-done((f32[3,4,8,128]{3,2,1,0:T(8,128)S(1)}, f32[3,4,8,128]{3,2,1,0:T(8,128)}, u32[]{:S(2)}) %copy-start.3) | copy-done | bytes 49176
  2.2 0.0 copy-done.4
  2.3 0.7 %collective-permute-start.1 = (f32[10,2,8,128]{3,2,1,0:T(8,128)S(1)}, f32[10,2,8,128]{3,2,1,0:T(8,128)S(1)}, u32[]{:S(2)}, u32[]{:S(2)}) collective-permute-start(f32[10,2,8,128]{3,2,1,0:T(8,128)S(1)} %get-tuple-element.11), channel_id=1, source_target_pairs={{4,8},{8,4},{12,16},{16,12},{20,24},{24,20},{5,9},{9,5},{13,17},{1... | collective-permute-start | bytes 245768 | tf_op jit(solution)/shard_map/ppermute | solution.py:54
  3.0 4.3 %collective-permute-start = (f32[10,2,8,128]{3,2,1,0:T(8,128)S(1)}, f32[10,2,8,128]{3,2,1,0:T(8,128)S(1)}, u32[]{:S(2)}, u32[]{:S(2)}) collective-permute-start(f32[10,2,8,128]{3,2,1,0:T(8,128)S(1)} %get-tuple-element.12), channel_id=1, source_target_pairs={{0,4},{4,0},{8,12},{12,8},{16,20},{20,16},{24,28},{28,24},{1,5},{5... | collective-permute-start | bytes 245768 | tf_op jit(solution)/shard_map/ppermute | solution.py:53
  7.4 0.7 %copy-done.8 = s32[1,1,8,8]{3,2,1,0:T(8,128)S(1)} copy-done((s32[1,1,8,8]{3,2,1,0:T(8,128)S(1)}, s32[1,1,8,8]{3,2,1,0:T(8,128)}, u32[]{:S(2)}) %copy-start.8) | copy-done | bytes 280
  8.1 1.9 %collective-permute-done.x_inner_ref = f32[10,2,8,128]{3,2,1,0:T(8,128)S(1)} collective-permute-done((f32[10,2,8,128]{3,2,1,0:T(8,128)S(1)}, f32[10,2,8,128]{3,2,1,0:T(8,128)S(1)}, u32[]{:S(2)}, u32[]{:S(2)}) %collective-permute-start) | collective-permute-done | bytes 81952 | tf_op jit(solution)/shard_map/ppermute | solution.py:53
  10.1 0.6 %copy-done.1 = f32[10,2,8,128]{3,2,1,0:T(8,128)} copy-done((f32[10,2,8,128]{3,2,1,0:T(8,128)}, f32[10,2,8,128]{3,2,1,0:T(8,128)S(1)}, u32[]{:S(2)}) %copy-start.1) | copy-done | bytes 81944
  10.7 0.1 broadcast_select_fusion
  10.8 0.1 broadcast_select_fusion.1
  10.9 0.1 collective-permute-start.2
  11.0 2.5 %collective-permute-start.3 = (f32[10,8,2,128]{3,2,1,0:T(2,128)S(1)}, f32[10,8,2,128]{3,2,1,0:T(2,128)S(1)}, u32[]{:S(2)}, u32[]{:S(2)}) collective-permute-start(f32[10,8,2,128]{3,2,1,0:T(2,128)S(1)} %broadcast_select_fusion), channel_id=1, source_target_pairs={{1,2},{2,1},{5,6},{6,5},{9,10},{10,9},{13,14},{14,13},{17,18},{18,... | collective-permute-start | bytes 245768 | tf_op jit(solution)/shard_map/ppermute | solution.py:54
  13.6 3.1 %collective-permute-done.3.y_outer_ref = f32[10,8,2,128]{3,2,1,0:T(2,128)S(1)} collective-permute-done((f32[10,8,2,128]{3,2,1,0:T(2,128)S(1)}, f32[10,8,2,128]{3,2,1,0:T(2,128)S(1)}, u32[]{:S(2)}, u32[]{:S(2)}) %collective-permute-start.3) | collective-permute-done | bytes 81952 | tf_op jit(solution)/shard_map/ppermute | solution.py:54
  16.7 0.6 %copy-done.7 = f32[10,8,2,128]{3,2,1,0:T(2,128)} copy-done((f32[10,8,2,128]{3,2,1,0:T(2,128)}, f32[10,8,2,128]{3,2,1,0:T(2,128)S(1)}, u32[]{:S(2)}) %copy-start.7) | copy-done | bytes 81944
  17.4 2.2 %shard_map.94 = (f32[3,4,8,128]{3,2,1,0:T(8,128)}, f32[3,4,8,128]{3,2,1,0:T(8,128)}, f32[2,64]{1,0:T(2,128)}) custom-call(f32[3,4,8,128]{3,2,1,0:T(8,128)} %e_ref.1, f32[3,4,8,128]{3,2,1,0:T(8,128)} %h_ref.1, f32[3,4,8,128]{3,2,1,0:T(8,128)} %perm_ref.1, f32[1,4,8,128]{3,2,1,0:T(8,128)} %bitcast.55, f32[10,2,8,128]{3,2,1,0:T(8,128)} %copy-done.1, ...), custom_call_target="tpu_custom_call" | custom-call | tf_op jit(solution)/shard_map/pallas_call | solution.py:159
  19.6 0.7 %copy-done.9 = f32[2,64]{1,0:T(2,128)S(1)} copy-done((f32[2,64]{1,0:T(2,128)S(1)}, f32[2,64]{1,0:T(2,128)}, u32[]{:S(2)}) %copy-start.9) | copy-done | bytes 536
  20.3 0.1 reshape.194
  20.3 0.1 reshape.190
  20.4 0.1 reshape.187
  20.5 0.1 reshape_reshape.8
  20.7 3.6 %collective-permute-start.4 = (f32[2,4,1,8]{3,1,0,2:T(4,128)S(1)}, f32[2,4,1,8]{3,1,0,2:T(4,128)S(1)}, u32[]{:S(2)}, u32[]{:S(2)}) collective-permute-start(f32[2,4,1,8]{3,1,0,2:T(4,128)S(1)} %get-tuple-element.38), channel_id=1, source_target_pairs={{0,16},{4,20},{8,24},{12,28},{16,0},{20,4},{24,8},{28,12},{1,17},{... | collective-permute-start | bytes 776 | tf_op jit(solution)/shard_map/ppermute | solution.py:192
  24.3 0.1 eq.46
  24.4 1.5 %collective-permute-done.4 = f32[2,4,1,8]{3,1,0,2:T(4,128)S(1)} collective-permute-done((f32[2,4,1,8]{3,1,0,2:T(4,128)S(1)}, f32[2,4,1,8]{3,1,0,2:T(4,128)S(1)}, u32[]{:S(2)}, u32[]{:S(2)}) %collective-permute-start.4) | collective-permute-done | bytes 288 | tf_op jit(solution)/shard_map/ppermute | solution.py:192
  26.0 2.9 %collective-permute-start.7 = (f32[2,2,8]{2,1,0:T(2,128)S(1)}, f32[2,2,8]{2,1,0:T(2,128)S(1)}, u32[]{:S(2)}, u32[]{:S(2)}) collective-permute-start(f32[2,2,8]{2,1,0:T(2,128)S(1)} %get-tuple-element.34), channel_id=1, source_target_pairs={{0,12},{4,8},{8,4},{12,0},{16,28},{20,24},{24,20},{28,16},{1,13},{... | collective-permute-start | bytes 392 | tf_op jit(solution)/shard_map/ppermute | solution.py:198
  28.9 0.5 %collective-permute-start.6 = (f32[2,2,8]{2,1,0:T(2,128)S(1)}, f32[2,2,8]{2,1,0:T(2,128)S(1)}, u32[]{:S(2)}, u32[]{:S(2)}) collective-permute-start(f32[2,2,8]{2,1,0:T(2,128)S(1)} %get-tuple-element.35), channel_id=1, source_target_pairs={{0,8},{4,12},{8,0},{12,4},{16,24},{20,28},{24,16},{28,20},{1,9},{5... | collective-permute-start | bytes 392 | tf_op jit(solution)/shard_map/ppermute | solution.py:198
  29.3 0.2 collective-permute-start.5
  29.5 1.0 %collective-permute-done.7 = f32[2,2,8]{2,1,0:T(2,128)S(1)} collective-permute-done((f32[2,2,8]{2,1,0:T(2,128)S(1)}, f32[2,2,8]{2,1,0:T(2,128)S(1)}, u32[]{:S(2)}, u32[]{:S(2)}) %collective-permute-start.7) | collective-permute-done | bytes 160 | tf_op jit(solution)/shard_map/ppermute | solution.py:198
  30.5 2.0 %collective-permute-done.6 = f32[2,2,8]{2,1,0:T(2,128)S(1)} collective-permute-done((f32[2,2,8]{2,1,0:T(2,128)S(1)}, f32[2,2,8]{2,1,0:T(2,128)S(1)}, u32[]{:S(2)}, u32[]{:S(2)}) %collective-permute-start.6) | collective-permute-done | bytes 160 | tf_op jit(solution)/shard_map/ppermute | solution.py:198
  32.5 0.5 %collective-permute-done.5 = f32[2,2,8]{2,1,0:T(2,128)S(1)} collective-permute-done((f32[2,2,8]{2,1,0:T(2,128)S(1)}, f32[2,2,8]{2,1,0:T(2,128)S(1)}, u32[]{:S(2)}, u32[]{:S(2)}) %collective-permute-start.5) | collective-permute-done | bytes 160 | tf_op jit(solution)/shard_map/ppermute | solution.py:198
  32.9 0.1 broadcast_in_dim.27
  33.0 0.6 %select_reduce_fusion = f32[128]{0:T(128)} fusion(f32[128]{0:T(128)S(1)} %broadcast_in_dim.27, s32[128]{0:T(128)S(1)} %eq.46), kind=kLoop, calls=%fused_computation.6 | loop fusion | flops 49024 | bytes 1536 | tf_op jit(solution)/shard_map/reduce_sum | solution.py:235
  (43 shorter events, 0.3 us)
Async XLA Ops:
  0.6 0.7 %copy-start.5 = (f32[4,8,128]{2,1,0:T(8,128)S(1)}, f32[4,8,128]{2,1,0:T(8,128)}, u32[]{:S(2)}) copy-start(f32[4,8,128]{2,1,0:T(8,128)} %param.10) | copy-start | bytes 49156
  0.6 0.8 %copy-start.2 = (f32[3,4,8,128]{3,2,1,0:T(8,128)S(1)}, f32[3,4,8,128]{3,2,1,0:T(8,128)}, u32[]{:S(2)}) copy-start(f32[3,4,8,128]{3,2,1,0:T(8,128)} %perm_ref.1) | copy-start | bytes 147460
  1.4 0.8 %copy-start.3 = (f32[3,4,8,128]{3,2,1,0:T(8,128)S(1)}, f32[3,4,8,128]{3,2,1,0:T(8,128)}, u32[]{:S(2)}) copy-start(f32[3,4,8,128]{3,2,1,0:T(8,128)} %e_ref.1) | copy-start | bytes 147460
  1.4 0.8 %copy-start.4 = (f32[3,4,8,128]{3,2,1,0:T(8,128)S(1)}, f32[3,4,8,128]{3,2,1,0:T(8,128)}, u32[]{:S(2)}) copy-start(f32[3,4,8,128]{3,2,1,0:T(8,128)} %h_ref.1) | copy-start | bytes 147460
  2.3 5.8 %collective-permute-start.1 = (f32[10,2,8,128]{3,2,1,0:T(8,128)S(1)}, f32[10,2,8,128]{3,2,1,0:T(8,128)S(1)}, u32[]{:S(2)}, u32[]{:S(2)}) collective-permute-start(f32[10,2,8,128]{3,2,1,0:T(8,128)S(1)} %get-tuple-element.11), channel_id=1, source_target_pairs={{4,8},{8,4},{12,16},{16,12},{20,24},{24,20},{5,9},{9,5},{13,17},{1... | collective-permute-start | bytes 245768 | tf_op jit(solution)/shard_map/ppermute | solution.py:54
  3.0 7.1 %collective-permute-start = (f32[10,2,8,128]{3,2,1,0:T(8,128)S(1)}, f32[10,2,8,128]{3,2,1,0:T(8,128)S(1)}, u32[]{:S(2)}, u32[]{:S(2)}) collective-permute-start(f32[10,2,8,128]{3,2,1,0:T(8,128)S(1)} %get-tuple-element.12), channel_id=1, source_target_pairs={{0,4},{4,0},{8,12},{12,8},{16,20},{20,16},{24,28},{28,24},{1,5},{5... | collective-permute-start | bytes 245768 | tf_op jit(solution)/shard_map/ppermute | solution.py:53
  7.3 0.7 %copy-start.8 = (s32[1,1,8,8]{3,2,1,0:T(8,128)S(1)}, s32[1,1,8,8]{3,2,1,0:T(8,128)}, u32[]{:S(2)}) copy-start(s32[1,1,8,8]{3,2,1,0:T(8,128)} %param.13) | copy-start | bytes 772
  8.1 2.0 %copy-start = (f32[10,2,8,128]{3,2,1,0:T(8,128)}, f32[10,2,8,128]{3,2,1,0:T(8,128)S(1)}, u32[]{:S(2)}) copy-start(f32[10,2,8,128]{3,2,1,0:T(8,128)S(1)} %collective-permute-done.1.x_outer_ref) | copy-start | bytes 245764
  10.1 0.6 %copy-start.1 = (f32[10,2,8,128]{3,2,1,0:T(8,128)}, f32[10,2,8,128]{3,2,1,0:T(8,128)S(1)}, u32[]{:S(2)}) copy-start(f32[10,2,8,128]{3,2,1,0:T(8,128)S(1)} %collective-permute-done.x_inner_ref) | copy-start | bytes 245764
  10.9 2.7 %collective-permute-start.2 = (f32[10,8,2,128]{3,2,1,0:T(2,128)S(1)}, f32[10,8,2,128]{3,2,1,0:T(2,128)S(1)}, u32[]{:S(2)}, u32[]{:S(2)}) collective-permute-start(f32[10,8,2,128]{3,2,1,0:T(2,128)S(1)} %broadcast_select_fusion.1), channel_id=1, source_target_pairs={{0,1},{1,0},{2,3},{3,2},{4,5},{5,4},{6,7},{7,6},{8,9},{9,8},{10,11... | collective-permute-start | bytes 245768 | tf_op jit(solution)/shard_map/ppermute | solution.py:53
  11.0 5.8 %collective-permute-start.3 = (f32[10,8,2,128]{3,2,1,0:T(2,128)S(1)}, f32[10,8,2,128]{3,2,1,0:T(2,128)S(1)}, u32[]{:S(2)}, u32[]{:S(2)}) collective-permute-start(f32[10,8,2,128]{3,2,1,0:T(2,128)S(1)} %broadcast_select_fusion), channel_id=1, source_target_pairs={{1,2},{2,1},{5,6},{6,5},{9,10},{10,9},{13,14},{14,13},{17,18},{18,... | collective-permute-start | bytes 245768 | tf_op jit(solution)/shard_map/ppermute | solution.py:54
  13.6 3.2 %copy-start.6 = (f32[10,8,2,128]{3,2,1,0:T(2,128)}, f32[10,8,2,128]{3,2,1,0:T(2,128)S(1)}, u32[]{:S(2)}) copy-start(f32[10,8,2,128]{3,2,1,0:T(2,128)S(1)} %collective-permute-done.2.y_inner_ref) | copy-start | bytes 245764
  16.7 0.6 %copy-start.7 = (f32[10,8,2,128]{3,2,1,0:T(2,128)}, f32[10,8,2,128]{3,2,1,0:T(2,128)S(1)}, u32[]{:S(2)}) copy-start(f32[10,8,2,128]{3,2,1,0:T(2,128)S(1)} %collective-permute-done.3.y_outer_ref) | copy-start | bytes 245764
  19.6 0.7 %copy-start.9 = (f32[2,64]{1,0:T(2,128)S(1)}, f32[2,64]{1,0:T(2,128)}, u32[]{:S(2)}) copy-start(f32[2,64]{1,0:T(2,128)} %get-tuple-element.8) | copy-start | bytes 1540
  20.7 5.2 %collective-permute-start.4 = (f32[2,4,1,8]{3,1,0,2:T(4,128)S(1)}, f32[2,4,1,8]{3,1,0,2:T(4,128)S(1)}, u32[]{:S(2)}, u32[]{:S(2)}) collective-permute-start(f32[2,4,1,8]{3,1,0,2:T(4,128)S(1)} %get-tuple-element.38), channel_id=1, source_target_pairs={{0,16},{4,20},{8,24},{12,28},{16,0},{20,4},{24,8},{28,12},{1,17},{... | collective-permute-start | bytes 776 | tf_op jit(solution)/shard_map/ppermute | solution.py:192
  26.0 4.5 %collective-permute-start.7 = (f32[2,2,8]{2,1,0:T(2,128)S(1)}, f32[2,2,8]{2,1,0:T(2,128)S(1)}, u32[]{:S(2)}, u32[]{:S(2)}) collective-permute-start(f32[2,2,8]{2,1,0:T(2,128)S(1)} %get-tuple-element.34), channel_id=1, source_target_pairs={{0,12},{4,8},{8,4},{12,0},{16,28},{20,24},{24,20},{28,16},{1,13},{... | collective-permute-start | bytes 392 | tf_op jit(solution)/shard_map/ppermute | solution.py:198
  28.9 3.6 %collective-permute-start.6 = (f32[2,2,8]{2,1,0:T(2,128)S(1)}, f32[2,2,8]{2,1,0:T(2,128)S(1)}, u32[]{:S(2)}, u32[]{:S(2)}) collective-permute-start(f32[2,2,8]{2,1,0:T(2,128)S(1)} %get-tuple-element.35), channel_id=1, source_target_pairs={{0,8},{4,12},{8,0},{12,4},{16,24},{20,28},{24,16},{28,20},{1,9},{5... | collective-permute-start | bytes 392 | tf_op jit(solution)/shard_map/ppermute | solution.py:198
  29.3 3.6 %collective-permute-start.5 = (f32[2,2,8]{2,1,0:T(2,128)S(1)}, f32[2,2,8]{2,1,0:T(2,128)S(1)}, u32[]{:S(2)}, u32[]{:S(2)}) collective-permute-start(f32[2,2,8]{2,1,0:T(2,128)S(1)} %get-tuple-element.36), channel_id=1, source_target_pairs={{0,4},{4,0},{8,12},{12,8},{16,20},{20,16},{24,28},{28,24},{1,5},{5... | collective-permute-start | bytes 392 | tf_op jit(solution)/shard_map/ppermute | solution.py:198

commit v13 on v11

--- a/solution.py
+++ b/solution.py
@@ -136,7 +136,15 @@
             picked = jnp.sum(jnp.where(row_pick, by_lane, 0.0), axis=0, keepdims=True)
             term = picked * fwd_ref[c, step_index : step_index + 1, :]
             product = term if product is None else product + term
-        prod_out[step_index : step_index + 1, :] = product
+        if owners & (owners - 1):
+            prod_out[step_index : step_index + 1, :] = product
+            continue
+        target = lax.broadcasted_iota(jnp.int32, (slots, slots), 1)
+        source = (jnp.bitwise_xor(target // capacity, slab)) * capacity + target % capacity
+        move = (lax.broadcasted_iota(jnp.int32, (slots, slots), 0) == source).astype(jnp.float32)
+        prod_out[step_index : step_index + 1, :] = jnp.dot(
+            product, move, precision=lax.Precision.HIGHEST, preferred_element_type=jnp.float32
+        )
 
     for c in range(3):
         e_out[c] = field_e[c][0:depth_x, 0:depth_y]
@@ -175,7 +183,7 @@
 
 def exchange_by_halving(products, segments, count):
     me = lax.axis_index("slab")
-    held = xor_rows(products, me, count, 1)[:, :, None]
+    held = products[:, :, None]
     bit = count // 2
     while bit >= RADIX:
         owners = held.shape[1]

time: 34.1 us -> 34.1 us (level)
  Pallas kernels: 2.34 us -> 2.73 us
    pallas_call x1, Pallas kernels: 2.34 us -> 2.73 us  [leapfrog(): pl.pallas_call(kernel, out_shape=(jax.ShapeDtypeStruct(field_e.shape, jnp...]
where the time goes in v13:
time: 34.1 us; the launch traced here: 33.7 us
  starting transfers between devices  14.8 us (43%)
  waiting for transfers between devices  9.96 us (29%)
  local copies, waits for them, and re-layouts  4.54 us (13%)
  Pallas kernels  2.73 us (8%)
  between operations  0.9 us (3%)
  other arithmetic  0.84 us (2%)
    ppermute x2, starting transfers between devices, swap_halos(): got_inner = lax.ppermute(jnp.where(odd, first, last), axis, inner)  4.42 us
    unnamed x20, local copies, waits for them, and re-layouts  4.15 us
    ppermute x1, starting transfers between devices, exchange_by_halving(): got = lax.ppermute(send, 'slab', pairs)  3.57 us
    ppermute x3, starting transfers between devices, exchange_by_halving(): lax.ppermute(held[:, q], 'slab', [(i, i ^ q) for i in range(count)])  3.57 us
    ppermute x3, waiting for transfers between devices, exchange_by_halving(): lax.ppermute(held[:, q], 'slab', [(i, i ^ q) for i in range(count)])  3.39 us
    ppermute x2, starting transfers between devices, swap_halos(): got_outer = lax.ppermute(jnp.where(odd, last, first), axis, outer)  3.2 us
    ppermute x2, waiting for transfers between devices, swap_halos(): got_outer = lax.ppermute(jnp.where(odd, last, first), axis, outer)  3.15 us
    pallas_call x1, Pallas kernels, leapfrog(): pl.pallas_call(kernel, out_shape=(jax.ShapeDtypeStruct(field_e.shape, jnp...  2.73 us
  transfers between devices with their start and end apart: 8, of which 6 were waited for; matrix products, arithmetic and copies ran while one was open for 1% of the time, Pallas kernels for 0%

profile of v13, /device:TPU:2, one launch (start us, length us, event | category | flops | bytes accessed | tf_op | source)
XLA Modules:
  0.0 33.7 jit_solution(14563290087401201318)
XLA Ops:
  0.6 0.0 copy-start.5
  0.6 0.0 copy-start.2
  0.7 0.7 %copy-done.5 = f32[4,8,128]{2,1,0:T(8,128)S(1)} copy-done((f32[4,8,128]{2,1,0:T(8,128)S(1)}, f32[4,8,128]{2,1,0:T(8,128)}, u32[]{:S(2)}) %copy-start.5) | copy-done | bytes 16408
  1.4 0.1 copy-done.2
  1.5 0.8 %copy-done.3 = f32[3,4,8,128]{3,2,1,0:T(8,128)S(1)} copy-done((f32[3,4,8,128]{3,2,1,0:T(8,128)S(1)}, f32[3,4,8,128]{3,2,1,0:T(8,128)}, u32[]{:S(2)}) %copy-start.3) | copy-done | bytes 49176
  2.2 0.0 copy-done.4
  2.3 0.7 %collective-permute-start.1 = (f32[10,2,8,128]{3,2,1,0:T(8,128)S(1)}, f32[10,2,8,128]{3,2,1,0:T(8,128)S(1)}, u32[]{:S(2)}, u32[]{:S(2)}) collective-permute-start(f32[10,2,8,128]{3,2,1,0:T(8,128)S(1)} %get-tuple-element.11), channel_id=1, source_target_pairs={{4,8},{8,4},{12,16},{16,12},{20,24},{24,20},{5,9},{9,5},{13,17},{1... | collective-permute-start | bytes 245768 | tf_op jit(solution)/shard_map/ppermute | solution.py:54
  3.0 4.3 %collective-permute-start = (f32[10,2,8,128]{3,2,1,0:T(8,128)S(1)}, f32[10,2,8,128]{3,2,1,0:T(8,128)S(1)}, u32[]{:S(2)}, u32[]{:S(2)}) collective-permute-start(f32[10,2,8,128]{3,2,1,0:T(8,128)S(1)} %get-tuple-element.12), channel_id=1, source_target_pairs={{0,4},{4,0},{8,12},{12,8},{16,20},{20,16},{24,28},{28,24},{1,5},{5... | collective-permute-start | bytes 245768 | tf_op jit(solution)/shard_map/ppermute | solution.py:53
  7.3 0.0 copy-start.8
  7.4 0.7 %copy-done.8 = s32[1,1,8,8]{3,2,1,0:T(8,128)S(1)} copy-done((s32[1,1,8,8]{3,2,1,0:T(8,128)S(1)}, s32[1,1,8,8]{3,2,1,0:T(8,128)}, u32[]{:S(2)}) %copy-start.8) | copy-done | bytes 280
  8.1 1.9 %collective-permute-done.x_inner_ref = f32[10,2,8,128]{3,2,1,0:T(8,128)S(1)} collective-permute-done((f32[10,2,8,128]{3,2,1,0:T(8,128)S(1)}, f32[10,2,8,128]{3,2,1,0:T(8,128)S(1)}, u32[]{:S(2)}, u32[]{:S(2)}) %collective-permute-start) | collective-permute-done | bytes 81952 | tf_op jit(solution)/shard_map/ppermute | solution.py:53
  10.1 0.6 %copy-done.1 = f32[10,2,8,128]{3,2,1,0:T(8,128)} copy-done((f32[10,2,8,128]{3,2,1,0:T(8,128)}, f32[10,2,8,128]{3,2,1,0:T(8,128)S(1)}, u32[]{:S(2)}) %copy-start.1) | copy-done | bytes 81944
  10.7 0.1 broadcast_select_fusion
  10.8 0.1 broadcast_select_fusion.1
  10.9 0.1 collective-permute-start.2
  11.0 2.5 %collective-permute-start.3 = (f32[10,8,2,128]{3,2,1,0:T(2,128)S(1)}, f32[10,8,2,128]{3,2,1,0:T(2,128)S(1)}, u32[]{:S(2)}, u32[]{:S(2)}) collective-permute-start(f32[10,8,2,128]{3,2,1,0:T(2,128)S(1)} %broadcast_select_fusion), channel_id=1, source_target_pairs={{1,2},{2,1},{5,6},{6,5},{9,10},{10,9},{13,14},{14,13},{17,18},{18,... | collective-permute-start | bytes 245768 | tf_op jit(solution)/shard_map/ppermute | solution.py:54
  13.6 3.1 %collective-permute-done.3.y_outer_ref = f32[10,8,2,128]{3,2,1,0:T(2,128)S(1)} collective-permute-done((f32[10,8,2,128]{3,2,1,0:T(2,128)S(1)}, f32[10,8,2,128]{3,2,1,0:T(2,128)S(1)}, u32[]{:S(2)}, u32[]{:S(2)}) %collective-permute-start.3) | collective-permute-done | bytes 81952 | tf_op jit(solution)/shard_map/ppermute | solution.py:54
  16.7 0.6 %copy-done.7 = f32[10,8,2,128]{3,2,1,0:T(2,128)} copy-done((f32[10,8,2,128]{3,2,1,0:T(2,128)}, f32[10,8,2,128]{3,2,1,0:T(2,128)S(1)}, u32[]{:S(2)}) %copy-start.7) | copy-done | bytes 81944
  17.4 2.7 %shard_map.94 = (f32[3,4,8,128]{3,2,1,0:T(8,128)}, f32[3,4,8,128]{3,2,1,0:T(8,128)}, f32[2,64]{1,0:T(2,128)}) custom-call(f32[3,4,8,128]{3,2,1,0:T(8,128)} %e_ref.1, f32[3,4,8,128]{3,2,1,0:T(8,128)} %h_ref.1, f32[3,4,8,128]{3,2,1,0:T(8,128)} %perm_ref.1, f32[1,4,8,128]{3,2,1,0:T(8,128)} %bitcast.42, f32[10,2,8,128]{3,2,1,0:T(8,128)} %copy-done.1, ...), custom_call_target="tpu_custom_call" | custom-call | tf_op jit(solution)/shard_map/pallas_call | solution.py:160
  20.1 0.7 %copy-done.9 = f32[2,64]{1,0:T(2,128)S(1)} copy-done((f32[2,64]{1,0:T(2,128)S(1)}, f32[2,64]{1,0:T(2,128)}, u32[]{:S(2)}) %copy-start.9) | copy-done | bytes 536
  20.8 0.1 broadcast_in_dim_reshape.3
  20.8 3.6 %collective-permute-start.4 = (f32[2,4,1,8]{3,1,0,2:T(4,128)S(1)}, f32[2,4,1,8]{3,1,0,2:T(4,128)S(1)}, u32[]{:S(2)}, u32[]{:S(2)}) collective-permute-start(f32[2,4,1,8]{3,1,0,2:T(4,128)S(1)} %get-tuple-element.38), channel_id=1, source_target_pairs={{0,16},{4,20},{8,24},{12,28},{16,0},{20,4},{24,8},{28,12},{1,17},{... | collective-permute-start | bytes 776 | tf_op jit(solution)/shard_map/ppermute | solution.py:193
  24.4 0.1 eq.40
  24.5 1.5 %collective-permute-done.4 = f32[2,4,1,8]{3,1,0,2:T(4,128)S(1)} collective-permute-done((f32[2,4,1,8]{3,1,0,2:T(4,128)S(1)}, f32[2,4,1,8]{3,1,0,2:T(4,128)S(1)}, u32[]{:S(2)}, u32[]{:S(2)}) %collective-permute-start.4) | collective-permute-done | bytes 288 | tf_op jit(solution)/shard_map/ppermute | solution.py:193
  26.0 2.9 %collective-permute-start.7 = (f32[2,2,8]{2,1,0:T(2,128)S(1)}, f32[2,2,8]{2,1,0:T(2,128)S(1)}, u32[]{:S(2)}, u32[]{:S(2)}) collective-permute-start(f32[2,2,8]{2,1,0:T(2,128)S(1)} %get-tuple-element.34), channel_id=1, source_target_pairs={{0,12},{4,8},{8,4},{12,0},{16,28},{20,24},{24,20},{28,16},{1,13},{... | collective-permute-start | bytes 392 | tf_op jit(solution)/shard_map/ppermute | solution.py:199
  28.9 0.4 %collective-permute-start.6 = (f32[2,2,8]{2,1,0:T(2,128)S(1)}, f32[2,2,8]{2,1,0:T(2,128)S(1)}, u32[]{:S(2)}, u32[]{:S(2)}) collective-permute-start(f32[2,2,8]{2,1,0:T(2,128)S(1)} %get-tuple-element.35), channel_id=1, source_target_pairs={{0,8},{4,12},{8,0},{12,4},{16,24},{20,28},{24,16},{28,20},{1,9},{5... | collective-permute-start | bytes 392 | tf_op jit(solution)/shard_map/ppermute | solution.py:199
  29.4 0.2 collective-permute-start.5
  29.6 1.0 %collective-permute-done.7 = f32[2,2,8]{2,1,0:T(2,128)S(1)} collective-permute-done((f32[2,2,8]{2,1,0:T(2,128)S(1)}, f32[2,2,8]{2,1,0:T(2,128)S(1)}, u32[]{:S(2)}, u32[]{:S(2)}) %collective-permute-start.7) | collective-permute-done | bytes 160 | tf_op jit(solution)/shard_map/ppermute | solution.py:199
  30.6 2.0 %collective-permute-done.6 = f32[2,2,8]{2,1,0:T(2,128)S(1)} collective-permute-done((f32[2,2,8]{2,1,0:T(2,128)S(1)}, f32[2,2,8]{2,1,0:T(2,128)S(1)}, u32[]{:S(2)}, u32[]{:S(2)}) %collective-permute-start.6) | collective-permute-done | bytes 160 | tf_op jit(solution)/shard_map/ppermute | solution.py:199
  32.5 0.4 %collective-permute-done.5 = f32[2,2,8]{2,1,0:T(2,128)S(1)} collective-permute-done((f32[2,2,8]{2,1,0:T(2,128)S(1)}, f32[2,2,8]{2,1,0:T(2,128)S(1)}, u32[]{:S(2)}, u32[]{:S(2)}) %collective-permute-start.5) | collective-permute-done | bytes 160 | tf_op jit(solution)/shard_map/ppermute | solution.py:199
  33.0 0.1 broadcast_in_dim.26
  33.1 0.6 %select_reduce_fusion = f32[128]{0:T(128)} fusion(f32[128]{0:T(128)S(1)} %broadcast_in_dim.26, s32[128]{0:T(128)S(1)} %eq.40), kind=kLoop, calls=%fused_computation.6 | loop fusion | flops 49024 | bytes 1536 | tf_op jit(solution)/shard_map/reduce_sum | solution.py:236
  (34 shorter events, 0.2 us)
Async XLA Ops:
  0.6 0.7 %copy-start.5 = (f32[4,8,128]{2,1,0:T(8,128)S(1)}, f32[4,8,128]{2,1,0:T(8,128)}, u32[]{:S(2)}) copy-start(f32[4,8,128]{2,1,0:T(8,128)} %param.10) | copy-start | bytes 49156
  0.6 0.8 %copy-start.2 = (f32[3,4,8,128]{3,2,1,0:T(8,128)S(1)}, f32[3,4,8,128]{3,2,1,0:T(8,128)}, u32[]{:S(2)}) copy-start(f32[3,4,8,128]{3,2,1,0:T(8,128)} %perm_ref.1) | copy-start | bytes 147460
  1.4 0.8 %copy-start.3 = (f32[3,4,8,128]{3,2,1,0:T(8,128)S(1)}, f32[3,4,8,128]{3,2,1,0:T(8,128)}, u32[]{:S(2)}) copy-start(f32[3,4,8,128]{3,2,1,0:T(8,128)} %e_ref.1) | copy-start | bytes 147460
  1.4 0.8 %copy-start.4 = (f32[3,4,8,128]{3,2,1,0:T(8,128)S(1)}, f32[3,4,8,128]{3,2,1,0:T(8,128)}, u32[]{:S(2)}) copy-start(f32[3,4,8,128]{3,2,1,0:T(8,128)} %h_ref.1) | copy-start | bytes 147460
  2.3 5.8 %collective-permute-start.1 = (f32[10,2,8,128]{3,2,1,0:T(8,128)S(1)}, f32[10,2,8,128]{3,2,1,0:T(8,128)S(1)}, u32[]{:S(2)}, u32[]{:S(2)}) collective-permute-start(f32[10,2,8,128]{3,2,1,0:T(8,128)S(1)} %get-tuple-element.11), channel_id=1, source_target_pairs={{4,8},{8,4},{12,16},{16,12},{20,24},{24,20},{5,9},{9,5},{13,17},{1... | collective-permute-start | bytes 245768 | tf_op jit(solution)/shard_map/ppermute | solution.py:54
  3.0 7.1 %collective-permute-start = (f32[10,2,8,128]{3,2,1,0:T(8,128)S(1)}, f32[10,2,8,128]{3,2,1,0:T(8,128)S(1)}, u32[]{:S(2)}, u32[]{:S(2)}) collective-permute-start(f32[10,2,8,128]{3,2,1,0:T(8,128)S(1)} %get-tuple-element.12), channel_id=1, source_target_pairs={{0,4},{4,0},{8,12},{12,8},{16,20},{20,16},{24,28},{28,24},{1,5},{5... | collective-permute-start | bytes 245768 | tf_op jit(solution)/shard_map/ppermute | solution.py:53
  7.3 0.7 %copy-start.8 = (s32[1,1,8,8]{3,2,1,0:T(8,128)S(1)}, s32[1,1,8,8]{3,2,1,0:T(8,128)}, u32[]{:S(2)}) copy-start(s32[1,1,8,8]{3,2,1,0:T(8,128)} %param.13) | copy-start | bytes 772
  8.1 2.0 %copy-start = (f32[10,2,8,128]{3,2,1,0:T(8,128)}, f32[10,2,8,128]{3,2,1,0:T(8,128)S(1)}, u32[]{:S(2)}) copy-start(f32[10,2,8,128]{3,2,1,0:T(8,128)S(1)} %collective-permute-done.1.x_outer_ref) | copy-start | bytes 245764
  10.1 0.6 %copy-start.1 = (f32[10,2,8,128]{3,2,1,0:T(8,128)}, f32[10,2,8,128]{3,2,1,0:T(8,128)S(1)}, u32[]{:S(2)}) copy-start(f32[10,2,8,128]{3,2,1,0:T(8,128)S(1)} %collective-permute-done.x_inner_ref) | copy-start | bytes 245764
  10.9 2.7 %collective-permute-start.2 = (f32[10,8,2,128]{3,2,1,0:T(2,128)S(1)}, f32[10,8,2,128]{3,2,1,0:T(2,128)S(1)}, u32[]{:S(2)}, u32[]{:S(2)}) collective-permute-start(f32[10,8,2,128]{3,2,1,0:T(2,128)S(1)} %broadcast_select_fusion.1), channel_id=1, source_target_pairs={{0,1},{1,0},{2,3},{3,2},{4,5},{5,4},{6,7},{7,6},{8,9},{9,8},{10,11... | collective-permute-start | bytes 245768 | tf_op jit(solution)/shard_map/ppermute | solution.py:53
  11.0 5.8 %collective-permute-start.3 = (f32[10,8,2,128]{3,2,1,0:T(2,128)S(1)}, f32[10,8,2,128]{3,2,1,0:T(2,128)S(1)}, u32[]{:S(2)}, u32[]{:S(2)}) collective-permute-start(f32[10,8,2,128]{3,2,1,0:T(2,128)S(1)} %broadcast_select_fusion), channel_id=1, source_target_pairs={{1,2},{2,1},{5,6},{6,5},{9,10},{10,9},{13,14},{14,13},{17,18},{18,... | collective-permute-start | bytes 245768 | tf_op jit(solution)/shard_map/ppermute | solution.py:54
  13.6 3.2 %copy-start.6 = (f32[10,8,2,128]{3,2,1,0:T(2,128)}, f32[10,8,2,128]{3,2,1,0:T(2,128)S(1)}, u32[]{:S(2)}) copy-start(f32[10,8,2,128]{3,2,1,0:T(2,128)S(1)} %collective-permute-done.2.y_inner_ref) | copy-start | bytes 245764
  16.7 0.6 %copy-start.7 = (f32[10,8,2,128]{3,2,1,0:T(2,128)}, f32[10,8,2,128]{3,2,1,0:T(2,128)S(1)}, u32[]{:S(2)}) copy-start(f32[10,8,2,128]{3,2,1,0:T(2,128)S(1)} %collective-permute-done.3.y_outer_ref) | copy-start | bytes 245764
  20.1 0.7 %copy-start.9 = (f32[2,64]{1,0:T(2,128)S(1)}, f32[2,64]{1,0:T(2,128)}, u32[]{:S(2)}) copy-start(f32[2,64]{1,0:T(2,128)} %get-tuple-element.8) | copy-start | bytes 1540
  20.8 5.2 %collective-permute-start.4 = (f32[2,4,1,8]{3,1,0,2:T(4,128)S(1)}, f32[2,4,1,8]{3,1,0,2:T(4,128)S(1)}, u32[]{:S(2)}, u32[]{:S(2)}) collective-permute-start(f32[2,4,1,8]{3,1,0,2:T(4,128)S(1)} %get-tuple-element.38), channel_id=1, source_target_pairs={{0,16},{4,20},{8,24},{12,28},{16,0},{20,4},{24,8},{28,12},{1,17},{... | collective-permute-start | bytes 776 | tf_op jit(solution)/shard_map/ppermute | solution.py:193
  26.0 4.5 %collective-permute-start.7 = (f32[2,2,8]{2,1,0:T(2,128)S(1)}, f32[2,2,8]{2,1,0:T(2,128)S(1)}, u32[]{:S(2)}, u32[]{:S(2)}) collective-permute-start(f32[2,2,8]{2,1,0:T(2,128)S(1)} %get-tuple-element.34), channel_id=1, source_target_pairs={{0,12},{4,8},{8,4},{12,0},{16,28},{20,24},{24,20},{28,16},{1,13},{... | collective-permute-start | bytes 392 | tf_op jit(solution)/shard_map/ppermute | solution.py:199
  28.9 3.6 %collective-permute-start.6 = (f32[2,2,8]{2,1,0:T(2,128)S(1)}, f32[2,2,8]{2,1,0:T(2,128)S(1)}, u32[]{:S(2)}, u32[]{:S(2)}) collective-permute-start(f32[2,2,8]{2,1,0:T(2,128)S(1)} %get-tuple-element.35), channel_id=1, source_target_pairs={{0,8},{4,12},{8,0},{12,4},{16,24},{20,28},{24,16},{28,20},{1,9},{5... | collective-permute-start | bytes 392 | tf_op jit(solution)/shard_map/ppermute | solution.py:199
  29.4 3.6 %collective-permute-start.5 = (f32[2,2,8]{2,1,0:T(2,128)S(1)}, f32[2,2,8]{2,1,0:T(2,128)S(1)}, u32[]{:S(2)}, u32[]{:S(2)}) collective-permute-start(f32[2,2,8]{2,1,0:T(2,128)S(1)} %get-tuple-element.36), channel_id=1, source_target_pairs={{0,4},{4,0},{8,12},{12,8},{16,20},{20,16},{24,28},{28,24},{1,5},{5... | collective-permute-start | bytes 392 | tf_op jit(solution)/shard_map/ppermute | solution.py:199

commit v14 on v11

--- a/solution.py
+++ b/solution.py
@@ -57,6 +57,37 @@
 
 def low_high(got_inner, got_outer, odd):
     return jnp.where(odd, got_inner, got_outer), jnp.where(odd, got_outer, got_inner)
+
+
+def pack_kernel(e_ref, h_ref, perm_ref, cond_ref, inner_ref, outer_ref, sems):
+    depth_x = e_ref.shape[1]
+    odd = lax.axis_index("slab") % 2
+    inner = (1 - odd) * (depth_x - HALO)
+    outer = odd * (depth_x - HALO)
+    copies = []
+    for out_ref, start in ((inner_ref, inner), (outer_ref, outer)):
+        planes = pl.ds(start, HALO)
+        for lo, src in ((0, e_ref), (3, h_ref), (6, perm_ref)):
+            copies.append((src.at[:, planes], out_ref.at[lo : lo + 3]))
+        copies.append((cond_ref.at[planes], out_ref.at[9]))
+    started = [pltpu.make_async_copy(a, b, sems.at[i]) for i, (a, b) in enumerate(copies)]
+    for copy in started:
+        copy.start()
+    for copy in started:
+        copy.wait()
+
+
+def pack_x_halos(field_e, field_h, permittivity, conductivity):
+    _, depth_x, depth_y, lanes = field_e.shape
+    anywhere = pl.BlockSpec(memory_space=pl.ANY)
+    piece = jax.ShapeDtypeStruct((10, HALO, depth_y, lanes), jnp.float32)
+    return pl.pallas_call(
+        pack_kernel,
+        out_shape=(piece, piece),
+        in_specs=[anywhere] * 4,
+        out_specs=(anywhere, anywhere),
+        scratch_shapes=[pltpu.SemaphoreType.DMA((8,))],
+    )(field_e, field_h, permittivity, conductivity)
 
 
 def leapfrog_kernel(
@@ -202,10 +233,11 @@
     n_x = lax.axis_size("slab") * depth_x
     n_y = lax.axis_size("yz") * depth_y
     parts = (field_e, field_h, permittivity, conductivity[None])
-    x_inner, x_outer = swap_halos(
-        jnp.concatenate([p[:, :HALO] for p in parts], 0),
-        jnp.concatenate([p[:, depth_x - HALO :] for p in parts], 0),
-        "slab",
+    send_inner, send_outer = pack_x_halos(field_e, field_h, permittivity, conductivity)
+    count = lax.axis_size("slab")
+    x_inner = lax.ppermute(send_inner, "slab", [(i, i ^ 1) for i in range(count) if i ^ 1 < count])
+    x_outer = lax.ppermute(
+        send_outer, "slab", [p for i in range(1, count - 1, 2) for p in ((i, i + 1), (i + 1, i))]
     )
     xlo, xhi = low_high(x_inner, x_outer, lax.axis_index("slab") % 2 == 1)
     def rows(start):

time: 34.1 us -> 37.9 us (1.11)
  Pallas kernels: 2.34 us -> 8.5 us
  local copies, waits for them, and re-layouts: 4.84 us -> 3.3 us
  waiting for transfers between devices: 9.96 us -> 9.09 us
    pallas_call x0 -> x1, Pallas kernels: none -> 6.15 us  [pack_x_halos(): pl.pallas_call(pack_kernel, out_shape=(piece, piece), in_specs=[anywhere]...]
    ppermute x2 -> x1, starting transfers between devices: 4.42 us -> 0.07 us  [swap_halos(): got_inner = lax.ppermute(jnp.where(odd, first, last), axis, inner)]
    ppermute x1, starting transfers between devices: 3.62 us -> 6.92 us  [exchange_by_halving(): got = lax.ppermute(send, 'slab', pairs)]
    ppermute x0 -> x2, starting transfers between devices: none -> 2.24 us  [the longest x1 1.58 us: shards(): lax.ppermute(send_inner, 'slab', [(i, i ^ 1) for i in range(count) if i ^...]
    ppermute x2 -> x1, waiting for transfers between devices: 1.93 us -> 0.01 us  [swap_halos(): got_inner = lax.ppermute(jnp.where(odd, first, last), axis, inner)]
    ppermute x0 -> x2, waiting for transfers between devices: none -> 1.59 us  [the longest x1 1.59 us: shards(): lax.ppermute(send_inner, 'slab', [(i, i ^ 1) for i in range(count) if i ^...]
    unnamed x20, local copies, waits for them, and re-layouts: 4.15 us -> 2.63 us
    ppermute x2 -> x1, starting transfers between devices: 3.2 us -> 2.05 us  [swap_halos(): got_outer = lax.ppermute(jnp.where(odd, last, first), axis, outer)]
  transfers between devices with their start and end apart: 8 -> 8, of which waited for: 6 -> 6; matrix products, arithmetic and copies ran while one was open for 1% -> 0% of each run, Pallas kernels for 0% -> 0%
where the time goes in v14:
time: 37.9 us; the launch traced here: 37.6 us
  starting transfers between devices  14.8 us (39%)
  waiting for transfers between devices  9.09 us (24%)
  Pallas kernels  8.5 us (22%)
  local copies, waits for them, and re-layouts  3.3 us (9%)
  between operations  0.99 us (3%)
  other arithmetic  0.84 us (2%)
    ppermute x1, starting transfers between devices, exchange_by_halving(): got = lax.ppermute(send, 'slab', pairs)  6.92 us
    pallas_call x1, Pallas kernels, pack_x_halos(): pl.pallas_call(pack_kernel, out_shape=(piece, piece), in_specs=[anywhere]...  6.15 us
    ppermute x1, waiting for transfers between devices, swap_halos(): got_outer = lax.ppermute(jnp.where(odd, last, first), axis, outer)  3.62 us
    ppermute x3, starting transfers between devices, exchange_by_halving(): lax.ppermute(held[:, q], 'slab', [(i, i ^ q) for i in range(count)])  3.55 us
    unnamed x20, local copies, waits for them, and re-layouts  2.63 us
    ppermute x3, waiting for transfers between devices, exchange_by_halving(): lax.ppermute(held[:, q], 'slab', [(i, i ^ q) for i in range(count)])  2.39 us
    pallas_call x1, Pallas kernels, leapfrog(): pl.pallas_call(kernel, out_shape=(jax.ShapeDtypeStruct(field_e.shape, jnp...  2.34 us
    ppermute x1, starting transfers between devices, swap_halos(): got_outer = lax.ppermute(jnp.where(odd, last, first), axis, outer)  2.05 us
  transfers between devices with their start and end apart: 8, of which 6 were waited for; matrix products, arithmetic and copies ran while one was open for 0% of the time, Pallas kernels for 0%

profile of v14, /device:TPU:2, one launch (start us, length us, event | category | flops | bytes accessed | tf_op | source)
XLA Modules:
  0.0 37.6 jit_solution(6971648627576709685)
XLA Ops:
  0.7 6.2 %shard_map.94 = (f32[10,2,8,128]{3,2,1,0:T(8,128)}, f32[10,2,8,128]{3,2,1,0:T(8,128)}) custom-call(f32[3,4,8,128]{3,2,1,0:T(8,128)} %e_ref.3, f32[3,4,8,128]{3,2,1,0:T(8,128)} %h_ref.3, f32[3,4,8,128]{3,2,1,0:T(8,128)} %perm_ref.3, f32[4,8,128]{2,1,0:T(8,128)} %cond_ref.1), custom_call_target="tpu_custom_call" | custom-call | tf_op jit(solution)/shard_map/pallas_call | solution.py:84
  6.8 0.0 copy-start.3
  6.8 1.6 %collective-permute-start = (f32[10,2,8,128]{3,2,1,0:T(8,128)}, f32[10,2,8,128]{3,2,1,0:T(8,128)S(1)}, u32[]{:S(2)}, u32[]{:S(2)}) collective-permute-start(f32[10,2,8,128]{3,2,1,0:T(8,128)} %get-tuple-element.8), channel_id=1, source_target_pairs={{0,4},{4,0},{8,12},{12,8},{16,20},{20,16},{24,28},{28,24},{1,5},{5... | collective-permute-start | bytes 245768 | tf_op jit(solution)/shard_map/ppermute | solution.py:238
  8.4 0.7 %collective-permute-start.1 = (f32[10,2,8,128]{3,2,1,0:T(8,128)}, f32[10,2,8,128]{3,2,1,0:T(8,128)S(1)}, u32[]{:S(2)}, u32[]{:S(2)}) collective-permute-start(f32[10,2,8,128]{3,2,1,0:T(8,128)} %get-tuple-element.9), channel_id=1, source_target_pairs={{4,8},{8,4},{12,16},{16,12},{20,24},{24,20},{5,9},{9,5},{13,17},{1... | collective-permute-start | bytes 245768 | tf_op jit(solution)/shard_map/ppermute | solution.py:239
  9.2 0.6 %copy-done.8 = s32[1,1,8,8]{3,2,1,0:T(8,128)S(1)} copy-done((s32[1,1,8,8]{3,2,1,0:T(8,128)S(1)}, s32[1,1,8,8]{3,2,1,0:T(8,128)}, u32[]{:S(2)}) %copy-start.8) | copy-done | bytes 280
  9.8 0.0 copy-done.5
  10.0 1.6 %collective-permute-done.x_inner_ref = f32[10,2,8,128]{3,2,1,0:T(8,128)S(1)} collective-permute-done((f32[10,2,8,128]{3,2,1,0:T(8,128)}, f32[10,2,8,128]{3,2,1,0:T(8,128)S(1)}, u32[]{:S(2)}, u32[]{:S(2)}) %collective-permute-start) | collective-permute-done | bytes 81952 | tf_op jit(solution)/shard_map/ppermute | solution.py:238
  11.6 0.6 %copy-done = f32[10,2,8,128]{3,2,1,0:T(8,128)} copy-done((f32[10,2,8,128]{3,2,1,0:T(8,128)}, f32[10,2,8,128]{3,2,1,0:T(8,128)S(1)}, u32[]{:S(2)}) %copy-start) | copy-done | bytes 81944
  12.2 0.0 copy-done.1
  12.2 0.1 broadcast_select_fusion
  12.3 0.1 broadcast_select_fusion.1
  12.4 0.1 collective-permute-start.2
  12.5 2.1 %collective-permute-start.3 = (f32[10,8,2,128]{3,2,1,0:T(2,128)S(1)}, f32[10,8,2,128]{3,2,1,0:T(2,128)S(1)}, u32[]{:S(2)}, u32[]{:S(2)}) collective-permute-start(f32[10,8,2,128]{3,2,1,0:T(2,128)S(1)} %broadcast_select_fusion), channel_id=1, source_target_pairs={{1,2},{2,1},{5,6},{6,5},{9,10},{10,9},{13,14},{14,13},{17,18},{18,... | collective-permute-start | bytes 245768 | tf_op jit(solution)/shard_map/ppermute | solution.py:54
  14.6 3.6 %collective-permute-done.3.y_outer_ref = f32[10,8,2,128]{3,2,1,0:T(2,128)S(1)} collective-permute-done((f32[10,8,2,128]{3,2,1,0:T(2,128)S(1)}, f32[10,8,2,128]{3,2,1,0:T(2,128)S(1)}, u32[]{:S(2)}, u32[]{:S(2)}) %collective-permute-start.3) | collective-permute-done | bytes 81952 | tf_op jit(solution)/shard_map/ppermute | solution.py:54
  18.2 0.6 %copy-done.7 = f32[10,8,2,128]{3,2,1,0:T(2,128)} copy-done((f32[10,8,2,128]{3,2,1,0:T(2,128)}, f32[10,8,2,128]{3,2,1,0:T(2,128)S(1)}, u32[]{:S(2)}) %copy-start.7) | copy-done | bytes 81944
  18.8 2.3 %shard_map.95 = (f32[3,4,8,128]{3,2,1,0:T(8,128)}, f32[3,4,8,128]{3,2,1,0:T(8,128)}, f32[2,64]{1,0:T(2,128)}) custom-call(f32[3,4,8,128]{3,2,1,0:T(8,128)} %e_ref.3, f32[3,4,8,128]{3,2,1,0:T(8,128)} %h_ref.3, f32[3,4,8,128]{3,2,1,0:T(8,128)} %perm_ref.3, f32[1,4,8,128]{3,2,1,0:T(8,128)} %bitcast.55, f32[10,2,8,128]{3,2,1,0:T(8,128)} %copy-done, ...), custom_call_target="tpu_custom_call" | custom-call | tf_op jit(solution)/shard_map/pallas_call | solution.py:183
  21.2 0.7 %copy-done.9 = f32[2,64]{1,0:T(2,128)S(1)} copy-done((f32[2,64]{1,0:T(2,128)S(1)}, f32[2,64]{1,0:T(2,128)}, u32[]{:S(2)}) %copy-start.9) | copy-done | bytes 536
  21.9 0.1 reshape.194
  21.9 0.1 reshape.190
  22.0 0.1 reshape.187
  22.1 0.1 reshape_reshape.8
  22.3 6.9 %collective-permute-start.4 = (f32[2,4,1,8]{3,1,0,2:T(4,128)S(1)}, f32[2,4,1,8]{3,1,0,2:T(4,128)S(1)}, u32[]{:S(2)}, u32[]{:S(2)}) collective-permute-start(f32[2,4,1,8]{3,1,0,2:T(4,128)S(1)} %get-tuple-element.32), channel_id=1, source_target_pairs={{0,16},{4,20},{8,24},{12,28},{16,0},{20,4},{24,8},{28,12},{1,17},{... | collective-permute-start | bytes 776 | tf_op jit(solution)/shard_map/ppermute | solution.py:216
  29.3 0.1 eq.44
  29.3 1.5 %collective-permute-done.4 = f32[2,4,1,8]{3,1,0,2:T(4,128)S(1)} collective-permute-done((f32[2,4,1,8]{3,1,0,2:T(4,128)S(1)}, f32[2,4,1,8]{3,1,0,2:T(4,128)S(1)}, u32[]{:S(2)}, u32[]{:S(2)}) %collective-permute-start.4) | collective-permute-done | bytes 288 | tf_op jit(solution)/shard_map/ppermute | solution.py:216
  30.9 1.9 %collective-permute-start.7 = (f32[2,2,8]{2,1,0:T(2,128)S(1)}, f32[2,2,8]{2,1,0:T(2,128)S(1)}, u32[]{:S(2)}, u32[]{:S(2)}) collective-permute-start(f32[2,2,8]{2,1,0:T(2,128)S(1)} %get-tuple-element.28), channel_id=1, source_target_pairs={{0,12},{4,8},{8,4},{12,0},{16,28},{20,24},{24,20},{28,16},{1,13},{... | collective-permute-start | bytes 392 | tf_op jit(solution)/shard_map/ppermute | solution.py:222
  32.8 0.4 %collective-permute-start.6 = (f32[2,2,8]{2,1,0:T(2,128)S(1)}, f32[2,2,8]{2,1,0:T(2,128)S(1)}, u32[]{:S(2)}, u32[]{:S(2)}) collective-permute-start(f32[2,2,8]{2,1,0:T(2,128)S(1)} %get-tuple-element.29), channel_id=1, source_target_pairs={{0,8},{4,12},{8,0},{12,4},{16,24},{20,28},{24,16},{28,20},{1,9},{5... | collective-permute-start | bytes 392 | tf_op jit(solution)/shard_map/ppermute | solution.py:222
  33.2 1.2 %collective-permute-start.5 = (f32[2,2,8]{2,1,0:T(2,128)S(1)}, f32[2,2,8]{2,1,0:T(2,128)S(1)}, u32[]{:S(2)}, u32[]{:S(2)}) collective-permute-start(f32[2,2,8]{2,1,0:T(2,128)S(1)} %get-tuple-element.30), channel_id=1, source_target_pairs={{0,4},{4,0},{8,12},{12,8},{16,20},{20,16},{24,28},{28,24},{1,5},{5... | collective-permute-start | bytes 392 | tf_op jit(solution)/shard_map/ppermute | solution.py:222
  34.4 1.0 %collective-permute-done.7 = f32[2,2,8]{2,1,0:T(2,128)S(1)} collective-permute-done((f32[2,2,8]{2,1,0:T(2,128)S(1)}, f32[2,2,8]{2,1,0:T(2,128)S(1)}, u32[]{:S(2)}, u32[]{:S(2)}) %collective-permute-start.7) | collective-permute-done | bytes 160 | tf_op jit(solution)/shard_map/ppermute | solution.py:222
  35.4 0.9 %collective-permute-done.6 = f32[2,2,8]{2,1,0:T(2,128)S(1)} collective-permute-done((f32[2,2,8]{2,1,0:T(2,128)S(1)}, f32[2,2,8]{2,1,0:T(2,128)S(1)}, u32[]{:S(2)}, u32[]{:S(2)}) %collective-permute-start.6) | collective-permute-done | bytes 160 | tf_op jit(solution)/shard_map/ppermute | solution.py:222
  36.4 0.4 %collective-permute-done.5 = f32[2,2,8]{2,1,0:T(2,128)S(1)} collective-permute-done((f32[2,2,8]{2,1,0:T(2,128)S(1)}, f32[2,2,8]{2,1,0:T(2,128)S(1)}, u32[]{:S(2)}, u32[]{:S(2)}) %collective-permute-start.5) | collective-permute-done | bytes 160 | tf_op jit(solution)/shard_map/ppermute | solution.py:222
  36.8 0.1 broadcast_in_dim.27
  36.9 0.6 %select_reduce_fusion = f32[128]{0:T(128)} fusion(f32[128]{0:T(128)S(1)} %broadcast_in_dim.27, s32[128]{0:T(128)S(1)} %eq.44), kind=kLoop, calls=%fused_computation.4 | loop fusion | flops 49024 | bytes 1536 | tf_op jit(solution)/shard_map/reduce_sum | solution.py:260
  (39 shorter events, 0.3 us)
Async XLA Ops:
  0.6 8.5 %copy-start.2 = (f32[3,4,8,128]{3,2,1,0:T(8,128)S(1)}, f32[3,4,8,128]{3,2,1,0:T(8,128)}, u32[]{:S(2)}) copy-start(f32[3,4,8,128]{3,2,1,0:T(8,128)} %perm_ref.3) | copy-start | bytes 147460
  0.6 8.5 %copy-start.4 = (f32[3,4,8,128]{3,2,1,0:T(8,128)S(1)}, f32[3,4,8,128]{3,2,1,0:T(8,128)}, u32[]{:S(2)}) copy-start(f32[3,4,8,128]{3,2,1,0:T(8,128)} %h_ref.3) | copy-start | bytes 147460
  6.8 2.3 %copy-start.3 = (f32[3,4,8,128]{3,2,1,0:T(8,128)S(1)}, f32[3,4,8,128]{3,2,1,0:T(8,128)}, u32[]{:S(2)}) copy-start(f32[3,4,8,128]{3,2,1,0:T(8,128)} %e_ref.3) | copy-start | bytes 147460
  6.8 4.7 %collective-permute-start = (f32[10,2,8,128]{3,2,1,0:T(8,128)}, f32[10,2,8,128]{3,2,1,0:T(8,128)S(1)}, u32[]{:S(2)}, u32[]{:S(2)}) collective-permute-start(f32[10,2,8,128]{3,2,1,0:T(8,128)} %get-tuple-element.8), channel_id=1, source_target_pairs={{0,4},{4,0},{8,12},{12,8},{16,20},{20,16},{24,28},{28,24},{1,5},{5... | collective-permute-start | bytes 245768 | tf_op jit(solution)/shard_map/ppermute | solution.py:238
  8.4 3.1 %collective-permute-start.1 = (f32[10,2,8,128]{3,2,1,0:T(8,128)}, f32[10,2,8,128]{3,2,1,0:T(8,128)S(1)}, u32[]{:S(2)}, u32[]{:S(2)}) collective-permute-start(f32[10,2,8,128]{3,2,1,0:T(8,128)} %get-tuple-element.9), channel_id=1, source_target_pairs={{4,8},{8,4},{12,16},{16,12},{20,24},{24,20},{5,9},{9,5},{13,17},{1... | collective-permute-start | bytes 245768 | tf_op jit(solution)/shard_map/ppermute | solution.py:239
  9.1 0.7 %copy-start.8 = (s32[1,1,8,8]{3,2,1,0:T(8,128)S(1)}, s32[1,1,8,8]{3,2,1,0:T(8,128)}, u32[]{:S(2)}) copy-start(s32[1,1,8,8]{3,2,1,0:T(8,128)} %param.13) | copy-start | bytes 772
  9.2 0.7 %copy-start.5 = (f32[4,8,128]{2,1,0:T(8,128)S(1)}, f32[4,8,128]{2,1,0:T(8,128)}, u32[]{:S(2)}) copy-start(f32[4,8,128]{2,1,0:T(8,128)} %cond_ref.1) | copy-start | bytes 49156
  11.5 0.6 %copy-start = (f32[10,2,8,128]{3,2,1,0:T(8,128)}, f32[10,2,8,128]{3,2,1,0:T(8,128)S(1)}, u32[]{:S(2)}) copy-start(f32[10,2,8,128]{3,2,1,0:T(8,128)S(1)} %collective-permute-done.x_inner_ref) | copy-start | bytes 245764
  11.5 0.7 %copy-start.1 = (f32[10,2,8,128]{3,2,1,0:T(8,128)}, f32[10,2,8,128]{3,2,1,0:T(8,128)S(1)}, u32[]{:S(2)}) copy-start(f32[10,2,8,128]{3,2,1,0:T(8,128)S(1)} %collective-permute-done.1.x_outer_ref) | copy-start | bytes 245764
  12.4 2.2 %collective-permute-start.2 = (f32[10,8,2,128]{3,2,1,0:T(2,128)S(1)}, f32[10,8,2,128]{3,2,1,0:T(2,128)S(1)}, u32[]{:S(2)}, u32[]{:S(2)}) collective-permute-start(f32[10,8,2,128]{3,2,1,0:T(2,128)S(1)} %broadcast_select_fusion.1), channel_id=1, source_target_pairs={{0,1},{1,0},{2,3},{3,2},{4,5},{5,4},{6,7},{7,6},{8,9},{9,8},{10,11... | collective-permute-start | bytes 245768 | tf_op jit(solution)/shard_map/ppermute | solution.py:53
  12.5 5.8 %collective-permute-start.3 = (f32[10,8,2,128]{3,2,1,0:T(2,128)S(1)}, f32[10,8,2,128]{3,2,1,0:T(2,128)S(1)}, u32[]{:S(2)}, u32[]{:S(2)}) collective-permute-start(f32[10,8,2,128]{3,2,1,0:T(2,128)S(1)} %broadcast_select_fusion), channel_id=1, source_target_pairs={{1,2},{2,1},{5,6},{6,5},{9,10},{10,9},{13,14},{14,13},{17,18},{18,... | collective-permute-start | bytes 245768 | tf_op jit(solution)/shard_map/ppermute | solution.py:54
  14.6 3.6 %copy-start.6 = (f32[10,8,2,128]{3,2,1,0:T(2,128)}, f32[10,8,2,128]{3,2,1,0:T(2,128)S(1)}, u32[]{:S(2)}) copy-start(f32[10,8,2,128]{3,2,1,0:T(2,128)S(1)} %collective-permute-done.2.y_inner_ref) | copy-start | bytes 245764
  18.2 0.6 %copy-start.7 = (f32[10,8,2,128]{3,2,1,0:T(2,128)}, f32[10,8,2,128]{3,2,1,0:T(2,128)S(1)}, u32[]{:S(2)}) copy-start(f32[10,8,2,128]{3,2,1,0:T(2,128)S(1)} %collective-permute-done.3.y_outer_ref) | copy-start | bytes 245764
  21.2 0.7 %copy-start.9 = (f32[2,64]{1,0:T(2,128)S(1)}, f32[2,64]{1,0:T(2,128)}, u32[]{:S(2)}) copy-start(f32[2,64]{1,0:T(2,128)} %get-tuple-element.12) | copy-start | bytes 1540
  22.3 8.5 %collective-permute-start.4 = (f32[2,4,1,8]{3,1,0,2:T(4,128)S(1)}, f32[2,4,1,8]{3,1,0,2:T(4,128)S(1)}, u32[]{:S(2)}, u32[]{:S(2)}) collective-permute-start(f32[2,4,1,8]{3,1,0,2:T(4,128)S(1)} %get-tuple-element.32), channel_id=1, source_target_pairs={{0,16},{4,20},{8,24},{12,28},{16,0},{20,4},{24,8},{28,12},{1,17},{... | collective-permute-start | bytes 776 | tf_op jit(solution)/shard_map/ppermute | solution.py:216
  30.9 4.5 %collective-permute-start.7 = (f32[2,2,8]{2,1,0:T(2,128)S(1)}, f32[2,2,8]{2,1,0:T(2,128)S(1)}, u32[]{:S(2)}, u32[]{:S(2)}) collective-permute-start(f32[2,2,8]{2,1,0:T(2,128)S(1)} %get-tuple-element.28), channel_id=1, source_target_pairs={{0,12},{4,8},{8,4},{12,0},{16,28},{20,24},{24,20},{28,16},{1,13},{... | collective-permute-start | bytes 392 | tf_op jit(solution)/shard_map/ppermute | solution.py:222
  32.8 3.6 %collective-permute-start.6 = (f32[2,2,8]{2,1,0:T(2,128)S(1)}, f32[2,2,8]{2,1,0:T(2,128)S(1)}, u32[]{:S(2)}, u32[]{:S(2)}) collective-permute-start(f32[2,2,8]{2,1,0:T(2,128)S(1)} %get-tuple-element.29), channel_id=1, source_target_pairs={{0,8},{4,12},{8,0},{12,4},{16,24},{20,28},{24,16},{28,20},{1,9},{5... | collective-permute-start | bytes 392 | tf_op jit(solution)/shard_map/ppermute | solution.py:222
  33.2 3.6 %collective-permute-start.5 = (f32[2,2,8]{2,1,0:T(2,128)S(1)}, f32[2,2,8]{2,1,0:T(2,128)S(1)}, u32[]{:S(2)}, u32[]{:S(2)}) collective-permute-start(f32[2,2,8]{2,1,0:T(2,128)S(1)} %get-tuple-element.30), channel_id=1, source_target_pairs={{0,4},{4,0},{8,12},{12,8},{16,20},{20,16},{24,28},{28,24},{1,5},{5... | collective-permute-start | bytes 392 | tf_op jit(solution)/shard_map/ppermute | solution.py:222

commit v15 on v11

--- a/solution.py
+++ b/solution.py
@@ -59,6 +59,21 @@
     return jnp.where(odd, got_inner, got_outer), jnp.where(odd, got_outer, got_inner)
 
 
+def pack_planes(parts, start, near):
+    fields = [p[:, start : start + HALO].reshape((-1,) + p.shape[2:]) for p in parts[:2]]
+    material = [parts[2][:, start + near], parts[3][:, start + near]]
+    return jnp.concatenate(fields + material, 0)
+
+
+def unpack_planes(piece, near):
+    rows = piece.shape[1:]
+    fields = piece[0:12].reshape((6, HALO) + rows)
+    material = piece[12:16][:, None]
+    filler = jnp.concatenate([jnp.ones((3, 1) + rows, jnp.float32), jnp.zeros((1, 1) + rows, jnp.float32)], 0)
+    planes = [material, filler] if near == 0 else [filler, material]
+    return jnp.concatenate([fields, jnp.concatenate(planes, 1)], 0)
+
+
 def leapfrog_kernel(
     dims, e_ref, h_ref, perm_ref, cond_ref, x_inner_ref, x_outer_ref, y_inner_ref, y_outer_ref,
     cell_ref, fwd_ref, e_out, h_out, prod_out, ring,
@@ -67,6 +82,7 @@
     ring_x, ring_y = ring.shape[1], ring.shape[2]
     slab, yz = lax.axis_index("slab"), lax.axis_index("yz")
     xlo, xhi = low_high(x_inner_ref[...], x_outer_ref[...], slab % 2 == 1)
+    xlo, xhi = unpack_planes(xlo, HALO - 1), unpack_planes(xhi, 0)
     ylo, yhi = low_high(y_inner_ref[...], y_outer_ref[...], yz % 2 == 1)
     ring[0:3, 0:depth_x, 0:depth_y] = e_ref[...]
     ring[3:6, 0:depth_x, 0:depth_y] = h_ref[...]
@@ -203,11 +219,10 @@
     n_y = lax.axis_size("yz") * depth_y
     parts = (field_e, field_h, permittivity, conductivity[None])
     x_inner, x_outer = swap_halos(
-        jnp.concatenate([p[:, :HALO] for p in parts], 0),
-        jnp.concatenate([p[:, depth_x - HALO :] for p in parts], 0),
-        "slab",
+        pack_planes(parts, 0, 0), pack_planes(parts, depth_x - HALO, HALO - 1), "slab"
     )
     xlo, xhi = low_high(x_inner, x_outer, lax.axis_index("slab") % 2 == 1)
+    xlo, xhi = unpack_planes(xlo, HALO - 1), unpack_planes(xhi, 0)
     def rows(start):
         center = jnp.concatenate([p[:, :, start : start + HALO] for p in parts], 0)
         return jnp.concatenate([center, xhi[:, :, start : start + HALO], xlo[:, :, start : start + HALO]], 1)

time: 34.1 us -> 34.1 us (level)
  local copies, waits for them, and re-layouts: 4.84 us -> 5.53 us
  waiting for transfers between devices: 9.96 us -> 9.45 us
    squeeze x0 -> x2, local copies, waits for them, and re-layouts: none -> 0.72 us  [pack_planes(): material = [parts[2][:, start + near], parts[3][:, start + near]]]
    ppermute x2, waiting for transfers between devices: 1.93 us -> 1.43 us  [swap_halos(): got_inner = lax.ppermute(jnp.where(odd, first, last), axis, inner)]
    unnamed x20 -> x24, local copies, waits for them, and re-layouts: 4.15 us -> 4.14 us
where the time goes in v15:
time: 34.1 us; the launch traced here: 33.7 us
  starting transfers between devices  14.6 us (43%)
  waiting for transfers between devices  9.45 us (28%)
  local copies, waits for them, and re-layouts  5.53 us (16%)
  Pallas kernels  2.32 us (7%)
  between operations  0.98 us (3%)
  other arithmetic  0.8 us (2%)
    ppermute x2, starting transfers between devices, swap_halos(): got_inner = lax.ppermute(jnp.where(odd, first, last), axis, inner)  4.42 us
    unnamed x24, local copies, waits for them, and re-layouts  4.14 us
    ppermute x3, starting transfers between devices, exchange_by_halving(): lax.ppermute(held[:, q], 'slab', [(i, i ^ q) for i in range(count)])  3.57 us
    ppermute x1, starting transfers between devices, exchange_by_halving(): got = lax.ppermute(send, 'slab', pairs)  3.42 us
    ppermute x3, waiting for transfers between devices, exchange_by_halving(): lax.ppermute(held[:, q], 'slab', [(i, i ^ q) for i in range(count)])  3.39 us
    ppermute x2, starting transfers between devices, swap_halos(): got_outer = lax.ppermute(jnp.where(odd, last, first), axis, outer)  3.2 us
    ppermute x2, waiting for transfers between devices, swap_halos(): got_outer = lax.ppermute(jnp.where(odd, last, first), axis, outer)  3.15 us
    pallas_call x1, Pallas kernels, leapfrog(): pl.pallas_call(kernel, out_shape=(jax.ShapeDtypeStruct(field_e.shape, jnp...  2.32 us
  transfers between devices with their start and end apart: 8, of which 6 were waited for; matrix products, arithmetic and copies ran while one was open for 1% of the time, Pallas kernels for 0%

profile of v15, /device:TPU:2, one launch (start us, length us, event | category | flops | bytes accessed | tf_op | source)
XLA Modules:
  0.0 33.7 jit_solution(9029610697898925138)
XLA Ops:
  0.7 0.7 %slice_bitcast_fusion.6 = (f32[1,8,128]{2,1,0:T(8,128)S(1)}, f32[1,8,128]{2,1,0:T(8,128)S(1)}) fusion(f32[1,4,8,128]{3,2,1,0:T(8,128)} %bitcast.92), kind=kLoop, calls=%fused_computation.33 | loop fusion | bytes 16384 | tf_op jit(solution)/shard_map/squeeze | solution.py:64
  1.4 0.0 copy-done.4
  1.5 0.8 %copy-done.1 = f32[3,4,8,128]{3,2,1,0:T(8,128)S(1)} copy-done((f32[3,4,8,128]{3,2,1,0:T(8,128)S(1)}, f32[3,4,8,128]{3,2,1,0:T(8,128)}, u32[]{:S(2)}) %copy-start.1) | copy-done | bytes 49176
  2.3 0.7 %collective-permute-start.1 = (f32[16,8,128]{2,1,0:T(8,128)S(1)}, f32[16,8,128]{2,1,0:T(8,128)S(1)}, u32[]{:S(2)}, u32[]{:S(2)}) collective-permute-start(f32[16,8,128]{2,1,0:T(8,128)S(1)} %get-tuple-element.14), channel_id=1, source_target_pairs={{4,8},{8,4},{12,16},{16,12},{20,24},{24,20},{5,9},{9,5},{13,17},{1... | collective-permute-start | bytes 196616 | tf_op jit(solution)/shard_map/ppermute | solution.py:54
  3.0 4.3 %collective-permute-start = (f32[16,8,128]{2,1,0:T(8,128)S(1)}, f32[16,8,128]{2,1,0:T(8,128)S(1)}, u32[]{:S(2)}, u32[]{:S(2)}) collective-permute-start(f32[16,8,128]{2,1,0:T(8,128)S(1)} %get-tuple-element.15), channel_id=1, source_target_pairs={{0,4},{4,0},{8,12},{12,8},{16,20},{20,16},{24,28},{28,24},{1,5},{5... | collective-permute-start | bytes 196616 | tf_op jit(solution)/shard_map/ppermute | solution.py:53
  7.4 0.7 %copy-done.8 = s32[1,1,8,8]{3,2,1,0:T(8,128)S(1)} copy-done((s32[1,1,8,8]{3,2,1,0:T(8,128)S(1)}, s32[1,1,8,8]{3,2,1,0:T(8,128)}, u32[]{:S(2)}) %copy-start.8) | copy-done | bytes 280
  8.1 1.4 %collective-permute-done.x_inner_ref = f32[16,8,128]{2,1,0:T(8,128)S(1)} collective-permute-done((f32[16,8,128]{2,1,0:T(8,128)S(1)}, f32[16,8,128]{2,1,0:T(8,128)S(1)}, u32[]{:S(2)}, u32[]{:S(2)}) %collective-permute-start) | collective-permute-done | bytes 65568 | tf_op jit(solution)/shard_map/ppermute | solution.py:53
  9.6 0.6 %copy-done.3 = f32[16,8,128]{2,1,0:T(8,128)} copy-done((f32[16,8,128]{2,1,0:T(8,128)}, f32[16,8,128]{2,1,0:T(8,128)S(1)}, u32[]{:S(2)}) %copy-start.3) | copy-done | bytes 65560
  10.2 0.7 %copy-done.10 = f32[4,1,8,128]{3,2,0,1:T(8,128)S(1)} copy-done((f32[4,1,8,128]{3,2,0,1:T(8,128)S(1)}, f32[4,1,8,128]{3,2,0,1:T(8,128)}, u32[]{:S(2)}) %copy-start.10) | copy-done | bytes 16408
  10.9 0.0 copy-done.9
  10.9 0.1 broadcast_select_fusion
  11.0 0.1 collective-permute-start.2
  11.1 2.5 %collective-permute-start.3 = (f32[10,8,2,128]{3,2,1,0:T(2,128)S(1)}, f32[10,8,2,128]{3,2,1,0:T(2,128)S(1)}, u32[]{:S(2)}, u32[]{:S(2)}) collective-permute-start(f32[10,8,2,128]{3,2,1,0:T(2,128)S(1)} %get-tuple-element.9), channel_id=1, source_target_pairs={{1,2},{2,1},{5,6},{6,5},{9,10},{10,9},{13,14},{14,13},{17,18},{18,... | collective-permute-start | bytes 245768 | tf_op jit(solution)/shard_map/ppermute | solution.py:54
  13.7 3.1 %collective-permute-done.3.y_outer_ref = f32[10,8,2,128]{3,2,1,0:T(2,128)S(1)} collective-permute-done((f32[10,8,2,128]{3,2,1,0:T(2,128)S(1)}, f32[10,8,2,128]{3,2,1,0:T(2,128)S(1)}, u32[]{:S(2)}, u32[]{:S(2)}) %collective-permute-start.3) | collective-permute-done | bytes 81952 | tf_op jit(solution)/shard_map/ppermute | solution.py:54
  16.9 0.6 %copy-done.6 = f32[10,8,2,128]{3,2,1,0:T(2,128)} copy-done((f32[10,8,2,128]{3,2,1,0:T(2,128)}, f32[10,8,2,128]{3,2,1,0:T(2,128)S(1)}, u32[]{:S(2)}) %copy-start.6) | copy-done | bytes 81944
  17.5 2.3 %shard_map.94 = (f32[3,4,8,128]{3,2,1,0:T(8,128)}, f32[3,4,8,128]{3,2,1,0:T(8,128)}, f32[2,64]{1,0:T(2,128)}) custom-call(f32[3,4,8,128]{3,2,1,0:T(8,128)} %e_ref.1, f32[3,4,8,128]{3,2,1,0:T(8,128)} %h_ref.1, f32[3,4,8,128]{3,2,1,0:T(8,128)} %perm_ref.1, f32[1,4,8,128]{3,2,1,0:T(8,128)} %bitcast.93, f32[16,8,128]{2,1,0:T(8,128)} %copy-done.3, ...), custom_call_target="tpu_custom_call" | custom-call | tf_op jit(solution)/shard_map/pallas_call | solution.py:168
  19.8 0.7 %copy-done.11 = f32[2,64]{1,0:T(2,128)S(1)} copy-done((f32[2,64]{1,0:T(2,128)S(1)}, f32[2,64]{1,0:T(2,128)}, u32[]{:S(2)}) %copy-start.11) | copy-done | bytes 536
  20.5 0.1 reshape.218
  20.6 0.1 reshape.214
  20.6 0.1 reshape.211
  20.7 0.1 reshape_reshape.8
  20.9 3.4 %collective-permute-start.4 = (f32[2,4,1,8]{3,1,0,2:T(4,128)S(1)}, f32[2,4,1,8]{3,1,0,2:T(4,128)S(1)}, u32[]{:S(2)}, u32[]{:S(2)}) collective-permute-start(f32[2,4,1,8]{3,1,0,2:T(4,128)S(1)} %get-tuple-element.37), channel_id=1, source_target_pairs={{0,16},{4,20},{8,24},{12,28},{16,0},{20,4},{24,8},{28,12},{1,17},{... | collective-permute-start | bytes 776 | tf_op jit(solution)/shard_map/ppermute | solution.py:201
  24.4 0.1 eq.46
  24.5 1.5 %collective-permute-done.4 = f32[2,4,1,8]{3,1,0,2:T(4,128)S(1)} collective-permute-done((f32[2,4,1,8]{3,1,0,2:T(4,128)S(1)}, f32[2,4,1,8]{3,1,0,2:T(4,128)S(1)}, u32[]{:S(2)}, u32[]{:S(2)}) %collective-permute-start.4) | collective-permute-done | bytes 288 | tf_op jit(solution)/shard_map/ppermute | solution.py:201
  26.0 2.9 %collective-permute-start.7 = (f32[2,2,8]{2,1,0:T(2,128)S(1)}, f32[2,2,8]{2,1,0:T(2,128)S(1)}, u32[]{:S(2)}, u32[]{:S(2)}) collective-permute-start(f32[2,2,8]{2,1,0:T(2,128)S(1)} %get-tuple-element.33), channel_id=1, source_target_pairs={{0,12},{4,8},{8,4},{12,0},{16,28},{20,24},{24,20},{28,16},{1,13},{... | collective-permute-start | bytes 392 | tf_op jit(solution)/shard_map/ppermute | solution.py:207
  28.9 0.4 %collective-permute-start.6 = (f32[2,2,8]{2,1,0:T(2,128)S(1)}, f32[2,2,8]{2,1,0:T(2,128)S(1)}, u32[]{:S(2)}, u32[]{:S(2)}) collective-permute-start(f32[2,2,8]{2,1,0:T(2,128)S(1)} %get-tuple-element.34), channel_id=1, source_target_pairs={{0,8},{4,12},{8,0},{12,4},{16,24},{20,28},{24,16},{28,20},{1,9},{5... | collective-permute-start | bytes 392 | tf_op jit(solution)/shard_map/ppermute | solution.py:207
  29.4 0.2 collective-permute-start.5
  29.5 1.0 %collective-permute-done.7 = f32[2,2,8]{2,1,0:T(2,128)S(1)} collective-permute-done((f32[2,2,8]{2,1,0:T(2,128)S(1)}, f32[2,2,8]{2,1,0:T(2,128)S(1)}, u32[]{:S(2)}, u32[]{:S(2)}) %collective-permute-start.7) | collective-permute-done | bytes 160 | tf_op jit(solution)/shard_map/ppermute | solution.py:207
  30.5 2.0 %collective-permute-done.6 = f32[2,2,8]{2,1,0:T(2,128)S(1)} collective-permute-done((f32[2,2,8]{2,1,0:T(2,128)S(1)}, f32[2,2,8]{2,1,0:T(2,128)S(1)}, u32[]{:S(2)}, u32[]{:S(2)}) %collective-permute-start.6) | collective-permute-done | bytes 160 | tf_op jit(solution)/shard_map/ppermute | solution.py:207
  32.5 0.4 %collective-permute-done.5 = f32[2,2,8]{2,1,0:T(2,128)S(1)} collective-permute-done((f32[2,2,8]{2,1,0:T(2,128)S(1)}, f32[2,2,8]{2,1,0:T(2,128)S(1)}, u32[]{:S(2)}, u32[]{:S(2)}) %collective-permute-start.5) | collective-permute-done | bytes 160 | tf_op jit(solution)/shard_map/ppermute | solution.py:207
  33.0 0.1 broadcast_in_dim.35
  33.0 0.6 %select_reduce_fusion = f32[128]{0:T(128)} fusion(f32[128]{0:T(128)S(1)} %broadcast_in_dim.35, s32[128]{0:T(128)S(1)} %eq.46), kind=kLoop, calls=%fused_computation.14 | loop fusion | flops 49024 | bytes 1536 | tf_op jit(solution)/shard_map/reduce_sum | solution.py:243
  (50 shorter events, 0.3 us)
Async XLA Ops:
  0.6 0.8 %copy-start.4 = (f32[3,4,8,128]{3,2,1,0:T(8,128)S(1)}, f32[3,4,8,128]{3,2,1,0:T(8,128)}, u32[]{:S(2)}) copy-start(f32[3,4,8,128]{3,2,1,0:T(8,128)} %perm_ref.1) | copy-start | bytes 147460
  0.6 0.8 %copy-start = (f32[3,4,8,128]{3,2,1,0:T(8,128)S(1)}, f32[3,4,8,128]{3,2,1,0:T(8,128)}, u32[]{:S(2)}) copy-start(f32[3,4,8,128]{3,2,1,0:T(8,128)} %e_ref.1) | copy-start | bytes 147460
  1.5 0.8 %copy-start.1 = (f32[3,4,8,128]{3,2,1,0:T(8,128)S(1)}, f32[3,4,8,128]{3,2,1,0:T(8,128)}, u32[]{:S(2)}) copy-start(f32[3,4,8,128]{3,2,1,0:T(8,128)} %h_ref.1) | copy-start | bytes 147460
  2.3 5.0 %copy-start.7 = (f32[4,8,128]{2,1,0:T(8,128)S(1)}, f32[4,8,128]{2,1,0:T(8,128)}, u32[]{:S(2)}) copy-start(f32[4,8,128]{2,1,0:T(8,128)} %param.10) | copy-start | bytes 49156
  2.3 5.8 %collective-permute-start.1 = (f32[16,8,128]{2,1,0:T(8,128)S(1)}, f32[16,8,128]{2,1,0:T(8,128)S(1)}, u32[]{:S(2)}, u32[]{:S(2)}) collective-permute-start(f32[16,8,128]{2,1,0:T(8,128)S(1)} %get-tuple-element.14), channel_id=1, source_target_pairs={{4,8},{8,4},{12,16},{16,12},{20,24},{24,20},{5,9},{9,5},{13,17},{1... | collective-permute-start | bytes 196616 | tf_op jit(solution)/shard_map/ppermute | solution.py:54
  3.0 6.6 %collective-permute-start = (f32[16,8,128]{2,1,0:T(8,128)S(1)}, f32[16,8,128]{2,1,0:T(8,128)S(1)}, u32[]{:S(2)}, u32[]{:S(2)}) collective-permute-start(f32[16,8,128]{2,1,0:T(8,128)S(1)} %get-tuple-element.15), channel_id=1, source_target_pairs={{0,4},{4,0},{8,12},{12,8},{16,20},{20,16},{24,28},{28,24},{1,5},{5... | collective-permute-start | bytes 196616 | tf_op jit(solution)/shard_map/ppermute | solution.py:53
  7.3 0.7 %copy-start.8 = (s32[1,1,8,8]{3,2,1,0:T(8,128)S(1)}, s32[1,1,8,8]{3,2,1,0:T(8,128)}, u32[]{:S(2)}) copy-start(s32[1,1,8,8]{3,2,1,0:T(8,128)} %param.13) | copy-start | bytes 772
  8.1 1.5 %copy-start.2 = (f32[16,8,128]{2,1,0:T(8,128)}, f32[16,8,128]{2,1,0:T(8,128)S(1)}, u32[]{:S(2)}) copy-start(f32[16,8,128]{2,1,0:T(8,128)S(1)} %collective-permute-done.1.x_outer_ref) | copy-start | bytes 196612
  9.5 0.6 %copy-start.3 = (f32[16,8,128]{2,1,0:T(8,128)}, f32[16,8,128]{2,1,0:T(8,128)S(1)}, u32[]{:S(2)}) copy-start(f32[16,8,128]{2,1,0:T(8,128)S(1)} %collective-permute-done.x_inner_ref) | copy-start | bytes 196612
  10.2 0.7 %copy-start.10 = (f32[4,1,8,128]{3,2,0,1:T(8,128)S(1)}, f32[4,1,8,128]{3,2,0,1:T(8,128)}, u32[]{:S(2)}) copy-start(f32[4,1,8,128]{3,2,0,1:T(8,128)} %constant.82.clone.1) | copy-start | bytes 49156
  10.2 0.7 %copy-start.9 = (f32[4,1,8,128]{3,2,1,0:T(8,128)S(1)}, f32[4,1,8,128]{3,2,1,0:T(8,128)}, u32[]{:S(2)}) copy-start(f32[4,1,8,128]{3,2,1,0:T(8,128)} %constant.93) | copy-start | bytes 49156
  11.0 2.7 %collective-permute-start.2 = (f32[10,8,2,128]{3,2,1,0:T(2,128)S(1)}, f32[10,8,2,128]{3,2,1,0:T(2,128)S(1)}, u32[]{:S(2)}, u32[]{:S(2)}) collective-permute-start(f32[10,8,2,128]{3,2,1,0:T(2,128)S(1)} %bitcast.89), channel_id=1, source_target_pairs={{0,1},{1,0},{2,3},{3,2},{4,5},{5,4},{6,7},{7,6},{8,9},{9,8},{10,11... | collective-permute-start | bytes 245768 | tf_op jit(solution)/shard_map/ppermute | solution.py:53
  11.1 5.8 %collective-permute-start.3 = (f32[10,8,2,128]{3,2,1,0:T(2,128)S(1)}, f32[10,8,2,128]{3,2,1,0:T(2,128)S(1)}, u32[]{:S(2)}, u32[]{:S(2)}) collective-permute-start(f32[10,8,2,128]{3,2,1,0:T(2,128)S(1)} %get-tuple-element.9), channel_id=1, source_target_pairs={{1,2},{2,1},{5,6},{6,5},{9,10},{10,9},{13,14},{14,13},{17,18},{18,... | collective-permute-start | bytes 245768 | tf_op jit(solution)/shard_map/ppermute | solution.py:54
  13.7 3.2 %copy-start.5 = (f32[10,8,2,128]{3,2,1,0:T(2,128)}, f32[10,8,2,128]{3,2,1,0:T(2,128)S(1)}, u32[]{:S(2)}) copy-start(f32[10,8,2,128]{3,2,1,0:T(2,128)S(1)} %collective-permute-done.2.y_inner_ref) | copy-start | bytes 245764
  16.9 0.6 %copy-start.6 = (f32[10,8,2,128]{3,2,1,0:T(2,128)}, f32[10,8,2,128]{3,2,1,0:T(2,128)S(1)}, u32[]{:S(2)}) copy-start(f32[10,8,2,128]{3,2,1,0:T(2,128)S(1)} %collective-permute-done.3.y_outer_ref) | copy-start | bytes 245764
  19.8 0.7 %copy-start.11 = (f32[2,64]{1,0:T(2,128)S(1)}, f32[2,64]{1,0:T(2,128)}, u32[]{:S(2)}) copy-start(f32[2,64]{1,0:T(2,128)} %get-tuple-element.8) | copy-start | bytes 1540
  20.9 5.0 %collective-permute-start.4 = (f32[2,4,1,8]{3,1,0,2:T(4,128)S(1)}, f32[2,4,1,8]{3,1,0,2:T(4,128)S(1)}, u32[]{:S(2)}, u32[]{:S(2)}) collective-permute-start(f32[2,4,1,8]{3,1,0,2:T(4,128)S(1)} %get-tuple-element.37), channel_id=1, source_target_pairs={{0,16},{4,20},{8,24},{12,28},{16,0},{20,4},{24,8},{28,12},{1,17},{... | collective-permute-start | bytes 776 | tf_op jit(solution)/shard_map/ppermute | solution.py:201
  26.0 4.5 %collective-permute-start.7 = (f32[2,2,8]{2,1,0:T(2,128)S(1)}, f32[2,2,8]{2,1,0:T(2,128)S(1)}, u32[]{:S(2)}, u32[]{:S(2)}) collective-permute-start(f32[2,2,8]{2,1,0:T(2,128)S(1)} %get-tuple-element.33), channel_id=1, source_target_pairs={{0,12},{4,8},{8,4},{12,0},{16,28},{20,24},{24,20},{28,16},{1,13},{... | collective-permute-start | bytes 392 | tf_op jit(solution)/shard_map/ppermute | solution.py:207
  28.9 3.6 %collective-permute-start.6 = (f32[2,2,8]{2,1,0:T(2,128)S(1)}, f32[2,2,8]{2,1,0:T(2,128)S(1)}, u32[]{:S(2)}, u32[]{:S(2)}) collective-permute-start(f32[2,2,8]{2,1,0:T(2,128)S(1)} %get-tuple-element.34), channel_id=1, source_target_pairs={{0,8},{4,12},{8,0},{12,4},{16,24},{20,28},{24,16},{28,20},{1,9},{5... | collective-permute-start | bytes 392 | tf_op jit(solution)/shard_map/ppermute | solution.py:207
  29.4 3.6 %collective-permute-start.5 = (f32[2,2,8]{2,1,0:T(2,128)S(1)}, f32[2,2,8]{2,1,0:T(2,128)S(1)}, u32[]{:S(2)}, u32[]{:S(2)}) collective-permute-start(f32[2,2,8]{2,1,0:T(2,128)S(1)} %get-tuple-element.35), channel_id=1, source_target_pairs={{0,4},{4,0},{8,12},{12,8},{16,20},{20,16},{24,28},{28,24},{1,5},{5... | collective-permute-start | bytes 392 | tf_op jit(solution)/shard_map/ppermute | solution.py:207

commit v16 on v11

--- a/solution.py
+++ b/solution.py
@@ -68,17 +68,24 @@
     slab, yz = lax.axis_index("slab"), lax.axis_index("yz")
     xlo, xhi = low_high(x_inner_ref[...], x_outer_ref[...], slab % 2 == 1)
     ylo, yhi = low_high(y_inner_ref[...], y_outer_ref[...], yz % 2 == 1)
+    y_far = {depth_y: depth_y + 1, ring_y - 1: ring_y - 2}
     ring[0:3, 0:depth_x, 0:depth_y] = e_ref[...]
     ring[3:6, 0:depth_x, 0:depth_y] = h_ref[...]
     ring[6:9, 0:depth_x, 0:depth_y] = perm_ref[...]
     ring[9:10, 0:depth_x, 0:depth_y] = cond_ref[...]
     ring[:, depth_x : depth_x + HALO, 0:depth_y] = xhi
     ring[:, ring_x - HALO : ring_x, 0:depth_y] = xlo
-    ring[:, :, depth_y : depth_y + HALO] = yhi
-    ring[:, :, depth_y + HALO : ring_y - HALO] = jnp.zeros(
-        (ring.shape[0], ring_x, ring_y - depth_y - 2 * HALO, LANES), jnp.float32
-    )
-    ring[:, :, ring_y - HALO : ring_y] = ylo
+    ring[:, :, depth_y:ring_y] = jnp.zeros((ring.shape[0], ring_x, ring_y - depth_y, LANES), jnp.float32)
+    for piece, first, near in ((yhi, depth_y, depth_y), (ylo, ring_y - HALO, ring_y - 1)):
+        for c in range(6):
+            for r in range(HALO):
+                for x in range(ring_x):
+                    ring[c, x, first + r : first + r + 1, :] = piece[2 * c + r, x : x + 1, :]
+        for c in range(4):
+            for x in range(ring_x):
+                ring[6 + c, x, near : near + 1, :] = piece[12 + c, x : x + 1, :]
+        for x in range(ring_x):
+            ring[6:9, x, y_far[near] : y_far[near] + 1, :] = jnp.ones((3, 1, LANES), jnp.float32)
 
     shape = (ring_x, ring_y, LANES)
     xi = lax.broadcasted_iota(jnp.int32, shape, 0)
@@ -208,11 +215,14 @@
         "slab",
     )
     xlo, xhi = low_high(x_inner, x_outer, lax.axis_index("slab") % 2 == 1)
-    def rows(start):
-        center = jnp.concatenate([p[:, :, start : start + HALO] for p in parts], 0)
-        return jnp.concatenate([center, xhi[:, :, start : start + HALO], xlo[:, :, start : start + HALO]], 1)
-
-    y_inner, y_outer = swap_halos(rows(0), rows(depth_y - HALO), "yz")
+    def rows(start, near):
+        stack = jnp.concatenate(parts, 0)
+        stack = jnp.concatenate([stack, xhi, xlo], 1)
+        fields = [stack[c, :, start + r] for c in range(6) for r in range(HALO)]
+        material = [stack[c, :, start + near] for c in range(6, 10)]
+        return jnp.stack(fields + material)
+
+    y_inner, y_outer = swap_halos(rows(0, 0), rows(depth_y - HALO, HALO - 1), "yz")
     new_e, new_h, products = leapfrog(
         field_e, field_h, permittivity, conductivity[None], x_inner, x_outer, y_inner, y_outer,
         slot_cell[0, 0], jnp.transpose(forward_e[0, 0], (1, 0, 2)), n_x, n_y,

time: 34.1 us -> 35.3 us (1.035)
  local copies, waits for them, and re-layouts: 4.84 us -> 6.18 us
    ppermute x2, waiting for transfers between devices: 3.15 us -> 1.14 us  [swap_halos(): got_outer = lax.ppermute(jnp.where(odd, last, first), axis, outer)]
    ppermute x0 -> x2, local copies, waits for them, and re-layouts: none -> 1.26 us  [the longest x1 0.63 us: swap_halos(): got_inner = lax.ppermute(jnp.where(odd, first, last), axis, inner)]
    ppermute x3, waiting for transfers between devices: 3.39 us -> 4.42 us  [exchange_by_halving(): lax.ppermute(held[:, q], 'slab', [(i, i ^ q) for i in range(count)])]
    ppermute x2, waiting for transfers between devices: 1.93 us -> 2.64 us  [swap_halos(): got_inner = lax.ppermute(jnp.where(odd, first, last), axis, inner)]
    broadcast_in_dim x0 -> x1, local copies, waits for them, and re-layouts: none -> 0.6 us  [shards(): conductivity[None]]
    unnamed x20 -> x18, local copies, waits for them, and re-layouts: 4.15 us -> 3.64 us
  transfers between devices with their start and end apart: 8 -> 8, of which waited for: 6 -> 6; matrix products, arithmetic and copies ran while one was open for 1% -> 6% of each run, Pallas kernels for 0% -> 0%
where the time goes in v16:
time: 35.3 us; the launch traced here: 35 us
  starting transfers between devices  14.8 us (42%)
  waiting for transfers between devices  9.69 us (27%)
  local copies, waits for them, and re-layouts  6.18 us (18%)
  Pallas kernels  2.29 us (6%)
  between operations  1.03 us (3%)
  other arithmetic  0.98 us (3%)
    ppermute x3, waiting for transfers between devices, exchange_by_halving(): lax.ppermute(held[:, q], 'slab', [(i, i ^ q) for i in range(count)])  4.42 us
    ppermute x2, starting transfers between devices, swap_halos(): got_inner = lax.ppermute(jnp.where(odd, first, last), axis, inner)  4.42 us
    unnamed x18, local copies, waits for them, and re-layouts  3.64 us
    ppermute x1, starting transfers between devices, exchange_by_halving(): got = lax.ppermute(send, 'slab', pairs)  3.62 us
    ppermute x3, starting transfers between devices, exchange_by_halving(): lax.ppermute(held[:, q], 'slab', [(i, i ^ q) for i in range(count)])  3.55 us
    ppermute x2, starting transfers between devices, swap_halos(): got_outer = lax.ppermute(jnp.where(odd, last, first), axis, outer)  3.2 us
    ppermute x2, waiting for transfers between devices, swap_halos(): got_inner = lax.ppermute(jnp.where(odd, first, last), axis, inner)  2.64 us
    pallas_call x1, Pallas kernels, leapfrog(): pl.pallas_call(kernel, out_shape=(jax.ShapeDtypeStruct(field_e.shape, jnp...  2.29 us
  transfers between devices with their start and end apart: 8, of which 6 were waited for; matrix products, arithmetic and copies ran while one was open for 6% of the time, Pallas kernels for 0%

profile of v16, /device:TPU:2, one launch (start us, length us, event | category | flops | bytes accessed | tf_op | source)
XLA Modules:
  0.0 35.0 jit_solution(7204276777740928970)
XLA Ops:
  0.7 0.8 %copy.26 = f32[3,4,8,128]{3,1,2,0:T(4,128)S(1)} copy(f32[3,4,8,128]{3,2,1,0:T(8,128)} %e_ref.1) | data formatting | bytes 98304 | tf_op args[0]
  1.5 0.7 %copy-done.6 = f32[4,8,128]{2,1,0:T(8,128)S(1)} copy-done((f32[4,8,128]{2,1,0:T(8,128)S(1)}, f32[4,8,128]{2,1,0:T(8,128)}, u32[]{:S(2)}) %copy-start.6) | copy-done | bytes 16408
  2.2 0.8 %copy-done.1 = f32[3,4,8,128]{3,2,1,0:T(8,128)S(1)} copy-done((f32[3,4,8,128]{3,2,1,0:T(8,128)S(1)}, f32[3,4,8,128]{3,2,1,0:T(8,128)}, u32[]{:S(2)}) %copy-start.1) | copy-done | bytes 49176
  3.1 0.1 broadcast_select_fusion.2
  3.2 0.0 copy-start.4
  3.2 0.7 %collective-permute-start.1 = (f32[10,2,8,128]{3,1,2,0:T(2,128)S(1)}, f32[10,2,8,128]{3,1,2,0:T(2,128)S(1)}, u32[]{:S(2)}, u32[]{:S(2)}) collective-permute-start(f32[10,2,8,128]{3,1,2,0:T(2,128)S(1)} %get-tuple-element.43), channel_id=1, source_target_pairs={{4,8},{8,4},{12,16},{16,12},{20,24},{24,20},{5,9},{9,5},{13,17},{1... | collective-permute-start | bytes 245768 | tf_op jit(solution)/shard_map/ppermute | solution.py:54
  3.9 4.3 %collective-permute-start = (f32[10,2,8,128]{3,1,2,0:T(2,128)S(1)}, f32[10,2,8,128]{3,1,2,0:T(2,128)S(1)}, u32[]{:S(2)}, u32[]{:S(2)}) collective-permute-start(f32[10,2,8,128]{3,1,2,0:T(2,128)S(1)} %get-tuple-element.44), channel_id=1, source_target_pairs={{0,4},{4,0},{8,12},{12,8},{16,20},{20,16},{24,28},{28,24},{1,5},{5... | collective-permute-start | bytes 245768 | tf_op jit(solution)/shard_map/ppermute | solution.py:53
  8.3 2.6 %collective-permute-done = f32[10,2,8,128]{3,1,2,0:T(2,128)S(1)} collective-permute-done((f32[10,2,8,128]{3,1,2,0:T(2,128)S(1)}, f32[10,2,8,128]{3,1,2,0:T(2,128)S(1)}, u32[]{:S(2)}, u32[]{:S(2)}) %collective-permute-start) | collective-permute-done | bytes 81952 | tf_op jit(solution)/shard_map/ppermute | solution.py:53
  11.3 0.1 collective-permute-start.2
  11.4 2.5 %collective-permute-start.3 = (f32[16,8,128]{2,1,0:T(8,128)S(1)}, f32[16,8,128]{2,1,0:T(8,128)S(1)}, u32[]{:S(2)}, u32[]{:S(2)}) collective-permute-start(f32[16,8,128]{2,1,0:T(8,128)S(1)} %get-tuple-element.45), channel_id=1, source_target_pairs={{1,2},{2,1},{5,6},{6,5},{9,10},{10,9},{13,14},{14,13},{17,18},{18,... | collective-permute-start | bytes 196616 | tf_op jit(solution)/shard_map/ppermute | solution.py:54
  14.0 0.6 %copy.35.cond_ref = f32[1,4,8,128]{3,2,1,0:T(8,128)} copy(f32[1,4,8,128]{3,1,2,0:T(4,128)S(1)} %bitcast.235) | data formatting | bytes 32768 | tf_op jit(solution)/shard_map/broadcast_in_dim | solution.py:227
  14.6 0.6 %copy.36.x_inner_ref = f32[10,2,8,128]{3,2,1,0:T(8,128)} copy(f32[10,2,8,128]{3,1,2,0:T(2,128)S(1)} %collective-permute-done) | data formatting | bytes 163840 | tf_op jit(solution)/shard_map/ppermute | solution.py:53
  15.2 0.6 %copy.37.x_outer_ref = f32[10,2,8,128]{3,2,1,0:T(8,128)} copy(f32[10,2,8,128]{3,1,2,0:T(2,128)S(1)} %collective-permute-done.1) | data formatting | bytes 163840 | tf_op jit(solution)/shard_map/ppermute | solution.py:54
  15.8 1.1 %collective-permute-done.3.y_outer_ref = f32[16,8,128]{2,1,0:T(8,128)S(1)} collective-permute-done((f32[16,8,128]{2,1,0:T(8,128)S(1)}, f32[16,8,128]{2,1,0:T(8,128)S(1)}, u32[]{:S(2)}, u32[]{:S(2)}) %collective-permute-start.3) | collective-permute-done | bytes 65568 | tf_op jit(solution)/shard_map/ppermute | solution.py:54
  17.0 0.6 %copy-done.3 = f32[16,8,128]{2,1,0:T(8,128)} copy-done((f32[16,8,128]{2,1,0:T(8,128)}, f32[16,8,128]{2,1,0:T(8,128)S(1)}, u32[]{:S(2)}) %copy-start.3) | copy-done | bytes 65560
  17.6 2.3 %shard_map.94 = (f32[3,4,8,128]{3,2,1,0:T(8,128)}, f32[3,4,8,128]{3,2,1,0:T(8,128)}, f32[2,64]{1,0:T(2,128)}) custom-call(f32[3,4,8,128]{3,2,1,0:T(8,128)} %e_ref.1, f32[3,4,8,128]{3,2,1,0:T(8,128)} %h_ref.1, f32[3,4,8,128]{3,2,1,0:T(8,128)} %perm_ref.1, f32[1,4,8,128]{3,2,1,0:T(8,128)} %copy.35.cond_ref, f32[10,2,8,128]{3,2,1,0:T(8,128)} %copy.36.x_inner_ref, ...), custom_call_target="tpu_custom_call" | custom-call | tf_op jit(solution)/shard_map/pallas_call | solution.py:159
  19.9 0.7 %copy-done.5 = f32[2,64]{1,0:T(2,128)S(1)} copy-done((f32[2,64]{1,0:T(2,128)S(1)}, f32[2,64]{1,0:T(2,128)}, u32[]{:S(2)}) %copy-start.5) | copy-done | bytes 536
  20.6 0.1 reshape_reshape.8
  20.6 0.1 reshape.187
  20.7 0.1 reshape.190
  20.8 0.1 reshape.194
  21.0 3.6 %collective-permute-start.4 = (f32[2,4,1,8]{3,1,0,2:T(4,128)S(1)}, f32[2,4,1,8]{3,1,0,2:T(4,128)S(1)}, u32[]{:S(2)}, u32[]{:S(2)}) collective-permute-start(f32[2,4,1,8]{3,1,0,2:T(4,128)S(1)} %get-tuple-element.60), channel_id=1, source_target_pairs={{0,16},{4,20},{8,24},{12,28},{16,0},{20,4},{24,8},{28,12},{1,17},{... | collective-permute-start | bytes 776 | tf_op jit(solution)/shard_map/ppermute | solution.py:192
  24.6 0.1 eq.46
  24.7 1.5 %collective-permute-done.4 = f32[2,4,1,8]{3,1,0,2:T(4,128)S(1)} collective-permute-done((f32[2,4,1,8]{3,1,0,2:T(4,128)S(1)}, f32[2,4,1,8]{3,1,0,2:T(4,128)S(1)}, u32[]{:S(2)}, u32[]{:S(2)}) %collective-permute-start.4) | collective-permute-done | bytes 288 | tf_op jit(solution)/shard_map/ppermute | solution.py:192
  26.2 1.9 %collective-permute-start.5 = (f32[2,2,8]{2,1,0:T(2,128)S(1)}, f32[2,2,8]{2,1,0:T(2,128)S(1)}, u32[]{:S(2)}, u32[]{:S(2)}) collective-permute-start(f32[2,2,8]{2,1,0:T(2,128)S(1)} %get-tuple-element.58), channel_id=1, source_target_pairs={{0,4},{4,0},{8,12},{12,8},{16,20},{20,16},{24,28},{28,24},{1,5},{5... | collective-permute-start | bytes 392 | tf_op jit(solution)/shard_map/ppermute | solution.py:198
  28.2 1.6 %collective-permute-start.6 = (f32[2,2,8]{2,1,0:T(2,128)S(1)}, f32[2,2,8]{2,1,0:T(2,128)S(1)}, u32[]{:S(2)}, u32[]{:S(2)}) collective-permute-start(f32[2,2,8]{2,1,0:T(2,128)S(1)} %get-tuple-element.57), channel_id=1, source_target_pairs={{0,8},{4,12},{8,0},{12,4},{16,24},{20,28},{24,16},{28,20},{1,9},{5... | collective-permute-start | bytes 392 | tf_op jit(solution)/shard_map/ppermute | solution.py:198
  29.7 0.1 collective-permute-start.7
  29.8 0.1 collective-permute-done.5
  29.9 1.8 %collective-permute-done.6 = f32[2,2,8]{2,1,0:T(2,128)S(1)} collective-permute-done((f32[2,2,8]{2,1,0:T(2,128)S(1)}, f32[2,2,8]{2,1,0:T(2,128)S(1)}, u32[]{:S(2)}, u32[]{:S(2)}) %collective-permute-start.6) | collective-permute-done | bytes 160 | tf_op jit(solution)/shard_map/ppermute | solution.py:198
  31.7 2.5 %collective-permute-done.7 = f32[2,2,8]{2,1,0:T(2,128)S(1)} collective-permute-done((f32[2,2,8]{2,1,0:T(2,128)S(1)}, f32[2,2,8]{2,1,0:T(2,128)S(1)}, u32[]{:S(2)}, u32[]{:S(2)}) %collective-permute-start.7) | collective-permute-done | bytes 160 | tf_op jit(solution)/shard_map/ppermute | solution.py:198
  34.2 0.1 broadcast_in_dim.27
  34.3 0.6 %select_reduce_fusion = f32[128]{0:T(128)} fusion(f32[128]{0:T(128)S(1)} %broadcast_in_dim.27, s32[128]{0:T(128)S(1)} %eq.46), kind=kLoop, calls=%fused_computation.38 | loop fusion | flops 49024 | bytes 1536 | tf_op jit(solution)/shard_map/reduce_sum | solution.py:238
  (54 shorter events, 0.5 us)
Async XLA Ops:
  0.6 0.8 %copy-start = (f32[3,4,8,128]{3,2,1,0:T(8,128)S(1)}, f32[3,4,8,128]{3,2,1,0:T(8,128)}, u32[]{:S(2)}) copy-start(f32[3,4,8,128]{3,2,1,0:T(8,128)} %h_ref.1) | copy-start | bytes 147460
  1.5 0.7 %copy-start.6 = (f32[4,8,128]{2,1,0:T(8,128)S(1)}, f32[4,8,128]{2,1,0:T(8,128)}, u32[]{:S(2)}) copy-start(f32[4,8,128]{2,1,0:T(8,128)} %param.10) | copy-start | bytes 49156
  2.2 0.8 %copy-start.1 = (f32[3,4,8,128]{3,2,1,0:T(8,128)S(1)}, f32[3,4,8,128]{3,2,1,0:T(8,128)}, u32[]{:S(2)}) copy-start(f32[3,4,8,128]{3,2,1,0:T(8,128)} %perm_ref.1) | copy-start | bytes 147460
  3.2 5.0 %copy-start.4 = (s32[1,1,8,8]{3,2,1,0:T(8,128)S(1)}, s32[1,1,8,8]{3,2,1,0:T(8,128)}, u32[]{:S(2)}) copy-start(s32[1,1,8,8]{3,2,1,0:T(8,128)} %param.13) | copy-start | bytes 772
  3.2 5.1 %collective-permute-start.1 = (f32[10,2,8,128]{3,1,2,0:T(2,128)S(1)}, f32[10,2,8,128]{3,1,2,0:T(2,128)S(1)}, u32[]{:S(2)}, u32[]{:S(2)}) collective-permute-start(f32[10,2,8,128]{3,1,2,0:T(2,128)S(1)} %get-tuple-element.43), channel_id=1, source_target_pairs={{4,8},{8,4},{12,16},{16,12},{20,24},{24,20},{5,9},{9,5},{13,17},{1... | collective-permute-start | bytes 245768 | tf_op jit(solution)/shard_map/ppermute | solution.py:54
  3.9 7.1 %collective-permute-start = (f32[10,2,8,128]{3,1,2,0:T(2,128)S(1)}, f32[10,2,8,128]{3,1,2,0:T(2,128)S(1)}, u32[]{:S(2)}, u32[]{:S(2)}) collective-permute-start(f32[10,2,8,128]{3,1,2,0:T(2,128)S(1)} %get-tuple-element.44), channel_id=1, source_target_pairs={{0,4},{4,0},{8,12},{12,8},{16,20},{20,16},{24,28},{28,24},{1,5},{5... | collective-permute-start | bytes 245768 | tf_op jit(solution)/shard_map/ppermute | solution.py:53
  11.3 4.5 %collective-permute-start.2 = (f32[16,8,128]{2,1,0:T(8,128)S(1)}, f32[16,8,128]{2,1,0:T(8,128)S(1)}, u32[]{:S(2)}, u32[]{:S(2)}) collective-permute-start(f32[16,8,128]{2,1,0:T(8,128)S(1)} %get-tuple-element.46), channel_id=1, source_target_pairs={{0,1},{1,0},{2,3},{3,2},{4,5},{5,4},{6,7},{7,6},{8,9},{9,8},{10,11... | collective-permute-start | bytes 196616 | tf_op jit(solution)/shard_map/ppermute | solution.py:53
  11.4 5.6 %collective-permute-start.3 = (f32[16,8,128]{2,1,0:T(8,128)S(1)}, f32[16,8,128]{2,1,0:T(8,128)S(1)}, u32[]{:S(2)}, u32[]{:S(2)}) collective-permute-start(f32[16,8,128]{2,1,0:T(8,128)S(1)} %get-tuple-element.45), channel_id=1, source_target_pairs={{1,2},{2,1},{5,6},{6,5},{9,10},{10,9},{13,14},{14,13},{17,18},{18,... | collective-permute-start | bytes 196616 | tf_op jit(solution)/shard_map/ppermute | solution.py:54
  15.8 1.1 %copy-start.2 = (f32[16,8,128]{2,1,0:T(8,128)}, f32[16,8,128]{2,1,0:T(8,128)S(1)}, u32[]{:S(2)}) copy-start(f32[16,8,128]{2,1,0:T(8,128)S(1)} %collective-permute-done.2.y_inner_ref) | copy-start | bytes 196612
  17.0 0.6 %copy-start.3 = (f32[16,8,128]{2,1,0:T(8,128)}, f32[16,8,128]{2,1,0:T(8,128)S(1)}, u32[]{:S(2)}) copy-start(f32[16,8,128]{2,1,0:T(8,128)S(1)} %collective-permute-done.3.y_outer_ref) | copy-start | bytes 196612
  19.9 0.7 %copy-start.5 = (f32[2,64]{1,0:T(2,128)S(1)}, f32[2,64]{1,0:T(2,128)}, u32[]{:S(2)}) copy-start(f32[2,64]{1,0:T(2,128)} %get-tuple-element.8) | copy-start | bytes 1540
  21.0 5.2 %collective-permute-start.4 = (f32[2,4,1,8]{3,1,0,2:T(4,128)S(1)}, f32[2,4,1,8]{3,1,0,2:T(4,128)S(1)}, u32[]{:S(2)}, u32[]{:S(2)}) collective-permute-start(f32[2,4,1,8]{3,1,0,2:T(4,128)S(1)} %get-tuple-element.60), channel_id=1, source_target_pairs={{0,16},{4,20},{8,24},{12,28},{16,0},{20,4},{24,8},{28,12},{1,17},{... | collective-permute-start | bytes 776 | tf_op jit(solution)/shard_map/ppermute | solution.py:192
  26.2 3.7 %collective-permute-start.5 = (f32[2,2,8]{2,1,0:T(2,128)S(1)}, f32[2,2,8]{2,1,0:T(2,128)S(1)}, u32[]{:S(2)}, u32[]{:S(2)}) collective-permute-start(f32[2,2,8]{2,1,0:T(2,128)S(1)} %get-tuple-element.58), channel_id=1, source_target_pairs={{0,4},{4,0},{8,12},{12,8},{16,20},{20,16},{24,28},{28,24},{1,5},{5... | collective-permute-start | bytes 392 | tf_op jit(solution)/shard_map/ppermute | solution.py:198
  28.2 3.6 %collective-permute-start.6 = (f32[2,2,8]{2,1,0:T(2,128)S(1)}, f32[2,2,8]{2,1,0:T(2,128)S(1)}, u32[]{:S(2)}, u32[]{:S(2)}) collective-permute-start(f32[2,2,8]{2,1,0:T(2,128)S(1)} %get-tuple-element.57), channel_id=1, source_target_pairs={{0,8},{4,12},{8,0},{12,4},{16,24},{20,28},{24,16},{28,20},{1,9},{5... | collective-permute-start | bytes 392 | tf_op jit(solution)/shard_map/ppermute | solution.py:198
  29.7 4.5 %collective-permute-start.7 = (f32[2,2,8]{2,1,0:T(2,128)S(1)}, f32[2,2,8]{2,1,0:T(2,128)S(1)}, u32[]{:S(2)}, u32[]{:S(2)}) collective-permute-start(f32[2,2,8]{2,1,0:T(2,128)S(1)} %get-tuple-element.56), channel_id=1, source_target_pairs={{0,12},{4,8},{8,4},{12,0},{16,28},{20,24},{24,20},{28,16},{1,13},{... | collective-permute-start | bytes 392 | tf_op jit(solution)/shard_map/ppermute | solution.py:198

commit v17 on v11

--- a/solution.py
+++ b/solution.py
@@ -61,13 +61,15 @@
 
 def leapfrog_kernel(
     dims, e_ref, h_ref, perm_ref, cond_ref, x_inner_ref, x_outer_ref, y_inner_ref, y_outer_ref,
-    cell_ref, fwd_ref, e_out, h_out, prod_out, ring,
+    y_inner2_ref, y_outer2_ref, cell_ref, fwd_ref, e_out, h_out, prod_out, ring,
 ):
     depth_x, depth_y, n_x, n_y = dims
     ring_x, ring_y = ring.shape[1], ring.shape[2]
     slab, yz = lax.axis_index("slab"), lax.axis_index("yz")
     xlo, xhi = low_high(x_inner_ref[...], x_outer_ref[...], slab % 2 == 1)
-    ylo, yhi = low_high(y_inner_ref[...], y_outer_ref[...], yz % 2 == 1)
+    y_inner = jnp.concatenate([y_inner_ref[...], y_inner2_ref[...]], 0)
+    y_outer = jnp.concatenate([y_outer_ref[...], y_outer2_ref[...]], 0)
+    ylo, yhi = low_high(y_inner, y_outer, yz % 2 == 1)
     ring[0:3, 0:depth_x, 0:depth_y] = e_ref[...]
     ring[3:6, 0:depth_x, 0:depth_y] = h_ref[...]
     ring[6:9, 0:depth_x, 0:depth_y] = perm_ref[...]
@@ -143,7 +145,7 @@
         h_out[c] = field_h[c][0:depth_x, 0:depth_y]
 
 
-def leapfrog(field_e, field_h, permittivity, conductivity, xlo, xhi, ylo, yhi, cells, fwd, n_x, n_y):
+def leapfrog(field_e, field_h, permittivity, conductivity, xlo, xhi, ylo, yhi, ylo2, yhi2, cells, fwd, n_x, n_y):
     _, depth_x, depth_y, _ = field_e.shape
     ring_x = depth_x + 2 * HALO
     ring_y = -(-(depth_y + 2 * HALO) // 8) * 8
@@ -156,10 +158,10 @@
             jax.ShapeDtypeStruct(field_h.shape, jnp.float32),
             jax.ShapeDtypeStruct((STEPS, cells.size), jnp.float32),
         ),
-        in_specs=[vmem] * 10,
+        in_specs=[vmem] * 12,
         out_specs=(vmem, vmem, vmem),
         scratch_shapes=[pltpu.VMEM((10, ring_x, ring_y, LANES), jnp.float32)],
-    )(field_e, field_h, permittivity, conductivity, xlo, xhi, ylo, yhi, cells, fwd)
+    )(field_e, field_h, permittivity, conductivity, xlo, xhi, ylo, yhi, ylo2, yhi2, cells, fwd)
 
 
 def xor_rows(array, me, count, axis):
@@ -212,9 +214,12 @@
         center = jnp.concatenate([p[:, :, start : start + HALO] for p in parts], 0)
         return jnp.concatenate([center, xhi[:, :, start : start + HALO], xlo[:, :, start : start + HALO]], 1)
 
-    y_inner, y_outer = swap_halos(rows(0), rows(depth_y - HALO), "yz")
+    first, last = rows(0), rows(depth_y - HALO)
+    split = first.shape[0] // 2
+    y_inner, y_outer = swap_halos(first[:split], last[:split], "yz")
+    y_inner2, y_outer2 = swap_halos(first[split:], last[split:], "yz")
     new_e, new_h, products = leapfrog(
-        field_e, field_h, permittivity, conductivity[None], x_inner, x_outer, y_inner, y_outer,
+        field_e, field_h, permittivity, conductivity[None], x_inner, x_outer, y_inner, y_outer, y_inner2, y_outer2,
         slot_cell[0, 0], jnp.transpose(forward_e[0, 0], (1, 0, 2)), n_x, n_y,
     )
     products = products.reshape(STEPS, sources, capacity)

time: 34.1 us -> 36.3 us (1.065)
  the two profiles are of different devices: /device:TPU:2 before, /device:TPU:0 now
where the time goes in v17:
time: 36.3 us; the launch traced here: 36 us
  starting transfers between devices  19.2 us (53%)
  waiting for transfers between devices  7.91 us (22%)
  local copies, waits for them, and re-layouts  4.79 us (13%)
  Pallas kernels  2.27 us (6%)
  between operations  0.94 us (3%)
  other arithmetic  0.85 us (2%)
    ppermute x3, starting transfers between devices, swap_halos(): got_inner = lax.ppermute(jnp.where(odd, first, last), axis, inner)  10 us
    unnamed x24, local copies, waits for them, and re-layouts  4.09 us
    ppermute x1, starting transfers between devices, exchange_by_halving(): got = lax.ppermute(send, 'slab', pairs)  3.62 us
    ppermute x3, starting transfers between devices, exchange_by_halving(): lax.ppermute(held[:, q], 'slab', [(i, i ^ q) for i in range(count)])  3.57 us
    ppermute x3, waiting for transfers between devices, exchange_by_halving(): lax.ppermute(held[:, q], 'slab', [(i, i ^ q) for i in range(count)])  3.39 us
    ppermute x3, waiting for transfers between devices, swap_halos(): got_inner = lax.ppermute(jnp.where(odd, first, last), axis, inner)  3.03 us
    pallas_call x1, Pallas kernels, leapfrog(): pl.pallas_call(kernel, out_shape=(jax.ShapeDtypeStruct(field_e.shape, jnp...  2.27 us
    ppermute x3, starting transfers between devices, swap_halos(): got_outer = lax.ppermute(jnp.where(odd, last, first), axis, outer)  1.99 us
  transfers between devices with their start and end apart: 10, of which 7 were waited for; matrix products, arithmetic and copies ran while one was open for 0% of the time, Pallas kernels for 0%

profile of v17, /device:TPU:0, one launch (start us, length us, event | category | flops | bytes accessed | tf_op | source)
XLA Modules:
  0.0 36.0 jit_solution(6213379167620937579)
XLA Ops:
  0.7 0.7 %copy-done.5 = f32[4,8,128]{2,1,0:T(8,128)S(1)} copy-done((f32[4,8,128]{2,1,0:T(8,128)S(1)}, f32[4,8,128]{2,1,0:T(8,128)}, u32[]{:S(2)}) %copy-start.5) | copy-done | bytes 16408
  1.4 0.1 copy-done.2
  1.5 0.8 %copy-done.3 = f32[3,4,8,128]{3,2,1,0:T(8,128)S(1)} copy-done((f32[3,4,8,128]{3,2,1,0:T(8,128)S(1)}, f32[3,4,8,128]{3,2,1,0:T(8,128)}, u32[]{:S(2)}) %copy-start.3) | copy-done | bytes 49176
  2.3 0.7 %collective-permute-start.1 = (f32[10,2,8,128]{3,2,1,0:T(8,128)S(1)}, f32[10,2,8,128]{3,2,1,0:T(8,128)S(1)}, u32[]{:S(2)}, u32[]{:S(2)}) collective-permute-start(f32[10,2,8,128]{3,2,1,0:T(8,128)S(1)} %get-tuple-element.15), channel_id=1, source_target_pairs={{4,8},{8,4},{12,16},{16,12},{20,24},{24,20},{5,9},{9,5},{13,17},{1... | collective-permute-start | bytes 245768 | tf_op jit(solution)/shard_map/ppermute | solution.py:54
  3.0 5.8 %collective-permute-start = (f32[10,2,8,128]{3,2,1,0:T(8,128)S(1)}, f32[10,2,8,128]{3,2,1,0:T(8,128)S(1)}, u32[]{:S(2)}, u32[]{:S(2)}) collective-permute-start(f32[10,2,8,128]{3,2,1,0:T(8,128)S(1)} %get-tuple-element.16), channel_id=1, source_target_pairs={{0,4},{4,0},{8,12},{12,8},{16,20},{20,16},{24,28},{28,24},{1,5},{5... | collective-permute-start | bytes 245768 | tf_op jit(solution)/shard_map/ppermute | solution.py:53
  8.8 0.7 %copy-done.6 = s32[1,1,8,8]{3,2,1,0:T(8,128)S(1)} copy-done((s32[1,1,8,8]{3,2,1,0:T(8,128)S(1)}, s32[1,1,8,8]{3,2,1,0:T(8,128)}, u32[]{:S(2)}) %copy-start.6) | copy-done | bytes 280
  9.6 1.9 %collective-permute-done.x_inner_ref = f32[10,2,8,128]{3,2,1,0:T(8,128)S(1)} collective-permute-done((f32[10,2,8,128]{3,2,1,0:T(8,128)S(1)}, f32[10,2,8,128]{3,2,1,0:T(8,128)S(1)}, u32[]{:S(2)}, u32[]{:S(2)}) %collective-permute-start) | collective-permute-done | bytes 81952 | tf_op jit(solution)/shard_map/ppermute | solution.py:53
  11.5 0.6 %copy-done.1 = f32[10,2,8,128]{3,2,1,0:T(8,128)} copy-done((f32[10,2,8,128]{3,2,1,0:T(8,128)}, f32[10,2,8,128]{3,2,1,0:T(8,128)S(1)}, u32[]{:S(2)}) %copy-start.1) | copy-done | bytes 81944
  12.3 0.7 %collective-permute-start.5 = (f32[5,8,2,128]{3,2,1,0:T(2,128)S(1)}, f32[5,8,2,128]{3,2,1,0:T(2,128)S(1)}, u32[]{:S(2)}, u32[]{:S(2)}) collective-permute-start(f32[5,8,2,128]{3,2,1,0:T(2,128)S(1)} %get-tuple-element.9), channel_id=1, source_target_pairs={{1,2},{2,1},{5,6},{6,5},{9,10},{10,9},{13,14},{14,13},{17,18},{18,... | collective-permute-start | bytes 122888 | tf_op jit(solution)/shard_map/ppermute | solution.py:54
  13.0 0.7 %collective-permute-start.3 = (f32[5,8,2,128]{3,2,1,0:T(2,128)S(1)}, f32[5,8,2,128]{3,2,1,0:T(2,128)S(1)}, u32[]{:S(2)}, u32[]{:S(2)}) collective-permute-start(f32[5,8,2,128]{3,2,1,0:T(2,128)S(1)} %get-tuple-element.10), channel_id=1, source_target_pairs={{1,2},{2,1},{5,6},{6,5},{9,10},{10,9},{13,14},{14,13},{17,18},{18,... | collective-permute-start | bytes 122888 | tf_op jit(solution)/shard_map/ppermute | solution.py:54
  13.7 4.2 %collective-permute-start.4 = (f32[5,8,2,128]{3,2,1,0:T(2,128)S(1)}, f32[5,8,2,128]{3,2,1,0:T(2,128)S(1)}, u32[]{:S(2)}, u32[]{:S(2)}) collective-permute-start(f32[5,8,2,128]{3,2,1,0:T(2,128)S(1)} %get-tuple-element.11), channel_id=1, source_target_pairs={{0,1},{1,0},{2,3},{3,2},{4,5},{5,4},{6,7},{7,6},{8,9},{9,8},{10,11... | collective-permute-start | bytes 122888 | tf_op jit(solution)/shard_map/ppermute | solution.py:53
  17.9 0.1 collective-permute-start.2
  18.0 0.7 %collective-permute-done.4.y_inner2_ref = f32[5,8,2,128]{3,2,1,0:T(2,128)S(1)} collective-permute-done((f32[5,8,2,128]{3,2,1,0:T(2,128)S(1)}, f32[5,8,2,128]{3,2,1,0:T(2,128)S(1)}, u32[]{:S(2)}, u32[]{:S(2)}) %collective-permute-start.4) | collective-permute-done | bytes 40992 | tf_op jit(solution)/shard_map/ppermute | solution.py:53
  18.7 0.3 collective-permute-done.2.y_inner_ref
  19.1 0.3 copy-done.9
  19.4 0.3 copy-done.10
  19.7 2.3 %shard_map.94 = (f32[3,4,8,128]{3,2,1,0:T(8,128)}, f32[3,4,8,128]{3,2,1,0:T(8,128)}, f32[2,64]{1,0:T(2,128)}) custom-call(f32[3,4,8,128]{3,2,1,0:T(8,128)} %e_ref.1, f32[3,4,8,128]{3,2,1,0:T(8,128)} %h_ref.1, f32[3,4,8,128]{3,2,1,0:T(8,128)} %perm_ref.1, f32[1,4,8,128]{3,2,1,0:T(8,128)} %bitcast.55, f32[10,2,8,128]{3,2,1,0:T(8,128)} %copy-done.1, ...), custom_call_target="tpu_custom_call" | custom-call | tf_op jit(solution)/shard_map/pallas_call | solution.py:154
  22.0 0.6 %copy-done.11 = f32[2,64]{1,0:T(2,128)S(1)} copy-done((f32[2,64]{1,0:T(2,128)S(1)}, f32[2,64]{1,0:T(2,128)}, u32[]{:S(2)}) %copy-start.11) | copy-done | bytes 536
  22.7 0.1 reshape.190
  22.7 0.1 reshape.187
  22.8 0.1 reshape_reshape.8
  23.1 3.6 %collective-permute-start.6 = (f32[2,4,1,8]{3,1,0,2:T(4,128)S(1)}, f32[2,4,1,8]{3,1,0,2:T(4,128)S(1)}, u32[]{:S(2)}, u32[]{:S(2)}) collective-permute-start(f32[2,4,1,8]{3,1,0,2:T(4,128)S(1)} %get-tuple-element.42), channel_id=1, source_target_pairs={{0,16},{4,20},{8,24},{12,28},{16,0},{20,4},{24,8},{28,12},{1,17},{... | collective-permute-start | bytes 776 | tf_op jit(solution)/shard_map/ppermute | solution.py:187
  26.7 0.1 eq.48
  26.8 1.5 %collective-permute-done.6 = f32[2,4,1,8]{3,1,0,2:T(4,128)S(1)} collective-permute-done((f32[2,4,1,8]{3,1,0,2:T(4,128)S(1)}, f32[2,4,1,8]{3,1,0,2:T(4,128)S(1)}, u32[]{:S(2)}, u32[]{:S(2)}) %collective-permute-start.6) | collective-permute-done | bytes 288 | tf_op jit(solution)/shard_map/ppermute | solution.py:187
  28.3 2.9 %collective-permute-start.9 = (f32[2,2,8]{2,1,0:T(2,128)S(1)}, f32[2,2,8]{2,1,0:T(2,128)S(1)}, u32[]{:S(2)}, u32[]{:S(2)}) collective-permute-start(f32[2,2,8]{2,1,0:T(2,128)S(1)} %get-tuple-element.38), channel_id=1, source_target_pairs={{0,12},{4,8},{8,4},{12,0},{16,28},{20,24},{24,20},{28,16},{1,13},{... | collective-permute-start | bytes 392 | tf_op jit(solution)/shard_map/ppermute | solution.py:193
  31.2 0.4 %collective-permute-start.8 = (f32[2,2,8]{2,1,0:T(2,128)S(1)}, f32[2,2,8]{2,1,0:T(2,128)S(1)}, u32[]{:S(2)}, u32[]{:S(2)}) collective-permute-start(f32[2,2,8]{2,1,0:T(2,128)S(1)} %get-tuple-element.39), channel_id=1, source_target_pairs={{0,8},{4,12},{8,0},{12,4},{16,24},{20,28},{24,16},{28,20},{1,9},{5... | collective-permute-start | bytes 392 | tf_op jit(solution)/shard_map/ppermute | solution.py:193
  31.7 0.2 collective-permute-start.7
  31.9 1.0 %collective-permute-done.9 = f32[2,2,8]{2,1,0:T(2,128)S(1)} collective-permute-done((f32[2,2,8]{2,1,0:T(2,128)S(1)}, f32[2,2,8]{2,1,0:T(2,128)S(1)}, u32[]{:S(2)}, u32[]{:S(2)}) %collective-permute-start.9) | collective-permute-done | bytes 160 | tf_op jit(solution)/shard_map/ppermute | solution.py:193
  32.8 2.0 %collective-permute-done.8 = f32[2,2,8]{2,1,0:T(2,128)S(1)} collective-permute-done((f32[2,2,8]{2,1,0:T(2,128)S(1)}, f32[2,2,8]{2,1,0:T(2,128)S(1)}, u32[]{:S(2)}, u32[]{:S(2)}) %collective-permute-start.8) | collective-permute-done | bytes 160 | tf_op jit(solution)/shard_map/ppermute | solution.py:193
  34.8 0.4 %collective-permute-done.7 = f32[2,2,8]{2,1,0:T(2,128)S(1)} collective-permute-done((f32[2,2,8]{2,1,0:T(2,128)S(1)}, f32[2,2,8]{2,1,0:T(2,128)S(1)}, u32[]{:S(2)}, u32[]{:S(2)}) %collective-permute-start.7) | collective-permute-done | bytes 160 | tf_op jit(solution)/shard_map/ppermute | solution.py:193
  35.3 0.1 broadcast_in_dim.27
  35.4 0.6 %select_reduce_fusion = f32[128]{0:T(128)} fusion(f32[128]{0:T(128)S(1)} %broadcast_in_dim.27, s32[128]{0:T(128)S(1)} %eq.48), kind=kLoop, calls=%fused_computation.4 | loop fusion | flops 49024 | bytes 1536 | tf_op jit(solution)/shard_map/reduce_sum | solution.py:233
  (52 shorter events, 0.5 us)
Async XLA Ops:
  0.6 0.7 %copy-start.5 = (f32[4,8,128]{2,1,0:T(8,128)S(1)}, f32[4,8,128]{2,1,0:T(8,128)}, u32[]{:S(2)}) copy-start(f32[4,8,128]{2,1,0:T(8,128)} %param.10) | copy-start | bytes 49156
  0.6 0.8 %copy-start.2 = (f32[3,4,8,128]{3,2,1,0:T(8,128)S(1)}, f32[3,4,8,128]{3,2,1,0:T(8,128)}, u32[]{:S(2)}) copy-start(f32[3,4,8,128]{3,2,1,0:T(8,128)} %perm_ref.1) | copy-start | bytes 147460
  1.4 0.8 %copy-start.3 = (f32[3,4,8,128]{3,2,1,0:T(8,128)S(1)}, f32[3,4,8,128]{3,2,1,0:T(8,128)}, u32[]{:S(2)}) copy-start(f32[3,4,8,128]{3,2,1,0:T(8,128)} %e_ref.1) | copy-start | bytes 147460
  1.4 0.8 %copy-start.4 = (f32[3,4,8,128]{3,2,1,0:T(8,128)S(1)}, f32[3,4,8,128]{3,2,1,0:T(8,128)}, u32[]{:S(2)}) copy-start(f32[3,4,8,128]{3,2,1,0:T(8,128)} %h_ref.1) | copy-start | bytes 147460
  2.3 7.3 %collective-permute-start.1 = (f32[10,2,8,128]{3,2,1,0:T(8,128)S(1)}, f32[10,2,8,128]{3,2,1,0:T(8,128)S(1)}, u32[]{:S(2)}, u32[]{:S(2)}) collective-permute-start(f32[10,2,8,128]{3,2,1,0:T(8,128)S(1)} %get-tuple-element.15), channel_id=1, source_target_pairs={{4,8},{8,4},{12,16},{16,12},{20,24},{24,20},{5,9},{9,5},{13,17},{1... | collective-permute-start | bytes 245768 | tf_op jit(solution)/shard_map/ppermute | solution.py:54
  3.0 8.5 %collective-permute-start = (f32[10,2,8,128]{3,2,1,0:T(8,128)S(1)}, f32[10,2,8,128]{3,2,1,0:T(8,128)S(1)}, u32[]{:S(2)}, u32[]{:S(2)}) collective-permute-start(f32[10,2,8,128]{3,2,1,0:T(8,128)S(1)} %get-tuple-element.16), channel_id=1, source_target_pairs={{0,4},{4,0},{8,12},{12,8},{16,20},{20,16},{24,28},{28,24},{1,5},{5... | collective-permute-start | bytes 245768 | tf_op jit(solution)/shard_map/ppermute | solution.py:53
  8.8 0.7 %copy-start.6 = (s32[1,1,8,8]{3,2,1,0:T(8,128)S(1)}, s32[1,1,8,8]{3,2,1,0:T(8,128)}, u32[]{:S(2)}) copy-start(s32[1,1,8,8]{3,2,1,0:T(8,128)} %param.13) | copy-start | bytes 772
  9.6 2.0 %copy-start = (f32[10,2,8,128]{3,2,1,0:T(8,128)}, f32[10,2,8,128]{3,2,1,0:T(8,128)S(1)}, u32[]{:S(2)}) copy-start(f32[10,2,8,128]{3,2,1,0:T(8,128)S(1)} %collective-permute-done.1.x_outer_ref) | copy-start | bytes 245764
  11.5 0.6 %copy-start.1 = (f32[10,2,8,128]{3,2,1,0:T(8,128)}, f32[10,2,8,128]{3,2,1,0:T(8,128)S(1)}, u32[]{:S(2)}) copy-start(f32[10,2,8,128]{3,2,1,0:T(8,128)S(1)} %collective-permute-done.x_inner_ref) | copy-start | bytes 245764
  12.3 5.6 %collective-permute-start.5 = (f32[5,8,2,128]{3,2,1,0:T(2,128)S(1)}, f32[5,8,2,128]{3,2,1,0:T(2,128)S(1)}, u32[]{:S(2)}, u32[]{:S(2)}) collective-permute-start(f32[5,8,2,128]{3,2,1,0:T(2,128)S(1)} %get-tuple-element.9), channel_id=1, source_target_pairs={{1,2},{2,1},{5,6},{6,5},{9,10},{10,9},{13,14},{14,13},{17,18},{18,... | collective-permute-start | bytes 122888 | tf_op jit(solution)/shard_map/ppermute | solution.py:54
  13.0 4.9 %collective-permute-start.3 = (f32[5,8,2,128]{3,2,1,0:T(2,128)S(1)}, f32[5,8,2,128]{3,2,1,0:T(2,128)S(1)}, u32[]{:S(2)}, u32[]{:S(2)}) collective-permute-start(f32[5,8,2,128]{3,2,1,0:T(2,128)S(1)} %get-tuple-element.10), channel_id=1, source_target_pairs={{1,2},{2,1},{5,6},{6,5},{9,10},{10,9},{13,14},{14,13},{17,18},{18,... | collective-permute-start | bytes 122888 | tf_op jit(solution)/shard_map/ppermute | solution.py:54
  13.7 5.0 %collective-permute-start.4 = (f32[5,8,2,128]{3,2,1,0:T(2,128)S(1)}, f32[5,8,2,128]{3,2,1,0:T(2,128)S(1)}, u32[]{:S(2)}, u32[]{:S(2)}) collective-permute-start(f32[5,8,2,128]{3,2,1,0:T(2,128)S(1)} %get-tuple-element.11), channel_id=1, source_target_pairs={{0,1},{1,0},{2,3},{3,2},{4,5},{5,4},{6,7},{7,6},{8,9},{9,8},{10,11... | collective-permute-start | bytes 122888 | tf_op jit(solution)/shard_map/ppermute | solution.py:53
  17.9 1.2 %collective-permute-start.2 = (f32[5,8,2,128]{3,2,1,0:T(2,128)S(1)}, f32[5,8,2,128]{3,2,1,0:T(2,128)S(1)}, u32[]{:S(2)}, u32[]{:S(2)}) collective-permute-start(f32[5,8,2,128]{3,2,1,0:T(2,128)S(1)} %get-tuple-element.12), channel_id=1, source_target_pairs={{0,1},{1,0},{2,3},{3,2},{4,5},{5,4},{6,7},{7,6},{8,9},{9,8},{10,11... | collective-permute-start | bytes 122888 | tf_op jit(solution)/shard_map/ppermute | solution.py:53
  18.0 1.1 %copy-start.7 = (f32[5,8,2,128]{3,2,1,0:T(2,128)}, f32[5,8,2,128]{3,2,1,0:T(2,128)S(1)}, u32[]{:S(2)}) copy-start(f32[5,8,2,128]{3,2,1,0:T(2,128)S(1)} %collective-permute-done.5.y_outer2_ref) | copy-start | bytes 122884
  18.0 1.1 %copy-start.8 = (f32[5,8,2,128]{3,2,1,0:T(2,128)}, f32[5,8,2,128]{3,2,1,0:T(2,128)S(1)}, u32[]{:S(2)}) copy-start(f32[5,8,2,128]{3,2,1,0:T(2,128)S(1)} %collective-permute-done.3.y_outer_ref) | copy-start | bytes 122884
  18.7 0.6 %copy-start.9 = (f32[5,8,2,128]{3,2,1,0:T(2,128)}, f32[5,8,2,128]{3,2,1,0:T(2,128)S(1)}, u32[]{:S(2)}) copy-start(f32[5,8,2,128]{3,2,1,0:T(2,128)S(1)} %collective-permute-done.4.y_inner2_ref) | copy-start | bytes 122884
  19.1 0.6 %copy-start.10 = (f32[5,8,2,128]{3,2,1,0:T(2,128)}, f32[5,8,2,128]{3,2,1,0:T(2,128)S(1)}, u32[]{:S(2)}) copy-start(f32[5,8,2,128]{3,2,1,0:T(2,128)S(1)} %collective-permute-done.2.y_inner_ref) | copy-start | bytes 122884
  22.0 0.6 %copy-start.11 = (f32[2,64]{1,0:T(2,128)S(1)}, f32[2,64]{1,0:T(2,128)}, u32[]{:S(2)}) copy-start(f32[2,64]{1,0:T(2,128)} %get-tuple-element.8) | copy-start | bytes 1540
  23.1 5.2 %collective-permute-start.6 = (f32[2,4,1,8]{3,1,0,2:T(4,128)S(1)}, f32[2,4,1,8]{3,1,0,2:T(4,128)S(1)}, u32[]{:S(2)}, u32[]{:S(2)}) collective-permute-start(f32[2,4,1,8]{3,1,0,2:T(4,128)S(1)} %get-tuple-element.42), channel_id=1, source_target_pairs={{0,16},{4,20},{8,24},{12,28},{16,0},{20,4},{24,8},{28,12},{1,17},{... | collective-permute-start | bytes 776 | tf_op jit(solution)/shard_map/ppermute | solution.py:187
  28.3 4.5 %collective-permute-start.9 = (f32[2,2,8]{2,1,0:T(2,128)S(1)}, f32[2,2,8]{2,1,0:T(2,128)S(1)}, u32[]{:S(2)}, u32[]{:S(2)}) collective-permute-start(f32[2,2,8]{2,1,0:T(2,128)S(1)} %get-tuple-element.38), channel_id=1, source_target_pairs={{0,12},{4,8},{8,4},{12,0},{16,28},{20,24},{24,20},{28,16},{1,13},{... | collective-permute-start | bytes 392 | tf_op jit(solution)/shard_map/ppermute | solution.py:193
  31.2 3.6 %collective-permute-start.8 = (f32[2,2,8]{2,1,0:T(2,128)S(1)}, f32[2,2,8]{2,1,0:T(2,128)S(1)}, u32[]{:S(2)}, u32[]{:S(2)}) collective-permute-start(f32[2,2,8]{2,1,0:T(2,128)S(1)} %get-tuple-element.39), channel_id=1, source_target_pairs={{0,8},{4,12},{8,0},{12,4},{16,24},{20,28},{24,16},{28,20},{1,9},{5... | collective-permute-start | bytes 392 | tf_op jit(solution)/shard_map/ppermute | solution.py:193
  31.7 3.6 %collective-permute-start.7 = (f32[2,2,8]{2,1,0:T(2,128)S(1)}, f32[2,2,8]{2,1,0:T(2,128)S(1)}, u32[]{:S(2)}, u32[]{:S(2)}) collective-permute-start(f32[2,2,8]{2,1,0:T(2,128)S(1)} %get-tuple-element.40), channel_id=1, source_target_pairs={{0,4},{4,0},{8,12},{12,8},{16,20},{20,16},{24,28},{28,24},{1,5},{5... | collective-permute-start | bytes 392 | tf_op jit(solution)/shard_map/ppermute | solution.py:193
